TPU v7x, 32 devices: a whole 2x2x4 slice. The times are simulated.
32 devices in a mesh: groups: 2 (over y), expert: 4 (over x, core), head: 4 (over z).
Axes of the slice: x: 2, y: 2, z: 4, core: 2. Of those that a mesh axis runs over, the one named last changes fastest.
Arguments:
- hidden_in: bfloat16 [512, 2048], P(('groups', 'expert', 'head')), parts along dimension 0, may hold values from -6 to 6
- out_grad: bfloat16 [512, 2048], P(('groups', 'expert', 'head')), parts along dimension 0, may hold values from -6 to 6
- loss_mask: int32 [512], P(('groups', 'expert', 'head')), parts along dimension 0, may hold values 0 or 1
- expert_ids: int32 [512, 8], P(('groups', 'expert', 'head')), parts along dimension 0, may hold values from 0 to 15, all different within a row; in each aligned block of 16 rows (0 to 15, 16 to 31, ...) at most 11 rows name the same one
- gate_weights: float32 [512, 8], P(('groups', 'expert', 'head')), parts along dimension 0, may hold values from 0.02 to 0.3
- cache_lengths: int32 [32], P(('groups', 'expert')), parts along dimension 0, may hold values from 1 to 32, as said below
- key_cache: bfloat16 [32, 32, 256], P(('groups', 'expert')), parts along dimension 0, may hold values from -94 to 94
- prefix_value_cache: bfloat16 [32, 32, 256], P(('groups', 'expert')), parts along dimension 0, may hold values from -6 to 6
- attn_gain: float32 [2048], replicated, may hold values from 0.1 to 1.9
- moe_gain: float32 [2048], replicated, may hold values from 0.1 to 1.9
- w_query: bfloat16 [2048, 2048], P(None, 'head'), may hold values from -0.125 to 0.125
- key_value_weight: bfloat16 [2048, 512], P(None, 'head'), may hold values from -0.125 to 0.125
- w_output: bfloat16 [2048, 2048], P('head'), may hold values from -0.125 to 0.125
- w_gate: bfloat16 [16, 2048, 768], P(('expert', 'head')), may hold values from -0.125 to 0.125
- w_up: bfloat16 [16, 2048, 768], P(('expert', 'head')), may hold values from -0.125 to 0.125
- w_down: bfloat16 [16, 768, 2048], P(('expert', 'head')), may hold values from -0.21875 to 0.21875
Outputs:
- layer_out: bfloat16 [512, 2048], P(('groups', 'expert', 'head')), parts along dimension 0
- input_grad: bfloat16 [512, 2048], P(('groups', 'expert', 'head')), parts along dimension 0
There are 2 independent parts, one for each index of `groups`. A program takes and returns all parts, laid end to end along the dimension named above; an argument that names none is the same for every part. Nothing has to cross between parts.
Inputs may be any that keep to these rules, and one draw needn't show every extreme that they name: `expert_ids`: each row names 8 different experts. Among the rows of one device no expert is named more than 11 times, and in every draw some expert is named exactly 11 times by the rows of some device. `cache_lengths`: some sequence uses all 32 positions.
All inputs are finite; a program needn't handle non-finite values. No bound on the sum of `loss_mask` on one device may be relied on, other than what follows from the above.
Results may differ from a plain program's by a relative error of at most 0.03.
Values may be sent and summed in bfloat16 or wider, within the bound.
No kernel may reach another device: no remote copies, remote signals or barrier semaphores. Data moves between devices by JAX's collectives and lax.ppermute only.
A program may use at most 64 MiB of HBM per device.

v0:
```python
import jax
import jax.numpy as jnp
from jax import lax
from jax.sharding import PartitionSpec as P

QUERY_HEADS = 16
KEY_VALUE_HEADS = 2
HEAD_SIZE = 128
TOP = 8
BLOCK = 16
PREFIX_SLOTS = 32


EPS = 1e-06
NEG_FILL = -1e30


def rms_forward(row_block, gain_vec):
    values = row_block.astype(jnp.float32)
    inverse = lax.rsqrt(jnp.mean(values * values, axis=-1, keepdims=True) + EPS)
    return (values * inverse * gain_vec, inverse)


def rms_backward(row_block, gain_vec, inverse, upstream):
    scaled_rows = row_block.astype(jnp.float32) * inverse
    weighted = upstream * gain_vec
    inner_mean = jnp.mean(weighted * scaled_rows, axis=-1, keepdims=True)
    return inverse * (weighted - scaled_rows * inner_mean)


def attend_forward(queries, key_rows, value_rows, usable):
    factor = queries.shape[-1] ** (-0.5)
    scores = (
        jnp.einsum("sbhd,skd->shbk", queries.astype(jnp.float32), key_rows.astype(jnp.float32))
        * factor
    )
    scores = jnp.where(usable[:, None, None, :], scores, NEG_FILL)
    highest = jnp.max(scores, axis=-1, keepdims=True)
    exponent_terms = jnp.exp(scores - highest)
    probabilities = exponent_terms / jnp.sum(exponent_terms, axis=-1, keepdims=True)
    probs_low = probabilities.astype(jnp.bfloat16)
    attended = jnp.einsum(
        "shbk,skd->sbhd", probs_low.astype(jnp.float32), value_rows.astype(jnp.float32)
    )
    return (probabilities, probs_low, attended.astype(jnp.bfloat16))


def attend_backward(queries, key_rows, value_rows, probabilities, probs_low, grad_attended):
    factor = queries.shape[-1] ** (-0.5)
    grad_probs = jnp.einsum(
        "sbhd,skd->shbk", grad_attended.astype(jnp.float32), value_rows.astype(jnp.float32)
    )
    inner_sum = jnp.sum(probabilities * grad_probs, axis=-1, keepdims=True)
    grad_scores = (probabilities * (grad_probs - inner_sum) * factor).astype(jnp.bfloat16)
    grad_queries = jnp.einsum(
        "shbk,skd->sbhd", grad_scores.astype(jnp.float32), key_rows.astype(jnp.float32)
    )
    grad_keys = jnp.einsum(
        "shbk,sbhd->skd", grad_scores.astype(jnp.float32), queries.astype(jnp.float32)
    )
    grad_values = jnp.einsum(
        "shbk,sbhd->skd", probs_low.astype(jnp.float32), grad_attended.astype(jnp.float32)
    )
    return (grad_queries.astype(jnp.bfloat16), grad_keys, grad_values)


def attention_forward(
    row_block, query_weights, kv_weights, key_cache, prefix_value_cache, lengths, first_head
):
    heads_here = query_weights.shape[1] // HEAD_SIZE
    query_group_count = QUERY_HEADS // KEY_VALUE_HEADS
    row_count = row_block.shape[0]
    seq_count = row_count // BLOCK
    key_value_width = KEY_VALUE_HEADS * HEAD_SIZE
    kv_first = first_head // query_group_count
    queries = jnp.dot(row_block, query_weights, preferred_element_type=jnp.float32).astype(
        jnp.bfloat16
    )
    queries = queries.reshape(seq_count, BLOCK, heads_here, HEAD_SIZE)
    usable = jnp.concatenate(
        [
            jnp.arange(PREFIX_SLOTS)[None, :] < lengths[:, None],
            jnp.ones((seq_count, BLOCK), dtype=jnp.bool_),
        ],
        axis=1,
    )
    kv_now = kv_first + 0
    pair_weights = jnp.concatenate(
        [
            lax.dynamic_slice_in_dim(kv_weights, kv_now * HEAD_SIZE, HEAD_SIZE, 1),
            lax.dynamic_slice_in_dim(
                kv_weights, key_value_width + kv_now * HEAD_SIZE, HEAD_SIZE, 1
            ),
        ],
        axis=1,
    )
    pair_rows = jnp.dot(row_block, pair_weights, preferred_element_type=jnp.float32).astype(
        jnp.bfloat16
    )
    key_rows = jnp.concatenate(
        [
            lax.dynamic_slice_in_dim(key_cache, kv_now * HEAD_SIZE, HEAD_SIZE, 2),
            pair_rows[:, :HEAD_SIZE].reshape(seq_count, BLOCK, HEAD_SIZE),
        ],
        axis=1,
    )
    value_rows = jnp.concatenate(
        [
            lax.dynamic_slice_in_dim(prefix_value_cache, kv_now * HEAD_SIZE, HEAD_SIZE, 2),
            pair_rows[:, HEAD_SIZE:].reshape(seq_count, BLOCK, HEAD_SIZE),
        ],
        axis=1,
    )
    probabilities, probs_low, attended = attend_forward(queries, key_rows, value_rows, usable)
    saved = [(queries, key_rows, value_rows, probabilities, probs_low, pair_weights)]
    joined = attended.reshape(row_count, heads_here * HEAD_SIZE)
    return (joined, saved)


def attention_backward(grad_rows, query_weights, output_weights, saved):
    heads_here = query_weights.shape[1] // HEAD_SIZE
    row_count = grad_rows.shape[0]
    seq_count = row_count // BLOCK
    grad_attn = jnp.einsum(
        "td,fd->tf", grad_rows, output_weights, preferred_element_type=jnp.float32
    ).astype(jnp.bfloat16)
    grad_attn = grad_attn.reshape(seq_count, BLOCK, heads_here, HEAD_SIZE)
    query_part, key_rows, value_rows, probabilities, probs_low, pair_weights = saved[0]
    grad_queries, grad_keys, grad_values = attend_backward(
        query_part, key_rows, value_rows, probabilities, probs_low, grad_attn
    )
    block_grads = jnp.concatenate(
        [
            grad_keys[:, PREFIX_SLOTS:].reshape(row_count, HEAD_SIZE),
            grad_values[:, PREFIX_SLOTS:].reshape(row_count, HEAD_SIZE),
        ],
        axis=1,
    )
    running = jnp.einsum(
        "tc,dc->td", block_grads, pair_weights.astype(jnp.float32), precision=lax.Precision.HIGHEST
    )
    query_flat = grad_queries.reshape(row_count, heads_here * HEAD_SIZE)
    return running + jnp.einsum(
        "tf,df->td", query_flat, query_weights, preferred_element_type=jnp.float32
    )


def head_rows(row_block):
    return lax.all_gather(row_block, "head", axis=0, tiled=True)


def head_sums(partial_rows):
    return lax.psum_scatter(partial_rows, "head", scatter_dimension=0, tiled=True)


def to_experts(outgoing):
    return lax.all_to_all(outgoing, ("expert", "head"), split_axis=0, concat_axis=0, tiled=True)


def from_experts(results):
    return lax.all_to_all(results, ("expert", "head"), split_axis=0, concat_axis=0, tiled=True)


def body(
    hidden_in,
    out_grad,
    loss_mask,
    expert_ids,
    gate_weights,
    cache_lengths,
    key_cache,
    prefix_value_cache,
    attn_gain,
    moe_gain,
    w_query,
    key_value_weight,
    w_output,
    w_gate,
    w_up,
    w_down,
):
    highest_prec = lax.Precision.HIGHEST
    owned = hidden_in.shape[0]
    width = hidden_in.shape[1]
    normed_one, inverse_one = rms_forward(hidden_in, attn_gain)
    attn_rows = normed_one.astype(jnp.bfloat16)
    kv_full = lax.all_gather(key_value_weight, "head", axis=1, tiled=True)
    heads_here = w_query.shape[1] // HEAD_SIZE
    first_head = lax.axis_index("head") * heads_here
    gathered_rows = head_rows(attn_rows)
    attended, saved = attention_forward(
        gathered_rows, w_query, kv_full, key_cache, prefix_value_cache, cache_lengths, first_head
    )
    mixed = head_sums(jnp.dot(attended, w_output, preferred_element_type=jnp.float32))
    hidden = (hidden_in.astype(jnp.float32) + mixed).astype(jnp.bfloat16)
    normed_two, inverse_two = rms_forward(hidden, moe_gain)
    moe_rows = normed_two.astype(jnp.bfloat16)
    device_count = lax.axis_size("expert") * lax.axis_size("head")
    capacity = (owned * TOP * 4 + 3 * device_count - 1) // (3 * device_count)
    slot_total = device_count * capacity
    flat_ids = expert_ids.reshape(-1)
    one_hot = (flat_ids[:, None] == jnp.arange(device_count, dtype=jnp.int32)[None, :]).astype(
        jnp.int32
    )
    earlier = jnp.cumsum(one_hot, axis=0) - one_hot
    position = jnp.sum(earlier * one_hot, axis=1)
    target = flat_ids * capacity + position
    matched = (jnp.arange(slot_total, dtype=jnp.int32)[:, None] == target[None, :]).reshape(
        slot_total, owned, TOP
    )
    placement = jnp.any(matched, axis=2).astype(jnp.bfloat16)
    weighting = jnp.sum(jnp.where(matched, gate_weights[None, :, :], 0.0), axis=2)
    outgoing = jnp.dot(placement, moe_rows, preferred_element_type=jnp.float32).astype(jnp.bfloat16)
    arrived = to_experts(outgoing.reshape(device_count, capacity, width)).reshape(slot_total, width)
    gate_matrix = w_gate[0]
    up_matrix = w_up[0]
    down_matrix = w_down[0]
    gate_pre = jnp.dot(arrived, gate_matrix, preferred_element_type=jnp.float32)
    up_pre = jnp.dot(arrived, up_matrix, preferred_element_type=jnp.float32)
    sigma = jax.nn.sigmoid(gate_pre)
    activated = (gate_pre * sigma * up_pre).astype(jnp.bfloat16)
    result = jnp.dot(activated, down_matrix, preferred_element_type=jnp.float32).astype(
        jnp.bfloat16
    )
    returned = from_experts(result.reshape(device_count, capacity, width)).reshape(
        slot_total, width
    )
    moe_sum = jnp.einsum(
        "rt,rd->td", weighting, returned.astype(jnp.float32), precision=highest_prec
    )
    layer_out = (hidden.astype(jnp.float32) + moe_sum).astype(jnp.bfloat16)
    cotangent = out_grad.astype(jnp.float32) * loss_mask.astype(jnp.float32)[:, None]
    grad_out = jnp.einsum("rt,td->rd", weighting, cotangent, precision=highest_prec).astype(
        jnp.bfloat16
    )
    grad_arrived = to_experts(grad_out.reshape(device_count, capacity, width)).reshape(
        slot_total, width
    )
    grad_act = jnp.einsum(
        "rd,fd->rf", grad_arrived, down_matrix, preferred_element_type=jnp.float32
    )
    grad_gate = (grad_act * up_pre * sigma * (1.0 + gate_pre * (1.0 - sigma))).astype(jnp.bfloat16)
    grad_up = (grad_act * gate_pre * sigma).astype(jnp.bfloat16)
    grad_back = jnp.einsum("rf,df->rd", grad_gate, gate_matrix, preferred_element_type=jnp.float32)
    grad_back = grad_back + jnp.einsum(
        "rf,df->rd", grad_up, up_matrix, preferred_element_type=jnp.float32
    )
    grad_back = grad_back.astype(jnp.bfloat16)
    grad_home = from_experts(grad_back.reshape(device_count, capacity, width)).reshape(
        slot_total, width
    )
    grad_moe = jnp.einsum("rt,rd->td", placement, grad_home, preferred_element_type=jnp.float32)
    grad_hidden = cotangent + rms_backward(hidden, moe_gain, inverse_two, grad_moe)
    grad_low = grad_hidden.astype(jnp.bfloat16)
    grad_gathered = head_rows(grad_low)
    grad_attn_rows = head_sums(attention_backward(grad_gathered, w_query, w_output, saved))
    input_grad = (
        grad_hidden + rms_backward(hidden_in, attn_gain, inverse_one, grad_attn_rows)
    ).astype(jnp.bfloat16)
    return (layer_out, input_grad)


def solution(mesh):
    in_specs = (
        P(("groups", "expert", "head"), None),
        P(("groups", "expert", "head"), None),
        P(("groups", "expert", "head")),
        P(("groups", "expert", "head"), None),
        P(("groups", "expert", "head"), None),
        P(("groups", "expert")),
        P(("groups", "expert"), None, None),
        P(("groups", "expert"), None, None),
        P(),
        P(),
        P(None, "head"),
        P(None, "head"),
        P("head", None),
        P(("expert", "head"), None, None),
        P(("expert", "head"), None, None),
        P(("expert", "head"), None, None),
    )
    out_specs = (P(("groups", "expert", "head"), None), P(("groups", "expert", "head"), None))
    return jax.shard_map(body, mesh=mesh, in_specs=in_specs, out_specs=out_specs, check_vma=False)
```

profile of v0, /device:TPU:0, one launch (start us, length us, event | category | flops | bytes accessed | tf_op | source)
XLA Modules:
  0.0 268.9 jit_solution(15294634260866818193)
XLA Ops:
  8.0 1.1 fusion.59
  9.1 0.9 fusion.53
  10.1 16.6 %all_gather.9 = bf16[64,2048]{1,0:T(8,128)(2,1)S(1)} all-gather(bf16[16,2048]{1,0:T(8,128)(2,1)S(1)} %fusion.53), channel_id=1, replica_groups=mesh['groups'=2,'expert'=4,'head'=4] {'head'}, dimensions={0}, use_global_device_ids=true | all-gather | bytes 327680 | tf_op jit(solution)/shard_map/all_gather | solution.py:149
  26.6 2.1 convolution_convert_fusion.5
  30.2 1.4 constant_dynamic-slice_fusion
  32.3 28.9 %all-gather.2.cloned.1.call-done = bf16[2048,512]{1,0:T(8,128)(2,1)} async-done(((bf16[2048,128]{1,0:T(8,128)(2,1)}), bf16[2048,512]{1,0:T(8,128)(2,1)}) %all-gather.2.cloned.1.call-update) | async-done | bytes 2097168 | tf_op jit(solution)/shard_map/all_gather | solution.py:187
  61.3 1.3 constant_dynamic-slice_fusion.2
  63.6 1.1 fusion.110
  65.0 2.9 %fusion.66 = f32[64,2048]{1,0:T(8,128)} fusion(bf16[512,2048]{1,0:T(8,128)(2,1)} %param.28, bf16[8,8,4,128]{3,2,1,0:T(4,128)(2,1)S(1)} %bitcast.90), kind=kOutput, calls=%fused_computation.85 | convolution fusion | flops 134217728 | bytes 2686976 | tf_op jit(solution)/shard_map/dot_general | solution.py:194
  68.2 2.2 convolution_convert_fusion
  70.4 2.4 reshape.112
  72.8 4.3 %all-to-all-start.2 = ((bf16[16,11,2048]{2,1,0:T(8,128)(2,1)}), bf16[16,11,2048]{2,1,0:T(8,128)(2,1)}, u32[]{:S(2)}, u32[]{:S(2)}) async-start(bf16[16,11,2048]{2,1,0:T(8,128)(2,1)} %reshape.112), calls=%async_computation.3 | async-start | bytes 2097152 | tf_op jit(solution)/shard_map/all_to_all | solution.py:157
  77.2 11.2 %reduce-scatter.3.cloned.1.call-done = f32[16,2048]{1,0:T(8,128)} async-done(((f32[64,2048]{1,0:T(8,128)}), f32[16,2048]{1,0:T(8,128)}) %reduce-scatter.3.cloned.1.call-update) | async-done | bytes 131088 | tf_op jit(solution)/shard_map/reduce_scatter | solution.py:153
  88.4 1.0 fusion.61
  89.4 1.3 convolution_convert_fusion.1
  90.7 2.3 reshape.108
  93.0 13.5 %all-to-all-done.2 = bf16[16,11,2048]{2,1,0:T(8,128)(2,1)} async-done(((bf16[16,11,2048]{2,1,0:T(8,128)(2,1)}), bf16[16,11,2048]{2,1,0:T(8,128)(2,1)}, u32[]{:S(2)}, u32[]{:S(2)}) %all-to-all-start.2) | async-done | bytes 720928 | tf_op jit(solution)/shard_map/all_to_all | solution.py:157
  106.6 4.3 %all-to-all-start = ((bf16[16,11,2048]{2,1,0:T(8,128)(2,1)}), bf16[16,11,2048]{2,1,0:T(8,128)(2,1)}, u32[]{:S(2)}, u32[]{:S(2)}) async-start(bf16[16,11,2048]{2,1,0:T(8,128)(2,1)} %reshape.108), calls=%async_computation.1 | async-start | bytes 2097152 | tf_op jit(solution)/shard_map/all_to_all | solution.py:157
  110.9 2.4 reshape.113
  113.3 4.1 %fusion.2 = f32[176,768]{1,0:T(8,128)} fusion(bf16[176,2048]{1,0:T(8,128)(2,1)} %reshape.113, bf16[1,768,2048]{2,1,0:T(8,128)(2,1)} %param.31), kind=kOutput, calls=%fused_computation.2 | convolution fusion | flops 553648128 | bytes 4407296 | tf_op jit(solution)/shard_map/rd,fd->rf/dot_general | solution.py:239
  117.5 20.4 %all-to-all-done = bf16[16,11,2048]{2,1,0:T(8,128)(2,1)} async-done(((bf16[16,11,2048]{2,1,0:T(8,128)(2,1)}), bf16[16,11,2048]{2,1,0:T(8,128)(2,1)}, u32[]{:S(2)}, u32[]{:S(2)}) %all-to-all-start) | async-done | bytes 720928 | tf_op jit(solution)/shard_map/all_to_all | solution.py:157
  137.9 2.4 reshape.109
  140.3 2.9 %fusion.12 = f32[176,768]{1,0:T(8,128)S(1)} fusion(bf16[176,2048]{1,0:T(8,128)(2,1)} %reshape.109, bf16[1,2048,768]{2,1,0:T(8,128)(2,1)} %param.29), kind=kOutput, calls=%fused_computation.12 | convolution fusion | flops 553648128 | bytes 4407296 | tf_op jit(solution)/shard_map/dot_general | solution.py:218
  144.4 1.2 fusion.6
  145.7 0.9 copy-done.1
  146.5 2.0 fusion.20
  148.6 2.4 reshape.114
  150.9 4.3 %all-to-all-start.3 = ((bf16[16,11,2048]{2,1,0:T(8,128)(2,1)}), bf16[16,11,2048]{2,1,0:T(8,128)(2,1)}, u32[]{:S(2)}, u32[]{:S(2)}) async-start(bf16[16,11,2048]{2,1,0:T(8,128)(2,1)} %reshape.114), calls=%async_computation.4 | async-start | bytes 2097152 | tf_op jit(solution)/shard_map/all_to_all | solution.py:161
  155.3 3.9 %fusion.17 = bf16[176,2048]{1,0:T(8,128)(2,1)} fusion(bf16[1,768,2048]{2,1,0:T(8,128)(2,1)} %param.31, f32[176,768]{1,0:T(8,128)} %copy-done.5, f32[176,768]{1,0:T(8,128)} %copy-done.4), kind=kOutput, calls=%fused_computation.15 | convolution fusion | flops 554819584 | bytes 4947968 | tf_op jit(solution)/shard_map/dot_general | solution.py:222
  159.1 2.3 reshape.110
  161.5 20.7 %all-to-all-done.3 = bf16[16,11,2048]{2,1,0:T(8,128)(2,1)} async-done(((bf16[16,11,2048]{2,1,0:T(8,128)(2,1)}), bf16[16,11,2048]{2,1,0:T(8,128)(2,1)}, u32[]{:S(2)}, u32[]{:S(2)}) %all-to-all-start.3) | async-done | bytes 720928 | tf_op jit(solution)/shard_map/all_to_all | solution.py:161
  182.2 4.3 %all-to-all-start.1 = ((bf16[16,11,2048]{2,1,0:T(8,128)(2,1)}), bf16[16,11,2048]{2,1,0:T(8,128)(2,1)}, u32[]{:S(2)}, u32[]{:S(2)}) async-start(bf16[16,11,2048]{2,1,0:T(8,128)(2,1)} %reshape.110), calls=%async_computation.2 | async-start | bytes 2097152 | tf_op jit(solution)/shard_map/all_to_all | solution.py:161
  186.6 2.4 reshape.115
  189.0 1.4 fusion.49
  190.9 29.2 %all_gather.11 = bf16[64,2048]{1,0:T(8,128)(2,1)S(1)} all-gather(bf16[16,2048]{1,0:T(8,128)(2,1)S(1)} %fusion.107), channel_id=1, replica_groups=mesh['groups'=2,'expert'=4,'head'=4] {'head'}, dimensions={0}, use_global_device_ids=true | all-gather | bytes 327680 | tf_op jit(solution)/shard_map/all_gather | solution.py:149
  220.2 2.3 convolution_convert_fusion.3
  223.2 1.7 convolution_bitcast_fusion
  224.9 2.9 %fusion.33 = bf16[4,16,4,128]{3,1,2,0:T(8,128)(2,1)} fusion(f32[4,4,16,48]{3,2,1,0:T(8,128)} %convolution_bitcast_fusion, bf16[4,16,128]{2,1,0:T(8,128)(2,1)} %bitcast.96, bf16[4,32,128]{2,1,0:T(8,128)(2,1)} %constant_dynamic-slice_fusion, f32[4,4,16,48]{3,2,1,0:T(8,128)} %copy-done.30, f32[4,4,16]{2,1,0:T(4,128)} %copy-done.31), kind=kOutput, calls=%fused_computation.40 | convolution fusion | flops 3363119 | bytes 214016 | tf_op jit(solution)/shard_map/shbk,skd->sbhd/dot_general | solution.py:55
  227.8 3.0 %convolution_bitcast_fusion.2 = f32[4,48,128]{2,1,0:T(8,128)} fusion(f32[4,4,16,48]{3,2,1,0:T(8,128)} %convolution_bitcast_fusion, bf16[4,16,4,128]{3,2,1,0:T(4,128)(2,1)} %reshape.106, f32[4,4,16,48]{3,2,1,0:T(8,128)} %copy-done.30, f32[4,4,16]{2,1,0:T(4,128)} %copy-done.31), kind=kOutput, calls=%fused_computation.35 | convolution fusion | flops 3232047 | bytes 263168 | tf_op jit(solution)/shard_map/shbk,sbhd->skd/dot_general | solution.py:58
  230.8 1.0 copy.42
  232.6 1.2 convolution_bitcast_fusion.1
  233.8 2.3 fusion.34
  236.0 1.5 convolution_add_fusion
  237.7 2.4 reshape.111
  240.0 2.1 fusion.23
  242.2 17.4 %reduce-scatter.5.cloned.1.call-done = f32[16,2048]{1,0:T(8,128)} async-done(((f32[64,2048]{1,0:T(8,128)}), f32[16,2048]{1,0:T(8,128)}) %reduce-scatter.5.cloned.1.call-update) | async-done | bytes 131088 | tf_op jit(solution)/shard_map/reduce_scatter | solution.py:153
  259.6 1.1 fusion.54
  260.7 1.7 fusion.58
  (98 shorter events, 7.8 us)
Async XLA Ops:
  7.2 136.0 %copy-start = (bf16[1,2048,768]{2,1,0:T(8,128)(2,1)S(1)}, bf16[1,2048,768]{2,1,0:T(8,128)(2,1)}, u32[]{:S(2)}) copy-start(bf16[1,2048,768]{2,1,0:T(8,128)(2,1)} %param.30) | copy-start | bytes 9437188
  7.2 22.2 %copy-start.24 = (s32[16,8]{0,1:T(8,128)S(1)}, s32[16,8]{0,1:T(8,128)}, u32[]{:S(2)}) copy-start(s32[16,8]{0,1:T(8,128)} %param.19) | copy-start | bytes 1540
  7.2 22.9 %copy-start.28 = (s32[4]{0:T(128)S(1)}, s32[4]{0:T(128)}, u32[]{:S(2)}) copy-start(s32[4]{0:T(128)} %param.21) | copy-start | bytes 52
  7.2 54.1 %all-gather.2.cloned.1.call-start = ((), (), s32[]{:S(2)}) async-start(), calls=%async_computation.6 | async-start | bytes 2621440 | tf_op jit(solution)/shard_map/all_gather | solution.py:187
  7.9 80.4 %reduce-scatter.3.cloned.1.call-start = ((), (), s32[]{:S(2)}) async-start(), calls=%async_computation.7 | async-start | bytes 655360 | tf_op jit(solution)/shard_map/reduce_scatter | solution.py:153
  9.1 0.9 copy-start.20
  30.2 33.4 %copy-start.14 = (bf16[4,16,4,128]{3,2,1,0:T(4,128)(2,1)S(1)}, bf16[4,16,4,128]{3,2,1,0:T(4,128)(2,1)}, u32[]{:S(2)}) copy-start(bf16[4,16,4,128]{3,2,1,0:T(4,128)(2,1)} %reshape.106) | copy-start | bytes 196612
  32.3 32.4 %copy-start.12 = (bf16[4,32,128]{2,1,0:T(8,128)(2,1)}, bf16[4,32,128]{2,1,0:T(8,128)(2,1)S(1)}, u32[]{:S(2)}) copy-start(bf16[4,32,128]{2,1,0:T(8,128)(2,1)S(1)} %constant_dynamic-slice_fusion.3) | copy-start | bytes 98308
  62.6 0.8 copy-start.9
  62.6 1.0 copy-start.10
  63.5 4.3 %copy-start.17 = (bf16[64,128]{1,0:T(8,128)(2,1)}, bf16[64,128]{1,0:T(8,128)(2,1)S(1)}, u32[]{:S(2)}) copy-start(bf16[64,128]{1,0:T(8,128)(2,1)S(1)} %get-tuple-element.6) | copy-start | bytes 49156
  63.5 4.4 %copy-start.15 = (bf16[64,128]{1,0:T(8,128)(2,1)}, bf16[64,128]{1,0:T(8,128)(2,1)S(1)}, u32[]{:S(2)}) copy-start(bf16[64,128]{1,0:T(8,128)(2,1)S(1)} %get-tuple-element.7) | copy-start | bytes 49156
  63.5 4.4 %copy-start.25 = (f32[16,8]{0,1:T(8,128)S(1)}, f32[16,8]{0,1:T(8,128)}, u32[]{:S(2)}) copy-start(f32[16,8]{0,1:T(8,128)} %param.20) | copy-start | bytes 1540
  63.5 4.5 %copy-start.29 = (s32[16]{0:T(128)S(1)}, s32[16]{0:T(128)}, u32[]{:S(2)}) copy-start(s32[16]{0:T(128)} %param.18) | copy-start | bytes 196
  64.7 3.5 %copy-start.30 = (f32[4,4,16,48]{3,2,1,0:T(8,128)}, f32[4,4,16,48]{3,2,1,0:T(8,128)S(1)}, u32[]{:S(2)}) copy-start(f32[4,4,16,48]{3,2,1,0:T(8,128)S(1)} %get-tuple-element.9) | copy-start | bytes 147460
  64.7 5.7 %copy-start.31 = (f32[4,4,16]{2,1,0:T(4,128)}, f32[4,4,16]{2,1,0:T(4,128)S(1)}, u32[]{:S(2)}) copy-start(f32[4,4,16]{2,1,0:T(4,128)S(1)} %get-tuple-element.8) | copy-start | bytes 3076
  64.7 3.5 %copy-start.8 = (bf16[16,2048]{1,0:T(8,128)(2,1)S(1)}, bf16[16,2048]{1,0:T(8,128)(2,1)}, u32[]{:S(2)}) copy-start(bf16[16,2048]{1,0:T(8,128)(2,1)} %param.17) | copy-start | bytes 196612
  68.0 122.4 %copy-start.22 = (f32[16]{0:T(128)}, f32[16]{0:T(128)S(1)}, u32[]{:S(2)}) copy-start(f32[16]{0:T(128)S(1)} %convert_element_type.116) | copy-start | bytes 196
  70.4 18.0 %copy-start.7 = (bf16[16,2048]{1,0:T(8,128)(2,1)S(1)}, bf16[16,2048]{1,0:T(8,128)(2,1)}, u32[]{:S(2)}) copy-start(bf16[16,2048]{1,0:T(8,128)(2,1)} %param.16) | copy-start | bytes 196612
  70.4 19.1 %copy-start.16 = (f32[2048]{0:T(1024)S(1)}, f32[2048]{0:T(1024)}, u32[]{:S(2)}) copy-start(f32[2048]{0:T(1024)} %param.25) | copy-start | bytes 24580
  72.8 33.8 %all-to-all-start.2 = ((bf16[16,11,2048]{2,1,0:T(8,128)(2,1)}), bf16[16,11,2048]{2,1,0:T(8,128)(2,1)}, u32[]{:S(2)}, u32[]{:S(2)}) async-start(bf16[16,11,2048]{2,1,0:T(8,128)(2,1)} %reshape.112), calls=%async_computation.3 | async-start | bytes 2097152 | tf_op jit(solution)/shard_map/all_to_all | solution.py:157
  89.4 101.0 %copy-start.18 = (f32[16]{0:T(128)}, f32[16]{0:T(128)S(1)}, u32[]{:S(2)}) copy-start(f32[16]{0:T(128)S(1)} %add_rsqrt_fusion) | copy-start | bytes 196
  106.6 31.3 %all-to-all-start = ((bf16[16,11,2048]{2,1,0:T(8,128)(2,1)}), bf16[16,11,2048]{2,1,0:T(8,128)(2,1)}, u32[]{:S(2)}, u32[]{:S(2)}) async-start(bf16[16,11,2048]{2,1,0:T(8,128)(2,1)} %reshape.108), calls=%async_computation.1 | async-start | bytes 2097152 | tf_op jit(solution)/shard_map/all_to_all | solution.py:157
  140.3 2.9 %copy-start.3 = (bf16[176,2048]{1,0:T(8,128)(2,1)S(1)}, bf16[176,2048]{1,0:T(8,128)(2,1)}, u32[]{:S(2)}) copy-start(bf16[176,2048]{1,0:T(8,128)(2,1)} %reshape.109) | copy-start | bytes 2162692
  143.2 2.4 copy-start.4
  143.2 1.2 copy-start.6
  144.4 1.2 copy-start.5
  144.4 2.1 copy-start.1
  150.9 31.3 %all-to-all-start.3 = ((bf16[16,11,2048]{2,1,0:T(8,128)(2,1)}), bf16[16,11,2048]{2,1,0:T(8,128)(2,1)}, u32[]{:S(2)}, u32[]{:S(2)}) async-start(bf16[16,11,2048]{2,1,0:T(8,128)(2,1)} %reshape.114), calls=%async_computation.4 | async-start | bytes 2097152 | tf_op jit(solution)/shard_map/all_to_all | solution.py:161
  182.2 55.4 %all-to-all-start.1 = ((bf16[16,11,2048]{2,1,0:T(8,128)(2,1)}), bf16[16,11,2048]{2,1,0:T(8,128)(2,1)}, u32[]{:S(2)}, u32[]{:S(2)}) async-start(bf16[16,11,2048]{2,1,0:T(8,128)(2,1)} %reshape.110), calls=%async_computation.2 | async-start | bytes 2097152 | tf_op jit(solution)/shard_map/all_to_all | solution.py:161
  186.6 73.0 %reduce-scatter.5.cloned.1.call-start = ((), (), s32[]{:S(2)}) async-start(), calls=%async_computation.8 | async-start | bytes 655360 | tf_op jit(solution)/shard_map/reduce_scatter | solution.py:153
  190.4 0.5 copy-start.26
  223.2 9.4 %copy-start.11 = (bf16[4,16,4,128]{3,2,1,0:T(4,128)(2,1)S(1)}, bf16[4,16,4,128]{3,2,1,0:T(4,128)(2,1)}, u32[]{:S(2)}) copy-start(bf16[4,16,4,128]{3,2,1,0:T(4,128)(2,1)} %reshape.116) | copy-start | bytes 196612
  230.8 5.3 %copy-start.2 = (bf16[2048,512]{1,0:T(8,128)(2,1)S(1)}, bf16[2048,512]{1,0:T(8,128)(2,1)}, u32[]{:S(2)}) copy-start(bf16[2048,512]{1,0:T(8,128)(2,1)} %param.26) | copy-start | bytes 6291460
  237.6 22.0 %copy-start.13 = (f32[2048]{0:T(1024)S(1)}, f32[2048]{0:T(1024)}, u32[]{:S(2)}) copy-start(f32[2048]{0:T(1024)} %param.24) | copy-start | bytes 24580
  237.6 22.0 %copy-start.21 = (f32[16]{0:T(128)S(1)}, f32[16]{0:T(128)}, u32[]{:S(2)}) copy-start(f32[16]{0:T(128)} %copy-done.20) | copy-start | bytes 196
  237.6 23.1 %copy-start.19 = (f32[16]{0:T(128)S(1)}, f32[16]{0:T(128)}, u32[]{:S(2)}) copy-start(f32[16]{0:T(128)} %copy-done.18) | copy-start | bytes 196
  237.6 23.1 %copy-start.23 = (f32[16]{0:T(128)S(1)}, f32[16]{0:T(128)}, u32[]{:S(2)}) copy-start(f32[16]{0:T(128)} %copy-done.22) | copy-start | bytes 196
  237.6 23.1 %copy-start.27 = (f32[16]{0:T(128)S(1)}, f32[16]{0:T(128)}, u32[]{:S(2)}) copy-start(f32[16]{0:T(128)} %copy-done.26) | copy-start | bytes 196
Sparse Core Ops, SparseCore 0:
  9.6 51.6 all-gather.1
  68.0 20.3 reduce-scatter.2
  237.8 21.7 reduce-scatter.4
where the time goes:
time: 270 us; the launch traced here: 269 us
  waiting for transfers between devices  113 us (42%)
  blocking collectives  45.8 us (17%)
  matrix products  43.4 us (16%)
  local copies, waits for them, and re-layouts  28.3 us (10%)
  starting transfers between devices  17.5 us (6%)
  between operations  14.2 us (5%)
  other arithmetic  6.73 us (2%)
    all_gather x2, blocking collectives, head_rows(): return lax.all_gather(row_block, 'head', axis=0, tiled=True)  45.8 us
    all_to_all x2, waiting for transfers between devices, to_experts(): lax.all_to_all(outgoing, ('expert', 'head'), split_axis=0, concat_axis=0,...  34 us
    all_gather x1, waiting for transfers between devices, body(): kv_full = lax.all_gather(key_value_weight, 'head', axis=1, tiled=True)  28.9 us
    reduce_scatter x2, waiting for transfers between devices, head_sums(): lax.psum_scatter(partial_rows, 'head', scatter_dimension=0, tiled=True)  28.6 us
    all_to_all x2, waiting for transfers between devices, from_experts(): lax.all_to_all(results, ('expert', 'head'), split_axis=0, concat_axis=0,...  20.7 us
    all_to_all x2, starting transfers between devices, to_experts(): lax.all_to_all(outgoing, ('expert', 'head'), split_axis=0, concat_axis=0,...  8.67 us
    all_to_all x2, starting transfers between devices, from_experts(): lax.all_to_all(results, ('expert', 'head'), split_axis=0, concat_axis=0,...  8.66 us
  transfers between devices with their start and end apart: 7, of which 6 were waited for; matrix products, arithmetic and copies ran while one was open for 21% of the time, Pallas kernels for 0%

commit v1 on v0

--- a/solution.py
+++ b/solution.py
@@ -206,50 +206,53 @@
     position = jnp.sum(earlier * one_hot, axis=1)
     target = flat_ids * capacity + position
     matched = (jnp.arange(slot_total, dtype=jnp.int32)[:, None] == target[None, :]).reshape(
-        slot_total, owned, TOP
-    )
-    placement = jnp.any(matched, axis=2).astype(jnp.bfloat16)
-    weighting = jnp.sum(jnp.where(matched, gate_weights[None, :, :], 0.0), axis=2)
-    outgoing = jnp.dot(placement, moe_rows, preferred_element_type=jnp.float32).astype(jnp.bfloat16)
-    arrived = to_experts(outgoing.reshape(device_count, capacity, width)).reshape(slot_total, width)
+        device_count, capacity, owned, TOP
+    )
+    placement = jnp.any(matched, axis=3).astype(jnp.bfloat16)
+    weighting = jnp.sum(jnp.where(matched, gate_weights[None, None, :, :], 0.0), axis=3)
+    cotangent = out_grad.astype(jnp.float32) * loss_mask.astype(jnp.float32)[:, None]
+    outgoing = jnp.einsum(
+        "dct,tw->dcw", placement, moe_rows, preferred_element_type=jnp.float32
+    ).astype(jnp.bfloat16)
+    grad_out = jnp.einsum(
+        "dct,tw->dcw", weighting, cotangent, precision=highest_prec
+    ).astype(jnp.bfloat16)
+    arrived = to_experts(jnp.concatenate([outgoing, grad_out], axis=2))
+    rows_in = arrived[:, :, :width]
+    grads_in = arrived[:, :, width:]
     gate_matrix = w_gate[0]
     up_matrix = w_up[0]
     down_matrix = w_down[0]
-    gate_pre = jnp.dot(arrived, gate_matrix, preferred_element_type=jnp.float32)
-    up_pre = jnp.dot(arrived, up_matrix, preferred_element_type=jnp.float32)
+    gate_pre = jnp.einsum("scw,wf->scf", rows_in, gate_matrix, preferred_element_type=jnp.float32)
+    up_pre = jnp.einsum("scw,wf->scf", rows_in, up_matrix, preferred_element_type=jnp.float32)
     sigma = jax.nn.sigmoid(gate_pre)
     activated = (gate_pre * sigma * up_pre).astype(jnp.bfloat16)
-    result = jnp.dot(activated, down_matrix, preferred_element_type=jnp.float32).astype(
-        jnp.bfloat16
-    )
-    returned = from_experts(result.reshape(device_count, capacity, width)).reshape(
-        slot_total, width
-    )
-    moe_sum = jnp.einsum(
-        "rt,rd->td", weighting, returned.astype(jnp.float32), precision=highest_prec
-    )
-    layer_out = (hidden.astype(jnp.float32) + moe_sum).astype(jnp.bfloat16)
-    cotangent = out_grad.astype(jnp.float32) * loss_mask.astype(jnp.float32)[:, None]
-    grad_out = jnp.einsum("rt,td->rd", weighting, cotangent, precision=highest_prec).astype(
-        jnp.bfloat16
-    )
-    grad_arrived = to_experts(grad_out.reshape(device_count, capacity, width)).reshape(
-        slot_total, width
-    )
+    result = jnp.einsum(
+        "scf,fw->scw", activated, down_matrix, preferred_element_type=jnp.float32
+    ).astype(jnp.bfloat16)
     grad_act = jnp.einsum(
-        "rd,fd->rf", grad_arrived, down_matrix, preferred_element_type=jnp.float32
+        "scw,fw->scf", grads_in, down_matrix, preferred_element_type=jnp.float32
     )
     grad_gate = (grad_act * up_pre * sigma * (1.0 + gate_pre * (1.0 - sigma))).astype(jnp.bfloat16)
     grad_up = (grad_act * gate_pre * sigma).astype(jnp.bfloat16)
-    grad_back = jnp.einsum("rf,df->rd", grad_gate, gate_matrix, preferred_element_type=jnp.float32)
+    grad_back = jnp.einsum(
+        "scf,wf->scw", grad_gate, gate_matrix, preferred_element_type=jnp.float32
+    )
     grad_back = grad_back + jnp.einsum(
-        "rf,df->rd", grad_up, up_matrix, preferred_element_type=jnp.float32
+        "scf,wf->scw", grad_up, up_matrix, preferred_element_type=jnp.float32
     )
     grad_back = grad_back.astype(jnp.bfloat16)
-    grad_home = from_experts(grad_back.reshape(device_count, capacity, width)).reshape(
-        slot_total, width
-    )
-    grad_moe = jnp.einsum("rt,rd->td", placement, grad_home, preferred_element_type=jnp.float32)
+    returned = from_experts(jnp.concatenate([result, grad_back], axis=2))
+    moe_sum = jnp.einsum(
+        "dct,dcw->tw",
+        weighting,
+        returned[:, :, :width].astype(jnp.float32),
+        precision=highest_prec,
+    )
+    layer_out = (hidden.astype(jnp.float32) + moe_sum).astype(jnp.bfloat16)
+    grad_moe = jnp.einsum(
+        "dct,dcw->tw", placement, returned[:, :, width:], preferred_element_type=jnp.float32
+    )
     grad_hidden = cotangent + rms_backward(hidden, moe_gain, inverse_two, grad_moe)
     grad_low = grad_hidden.astype(jnp.bfloat16)
     grad_gathered = head_rows(grad_low)

time: 270 us -> 276 us (1.022)
  blocking collectives: 45.8 us -> 136 us
  waiting for transfers between devices: 113 us -> 61.4 us
  starting transfers between devices: 17.5 us -> 0.12 us
  local copies, waits for them, and re-layouts: 28.3 us -> 15.7 us
  matrix products: 43.4 us -> 37.5 us
    all_to_all x0 -> x2, blocking collectives: none -> 105 us  [the longest x1 52.7 us: from_experts(): lax.all_to_all(results, ('expert', 'head'), split_axis=0, concat_axis=0,...]
    all_to_all x4 -> x0, waiting for transfers between devices: 54.7 us -> none  [the longest x2 34 us: to_experts(): lax.all_to_all(outgoing, ('expert', 'head'), split_axis=0, concat_axis=0,...]
    reshape x8 -> x0, local copies, waits for them, and re-layouts: 18.9 us -> none  [the longest x1 2.39 us: body(): grad_out.reshape(device_count, capacity, width)]
    all_to_all x4 -> x0, starting transfers between devices: 17.3 us -> none  [the longest x2 8.67 us: to_experts(): lax.all_to_all(outgoing, ('expert', 'head'), split_axis=0, concat_axis=0,...]
    all_gather x2, blocking collectives: 45.8 us -> 31.4 us  [head_rows(): return lax.all_gather(row_block, 'head', axis=0, tiled=True)]
    dot_general x10, matrix products: 21.9 us -> 13.3 us  [the longest x1 2.43 us: body(): jnp.einsum('dct,dcw->tw', weighting, returned[:, :, :width].astype(jnp.fl...]
    reduce_scatter x2, waiting for transfers between devices: 28.6 us -> 33.2 us  [head_sums(): lax.psum_scatter(partial_rows, 'head', scatter_dimension=0, tiled=True)]
    unnamed x66 -> x63, local copies, waits for them, and re-layouts: 2.68 us -> 5.77 us
  transfers between devices with their start and end apart: 7 -> 3, of which waited for: 6 -> 3; matrix products, arithmetic and copies ran while one was open for 21% -> 5% of each run, Pallas kernels for 0% -> 0%
where the time goes in v1:
time: 276 us; the launch traced here: 274 us
  blocking collectives  136 us (49%)
  waiting for transfers between devices  61.4 us (22%)
  matrix products  37.5 us (14%)
  local copies, waits for them, and re-layouts  15.7 us (6%)
  between operations  14.2 us (5%)
  other arithmetic  9.03 us (3%)
    all_to_all x1, blocking collectives, from_experts(): lax.all_to_all(results, ('expert', 'head'), split_axis=0, concat_axis=0,...  52.7 us
    all_to_all x1, blocking collectives, to_experts(): lax.all_to_all(outgoing, ('expert', 'head'), split_axis=0, concat_axis=0,...  52.3 us
    reduce_scatter x2, waiting for transfers between devices, head_sums(): lax.psum_scatter(partial_rows, 'head', scatter_dimension=0, tiled=True)  33.2 us
    all_gather x2, blocking collectives, head_rows(): return lax.all_gather(row_block, 'head', axis=0, tiled=True)  31.4 us
    all_gather x1, waiting for transfers between devices, body(): kv_full = lax.all_gather(key_value_weight, 'head', axis=1, tiled=True)  27.5 us
    unnamed x63, local copies, waits for them, and re-layouts  5.77 us
  transfers between devices with their start and end apart: 3, of which 3 were waited for; matrix products, arithmetic and copies ran while one was open for 5% of the time, Pallas kernels for 0%

profile of v1, /device:TPU:0, one launch (start us, length us, event | category | flops | bytes accessed | tf_op | source)
XLA Modules:
  0.0 274.5 jit_solution(4676512596137165730)
XLA Ops:
  7.2 0.7 all-gather.2.cloned.1.call-update
  8.0 0.9 copy.76
  9.5 1.0 fusion.67
  10.5 0.9 fusion.61
  11.4 16.9 %all_gather.9 = bf16[64,2048]{1,0:T(8,128)(2,1)S(1)} all-gather(bf16[16,2048]{1,0:T(8,128)(2,1)S(1)} %fusion.61), channel_id=1, replica_groups=mesh['groups'=2,'expert'=4,'head'=4] {'head'}, dimensions={0}, use_global_device_ids=true | all-gather | bytes 327680 | tf_op jit(solution)/shard_map/all_gather | solution.py:149
  28.4 2.1 convolution_convert_fusion.5
  31.1 0.8 constant_dynamic-slice_fusion.3
  31.8 0.8 constant_dynamic-slice_fusion
  32.6 27.5 %all-gather.2.cloned.1.call-done = bf16[2048,512]{1,0:T(8,128)(2,1)} async-done(((bf16[2048,128]{1,0:T(8,128)(2,1)}), bf16[2048,512]{1,0:T(8,128)(2,1)}) %all-gather.2.cloned.1.call-update) | async-done | bytes 2097168 | tf_op jit(solution)/shard_map/all_gather | solution.py:187
  60.1 1.3 constant_dynamic-slice_fusion.2
  62.4 1.6 fusion.122
  64.1 1.2 fusion.34
  65.3 2.9 %fusion.77 = f32[64,2048]{1,0:T(8,128)} fusion(bf16[512,2048]{1,0:T(8,128)(2,1)} %param.28, bf16[8,8,4,128]{3,2,1,0:T(4,128)(2,1)S(1)} %bitcast.102), kind=kOutput, calls=%fused_computation.98 | convolution fusion | flops 134217728 | bytes 2686976 | tf_op jit(solution)/shard_map/dot_general | solution.py:194
  69.3 1.0 fusion.38
  70.3 2.2 convolution_convert_fusion
  72.5 15.8 %reduce-scatter.3.cloned.1.call-done = f32[16,2048]{1,0:T(8,128)} async-done(((f32[64,2048]{1,0:T(8,128)}), f32[16,2048]{1,0:T(8,128)}) %reduce-scatter.3.cloned.1.call-update) | async-done | bytes 131088 | tf_op jit(solution)/shard_map/reduce_scatter | solution.py:153
  88.3 1.0 fusion.69
  89.3 1.1 convolution_convert_fusion.1
  90.4 1.2 pad_maximum_fusion
  91.7 0.9 copy.80
  92.5 52.3 %all_to_all.10 = bf16[16,11,4096]{2,1,0:T(8,128)(2,1)S(1)} all-to-all(bf16[16,11,4096]{2,1,0:T(8,128)(2,1)S(1)} %copy.80), channel_id=1, replica_groups=mesh['groups'=2,'expert'=4,'head'=4] {'expert','head'}, dimensions={0} | all-to-all | bytes 2883584 | tf_op jit(solution)/shard_map/all_to_all | solution.py:157
  145.0 1.7 copy-done.3
  146.7 1.2 fusion.12
  147.9 1.2 fusion.8
  149.2 0.6 copy-done.4
  149.8 1.7 fusion.2
  151.5 1.2 fusion.6
  152.7 0.8 fusion.17
  153.5 1.2 fusion.20
  154.7 0.9 copy.83
  155.7 52.7 %all_to_all.11 = bf16[16,11,4096]{2,1,0:T(8,128)(2,1)S(1)} all-to-all(bf16[16,11,4096]{2,1,0:T(8,128)(2,1)S(1)} %copy.83), channel_id=1, replica_groups=mesh['groups'=2,'expert'=4,'head'=4] {'expert','head'}, dimensions={0} | all-to-all | bytes 2883584 | tf_op jit(solution)/shard_map/all_to_all | solution.py:161
  208.4 1.3 copy-done.1
  210.7 14.4 %all_gather.11 = bf16[64,2048]{1,0:T(8,128)(2,1)S(1)} all-gather(bf16[16,2048]{1,0:T(8,128)(2,1)S(1)} %fusion.118), channel_id=1, replica_groups=mesh['groups'=2,'expert'=4,'head'=4] {'head'}, dimensions={0}, use_global_device_ids=true | all-gather | bytes 327680 | tf_op jit(solution)/shard_map/all_gather | solution.py:149
  225.1 1.4 convolution_convert_fusion.3
  226.5 1.5 reshape.90
  228.0 1.8 convolution_bitcast_fusion.3
  229.8 1.7 convolution_bitcast_fusion.2
  231.5 3.0 %convolution_bitcast_fusion.4 = f32[4,48,128]{2,1,0:T(8,128)} fusion(f32[4,4,16,48]{3,2,1,0:T(8,128)} %convolution_bitcast_fusion.2, bf16[4,16,4,128]{3,2,1,0:T(4,128)(2,1)} %copy-done.14, f32[4,4,16,48]{3,2,1,0:T(8,128)} %get-tuple-element.11, f32[4,4,16]{2,1,0:T(4,128)} %copy-done.30), kind=kOutput, calls=%fused_computation.39 | convolution fusion | flops 3232047 | bytes 263168 | tf_op jit(solution)/shard_map/shbk,sbhd->skd/dot_general | solution.py:58
  234.5 2.9 %fusion.35 = bf16[4,16,4,128]{3,1,2,0:T(8,128)(2,1)} fusion(f32[4,4,16,48]{3,2,1,0:T(8,128)} %convolution_bitcast_fusion.2, bf16[4,16,128]{2,1,0:T(8,128)(2,1)} %bitcast.108, bf16[4,32,128]{2,1,0:T(8,128)(2,1)} %copy-done.16, f32[4,4,16,48]{3,2,1,0:T(8,128)} %get-tuple-element.11, f32[4,4,16]{2,1,0:T(4,128)} %copy-done.30), kind=kOutput, calls=%fused_computation.44 | convolution fusion | flops 3363119 | bytes 214016 | tf_op jit(solution)/shard_map/shbk,skd->sbhd/dot_general | solution.py:55
  237.4 0.8 slice.39
  238.2 0.8 slice.38
  238.9 0.9 copy.89
  239.8 2.3 fusion.40
  242.1 3.1 %convolution_add_fusion = f32[64,2048]{1,0:T(8,128)} fusion(f32[64,2048]{1,0:T(8,128)S(1)} %fusion.40, bf16[2048,512]{1,0:T(8,128)(2,1)} %param.26, bf16[8,8,4,128]{3,2,1,0:T(4,128)(2,1)S(1)} %bitcast.101), kind=kOutput, calls=%fused_computation.19 | convolution fusion | flops 134348800 | bytes 3211264 | tf_op jit(solution)/shard_map/tf,df->td/dot_general | solution.py:143
  245.3 2.4 fusion.25
  247.7 17.4 %reduce-scatter.5.cloned.1.call-done = f32[16,2048]{1,0:T(8,128)} async-done(((f32[64,2048]{1,0:T(8,128)}), f32[16,2048]{1,0:T(8,128)}) %reduce-scatter.5.cloned.1.call-update) | async-done | bytes 131088 | tf_op jit(solution)/shard_map/reduce_scatter | solution.py:153
  265.1 1.1 fusion.62
  266.3 1.7 fusion.66
  (88 shorter events, 4.7 us)
Async XLA Ops:
  7.2 140.8 %copy-start = (bf16[1,2048,768]{2,1,0:T(8,128)(2,1)S(1)}, bf16[1,2048,768]{2,1,0:T(8,128)(2,1)}, u32[]{:S(2)}) copy-start(bf16[1,2048,768]{2,1,0:T(8,128)(2,1)} %param.30) | copy-start | bytes 9437188
  7.2 23.3 %copy-start.28 = (s32[4]{0:T(128)S(1)}, s32[4]{0:T(128)}, u32[]{:S(2)}) copy-start(s32[4]{0:T(128)} %param.21) | copy-start | bytes 52
  7.2 53.0 %all-gather.2.cloned.1.call-start = ((), (), s32[]{:S(2)}) async-start(), calls=%async_computation.4 | async-start | bytes 2621440 | tf_op jit(solution)/shard_map/all_gather | solution.py:187
  7.9 80.3 %reduce-scatter.3.cloned.1.call-start = ((), (), s32[]{:S(2)}) async-start(), calls=%async_computation.5 | async-start | bytes 655360 | tf_op jit(solution)/shard_map/reduce_scatter | solution.py:153
  10.5 0.9 copy-start.21
  30.5 32.0 %copy-start.14 = (bf16[4,16,4,128]{3,2,1,0:T(4,128)(2,1)}, bf16[4,16,4,128]{3,2,1,0:T(4,128)(2,1)S(1)}, u32[]{:S(2)}) copy-start(bf16[4,16,4,128]{3,2,1,0:T(4,128)(2,1)S(1)} %reshape.88) | copy-start | bytes 196612
  31.8 32.2 %copy-start.12 = (bf16[4,32,128]{2,1,0:T(8,128)(2,1)}, bf16[4,32,128]{2,1,0:T(8,128)(2,1)S(1)}, u32[]{:S(2)}) copy-start(bf16[4,32,128]{2,1,0:T(8,128)(2,1)S(1)} %constant_dynamic-slice_fusion.3) | copy-start | bytes 98308
  32.6 31.4 %copy-start.16 = (bf16[4,32,128]{2,1,0:T(8,128)(2,1)}, bf16[4,32,128]{2,1,0:T(8,128)(2,1)S(1)}, u32[]{:S(2)}) copy-start(bf16[4,32,128]{2,1,0:T(8,128)(2,1)S(1)} %constant_dynamic-slice_fusion) | copy-start | bytes 98308
  61.4 0.8 copy-start.8
  61.4 1.0 copy-start.9
  62.4 1.6 copy-start.18
  62.4 5.9 %copy-start.25 = (s32[128]{0:T(128)S(1)}, s32[128]{0:T(128)}, u32[]{:S(2)}) copy-start(s32[128]{0:T(128)} %eq.39) | copy-start | bytes 1540
  64.0 4.3 %copy-start.30 = (f32[4,4,16]{2,1,0:T(4,128)}, f32[4,4,16]{2,1,0:T(4,128)S(1)}, u32[]{:S(2)}) copy-start(f32[4,4,16]{2,1,0:T(4,128)S(1)} %get-tuple-element.10) | copy-start | bytes 3076
  64.0 4.5 %copy-start.26 = (s32[128]{0:T(128)S(1)}, s32[128]{0:T(128)}, u32[]{:S(2)}) copy-start(s32[128]{0:T(128)} %eq.39) | copy-start | bytes 1540
  64.1 4.8 %copy-start.29 = (s32[16]{0:T(128)S(1)}, s32[16]{0:T(128)}, u32[]{:S(2)}) copy-start(s32[16]{0:T(128)} %param.18) | copy-start | bytes 196
  64.1 4.9 %copy-start.17 = (s32[16,8]{0,1:T(8,128)S(1)}, s32[16,8]{0,1:T(8,128)}, u32[]{:S(2)}) copy-start(s32[16,8]{0,1:T(8,128)} %param.19) | copy-start | bytes 1540
  64.1 6.2 %copy-start.6 = (bf16[16,2048]{1,0:T(8,128)(2,1)S(1)}, bf16[16,2048]{1,0:T(8,128)(2,1)}, u32[]{:S(2)}) copy-start(bf16[16,2048]{1,0:T(8,128)(2,1)} %param.17) | copy-start | bytes 196612
  65.3 23.0 %copy-start.5 = (bf16[16,2048]{1,0:T(8,128)(2,1)S(1)}, bf16[16,2048]{1,0:T(8,128)(2,1)}, u32[]{:S(2)}) copy-start(bf16[16,2048]{1,0:T(8,128)(2,1)} %param.16) | copy-start | bytes 196612
  68.2 196.9 %reduce-scatter.5.cloned.1.call-start = ((), (), s32[]{:S(2)}) async-start(), calls=%async_computation.6 | async-start | bytes 655360 | tf_op jit(solution)/shard_map/reduce_scatter | solution.py:153
  68.9 22.7 %copy-start.23 = (f32[16]{0:T(128)}, f32[16]{0:T(128)S(1)}, u32[]{:S(2)}) copy-start(f32[16]{0:T(128)S(1)} %convert_element_type.113) | copy-start | bytes 196
  69.3 22.4 %copy-start.10 = (pred[16,11,16]{2,1,0:T(8,128)(4,1)}, pred[16,11,16]{2,1,0:T(8,128)(4,1)S(1)}, u32[]{:S(2)}) copy-start(pred[16,11,16]{2,1,0:T(8,128)(4,1)S(1)} %compare_reduce_fusion) | copy-start | bytes 8452
  89.3 120.8 %copy-start.19 = (f32[16]{0:T(128)}, f32[16]{0:T(128)S(1)}, u32[]{:S(2)}) copy-start(f32[16]{0:T(128)S(1)} %add_rsqrt_fusion) | copy-start | bytes 196
  144.8 1.9 copy-start.3
  147.9 1.9 copy-start.4
  155.6 54.1 %copy-start.11 = (pred[16,11,16]{2,1,0:T(8,128)(4,1)S(1)}, pred[16,11,16]{2,1,0:T(8,128)(4,1)}, u32[]{:S(2)}) copy-start(pred[16,11,16]{2,1,0:T(8,128)(4,1)} %copy-done.10) | copy-start | bytes 8452
  155.6 54.1 %copy-start.15 = (f32[2048]{0:T(1024)S(1)}, f32[2048]{0:T(1024)}, u32[]{:S(2)}) copy-start(f32[2048]{0:T(1024)} %param.25) | copy-start | bytes 24580
  155.6 54.5 %copy-start.7 = (bf16[16,2048]{1,0:T(8,128)(2,1)S(1)}, bf16[16,2048]{1,0:T(8,128)(2,1)}, u32[]{:S(2)}) copy-start(bf16[16,2048]{1,0:T(8,128)(2,1)} %param.17) | copy-start | bytes 196612
  155.7 54.5 %copy-start.24 = (f32[16]{0:T(128)S(1)}, f32[16]{0:T(128)}, u32[]{:S(2)}) copy-start(f32[16]{0:T(128)} %copy-done.23) | copy-start | bytes 196
  155.7 69.5 %copy-start.2 = (bf16[512,2048]{1,0:T(8,128)(2,1)S(1)}, bf16[512,2048]{1,0:T(8,128)(2,1)}, u32[]{:S(2)}) copy-start(bf16[512,2048]{1,0:T(8,128)(2,1)} %param.28) | copy-start | bytes 6291460
  208.4 1.3 copy-start.1
  210.2 0.5 copy-start.27
  242.1 23.1 %copy-start.13 = (f32[2048]{0:T(1024)S(1)}, f32[2048]{0:T(1024)}, u32[]{:S(2)}) copy-start(f32[2048]{0:T(1024)} %param.24) | copy-start | bytes 24580
  242.1 23.1 %copy-start.22 = (f32[16]{0:T(128)S(1)}, f32[16]{0:T(128)}, u32[]{:S(2)}) copy-start(f32[16]{0:T(128)} %copy-done.21) | copy-start | bytes 196
  242.1 24.2 %copy-start.20 = (f32[16]{0:T(128)S(1)}, f32[16]{0:T(128)}, u32[]{:S(2)}) copy-start(f32[16]{0:T(128)} %copy-done.19) | copy-start | bytes 196
Sparse Core Ops, SparseCore 0:
  9.6 50.5 all-gather.1
  68.4 19.8 reduce-scatter.2
  245.4 19.7 reduce-scatter.4

commit v2 on v1

--- a/solution.py
+++ b/solution.py
@@ -153,12 +153,18 @@
     return lax.psum_scatter(partial_rows, "head", scatter_dimension=0, tiled=True)
 
 
-def to_experts(outgoing):
-    return lax.all_to_all(outgoing, ("expert", "head"), split_axis=0, concat_axis=0, tiled=True)
-
-
-def from_experts(results):
-    return lax.all_to_all(results, ("expert", "head"), split_axis=0, concat_axis=0, tiled=True)
+EXPERT_AXES = ("expert", "head")
+
+
+def shift_send(block, axes, count, shift):
+    return lax.ppermute(block, axes, perm=[(j, (j + shift) % count) for j in range(count)])
+
+
+def exchange(slots, axes, count, sign):
+    moved = [slots[0]]
+    for shift in range(1, count):
+        moved.append(shift_send(slots[shift], axes, count, (sign * shift) % count))
+    return jnp.stack(moved)
 
 
 def body(
@@ -204,7 +210,8 @@
     )
     earlier = jnp.cumsum(one_hot, axis=0) - one_hot
     position = jnp.sum(earlier * one_hot, axis=1)
-    target = flat_ids * capacity + position
+    me = lax.axis_index(EXPERT_AXES)
+    target = ((flat_ids - me) % device_count) * capacity + position
     matched = (jnp.arange(slot_total, dtype=jnp.int32)[:, None] == target[None, :]).reshape(
         device_count, capacity, owned, TOP
     )
@@ -217,7 +224,7 @@
     grad_out = jnp.einsum(
         "dct,tw->dcw", weighting, cotangent, precision=highest_prec
     ).astype(jnp.bfloat16)
-    arrived = to_experts(jnp.concatenate([outgoing, grad_out], axis=2))
+    arrived = exchange(jnp.concatenate([outgoing, grad_out], axis=2), EXPERT_AXES, device_count, 1)
     rows_in = arrived[:, :, :width]
     grads_in = arrived[:, :, width:]
     gate_matrix = w_gate[0]
@@ -242,7 +249,7 @@
         "scf,wf->scw", grad_up, up_matrix, preferred_element_type=jnp.float32
     )
     grad_back = grad_back.astype(jnp.bfloat16)
-    returned = from_experts(jnp.concatenate([result, grad_back], axis=2))
+    returned = exchange(jnp.concatenate([result, grad_back], axis=2), EXPERT_AXES, device_count, -1)
     moe_sum = jnp.einsum(
         "dct,dcw->tw",
         weighting,

time: 276 us -> 298 us (1.080)
  blocking collectives: 136 us -> 31 us
  starting transfers between devices: 0.12 us -> 54.6 us
  local copies, waits for them, and re-layouts: 15.7 us -> 61.8 us
  waiting for transfers between devices: 61.4 us -> 79.9 us
  other arithmetic: 9.03 us -> 19.3 us
  matrix products: 37.5 us -> 34.5 us
    all_to_all x2 -> x0, blocking collectives: 105 us -> none  [the longest x1 52.7 us: from_experts(): lax.all_to_all(results, ('expert', 'head'), split_axis=0, concat_axis=0,...]
    ppermute x0 -> x30, starting transfers between devices: none -> 54.5 us  [shift_send(): lax.ppermute(block, axes, perm=[(j, (j + shift) % count) for j in range(c...]
    another operation x0 -> x32, local copies, waits for them, and re-layouts: none -> 45.4 us  [exchange(): return jnp.stack(moved)]
    ppermute x0 -> x30, waiting for transfers between devices: none -> 17.6 us  [shift_send(): lax.ppermute(block, axes, perm=[(j, (j + shift) % count) for j in range(c...]
    concatenate x2 -> x4, other arithmetic: 1.32 us -> 11.5 us  [the longest x2 5.77 us: body(): jnp.concatenate([outgoing, grad_out], axis=2)]
    unnamed x63 -> x95, local copies, waits for them, and re-layouts: 5.77 us -> 7.01 us
  transfers between devices with their start and end apart: 3 -> 33, of which waited for: 3 -> 9; matrix products, arithmetic and copies ran while one was open for 5% -> 16% of each run, Pallas kernels for 0% -> 0%
where the time goes in v2:
time: 298 us; the launch traced here: 296 us
  waiting for transfers between devices  79.9 us (27%)
  local copies, waits for them, and re-layouts  61.8 us (21%)
  starting transfers between devices  54.6 us (18%)
  matrix products  34.5 us (12%)
  blocking collectives  31 us (10%)
  other arithmetic  19.3 us (6%)
  between operations  14.5 us (5%)
    ppermute x30, starting transfers between devices, shift_send(): lax.ppermute(block, axes, perm=[(j, (j + shift) % count) for j in range(c...  54.5 us
    another operation x32, local copies, waits for them, and re-layouts, exchange(): return jnp.stack(moved)  45.4 us
    reduce_scatter x2, waiting for transfers between devices, head_sums(): lax.psum_scatter(partial_rows, 'head', scatter_dimension=0, tiled=True)  33.7 us
    all_gather x2, blocking collectives, head_rows(): return lax.all_gather(row_block, 'head', axis=0, tiled=True)  31 us
    all_gather x1, waiting for transfers between devices, body(): kv_full = lax.all_gather(key_value_weight, 'head', axis=1, tiled=True)  27.8 us
    ppermute x30, waiting for transfers between devices, shift_send(): lax.ppermute(block, axes, perm=[(j, (j + shift) % count) for j in range(c...  17.6 us
    unnamed x95, local copies, waits for them, and re-layouts  7.01 us
  transfers between devices with their start and end apart: 33, of which 9 were waited for; matrix products, arithmetic and copies ran while one was open for 16% of the time, Pallas kernels for 0%

profile of v2, /device:TPU:0, one launch (start us, length us, event | category | flops | bytes accessed | tf_op | source)
XLA Modules:
  0.0 295.7 jit_solution(11274929545748727794)
XLA Ops:
  10.9 16.6 %all_gather.9 = bf16[64,2048]{1,0:T(8,128)(2,1)S(1)} all-gather(bf16[16,2048]{1,0:T(8,128)(2,1)S(1)} %fusion.91), channel_id=1, replica_groups=mesh['groups'=2,'expert'=4,'head'=4] {'head'}, dimensions={0}, use_global_device_ids=true | all-gather | bytes 327680 | tf_op jit(solution)/shard_map/all_gather | solution.py:149
  27.5 2.1 convolution_convert_fusion.5
  29.7 1.4 constant_dynamic-slice_fusion
  31.8 27.8 %all-gather.2.cloned.1.call-done = bf16[2048,512]{1,0:T(8,128)(2,1)} async-done(((bf16[2048,128]{1,0:T(8,128)(2,1)}), bf16[2048,512]{1,0:T(8,128)(2,1)}) %all-gather.2.cloned.1.call-update) | async-done | bytes 2097168 | tf_op jit(solution)/shard_map/all_gather | solution.py:193
  63.7 2.9 fusion.107
  68.8 2.2 convolution_convert_fusion
  71.0 15.9 %reduce-scatter.3.cloned.1.call-done = f32[16,2048]{1,0:T(8,128)} async-done(((f32[64,2048]{1,0:T(8,128)}), f32[16,2048]{1,0:T(8,128)}) %reduce-scatter.3.cloned.1.call-update) | async-done | bytes 131088 | tf_op jit(solution)/shard_map/reduce_scatter | solution.py:153
  88.4 2.1 fusion.71
  91.3 4.6 %collective-permute-start.10 = (bf16[11,4096]{1,0:T(8,128)(2,1)S(1)}, bf16[11,4096]{1,0:T(8,128)(2,1)S(1)}, u32[]{:S(2)}, u32[]{:S(2)}) collective-permute-start(bf16[11,4096]{1,0:T(8,128)(2,1)S(1)} %bitcast.263), channel_id=1, source_target_pairs={{0,11},{1,12},{2,13},{3,14},{4,15},{5,0},{6,1},{7,2},{8,3},{9,4},{... | collective-permute-start | bytes 270344 | tf_op jit(solution)/shard_map/ppermute | solution.py:160
  96.5 3.7 %pad_maximum_fusion.4 = (bf16[1,11,4096]{2,0,1:T(2,128)(2,1)S(1)}, bf16[1,11,4096]{2,0,1:T(2,128)(2,1)}, bf16[1,11,4096]{2,0,1:T(2,128)(2,1)S(1)}, bf16[1,11,409...) fusion(bf16[16,11,2048]{2,0,1:T(8,128)(2,1)S(1)} %copy-done.3, ...), kind=kLoop, calls=%fused_computation.166 | loop fusion | flops 1622016 | bytes 2252800 | tf_op jit(solution)/shard_map/concatenate | solution.py:227
  100.7 1.5 collective-permute-start.7
  102.2 1.8 collective-permute-start.13
  104.0 2.4 collective-permute-start.6
  106.4 4.9 %collective-permute-done.9 = bf16[11,4096]{1,0:T(8,128)(2,1)S(1)} collective-permute-done((bf16[11,4096]{1,0:T(8,128)(2,1)S(1)}, bf16[11,4096]{1,0:T(8,128)(2,1)S(1)}, u32[]{:S(2)}, u32[]{:S(2)}) %collective-permute-start.9) | collective-permute-done | bytes 90144 | tf_op jit(solution)/shard_map/ppermute | solution.py:160
  111.2 5.0 %collective-permute-start.4 = (bf16[11,4096]{1,0:T(8,128)(2,1)S(1)}, bf16[11,4096]{1,0:T(8,128)(2,1)S(1)}, u32[]{:S(2)}, u32[]{:S(2)}) collective-permute-start(bf16[11,4096]{1,0:T(8,128)(2,1)S(1)} %bitcast.237), channel_id=1, source_target_pairs={{0,5},{1,6},{2,7},{3,8},{4,9},{5,10},{6,11},{7,12},{8,13},{9,14},{... | collective-permute-start | bytes 270344 | tf_op jit(solution)/shard_map/ppermute | solution.py:160
  117.9 2.0 collective-permute-done.13
  119.9 2.3 collective-permute-start.2
  123.5 3.3 %collective-permute-done.5 = bf16[11,4096]{1,0:T(8,128)(2,1)S(1)} collective-permute-done((bf16[11,4096]{1,0:T(8,128)(2,1)S(1)}, bf16[11,4096]{1,0:T(8,128)(2,1)S(1)}, u32[]{:S(2)}, u32[]{:S(2)}) %collective-permute-start.5) | collective-permute-done | bytes 90144 | tf_op jit(solution)/shard_map/ppermute | solution.py:160
  126.8 4.4 %collective-permute-start.14 = (bf16[11,4096]{1,0:T(8,128)(2,1)S(1)}, bf16[11,4096]{1,0:T(8,128)(2,1)S(1)}, u32[]{:S(2)}, u32[]{:S(2)}) collective-permute-start(bf16[11,4096]{1,0:T(8,128)(2,1)S(1)} %bitcast.234), channel_id=1, source_target_pairs={{0,15},{1,0},{2,1},{3,2},{4,3},{5,4},{6,5},{7,6},{8,7},{9,8},{10,9... | collective-permute-start | bytes 270344 | tf_op jit(solution)/shard_map/ppermute | solution.py:160
  143.9 10.1 %stack.111 = bf16[16,11,4096]{2,0,1:T(8,128)(2,1)} concatenate(bf16[1,11,4096]{2,0,1:T(2,128)(2,1)} %get-tuple-element.25, bf16[1,11,4096]{2,0,1:T(2,128)(2,1)} %copy.555, bf16[1,11,4096]{2,0,1:T(2,128)(2,1)} %copy.556, bf16[1,11,4096]{2,0,1:T(2,128)(2,1)} %copy.557, bf16[1,11,4096]{2,0,1:T(2,128)(2,1)} %copy.558, bf16[1,11,4096]{2,0,1:T(2,128)(2,1)} %copy.559, ...), dimensions={0} | concatenate | bytes 2883584 | tf_op jit(solution)/shard_map/stack | solution.py:167
  154.0 3.0 %fusion.12 = f32[16,11,768]{2,0,1:T(8,128)S(1)} fusion(bf16[1,2048,768]{2,1,0:T(8,128)(2,1)} %param.29, bf16[16,11,4096]{2,0,1:T(8,128)(2,1)} %stack.111), kind=kOutput, calls=%fused_computation.72 | convolution fusion | flops 553648128 | bytes 4407296 | tf_op jit(solution)/shard_map/scw,wf->scf/dot_general | solution.py:233
  163.3 2.1 fusion.56
  166.0 2.7 collective-permute-start.27
  168.9 1.6 collective-permute-start.24
  170.4 3.0 %collective-permute-start.23 = (bf16[11,4096]{1,0:T(8,128)(2,1)S(1)}, bf16[11,4096]{1,0:T(8,128)(2,1)S(1)}, u32[]{:S(2)}, u32[]{:S(2)}) collective-permute-start(bf16[11,4096]{1,0:T(8,128)(2,1)S(1)} %bitcast.244), channel_id=1, source_target_pairs={{0,7},{1,8},{2,9},{3,10},{4,11},{5,12},{6,13},{7,14},{8,15},{9,0},... | collective-permute-start | bytes 270344 | tf_op jit(solution)/shard_map/ppermute | solution.py:160
  173.4 3.7 %pad_maximum_fusion.3 = (bf16[1,11,4096]{2,0,1:T(2,128)(2,1)S(1)}, bf16[1,11,4096]{2,0,1:T(2,128)(2,1)}, bf16[1,11,4096]{2,0,1:T(2,128)(2,1)S(1)}, bf16[1,11,409...) fusion(bf16[16,11,2048]{2,0,1:T(8,128)(2,1)S(1)} %fusion.20, ...), kind=kLoop, calls=%fused_computation.165 | loop fusion | flops 1622016 | bytes 2252800 | tf_op jit(solution)/shard_map/concatenate | solution.py:252
  177.7 1.6 collective-permute-start.22
  179.3 1.9 collective-permute-start.28
  183.1 6.3 %collective-permute-start.19 = (bf16[11,4096]{1,0:T(8,128)(2,1)S(1)}, bf16[11,4096]{1,0:T(8,128)(2,1)S(1)}, u32[]{:S(2)}, u32[]{:S(2)}) collective-permute-start(bf16[11,4096]{1,0:T(8,128)(2,1)S(1)} %bitcast.239), channel_id=1, source_target_pairs={{0,11},{1,12},{2,13},{3,14},{4,15},{5,0},{6,1},{7,2},{8,3},{9,4},{... | collective-permute-start | bytes 270344 | tf_op jit(solution)/shard_map/ppermute | solution.py:160
  190.0 1.6 collective-permute-start.18
  191.6 5.7 %collective-permute-done.28 = bf16[11,4096]{1,0:T(8,128)(2,1)S(1)} collective-permute-done((bf16[11,4096]{1,0:T(8,128)(2,1)S(1)}, bf16[11,4096]{1,0:T(8,128)(2,1)S(1)}, u32[]{:S(2)}, u32[]{:S(2)}) %collective-permute-start.28) | collective-permute-done | bytes 90144 | tf_op jit(solution)/shard_map/ppermute | solution.py:160
  197.3 3.6 %collective-permute-start.16 = (bf16[11,4096]{1,0:T(8,128)(2,1)S(1)}, bf16[11,4096]{1,0:T(8,128)(2,1)S(1)}, u32[]{:S(2)}, u32[]{:S(2)}) collective-permute-start(bf16[11,4096]{1,0:T(8,128)(2,1)S(1)} %bitcast.250), channel_id=1, source_target_pairs={{0,14},{1,15},{2,0},{3,1},{4,2},{5,3},{6,4},{7,5},{8,6},{9,7},{10,... | collective-permute-start | bytes 270344 | tf_op jit(solution)/shard_map/ppermute | solution.py:160
  201.0 3.2 %collective-permute-start.15 = (bf16[11,4096]{1,0:T(8,128)(2,1)S(1)}, bf16[11,4096]{1,0:T(8,128)(2,1)S(1)}, u32[]{:S(2)}, u32[]{:S(2)}) collective-permute-start(bf16[11,4096]{1,0:T(8,128)(2,1)S(1)} %bitcast.242), channel_id=1, source_target_pairs={{0,15},{1,0},{2,1},{3,2},{4,3},{5,4},{6,5},{7,6},{8,7},{9,8},{10,9... | collective-permute-start | bytes 270344 | tf_op jit(solution)/shard_map/ppermute | solution.py:160
  204.8 2.8 collective-permute-start.29
  220.2 10.1 %stack.127 = bf16[16,11,4096]{2,0,1:T(8,128)(2,1)} concatenate(bf16[1,11,4096]{2,0,1:T(2,128)(2,1)} %get-tuple-element.9, bf16[1,11,4096]{2,0,1:T(2,128)(2,1)} %copy.570, bf16[1,11,4096]{2,0,1:T(2,128)(2,1)} %copy.571, bf16[1,11,4096]{2,0,1:T(2,128)(2,1)} %copy.572, bf16[1,11,4096]{2,0,1:T(2,128)(2,1)} %copy.573, bf16[1,11,4096]{2,0,1:T(2,128)(2,1)} %copy.574, ...), dimensions={0} | concatenate | bytes 2883584 | tf_op jit(solution)/shard_map/stack | solution.py:167
  230.4 2.5 fusion.153
  234.2 14.5 %all_gather.11 = bf16[64,2048]{1,0:T(8,128)(2,1)S(1)} all-gather(bf16[16,2048]{1,0:T(8,128)(2,1)S(1)} %fusion.151), channel_id=1, replica_groups=mesh['groups'=2,'expert'=4,'head'=4] {'head'}, dimensions={0}, use_global_device_ids=true | all-gather | bytes 327680 | tf_op jit(solution)/shard_map/all_gather | solution.py:149
  248.7 1.4 convolution_convert_fusion.3
  250.1 1.5 reshape.102
  251.6 1.6 convolution_bitcast_fusion.2
  253.2 2.9 fusion.35
  256.1 3.0 %convolution_bitcast_fusion.4 = f32[4,48,128]{2,1,0:T(8,128)} fusion(f32[4,4,16,48]{3,2,1,0:T(8,128)} %convolution_bitcast_fusion.2, bf16[4,16,4,128]{3,2,1,0:T(4,128)(2,1)} %copy-done.15, f32[4,4,16,48]{3,2,1,0:T(8,128)} %copy-done.29, f32[4,4,16]{2,1,0:T(4,128)} %copy-done.30), kind=kOutput, calls=%fused_computation.97 | convolution fusion | flops 3232047 | bytes 263168 | tf_op jit(solution)/shard_map/shbk,sbhd->skd/dot_general | solution.py:58
  259.1 1.3 convolution_bitcast_fusion.3
  262.1 2.3 fusion.40
  264.4 1.5 convolution_add_fusion
  266.0 2.6 fusion.25
  268.6 17.8 %reduce-scatter.5.cloned.1.call-done = f32[16,2048]{1,0:T(8,128)} async-done(((f32[64,2048]{1,0:T(8,128)}), f32[16,2048]{1,0:T(8,128)}) %reduce-scatter.5.cloned.1.call-update) | async-done | bytes 131088 | tf_op jit(solution)/shard_map/reduce_scatter | solution.py:153
  287.5 1.7 fusion.96
  (210 shorter events, 56.8 us)
Async XLA Ops:
  7.2 151.1 %copy-start = (bf16[1,768,2048]{2,1,0:T(8,128)(2,1)S(1)}, bf16[1,768,2048]{2,1,0:T(8,128)(2,1)}, u32[]{:S(2)}) copy-start(bf16[1,768,2048]{2,1,0:T(8,128)(2,1)} %param.31) | copy-start | bytes 9437188
  7.2 52.5 %all-gather.2.cloned.1.call-start = ((), (), s32[]{:S(2)}) async-start(), calls=%async_computation.2 | async-start | bytes 2621440 | tf_op jit(solution)/shard_map/all_gather | solution.py:193
  7.9 79.0 %reduce-scatter.3.cloned.1.call-start = ((), (), s32[]{:S(2)}) async-start(), calls=%async_computation.3 | async-start | bytes 655360 | tf_op jit(solution)/shard_map/reduce_scatter | solution.py:153
  10.9 18.7 %copy-start.27 = (s32[4]{0:T(128)S(1)}, s32[4]{0:T(128)}, u32[]{:S(2)}) copy-start(s32[4]{0:T(128)} %param.21) | copy-start | bytes 52
  29.6 32.4 %copy-start.15 = (bf16[4,16,4,128]{3,2,1,0:T(4,128)(2,1)}, bf16[4,16,4,128]{3,2,1,0:T(4,128)(2,1)S(1)}, u32[]{:S(2)}) copy-start(bf16[4,16,4,128]{3,2,1,0:T(4,128)(2,1)S(1)} %reshape.100) | copy-start | bytes 196612
  31.8 31.3 %copy-start.13 = (bf16[4,32,128]{2,1,0:T(8,128)(2,1)}, bf16[4,32,128]{2,1,0:T(8,128)(2,1)S(1)}, u32[]{:S(2)}) copy-start(bf16[4,32,128]{2,1,0:T(8,128)(2,1)S(1)} %constant_dynamic-slice_fusion.3) | copy-start | bytes 98308
  66.7 20.2 %copy-start.6 = (bf16[16,2048]{1,0:T(8,128)(2,1)S(1)}, bf16[16,2048]{1,0:T(8,128)(2,1)}, u32[]{:S(2)}) copy-start(bf16[16,2048]{1,0:T(8,128)(2,1)} %param.16) | copy-start | bytes 196612
  66.7 21.3 %copy-start.18 = (f32[2048]{0:T(1024)S(1)}, f32[2048]{0:T(1024)}, u32[]{:S(2)}) copy-start(f32[2048]{0:T(1024)} %param.25) | copy-start | bytes 24580
  66.7 219.7 %reduce-scatter.5.cloned.1.call-start = ((), (), s32[]{:S(2)}) async-start(), calls=%async_computation.4 | async-start | bytes 655360 | tf_op jit(solution)/shard_map/reduce_scatter | solution.py:153
  66.9 166.7 %copy-start.24 = (f32[16]{0:T(128)}, f32[16]{0:T(128)S(1)}, u32[]{:S(2)}) copy-start(f32[16]{0:T(128)S(1)} %convert_element_type.113) | copy-start | bytes 196
  67.8 22.8 %copy-start.11 = (pred[16,11,16]{2,1,0:T(8,128)(4,1)}, pred[16,11,16]{2,1,0:T(8,128)(4,1)S(1)}, u32[]{:S(2)}) copy-start(pred[16,11,16]{2,1,0:T(8,128)(4,1)S(1)} %compare_reduce_fusion) | copy-start | bytes 8452
  88.0 145.6 %copy-start.20 = (f32[16]{0:T(128)}, f32[16]{0:T(128)S(1)}, u32[]{:S(2)}) copy-start(f32[16]{0:T(128)S(1)} %add_rsqrt_fusion) | copy-start | bytes 196
  91.1 9.6 %collective-permute-start.12 = (bf16[11,4096]{1,0:T(8,128)(2,1)S(1)}, bf16[11,4096]{1,0:T(8,128)(2,1)S(1)}, u32[]{:S(2)}, u32[]{:S(2)}) collective-permute-start(bf16[11,4096]{1,0:T(8,128)(2,1)S(1)} %bitcast.281), channel_id=1, source_target_pairs={{0,13},{1,14},{2,15},{3,0},{4,1},{5,2},{6,3},{7,4},{8,5},{9,6},{10... | collective-permute-start | bytes 270344 | tf_op jit(solution)/shard_map/ppermute | solution.py:160
  91.2 11.0 %collective-permute-start.11 = (bf16[11,4096]{1,0:T(8,128)(2,1)S(1)}, bf16[11,4096]{1,0:T(8,128)(2,1)S(1)}, u32[]{:S(2)}, u32[]{:S(2)}) collective-permute-start(bf16[11,4096]{1,0:T(8,128)(2,1)S(1)} %bitcast.273), channel_id=1, source_target_pairs={{0,12},{1,13},{2,14},{3,15},{4,0},{5,1},{6,2},{7,3},{8,4},{9,5},{1... | collective-permute-start | bytes 270344 | tf_op jit(solution)/shard_map/ppermute | solution.py:160
  91.3 12.7 %collective-permute-start.10 = (bf16[11,4096]{1,0:T(8,128)(2,1)S(1)}, bf16[11,4096]{1,0:T(8,128)(2,1)S(1)}, u32[]{:S(2)}, u32[]{:S(2)}) collective-permute-start(bf16[11,4096]{1,0:T(8,128)(2,1)S(1)} %bitcast.263), channel_id=1, source_target_pairs={{0,11},{1,12},{2,13},{3,14},{4,15},{5,0},{6,1},{7,2},{8,3},{9,4},{... | collective-permute-start | bytes 270344 | tf_op jit(solution)/shard_map/ppermute | solution.py:160
  95.9 15.4 %collective-permute-start.9 = (bf16[11,4096]{1,0:T(8,128)(2,1)S(1)}, bf16[11,4096]{1,0:T(8,128)(2,1)S(1)}, u32[]{:S(2)}, u32[]{:S(2)}) collective-permute-start(bf16[11,4096]{1,0:T(8,128)(2,1)S(1)} %bitcast.253), channel_id=1, source_target_pairs={{0,10},{1,11},{2,12},{3,13},{4,14},{5,15},{6,0},{7,1},{8,2},{9,3},... | collective-permute-start | bytes 270344 | tf_op jit(solution)/shard_map/ppermute | solution.py:160
  95.9 15.4 %collective-permute-start.8 = (bf16[11,4096]{1,0:T(8,128)(2,1)S(1)}, bf16[11,4096]{1,0:T(8,128)(2,1)S(1)}, u32[]{:S(2)}, u32[]{:S(2)}) collective-permute-start(bf16[11,4096]{1,0:T(8,128)(2,1)S(1)} %bitcast.243), channel_id=1, source_target_pairs={{0,9},{1,10},{2,11},{3,12},{4,13},{5,14},{6,15},{7,0},{8,1},{9,2},... | collective-permute-start | bytes 270344 | tf_op jit(solution)/shard_map/ppermute | solution.py:160
  100.7 16.1 %collective-permute-start.7 = (bf16[11,4096]{1,0:T(8,128)(2,1)S(1)}, bf16[11,4096]{1,0:T(8,128)(2,1)S(1)}, u32[]{:S(2)}, u32[]{:S(2)}) collective-permute-start(bf16[11,4096]{1,0:T(8,128)(2,1)S(1)} %bitcast.267), channel_id=1, source_target_pairs={{0,8},{1,9},{2,10},{3,11},{4,12},{5,13},{6,14},{7,15},{8,0},{9,1},... | collective-permute-start | bytes 270344 | tf_op jit(solution)/shard_map/ppermute | solution.py:160
  102.2 17.8 %collective-permute-start.13 = (bf16[11,4096]{1,0:T(8,128)(2,1)S(1)}, bf16[11,4096]{1,0:T(8,128)(2,1)S(1)}, u32[]{:S(2)}, u32[]{:S(2)}) collective-permute-start(bf16[11,4096]{1,0:T(8,128)(2,1)S(1)} %bitcast.259), channel_id=1, source_target_pairs={{0,14},{1,15},{2,0},{3,1},{4,2},{5,3},{6,4},{7,5},{8,6},{9,7},{10,... | collective-permute-start | bytes 270344 | tf_op jit(solution)/shard_map/ppermute | solution.py:160
  104.0 18.3 %collective-permute-start.6 = (bf16[11,4096]{1,0:T(8,128)(2,1)S(1)}, bf16[11,4096]{1,0:T(8,128)(2,1)S(1)}, u32[]{:S(2)}, u32[]{:S(2)}) collective-permute-start(bf16[11,4096]{1,0:T(8,128)(2,1)S(1)} %bitcast.261), channel_id=1, source_target_pairs={{0,7},{1,8},{2,9},{3,10},{4,11},{5,12},{6,13},{7,14},{8,15},{9,0},... | collective-permute-start | bytes 270344 | tf_op jit(solution)/shard_map/ppermute | solution.py:160
  111.2 15.6 %collective-permute-start.5 = (bf16[11,4096]{1,0:T(8,128)(2,1)S(1)}, bf16[11,4096]{1,0:T(8,128)(2,1)S(1)}, u32[]{:S(2)}, u32[]{:S(2)}) collective-permute-start(bf16[11,4096]{1,0:T(8,128)(2,1)S(1)} %bitcast.247), channel_id=1, source_target_pairs={{0,6},{1,7},{2,8},{3,9},{4,10},{5,11},{6,12},{7,13},{8,14},{9,15},... | collective-permute-start | bytes 270344 | tf_op jit(solution)/shard_map/ppermute | solution.py:160
  111.2 15.6 %collective-permute-start.4 = (bf16[11,4096]{1,0:T(8,128)(2,1)S(1)}, bf16[11,4096]{1,0:T(8,128)(2,1)S(1)}, u32[]{:S(2)}, u32[]{:S(2)}) collective-permute-start(bf16[11,4096]{1,0:T(8,128)(2,1)S(1)} %bitcast.237), channel_id=1, source_target_pairs={{0,5},{1,6},{2,7},{3,8},{4,9},{5,10},{6,11},{7,12},{8,13},{9,14},{... | collective-permute-start | bytes 270344 | tf_op jit(solution)/shard_map/ppermute | solution.py:160
  116.8 22.9 %collective-permute-start.3 = (bf16[11,4096]{1,0:T(8,128)(2,1)S(1)}, bf16[11,4096]{1,0:T(8,128)(2,1)S(1)}, u32[]{:S(2)}, u32[]{:S(2)}) collective-permute-start(bf16[11,4096]{1,0:T(8,128)(2,1)S(1)} %bitcast.265), channel_id=1, source_target_pairs={{0,4},{1,5},{2,6},{3,7},{4,8},{5,9},{6,10},{7,11},{8,12},{9,13},{1... | collective-permute-start | bytes 270344 | tf_op jit(solution)/shard_map/ppermute | solution.py:160
  119.9 20.6 %collective-permute-start.2 = (bf16[11,4096]{1,0:T(8,128)(2,1)S(1)}, bf16[11,4096]{1,0:T(8,128)(2,1)S(1)}, u32[]{:S(2)}, u32[]{:S(2)}) collective-permute-start(bf16[11,4096]{1,0:T(8,128)(2,1)S(1)} %bitcast.256), channel_id=1, source_target_pairs={{0,3},{1,4},{2,5},{3,6},{4,7},{5,8},{6,9},{7,10},{8,11},{9,12},{10... | collective-permute-start | bytes 270344 | tf_op jit(solution)/shard_map/ppermute | solution.py:160
  122.3 19.1 %collective-permute-start.1 = (bf16[11,4096]{1,0:T(8,128)(2,1)S(1)}, bf16[11,4096]{1,0:T(8,128)(2,1)S(1)}, u32[]{:S(2)}, u32[]{:S(2)}) collective-permute-start(bf16[11,4096]{1,0:T(8,128)(2,1)S(1)} %bitcast.248), channel_id=1, source_target_pairs={{0,2},{1,3},{2,4},{3,5},{4,6},{5,7},{6,8},{7,9},{8,10},{9,11},{10,... | collective-permute-start | bytes 270344 | tf_op jit(solution)/shard_map/ppermute | solution.py:160
  126.8 15.4 %collective-permute-start = (bf16[11,4096]{1,0:T(8,128)(2,1)S(1)}, bf16[11,4096]{1,0:T(8,128)(2,1)S(1)}, u32[]{:S(2)}, u32[]{:S(2)}) collective-permute-start(bf16[11,4096]{1,0:T(8,128)(2,1)S(1)} %bitcast.241), channel_id=1, source_target_pairs={{0,1},{1,2},{2,3},{3,4},{4,5},{5,6},{6,7},{7,8},{8,9},{9,10},{10,1... | collective-permute-start | bytes 270344 | tf_op jit(solution)/shard_map/ppermute | solution.py:160
  126.8 16.2 %collective-permute-start.14 = (bf16[11,4096]{1,0:T(8,128)(2,1)S(1)}, bf16[11,4096]{1,0:T(8,128)(2,1)S(1)}, u32[]{:S(2)}, u32[]{:S(2)}) collective-permute-start(bf16[11,4096]{1,0:T(8,128)(2,1)S(1)} %bitcast.234), channel_id=1, source_target_pairs={{0,15},{1,0},{2,1},{3,2},{4,3},{5,4},{6,5},{7,6},{8,7},{9,8},{10,9... | collective-permute-start | bytes 270344 | tf_op jit(solution)/shard_map/ppermute | solution.py:160
  166.0 11.6 %collective-permute-start.27 = (bf16[11,4096]{1,0:T(8,128)(2,1)S(1)}, bf16[11,4096]{1,0:T(8,128)(2,1)S(1)}, u32[]{:S(2)}, u32[]{:S(2)}) collective-permute-start(bf16[11,4096]{1,0:T(8,128)(2,1)S(1)} %bitcast.282), channel_id=1, source_target_pairs={{0,3},{1,4},{2,5},{3,6},{4,7},{5,8},{6,9},{7,10},{8,11},{9,12},{10... | collective-permute-start | bytes 270344 | tf_op jit(solution)/shard_map/ppermute | solution.py:160
  168.7 10.6 %collective-permute-start.26 = (bf16[11,4096]{1,0:T(8,128)(2,1)S(1)}, bf16[11,4096]{1,0:T(8,128)(2,1)S(1)}, u32[]{:S(2)}, u32[]{:S(2)}) collective-permute-start(bf16[11,4096]{1,0:T(8,128)(2,1)S(1)} %bitcast.274), channel_id=1, source_target_pairs={{0,4},{1,5},{2,6},{3,7},{4,8},{5,9},{6,10},{7,11},{8,12},{9,13},{1... | collective-permute-start | bytes 270344 | tf_op jit(solution)/shard_map/ppermute | solution.py:160
  168.9 12.4 %collective-permute-start.25 = (bf16[11,4096]{1,0:T(8,128)(2,1)S(1)}, bf16[11,4096]{1,0:T(8,128)(2,1)S(1)}, u32[]{:S(2)}, u32[]{:S(2)}) collective-permute-start(bf16[11,4096]{1,0:T(8,128)(2,1)S(1)} %bitcast.264), channel_id=1, source_target_pairs={{0,5},{1,6},{2,7},{3,8},{4,9},{5,10},{6,11},{7,12},{8,13},{9,14},{... | collective-permute-start | bytes 270344 | tf_op jit(solution)/shard_map/ppermute | solution.py:160
  168.9 13.4 %collective-permute-start.24 = (bf16[11,4096]{1,0:T(8,128)(2,1)S(1)}, bf16[11,4096]{1,0:T(8,128)(2,1)S(1)}, u32[]{:S(2)}, u32[]{:S(2)}) collective-permute-start(bf16[11,4096]{1,0:T(8,128)(2,1)S(1)} %bitcast.254), channel_id=1, source_target_pairs={{0,6},{1,7},{2,8},{3,9},{4,10},{5,11},{6,12},{7,13},{8,14},{9,15},... | collective-permute-start | bytes 270344 | tf_op jit(solution)/shard_map/ppermute | solution.py:160
  170.4 12.7 %collective-permute-start.23 = (bf16[11,4096]{1,0:T(8,128)(2,1)S(1)}, bf16[11,4096]{1,0:T(8,128)(2,1)S(1)}, u32[]{:S(2)}, u32[]{:S(2)}) collective-permute-start(bf16[11,4096]{1,0:T(8,128)(2,1)S(1)} %bitcast.244), channel_id=1, source_target_pairs={{0,7},{1,8},{2,9},{3,10},{4,11},{5,12},{6,13},{7,14},{8,15},{9,0},... | collective-permute-start | bytes 270344 | tf_op jit(solution)/shard_map/ppermute | solution.py:160
  177.7 12.4 %collective-permute-start.22 = (bf16[11,4096]{1,0:T(8,128)(2,1)S(1)}, bf16[11,4096]{1,0:T(8,128)(2,1)S(1)}, u32[]{:S(2)}, u32[]{:S(2)}) collective-permute-start(bf16[11,4096]{1,0:T(8,128)(2,1)S(1)} %bitcast.269), channel_id=1, source_target_pairs={{0,8},{1,9},{2,10},{3,11},{4,12},{5,13},{6,14},{7,15},{8,0},{9,1},... | collective-permute-start | bytes 270344 | tf_op jit(solution)/shard_map/ppermute | solution.py:160
  179.3 18.0 %collective-permute-start.28 = (bf16[11,4096]{1,0:T(8,128)(2,1)S(1)}, bf16[11,4096]{1,0:T(8,128)(2,1)S(1)}, u32[]{:S(2)}, u32[]{:S(2)}) collective-permute-start(bf16[11,4096]{1,0:T(8,128)(2,1)S(1)} %bitcast.260), channel_id=1, source_target_pairs={{0,2},{1,3},{2,4},{3,5},{4,6},{5,7},{6,8},{7,9},{8,10},{9,11},{10,... | collective-permute-start | bytes 270344 | tf_op jit(solution)/shard_map/ppermute | solution.py:160
  181.2 16.1 %collective-permute-start.21 = (bf16[11,4096]{1,0:T(8,128)(2,1)S(1)}, bf16[11,4096]{1,0:T(8,128)(2,1)S(1)}, u32[]{:S(2)}, u32[]{:S(2)}) collective-permute-start(bf16[11,4096]{1,0:T(8,128)(2,1)S(1)} %bitcast.262), channel_id=1, source_target_pairs={{0,9},{1,10},{2,11},{3,12},{4,13},{5,14},{6,15},{7,0},{8,1},{9,2},... | collective-permute-start | bytes 270344 | tf_op jit(solution)/shard_map/ppermute | solution.py:160
  182.2 18.7 %collective-permute-start.20 = (bf16[11,4096]{1,0:T(8,128)(2,1)S(1)}, bf16[11,4096]{1,0:T(8,128)(2,1)S(1)}, u32[]{:S(2)}, u32[]{:S(2)}) collective-permute-start(bf16[11,4096]{1,0:T(8,128)(2,1)S(1)} %bitcast.249), channel_id=1, source_target_pairs={{0,10},{1,11},{2,12},{3,13},{4,14},{5,15},{6,0},{7,1},{8,2},{9,3},... | collective-permute-start | bytes 270344 | tf_op jit(solution)/shard_map/ppermute | solution.py:160
  183.1 21.7 %collective-permute-start.19 = (bf16[11,4096]{1,0:T(8,128)(2,1)S(1)}, bf16[11,4096]{1,0:T(8,128)(2,1)S(1)}, u32[]{:S(2)}, u32[]{:S(2)}) collective-permute-start(bf16[11,4096]{1,0:T(8,128)(2,1)S(1)} %bitcast.239), channel_id=1, source_target_pairs={{0,11},{1,12},{2,13},{3,14},{4,15},{5,0},{6,1},{7,2},{8,3},{9,4},{... | collective-permute-start | bytes 270344 | tf_op jit(solution)/shard_map/ppermute | solution.py:160
  190.0 26.0 %collective-permute-start.18 = (bf16[11,4096]{1,0:T(8,128)(2,1)S(1)}, bf16[11,4096]{1,0:T(8,128)(2,1)S(1)}, u32[]{:S(2)}, u32[]{:S(2)}) collective-permute-start(bf16[11,4096]{1,0:T(8,128)(2,1)S(1)} %bitcast.266), channel_id=1, source_target_pairs={{0,12},{1,13},{2,14},{3,15},{4,0},{5,1},{6,2},{7,3},{8,4},{9,5},{1... | collective-permute-start | bytes 270344 | tf_op jit(solution)/shard_map/ppermute | solution.py:160
  197.3 19.6 %collective-permute-start.17 = (bf16[11,4096]{1,0:T(8,128)(2,1)S(1)}, bf16[11,4096]{1,0:T(8,128)(2,1)S(1)}, u32[]{:S(2)}, u32[]{:S(2)}) collective-permute-start(bf16[11,4096]{1,0:T(8,128)(2,1)S(1)} %bitcast.258), channel_id=1, source_target_pairs={{0,13},{1,14},{2,15},{3,0},{4,1},{5,2},{6,3},{7,4},{8,5},{9,6},{10... | collective-permute-start | bytes 270344 | tf_op jit(solution)/shard_map/ppermute | solution.py:160
  197.3 20.4 %collective-permute-start.16 = (bf16[11,4096]{1,0:T(8,128)(2,1)S(1)}, bf16[11,4096]{1,0:T(8,128)(2,1)S(1)}, u32[]{:S(2)}, u32[]{:S(2)}) collective-permute-start(bf16[11,4096]{1,0:T(8,128)(2,1)S(1)} %bitcast.250), channel_id=1, source_target_pairs={{0,14},{1,15},{2,0},{3,1},{4,2},{5,3},{6,4},{7,5},{8,6},{9,7},{10,... | collective-permute-start | bytes 270344 | tf_op jit(solution)/shard_map/ppermute | solution.py:160
  201.0 17.6 %collective-permute-start.15 = (bf16[11,4096]{1,0:T(8,128)(2,1)S(1)}, bf16[11,4096]{1,0:T(8,128)(2,1)S(1)}, u32[]{:S(2)}, u32[]{:S(2)}) collective-permute-start(bf16[11,4096]{1,0:T(8,128)(2,1)S(1)} %bitcast.242), channel_id=1, source_target_pairs={{0,15},{1,0},{2,1},{3,2},{4,3},{5,4},{6,5},{7,6},{8,7},{9,8},{10,9... | collective-permute-start | bytes 270344 | tf_op jit(solution)/shard_map/ppermute | solution.py:160
  204.8 14.6 %collective-permute-start.29 = (bf16[11,4096]{1,0:T(8,128)(2,1)S(1)}, bf16[11,4096]{1,0:T(8,128)(2,1)S(1)}, u32[]{:S(2)}, u32[]{:S(2)}) collective-permute-start(bf16[11,4096]{1,0:T(8,128)(2,1)S(1)} %bitcast.236), channel_id=1, source_target_pairs={{0,1},{1,2},{2,3},{3,4},{4,5},{5,6},{6,7},{7,8},{8,9},{9,10},{10,1... | collective-permute-start | bytes 270344 | tf_op jit(solution)/shard_map/ppermute | solution.py:160
  230.4 18.3 %copy-start.1 = (bf16[512,2048]{1,0:T(8,128)(2,1)S(1)}, bf16[512,2048]{1,0:T(8,128)(2,1)}, u32[]{:S(2)}) copy-start(bf16[512,2048]{1,0:T(8,128)(2,1)} %param.28) | copy-start | bytes 6291460
  234.2 17.4 %copy-start.17 = (bf16[64,128]{1,0:T(8,128)(2,1)S(1)}, bf16[64,128]{1,0:T(8,128)(2,1)}, u32[]{:S(2)}) copy-start(bf16[64,128]{1,0:T(8,128)(2,1)} %copy-done.16) | copy-start | bytes 49156
  253.2 5.9 %copy-start.31 = (f32[4,4,16]{2,1,0:T(4,128)S(1)}, f32[4,4,16]{2,1,0:T(4,128)}, u32[]{:S(2)}) copy-start(f32[4,4,16]{2,1,0:T(4,128)} %copy-done.30) | copy-start | bytes 3076
  265.9 20.4 %copy-start.14 = (f32[2048]{0:T(1024)S(1)}, f32[2048]{0:T(1024)}, u32[]{:S(2)}) copy-start(f32[2048]{0:T(1024)} %param.24) | copy-start | bytes 24580
  265.9 20.4 %copy-start.23 = (f32[16]{0:T(128)S(1)}, f32[16]{0:T(128)}, u32[]{:S(2)}) copy-start(f32[16]{0:T(128)} %copy-done.22) | copy-start | bytes 196
  266.0 21.5 %copy-start.21 = (f32[16]{0:T(128)S(1)}, f32[16]{0:T(128)}, u32[]{:S(2)}) copy-start(f32[16]{0:T(128)} %copy-done.20) | copy-start | bytes 196
  (17 other events, 46.6 us)
Sparse Core Ops, SparseCore 0:
  9.6 50.0 all-gather.1
  66.8 20.0 reduce-scatter.2
  266.1 20.2 reduce-scatter.4

commit v3 on v1

--- a/solution.py
+++ b/solution.py
@@ -217,9 +217,8 @@
     grad_out = jnp.einsum(
         "dct,tw->dcw", weighting, cotangent, precision=highest_prec
     ).astype(jnp.bfloat16)
-    arrived = to_experts(jnp.concatenate([outgoing, grad_out], axis=2))
-    rows_in = arrived[:, :, :width]
-    grads_in = arrived[:, :, width:]
+    rows_in = to_experts(outgoing)
+    grads_in = to_experts(grad_out)
     gate_matrix = w_gate[0]
     up_matrix = w_up[0]
     down_matrix = w_down[0]
@@ -242,16 +241,17 @@
         "scf,wf->scw", grad_up, up_matrix, preferred_element_type=jnp.float32
     )
     grad_back = grad_back.astype(jnp.bfloat16)
-    returned = from_experts(jnp.concatenate([result, grad_back], axis=2))
+    result_home = from_experts(result)
+    grad_home = from_experts(grad_back)
     moe_sum = jnp.einsum(
         "dct,dcw->tw",
         weighting,
-        returned[:, :, :width].astype(jnp.float32),
+        result_home.astype(jnp.float32),
         precision=highest_prec,
     )
     layer_out = (hidden.astype(jnp.float32) + moe_sum).astype(jnp.bfloat16)
     grad_moe = jnp.einsum(
-        "dct,dcw->tw", placement, returned[:, :, width:], preferred_element_type=jnp.float32
+        "dct,dcw->tw", placement, grad_home, preferred_element_type=jnp.float32
     )
     grad_hidden = cotangent + rms_backward(hidden, moe_gain, inverse_two, grad_moe)
     grad_low = grad_hidden.astype(jnp.bfloat16)

time: 276 us -> 275 us (level)
  blocking collectives: 136 us -> 47.6 us
  waiting for transfers between devices: 61.4 us -> 121 us
  starting transfers between devices: 0.12 us -> 17.7 us
  matrix products: 37.5 us -> 47.2 us
    all_to_all x2 -> x0, blocking collectives: 105 us -> none  [the longest x1 52.7 us: from_experts(): lax.all_to_all(results, ('expert', 'head'), split_axis=0, concat_axis=0,...]
    all_to_all x0 -> x4, waiting for transfers between devices: none -> 59.1 us  [the longest x2 36.5 us: to_experts(): lax.all_to_all(outgoing, ('expert', 'head'), split_axis=0, concat_axis=0,...]
    all_to_all x0 -> x4, starting transfers between devices: none -> 17.6 us  [the longest x2 8.86 us: from_experts(): lax.all_to_all(results, ('expert', 'head'), split_axis=0, concat_axis=0,...]
    all_gather x2, blocking collectives: 31.4 us -> 47.6 us  [head_rows(): return lax.all_gather(row_block, 'head', axis=0, tiled=True)]
    convert_element_type x0 -> x4, local copies, waits for them, and re-layouts: none -> 5.74 us  [the longest x1 1.46 us: body(): grad_out = jnp.einsum('dct,tw->dcw', weighting, cotangent, precision=high...]
    unnamed x63 -> x57, local copies, waits for them, and re-layouts: 5.77 us -> 2.44 us
    dot_general x1, matrix products: 1.67 us -> 4.44 us  [body(): jnp.einsum('scw,fw->scf', grads_in, down_matrix, preferred_element_type=j...]
  transfers between devices with their start and end apart: 3 -> 7, of which waited for: 3 -> 6; matrix products, arithmetic and copies ran while one was open for 5% -> 19% of each run, Pallas kernels for 0% -> 0%
where the time goes in v3:
time: 275 us; the launch traced here: 273 us
  waiting for transfers between devices  121 us (44%)
  blocking collectives  47.6 us (17%)
  matrix products  47.2 us (17%)
  starting transfers between devices  17.7 us (6%)
  local copies, waits for them, and re-layouts  16.9 us (6%)
  between operations  14.3 us (5%)
  other arithmetic  8.46 us (3%)
    all_gather x2, blocking collectives, head_rows(): return lax.all_gather(row_block, 'head', axis=0, tiled=True)  47.6 us
    all_to_all x2, waiting for transfers between devices, to_experts(): lax.all_to_all(outgoing, ('expert', 'head'), split_axis=0, concat_axis=0,...  36.5 us
    reduce_scatter x2, waiting for transfers between devices, head_sums(): lax.psum_scatter(partial_rows, 'head', scatter_dimension=0, tiled=True)  32.9 us
    all_gather x1, waiting for transfers between devices, body(): kv_full = lax.all_gather(key_value_weight, 'head', axis=1, tiled=True)  28.5 us
    all_to_all x2, waiting for transfers between devices, from_experts(): lax.all_to_all(results, ('expert', 'head'), split_axis=0, concat_axis=0,...  22.6 us
    all_to_all x2, starting transfers between devices, from_experts(): lax.all_to_all(results, ('expert', 'head'), split_axis=0, concat_axis=0,...  8.86 us
    all_to_all x2, starting transfers between devices, to_experts(): lax.all_to_all(outgoing, ('expert', 'head'), split_axis=0, concat_axis=0,...  8.69 us
  transfers between devices with their start and end apart: 7, of which 6 were waited for; matrix products, arithmetic and copies ran while one was open for 19% of the time, Pallas kernels for 0%

profile of v3, /device:TPU:0, one launch (start us, length us, event | category | flops | bytes accessed | tf_op | source)
XLA Modules:
  0.0 273.4 jit_solution(7430141480536948963)
XLA Ops:
  8.0 0.9 copy.80
  9.6 1.0 fusion.65
  10.6 0.9 fusion.59
  11.5 17.2 %all_gather.9 = bf16[64,2048]{1,0:T(8,128)(2,1)S(1)} all-gather(bf16[16,2048]{1,0:T(8,128)(2,1)S(1)} %fusion.59), channel_id=1, replica_groups=mesh['groups'=2,'expert'=4,'head'=4] {'head'}, dimensions={0}, use_global_device_ids=true | all-gather | bytes 327680 | tf_op jit(solution)/shard_map/all_gather | solution.py:149
  28.7 2.1 convolution_convert_fusion.5
  33.6 28.5 %all-gather.2.cloned.1.call-done = bf16[2048,512]{1,0:T(8,128)(2,1)} async-done(((bf16[2048,128]{1,0:T(8,128)(2,1)}), bf16[2048,512]{1,0:T(8,128)(2,1)}) %all-gather.2.cloned.1.call-update) | async-done | bytes 2097168 | tf_op jit(solution)/shard_map/all_gather | solution.py:187
  62.1 1.3 constant_dynamic-slice_fusion.2
  64.4 1.6 fusion.119
  66.0 1.2 fusion.34
  67.2 2.9 %fusion.75 = f32[64,2048]{1,0:T(8,128)} fusion(bf16[512,2048]{1,0:T(8,128)(2,1)} %param.28, bf16[8,8,4,128]{3,2,1,0:T(4,128)(2,1)S(1)} %bitcast.104), kind=kOutput, calls=%fused_computation.94 | convolution fusion | flops 134217728 | bytes 2686976 | tf_op jit(solution)/shard_map/dot_general | solution.py:194
  70.8 1.3 convolution_convert_fusion
  72.2 1.5 copy.89
  73.6 4.3 %all-to-all-start.2 = ((bf16[16,11,2048]{2,1,0:T(8,128)(2,1)}), bf16[16,11,2048]{2,1,0:T(8,128)(2,1)}, u32[]{:S(2)}, u32[]{:S(2)}) async-start(bf16[16,11,2048]{2,1,0:T(8,128)(2,1)} %copy.89), calls=%async_computation.3 | async-start | bytes 2097152 | tf_op jit(solution)/shard_map/all_to_all | solution.py:157
  78.3 13.0 %reduce-scatter.3.cloned.1.call-done = f32[16,2048]{1,0:T(8,128)} async-done(((f32[64,2048]{1,0:T(8,128)}), f32[16,2048]{1,0:T(8,128)}) %reduce-scatter.3.cloned.1.call-update) | async-done | bytes 131088 | tf_op jit(solution)/shard_map/reduce_scatter | solution.py:153
  91.3 1.0 fusion.67
  92.8 1.4 copy.83
  94.2 14.0 %all-to-all-done.2 = bf16[16,11,2048]{2,1,0:T(8,128)(2,1)} async-done(((bf16[16,11,2048]{2,1,0:T(8,128)(2,1)}), bf16[16,11,2048]{2,1,0:T(8,128)(2,1)}, u32[]{:S(2)}, u32[]{:S(2)}) %all-to-all-start.2) | async-done | bytes 720928 | tf_op jit(solution)/shard_map/all_to_all | solution.py:157
  108.3 4.3 %all-to-all-start = ((bf16[16,11,2048]{2,1,0:T(8,128)(2,1)}), bf16[16,11,2048]{2,1,0:T(8,128)(2,1)}, u32[]{:S(2)}, u32[]{:S(2)}) async-start(bf16[16,11,2048]{2,1,0:T(8,128)(2,1)} %copy.83), calls=%async_computation.1 | async-start | bytes 2097152 | tf_op jit(solution)/shard_map/all_to_all | solution.py:157
  112.6 4.4 %fusion.2 = f32[16,11,768]{2,0,1:T(8,128)} fusion(bf16[1,768,2048]{2,1,0:T(8,128)(2,1)} %param.31, bf16[16,11,2048]{2,1,0:T(8,128)(2,1)} %all-to-all-done.2), kind=kOutput, calls=%fused_computation.2 | convolution fusion | flops 553648128 | bytes 4407296 | tf_op jit(solution)/shard_map/scw,fw->scf/dot_general | solution.py:232
  117.0 22.5 %all-to-all-done = bf16[16,11,2048]{2,1,0:T(8,128)(2,1)} async-done(((bf16[16,11,2048]{2,1,0:T(8,128)(2,1)}), bf16[16,11,2048]{2,1,0:T(8,128)(2,1)}, u32[]{:S(2)}, u32[]{:S(2)}) %all-to-all-start) | async-done | bytes 720928 | tf_op jit(solution)/shard_map/all_to_all | solution.py:157
  139.6 3.3 %fusion.12 = f32[16,11,768]{2,0,1:T(8,128)S(1)} fusion(bf16[1,2048,768]{2,1,0:T(8,128)(2,1)} %param.29, bf16[16,11,2048]{2,1,0:T(8,128)(2,1)} %all-to-all-done), kind=kOutput, calls=%fused_computation.12 | convolution fusion | flops 553648128 | bytes 4407296 | tf_op jit(solution)/shard_map/scw,wf->scf/dot_general | solution.py:225
  142.9 1.2 fusion.6
  144.1 2.5 fusion.8
  146.6 1.2 fusion.20
  147.8 1.5 copy.91
  149.3 4.3 %all-to-all-start.3 = ((bf16[16,11,2048]{2,1,0:T(8,128)(2,1)}), bf16[16,11,2048]{2,1,0:T(8,128)(2,1)}, u32[]{:S(2)}, u32[]{:S(2)}) async-start(bf16[16,11,2048]{2,1,0:T(8,128)(2,1)} %copy.91), calls=%async_computation.4 | async-start | bytes 2097152 | tf_op jit(solution)/shard_map/all_to_all | solution.py:161
  153.6 3.0 %fusion.17 = bf16[16,11,2048]{2,0,1:T(8,128)(2,1)S(1)} fusion(bf16[1,768,2048]{2,1,0:T(8,128)(2,1)} %param.31, f32[16,11,768]{2,0,1:T(8,128)} %copy-done.6, f32[16,11,768]{2,0,1:T(8,128)} %copy-done.5), kind=kOutput, calls=%fused_computation.15 | convolution fusion | flops 554819584 | bytes 4947968 | tf_op jit(solution)/shard_map/scf,fw->scw/dot_general | solution.py:229
  156.6 1.4 copy.86
  158.0 22.6 %all-to-all-done.3 = bf16[16,11,2048]{2,1,0:T(8,128)(2,1)} async-done(((bf16[16,11,2048]{2,1,0:T(8,128)(2,1)}), bf16[16,11,2048]{2,1,0:T(8,128)(2,1)}, u32[]{:S(2)}, u32[]{:S(2)}) %all-to-all-start.3) | async-done | bytes 720928 | tf_op jit(solution)/shard_map/all_to_all | solution.py:161
  180.6 4.5 %all-to-all-start.1 = ((bf16[16,11,2048]{2,1,0:T(8,128)(2,1)}), bf16[16,11,2048]{2,1,0:T(8,128)(2,1)}, u32[]{:S(2)}, u32[]{:S(2)}) async-start(bf16[16,11,2048]{2,1,0:T(8,128)(2,1)} %copy.86), calls=%async_computation.2 | async-start | bytes 2097152 | tf_op jit(solution)/shard_map/all_to_all | solution.py:161
  185.2 1.6 fusion.55
  187.3 1.0 fusion.116
  188.3 30.5 %all_gather.11 = bf16[64,2048]{1,0:T(8,128)(2,1)S(1)} all-gather(bf16[16,2048]{1,0:T(8,128)(2,1)S(1)} %fusion.116), channel_id=1, replica_groups=mesh['groups'=2,'expert'=4,'head'=4] {'head'}, dimensions={0}, use_global_device_ids=true | all-gather | bytes 327680 | tf_op jit(solution)/shard_map/all_gather | solution.py:149
  218.7 3.0 %convolution_convert_fusion.3 = bf16[64,512]{1,0:T(8,128)(2,1)} fusion(bf16[64,2048]{1,0:T(8,128)(2,1)S(1)} %all_gather.11, bf16[512,2048]{1,0:T(8,128)(2,1)} %param.28), kind=kOutput, calls=%fused_computation.38 | convolution fusion | flops 134250496 | bytes 2424832 | tf_op jit(solution)/shard_map/td,fd->tf/dot_general | solution.py:124
  221.7 1.5 reshape.90
  223.2 1.7 convolution_bitcast_fusion.2
  224.8 1.8 convolution_bitcast_fusion.3
  226.7 3.0 %convolution_bitcast_fusion.4 = f32[4,48,128]{2,1,0:T(8,128)} fusion(f32[4,4,16,48]{3,2,1,0:T(8,128)} %convolution_bitcast_fusion.2, bf16[4,16,4,128]{3,2,1,0:T(4,128)(2,1)} %copy-done.12, f32[4,4,16,48]{3,2,1,0:T(8,128)} %get-tuple-element.9, f32[4,4,16]{2,1,0:T(4,128)} %copy-done.27), kind=kOutput, calls=%fused_computation.37 | convolution fusion | flops 3232047 | bytes 263168 | tf_op jit(solution)/shard_map/shbk,sbhd->skd/dot_general | solution.py:58
  229.7 1.4 slice.19
  231.1 1.4 slice.18
  232.4 2.9 %fusion.35 = bf16[4,16,4,128]{3,1,2,0:T(8,128)(2,1)} fusion(f32[4,4,16,48]{3,2,1,0:T(8,128)} %convolution_bitcast_fusion.2, bf16[4,16,128]{2,1,0:T(8,128)(2,1)} %bitcast.110, bf16[4,32,128]{2,1,0:T(8,128)(2,1)} %copy-done.15, f32[4,4,16,48]{3,2,1,0:T(8,128)} %get-tuple-element.9, f32[4,4,16]{2,1,0:T(4,128)} %copy-done.27), kind=kOutput, calls=%fused_computation.42 | convolution fusion | flops 3363119 | bytes 214016 | tf_op jit(solution)/shard_map/shbk,skd->sbhd/dot_general | solution.py:55
  235.3 0.9 copy.96
  236.2 2.3 fusion.38
  238.5 3.2 %convolution_add_fusion = f32[64,2048]{1,0:T(8,128)} fusion(f32[64,2048]{1,0:T(8,128)S(1)} %fusion.38, bf16[2048,512]{1,0:T(8,128)(2,1)} %param.26, bf16[8,8,4,128]{3,2,1,0:T(4,128)(2,1)S(1)} %bitcast.103), kind=kOutput, calls=%fused_computation.19 | convolution fusion | flops 134348800 | bytes 3211264 | tf_op jit(solution)/shard_map/tf,df->td/dot_general | solution.py:143
  241.7 2.4 fusion.25
  244.2 19.9 %reduce-scatter.5.cloned.1.call-done = f32[16,2048]{1,0:T(8,128)} async-done(((f32[64,2048]{1,0:T(8,128)}), f32[16,2048]{1,0:T(8,128)}) %reduce-scatter.5.cloned.1.call-update) | async-done | bytes 131088 | tf_op jit(solution)/shard_map/reduce_scatter | solution.py:153
  264.0 1.1 fusion.60
  265.2 1.7 fusion.64
  (87 shorter events, 7.2 us)
Async XLA Ops:
  7.2 135.8 %copy-start = (bf16[1,2048,768]{2,1,0:T(8,128)(2,1)S(1)}, bf16[1,2048,768]{2,1,0:T(8,128)(2,1)}, u32[]{:S(2)}) copy-start(bf16[1,2048,768]{2,1,0:T(8,128)(2,1)} %param.30) | copy-start | bytes 9437188
  7.2 25.8 %copy-start.16 = (s32[16,8]{0,1:T(8,128)S(1)}, s32[16,8]{0,1:T(8,128)}, u32[]{:S(2)}) copy-start(s32[16,8]{0,1:T(8,128)} %param.19) | copy-start | bytes 1540
  7.2 23.7 %copy-start.25 = (s32[4]{0:T(128)S(1)}, s32[4]{0:T(128)}, u32[]{:S(2)}) copy-start(s32[4]{0:T(128)} %param.21) | copy-start | bytes 52
  7.2 54.9 %all-gather.2.cloned.1.call-start = ((), (), s32[]{:S(2)}) async-start(), calls=%async_computation.6 | async-start | bytes 2621440 | tf_op jit(solution)/shard_map/all_gather | solution.py:187
  7.9 83.4 %reduce-scatter.3.cloned.1.call-start = ((), (), s32[]{:S(2)}) async-start(), calls=%async_computation.7 | async-start | bytes 655360 | tf_op jit(solution)/shard_map/reduce_scatter | solution.py:153
  10.6 0.9 copy-start.20
  30.8 33.6 %copy-start.12 = (bf16[4,16,4,128]{3,2,1,0:T(4,128)(2,1)}, bf16[4,16,4,128]{3,2,1,0:T(4,128)(2,1)S(1)}, u32[]{:S(2)}) copy-start(bf16[4,16,4,128]{3,2,1,0:T(4,128)(2,1)S(1)} %reshape.88) | copy-start | bytes 196612
  32.2 33.8 %copy-start.15 = (bf16[4,32,128]{2,1,0:T(8,128)(2,1)}, bf16[4,32,128]{2,1,0:T(8,128)(2,1)S(1)}, u32[]{:S(2)}) copy-start(bf16[4,32,128]{2,1,0:T(8,128)(2,1)S(1)} %constant_dynamic-slice_fusion) | copy-start | bytes 98308
  33.0 33.1 %copy-start.10 = (bf16[4,32,128]{2,1,0:T(8,128)(2,1)}, bf16[4,32,128]{2,1,0:T(8,128)(2,1)S(1)}, u32[]{:S(2)}) copy-start(bf16[4,32,128]{2,1,0:T(8,128)(2,1)S(1)} %constant_dynamic-slice_fusion.3) | copy-start | bytes 98308
  63.4 0.8 copy-start.7
  63.4 1.0 copy-start.8
  64.4 5.8 %copy-start.17 = (bf16[64,128]{1,0:T(8,128)(2,1)}, bf16[64,128]{1,0:T(8,128)(2,1)S(1)}, u32[]{:S(2)}) copy-start(bf16[64,128]{1,0:T(8,128)(2,1)S(1)} %get-tuple-element.6) | copy-start | bytes 49156
  64.4 5.8 %copy-start.26 = (s32[16]{0:T(128)S(1)}, s32[16]{0:T(128)}, u32[]{:S(2)}) copy-start(s32[16]{0:T(128)} %param.18) | copy-start | bytes 196
  64.4 5.8 %copy-start.13 = (s32[16,8]{0,1:T(8,128)S(1)}, s32[16,8]{0,1:T(8,128)}, u32[]{:S(2)}) copy-start(s32[16,8]{0,1:T(8,128)} %multiply_add_fusion.1) | copy-start | bytes 1540
  64.4 5.8 %copy-start.23 = (f32[16,8]{0,1:T(8,128)S(1)}, f32[16,8]{0,1:T(8,128)}, u32[]{:S(2)}) copy-start(f32[16,8]{0,1:T(8,128)} %param.20) | copy-start | bytes 1540
  66.0 6.1 %copy-start.27 = (f32[4,4,16]{2,1,0:T(4,128)}, f32[4,4,16]{2,1,0:T(4,128)S(1)}, u32[]{:S(2)}) copy-start(f32[4,4,16]{2,1,0:T(4,128)S(1)} %get-tuple-element.8) | copy-start | bytes 3076
  66.0 4.8 %copy-start.4 = (bf16[16,2048]{1,0:T(8,128)(2,1)S(1)}, bf16[16,2048]{1,0:T(8,128)(2,1)}, u32[]{:S(2)}) copy-start(bf16[16,2048]{1,0:T(8,128)(2,1)} %param.17) | copy-start | bytes 196612
  70.2 0.6 copy-start.22
  72.1 19.2 %copy-start.3 = (bf16[16,2048]{1,0:T(8,128)(2,1)S(1)}, bf16[16,2048]{1,0:T(8,128)(2,1)}, u32[]{:S(2)}) copy-start(bf16[16,2048]{1,0:T(8,128)(2,1)} %param.16) | copy-start | bytes 196612
  72.2 20.2 %copy-start.14 = (f32[2048]{0:T(1024)S(1)}, f32[2048]{0:T(1024)}, u32[]{:S(2)}) copy-start(f32[2048]{0:T(1024)} %param.25) | copy-start | bytes 24580
  73.6 34.6 %all-to-all-start.2 = ((bf16[16,11,2048]{2,1,0:T(8,128)(2,1)}), bf16[16,11,2048]{2,1,0:T(8,128)(2,1)}, u32[]{:S(2)}, u32[]{:S(2)}) async-start(bf16[16,11,2048]{2,1,0:T(8,128)(2,1)} %copy.89), calls=%async_computation.3 | async-start | bytes 2097152 | tf_op jit(solution)/shard_map/all_to_all | solution.py:157
  78.3 29.9 %copy-start.9 = (pred[16,11,16]{2,1,0:T(8,128)(4,1)}, pred[16,11,16]{2,1,0:T(8,128)(4,1)S(1)}, u32[]{:S(2)}) copy-start(pred[16,11,16]{2,1,0:T(8,128)(4,1)S(1)} %compare_reduce_fusion) | copy-start | bytes 8452
  92.4 15.9 %copy-start.18 = (f32[16]{0:T(128)}, f32[16]{0:T(128)S(1)}, u32[]{:S(2)}) copy-start(f32[16]{0:T(128)S(1)} %add_rsqrt_fusion) | copy-start | bytes 196
  108.3 31.3 %all-to-all-start = ((bf16[16,11,2048]{2,1,0:T(8,128)(2,1)}), bf16[16,11,2048]{2,1,0:T(8,128)(2,1)}, u32[]{:S(2)}, u32[]{:S(2)}) async-start(bf16[16,11,2048]{2,1,0:T(8,128)(2,1)} %copy.83), calls=%async_computation.1 | async-start | bytes 2097152 | tf_op jit(solution)/shard_map/all_to_all | solution.py:157
  139.6 3.4 %copy-start.2 = (f32[16,11,768]{2,0,1:T(8,128)S(1)}, f32[16,11,768]{2,0,1:T(8,128)}, u32[]{:S(2)}) copy-start(f32[16,11,768]{2,0,1:T(8,128)} %fusion.2) | copy-start | bytes 1622020
  142.9 3.7 %copy-start.5 = (f32[16,11,768]{2,0,1:T(8,128)}, f32[16,11,768]{2,0,1:T(8,128)S(1)}, u32[]{:S(2)}) copy-start(f32[16,11,768]{2,0,1:T(8,128)S(1)} %fusion.12) | copy-start | bytes 1622020
  144.1 2.5 copy-start.1
  146.6 1.2 copy-start.6
  149.3 31.3 %all-to-all-start.3 = ((bf16[16,11,2048]{2,1,0:T(8,128)(2,1)}), bf16[16,11,2048]{2,1,0:T(8,128)(2,1)}, u32[]{:S(2)}, u32[]{:S(2)}) async-start(bf16[16,11,2048]{2,1,0:T(8,128)(2,1)} %copy.91), calls=%async_computation.4 | async-start | bytes 2097152 | tf_op jit(solution)/shard_map/all_to_all | solution.py:161
  180.6 61.2 %all-to-all-start.1 = ((bf16[16,11,2048]{2,1,0:T(8,128)(2,1)}), bf16[16,11,2048]{2,1,0:T(8,128)(2,1)}, u32[]{:S(2)}, u32[]{:S(2)}) async-start(bf16[16,11,2048]{2,1,0:T(8,128)(2,1)} %copy.86), calls=%async_computation.2 | async-start | bytes 2097152 | tf_op jit(solution)/shard_map/all_to_all | solution.py:161
  185.1 78.9 %reduce-scatter.5.cloned.1.call-start = ((), (), s32[]{:S(2)}) async-start(), calls=%async_computation.8 | async-start | bytes 655360 | tf_op jit(solution)/shard_map/reduce_scatter | solution.py:153
  186.8 0.5 copy-start.24
  238.5 25.5 %copy-start.11 = (f32[2048]{0:T(1024)S(1)}, f32[2048]{0:T(1024)}, u32[]{:S(2)}) copy-start(f32[2048]{0:T(1024)} %param.24) | copy-start | bytes 24580
  238.5 25.5 %copy-start.21 = (f32[16]{0:T(128)S(1)}, f32[16]{0:T(128)}, u32[]{:S(2)}) copy-start(f32[16]{0:T(128)} %copy-done.20) | copy-start | bytes 196
  238.5 26.6 %copy-start.19 = (f32[16]{0:T(128)S(1)}, f32[16]{0:T(128)}, u32[]{:S(2)}) copy-start(f32[16]{0:T(128)} %copy-done.18) | copy-start | bytes 196
Sparse Core Ops, SparseCore 0:
  9.6 52.4 all-gather.1
  70.3 21.0 reduce-scatter.2
  241.8 22.1 reduce-scatter.4

commit v4 on v3

--- a/solution.py
+++ b/solution.py
@@ -65,7 +65,14 @@
 
 
 def attention_forward(
-    row_block, query_weights, kv_weights, key_cache, prefix_value_cache, lengths, first_head
+    row_block,
+    query_weights,
+    kv_weights,
+    own_kv_weights,
+    key_cache,
+    prefix_value_cache,
+    lengths,
+    first_head,
 ):
     heads_here = query_weights.shape[1] // HEAD_SIZE
     query_group_count = QUERY_HEADS // KEY_VALUE_HEADS
@@ -94,8 +101,16 @@
         ],
         axis=1,
     )
-    pair_rows = jnp.dot(row_block, pair_weights, preferred_element_type=jnp.float32).astype(
+    own_rows = jnp.dot(row_block, own_kv_weights, preferred_element_type=jnp.float32).astype(
         jnp.bfloat16
+    )
+    kv_rows = lax.all_gather(own_rows, "head", axis=1, tiled=True)
+    pair_rows = jnp.concatenate(
+        [
+            lax.dynamic_slice_in_dim(kv_rows, kv_now * HEAD_SIZE, HEAD_SIZE, 1),
+            lax.dynamic_slice_in_dim(kv_rows, key_value_width + kv_now * HEAD_SIZE, HEAD_SIZE, 1),
+        ],
+        axis=1,
     )
     key_rows = jnp.concatenate(
         [
@@ -189,7 +204,7 @@
     first_head = lax.axis_index("head") * heads_here
     gathered_rows = head_rows(attn_rows)
     attended, saved = attention_forward(
-        gathered_rows, w_query, kv_full, key_cache, prefix_value_cache, cache_lengths, first_head
+        gathered_rows, w_query, kv_full, key_value_weight, key_cache, prefix_value_cache, cache_lengths, first_head
     )
     mixed = head_sums(jnp.dot(attended, w_output, preferred_element_type=jnp.float32))
     hidden = (hidden_in.astype(jnp.float32) + mixed).astype(jnp.bfloat16)

time: 275 us -> 267 us (0.971)
  waiting for transfers between devices: 121 us -> 110 us
  blocking collectives: 47.6 us -> 58.1 us
  matrix products: 47.2 us -> 43.7 us
  local copies, waits for them, and re-layouts: 16.9 us -> 13.6 us
    all_gather x1, waiting for transfers between devices: 28.5 us -> 0.01 us  [body(): kv_full = lax.all_gather(key_value_weight, 'head', axis=1, tiled=True)]
    all_gather x0 -> x1, blocking collectives: none -> 12.1 us  [attention_forward(): kv_rows = lax.all_gather(own_rows, 'head', axis=1, tiled=True)]
    all_to_all x2, waiting for transfers between devices: 36.5 us -> 46.6 us  [to_experts(): lax.all_to_all(outgoing, ('expert', 'head'), split_axis=0, concat_axis=0,...]
    reduce_scatter x2, waiting for transfers between devices: 32.9 us -> 42.5 us  [head_sums(): lax.psum_scatter(partial_rows, 'head', scatter_dimension=0, tiled=True)]
  transfers between devices with their start and end apart: 7 -> 7, of which waited for: 6 -> 5; matrix products, arithmetic and copies ran while one was open for 19% -> 19% of each run, Pallas kernels for 0% -> 0%
where the time goes in v4:
time: 267 us; the launch traced here: 266 us
  waiting for transfers between devices  110 us (41%)
  blocking collectives  58.1 us (22%)
  matrix products  43.7 us (16%)
  starting transfers between devices  18.3 us (7%)
  between operations  14.3 us (5%)
  local copies, waits for them, and re-layouts  13.6 us (5%)
  other arithmetic  8 us (3%)
    all_to_all x2, waiting for transfers between devices, to_experts(): lax.all_to_all(outgoing, ('expert', 'head'), split_axis=0, concat_axis=0,...  46.6 us
    all_gather x2, blocking collectives, head_rows(): return lax.all_gather(row_block, 'head', axis=0, tiled=True)  46 us
    reduce_scatter x2, waiting for transfers between devices, head_sums(): lax.psum_scatter(partial_rows, 'head', scatter_dimension=0, tiled=True)  42.5 us
    all_to_all x2, waiting for transfers between devices, from_experts(): lax.all_to_all(results, ('expert', 'head'), split_axis=0, concat_axis=0,...  20.2 us
    all_gather x1, blocking collectives, attention_forward(): kv_rows = lax.all_gather(own_rows, 'head', axis=1, tiled=True)  12.1 us
    all_to_all x2, starting transfers between devices, to_experts(): lax.all_to_all(outgoing, ('expert', 'head'), split_axis=0, concat_axis=0,...  9.31 us
    all_to_all x2, starting transfers between devices, from_experts(): lax.all_to_all(results, ('expert', 'head'), split_axis=0, concat_axis=0,...  8.86 us
  transfers between devices with their start and end apart: 7, of which 5 were waited for; matrix products, arithmetic and copies ran while one was open for 19% of the time, Pallas kernels for 0%

profile of v4, /device:TPU:0, one launch (start us, length us, event | category | flops | bytes accessed | tf_op | source)
XLA Modules:
  0.0 266.2 jit_solution(12603720725292792029)
XLA Ops:
  7.3 1.1 fusion.68
  8.4 0.9 fusion.62
  9.4 15.6 %all_gather.12 = bf16[64,2048]{1,0:T(8,128)(2,1)S(1)} all-gather(bf16[16,2048]{1,0:T(8,128)(2,1)S(1)} %fusion.62), channel_id=1, replica_groups=mesh['groups'=2,'expert'=4,'head'=4] {'head'}, dimensions={0}, use_global_device_ids=true | all-gather | bytes 327680 | tf_op jit(solution)/shard_map/all_gather | solution.py:164
  25.0 1.3 convolution_convert_fusion.6
  26.3 12.1 %all_gather.13 = bf16[64,512]{1,0:T(8,128)(2,1)S(1)} all-gather(bf16[64,128]{1,0:T(8,128)(2,1)S(1)} %convolution_convert_fusion.6), channel_id=1, replica_groups=mesh['groups'=2,'expert'=4,'head'=4] {'head'}, dimensions={1}, use_global_device_ids=true | all-gather | bytes 81920 | tf_op jit(solution)/shard_map/all_gather | solution.py:107
  38.3 2.1 convolution_convert_fusion.5
  41.5 2.9 %fusion.78 = f32[64,2048]{1,0:T(8,128)} fusion(bf16[512,2048]{1,0:T(8,128)(2,1)} %param.28, bf16[8,8,4,128]{3,2,1,0:T(4,128)(2,1)S(1)} %bitcast.105), kind=kOutput, calls=%fused_computation.96 | convolution fusion | flops 134217728 | bytes 2686976 | tf_op jit(solution)/shard_map/dot_general | solution.py:209
  45.8 1.3 convolution_convert_fusion
  47.2 1.4 copy.89
  48.6 5.0 %all-to-all-start.2 = ((bf16[16,11,2048]{2,1,0:T(8,128)(2,1)}), bf16[16,11,2048]{2,1,0:T(8,128)(2,1)}, u32[]{:S(2)}, u32[]{:S(2)}) async-start(bf16[16,11,2048]{2,1,0:T(8,128)(2,1)} %copy.89), calls=%async_computation.3 | async-start | bytes 2097152 | tf_op jit(solution)/shard_map/all_to_all | solution.py:172
  53.9 22.7 %reduce-scatter.3.cloned.1.call-done = f32[16,2048]{1,0:T(8,128)} async-done(((f32[64,2048]{1,0:T(8,128)}), f32[16,2048]{1,0:T(8,128)}) %reduce-scatter.3.cloned.1.call-update) | async-done | bytes 131088 | tf_op jit(solution)/shard_map/reduce_scatter | solution.py:168
  76.6 1.0 fusion.70
  78.1 1.4 copy.83
  79.5 6.8 %all-to-all-done.2 = bf16[16,11,2048]{2,1,0:T(8,128)(2,1)} async-done(((bf16[16,11,2048]{2,1,0:T(8,128)(2,1)}), bf16[16,11,2048]{2,1,0:T(8,128)(2,1)}, u32[]{:S(2)}, u32[]{:S(2)}) %all-to-all-start.2) | async-done | bytes 720928 | tf_op jit(solution)/shard_map/all_to_all | solution.py:172
  86.2 4.3 %all-to-all-start = ((bf16[16,11,2048]{2,1,0:T(8,128)(2,1)}), bf16[16,11,2048]{2,1,0:T(8,128)(2,1)}, u32[]{:S(2)}, u32[]{:S(2)}) async-start(bf16[16,11,2048]{2,1,0:T(8,128)(2,1)} %copy.83), calls=%async_computation.1 | async-start | bytes 2097152 | tf_op jit(solution)/shard_map/all_to_all | solution.py:172
  90.6 0.7 all-gather.2.cloned.1.call-update
  91.3 4.5 %fusion.2 = f32[16,11,768]{2,0,1:T(8,128)} fusion(bf16[1,768,2048]{2,1,0:T(8,128)(2,1)} %param.31, bf16[16,11,2048]{2,1,0:T(8,128)(2,1)} %all-to-all-done.2), kind=kOutput, calls=%fused_computation.2 | convolution fusion | flops 553648128 | bytes 4407296 | tf_op jit(solution)/shard_map/scw,fw->scf/dot_general | solution.py:247
  95.8 39.9 %all-to-all-done = bf16[16,11,2048]{2,1,0:T(8,128)(2,1)} async-done(((bf16[16,11,2048]{2,1,0:T(8,128)(2,1)}), bf16[16,11,2048]{2,1,0:T(8,128)(2,1)}, u32[]{:S(2)}, u32[]{:S(2)}) %all-to-all-start) | async-done | bytes 720928 | tf_op jit(solution)/shard_map/all_to_all | solution.py:172
  135.7 3.3 %fusion.12 = f32[16,11,768]{2,0,1:T(8,128)S(1)} fusion(bf16[1,2048,768]{2,1,0:T(8,128)(2,1)} %param.29, bf16[16,11,2048]{2,1,0:T(8,128)(2,1)} %all-to-all-done), kind=kOutput, calls=%fused_computation.12 | convolution fusion | flops 553648128 | bytes 4407296 | tf_op jit(solution)/shard_map/scw,wf->scf/dot_general | solution.py:240
  139.0 2.5 fusion.8
  141.6 1.2 fusion.6
  142.8 0.9 copy-done.2
  143.7 1.2 fusion.20
  144.8 1.4 copy.91
  146.2 4.3 %all-to-all-start.3 = ((bf16[16,11,2048]{2,1,0:T(8,128)(2,1)}), bf16[16,11,2048]{2,1,0:T(8,128)(2,1)}, u32[]{:S(2)}, u32[]{:S(2)}) async-start(bf16[16,11,2048]{2,1,0:T(8,128)(2,1)} %copy.91), calls=%async_computation.4 | async-start | bytes 2097152 | tf_op jit(solution)/shard_map/all_to_all | solution.py:176
  150.6 3.0 %fusion.17 = bf16[16,11,2048]{2,0,1:T(8,128)(2,1)S(1)} fusion(bf16[1,768,2048]{2,1,0:T(8,128)(2,1)} %param.31, f32[16,11,768]{2,0,1:T(8,128)} %copy-done.7, f32[16,11,768]{2,0,1:T(8,128)} %copy-done.6), kind=kOutput, calls=%fused_computation.15 | convolution fusion | flops 554819584 | bytes 4947968 | tf_op jit(solution)/shard_map/scf,fw->scw/dot_general | solution.py:244
  153.5 1.4 copy.86
  155.0 2.3 constant_dynamic-slice_fusion
  157.3 20.2 %all-to-all-done.3 = bf16[16,11,2048]{2,1,0:T(8,128)(2,1)} async-done(((bf16[16,11,2048]{2,1,0:T(8,128)(2,1)}), bf16[16,11,2048]{2,1,0:T(8,128)(2,1)}, u32[]{:S(2)}, u32[]{:S(2)}) %all-to-all-start.3) | async-done | bytes 720928 | tf_op jit(solution)/shard_map/all_to_all | solution.py:176
  177.5 4.5 %all-to-all-start.1 = ((bf16[16,11,2048]{2,1,0:T(8,128)(2,1)}), bf16[16,11,2048]{2,1,0:T(8,128)(2,1)}, u32[]{:S(2)}, u32[]{:S(2)}) async-start(bf16[16,11,2048]{2,1,0:T(8,128)(2,1)} %copy.86), calls=%async_computation.2 | async-start | bytes 2097152 | tf_op jit(solution)/shard_map/all_to_all | solution.py:176
  182.1 1.6 fusion.58
  183.8 0.6 copy-done.24
  184.3 1.0 fusion.118
  185.3 30.4 %all_gather.14 = bf16[64,2048]{1,0:T(8,128)(2,1)S(1)} all-gather(bf16[16,2048]{1,0:T(8,128)(2,1)S(1)} %fusion.118), channel_id=1, replica_groups=mesh['groups'=2,'expert'=4,'head'=4] {'head'}, dimensions={0}, use_global_device_ids=true | all-gather | bytes 327680 | tf_op jit(solution)/shard_map/all_gather | solution.py:164
  215.7 3.0 %convolution_convert_fusion.3 = bf16[64,512]{1,0:T(8,128)(2,1)} fusion(bf16[64,2048]{1,0:T(8,128)(2,1)S(1)} %all_gather.14, bf16[512,2048]{1,0:T(8,128)(2,1)} %param.28), kind=kOutput, calls=%fused_computation.38 | convolution fusion | flops 134250496 | bytes 2424832 | tf_op jit(solution)/shard_map/td,fd->tf/dot_general | solution.py:139
  218.7 1.5 reshape.90
  220.1 1.7 convolution_bitcast_fusion.2
  221.8 2.9 %fusion.35 = bf16[4,16,4,128]{3,1,2,0:T(8,128)(2,1)} fusion(f32[4,4,16,48]{3,2,1,0:T(8,128)} %convolution_bitcast_fusion.2, bf16[4,16,128]{2,1,0:T(8,128)(2,1)} %bitcast.111, bf16[4,32,128]{2,1,0:T(8,128)(2,1)} %copy-done.13, f32[4,4,16,48]{3,2,1,0:T(8,128)} %copy-done.27, f32[4,4,16]{2,1,0:T(4,128)} %copy-done.28), kind=kOutput, calls=%fused_computation.42 | convolution fusion | flops 3363119 | bytes 214016 | tf_op jit(solution)/shard_map/shbk,skd->sbhd/dot_general | solution.py:55
  224.7 3.0 %convolution_bitcast_fusion.4 = f32[4,48,128]{2,1,0:T(8,128)} fusion(f32[4,4,16,48]{3,2,1,0:T(8,128)} %convolution_bitcast_fusion.2, bf16[4,16,4,128]{3,2,1,0:T(4,128)(2,1)} %copy-done.11, f32[4,4,16,48]{3,2,1,0:T(8,128)} %copy-done.27, f32[4,4,16]{2,1,0:T(4,128)} %copy-done.28), kind=kOutput, calls=%fused_computation.37 | convolution fusion | flops 3232047 | bytes 263168 | tf_op jit(solution)/shard_map/shbk,sbhd->skd/dot_general | solution.py:58
  227.7 1.0 copy.96
  228.8 0.8 slice.8
  229.5 1.2 convolution_bitcast_fusion.3
  230.7 2.3 fusion.36
  233.0 1.6 convolution_add_fusion
  234.7 2.4 fusion.25
  237.1 19.8 %reduce-scatter.5.cloned.1.call-done = f32[16,2048]{1,0:T(8,128)} async-done(((f32[64,2048]{1,0:T(8,128)}), f32[16,2048]{1,0:T(8,128)}) %reduce-scatter.5.cloned.1.call-update) | async-done | bytes 131088 | tf_op jit(solution)/shard_map/reduce_scatter | solution.py:168
  256.9 1.1 fusion.63
  258.0 1.7 fusion.67
  (92 shorter events, 3.3 us)
Async XLA Ops:
  7.2 131.8 %copy-start = (bf16[1,2048,768]{2,1,0:T(8,128)(2,1)S(1)}, bf16[1,2048,768]{2,1,0:T(8,128)(2,1)}, u32[]{:S(2)}) copy-start(bf16[1,2048,768]{2,1,0:T(8,128)(2,1)} %param.30) | copy-start | bytes 9437188
  7.2 33.3 %copy-start.25 = (s32[4]{0:T(128)S(1)}, s32[4]{0:T(128)}, u32[]{:S(2)}) copy-start(s32[4]{0:T(128)} %param.21) | copy-start | bytes 52
  7.2 33.3 %copy-start.15 = (bf16[4,32,256]{2,1,0:T(8,128)(2,1)S(1)}, bf16[4,32,256]{2,1,0:T(8,128)(2,1)}, u32[]{:S(2)}) copy-start(bf16[4,32,256]{2,1,0:T(8,128)(2,1)} %param.22) | copy-start | bytes 196612
  7.2 33.3 %copy-start.16 = (bf16[4,32,256]{2,1,0:T(8,128)(2,1)S(1)}, bf16[4,32,256]{2,1,0:T(8,128)(2,1)}, u32[]{:S(2)}) copy-start(bf16[4,32,256]{2,1,0:T(8,128)(2,1)} %param.23) | copy-start | bytes 196612
  7.2 69.4 %reduce-scatter.3.cloned.1.call-start = ((), (), s32[]{:S(2)}) async-start(), calls=%async_computation.6 | async-start | bytes 655360 | tf_op jit(solution)/shard_map/reduce_scatter | solution.py:168
  8.4 17.8 %copy-start.20 = (f32[16]{0:T(128)}, f32[16]{0:T(128)S(1)}, u32[]{:S(2)}) copy-start(f32[16]{0:T(128)S(1)} %add_rsqrt_fusion.1) | copy-start | bytes 196
  40.4 4.0 %copy-start.11 = (bf16[4,16,4,128]{3,2,1,0:T(4,128)(2,1)}, bf16[4,16,4,128]{3,2,1,0:T(4,128)(2,1)S(1)}, u32[]{:S(2)}) copy-start(bf16[4,16,4,128]{3,2,1,0:T(4,128)(2,1)S(1)} %reshape.88) | copy-start | bytes 196612
  40.6 0.6 copy-start.13
  40.6 3.8 %copy-start.9 = (bf16[4,32,128]{2,1,0:T(8,128)(2,1)}, bf16[4,32,128]{2,1,0:T(8,128)(2,1)S(1)}, u32[]{:S(2)}) copy-start(bf16[4,32,128]{2,1,0:T(8,128)(2,1)S(1)} %constant_dynamic-slice_fusion.5) | copy-start | bytes 98308
  40.6 0.6 copy-start.17
  40.7 3.8 %copy-start.14 = (s32[16,8]{0,1:T(8,128)S(1)}, s32[16,8]{0,1:T(8,128)}, u32[]{:S(2)}) copy-start(s32[16,8]{0,1:T(8,128)} %param.19) | copy-start | bytes 1540
  41.0 4.0 %copy-start.27 = (f32[4,4,16,48]{3,2,1,0:T(8,128)}, f32[4,4,16,48]{3,2,1,0:T(8,128)S(1)}, u32[]{:S(2)}) copy-start(f32[4,4,16,48]{3,2,1,0:T(8,128)S(1)} %get-tuple-element.9) | copy-start | bytes 147460
  41.0 4.0 %copy-start.28 = (f32[4,4,16]{2,1,0:T(4,128)}, f32[4,4,16]{2,1,0:T(4,128)S(1)}, u32[]{:S(2)}) copy-start(f32[4,4,16]{2,1,0:T(4,128)S(1)} %get-tuple-element.8) | copy-start | bytes 3076
  41.2 4.0 %copy-start.26 = (s32[16]{0:T(128)S(1)}, s32[16]{0:T(128)}, u32[]{:S(2)}) copy-start(s32[16]{0:T(128)} %param.18) | copy-start | bytes 196
  41.2 4.0 %copy-start.23 = (f32[16,8]{0,1:T(8,128)S(1)}, f32[16,8]{0,1:T(8,128)}, u32[]{:S(2)}) copy-start(f32[16,8]{0,1:T(8,128)} %param.20) | copy-start | bytes 1540
  41.2 4.6 %copy-start.5 = (bf16[16,2048]{1,0:T(8,128)(2,1)S(1)}, bf16[16,2048]{1,0:T(8,128)(2,1)}, u32[]{:S(2)}) copy-start(bf16[16,2048]{1,0:T(8,128)(2,1)} %param.17) | copy-start | bytes 196612
  45.3 0.5 copy-start.22
  47.1 29.5 %copy-start.4 = (bf16[16,2048]{1,0:T(8,128)(2,1)S(1)}, bf16[16,2048]{1,0:T(8,128)(2,1)}, u32[]{:S(2)}) copy-start(bf16[16,2048]{1,0:T(8,128)(2,1)} %param.16) | copy-start | bytes 196612
  47.1 30.5 %copy-start.12 = (f32[2048]{0:T(1024)S(1)}, f32[2048]{0:T(1024)}, u32[]{:S(2)}) copy-start(f32[2048]{0:T(1024)} %param.25) | copy-start | bytes 24580
  48.6 37.7 %all-to-all-start.2 = ((bf16[16,11,2048]{2,1,0:T(8,128)(2,1)}), bf16[16,11,2048]{2,1,0:T(8,128)(2,1)}, u32[]{:S(2)}, u32[]{:S(2)}) async-start(bf16[16,11,2048]{2,1,0:T(8,128)(2,1)} %copy.89), calls=%async_computation.3 | async-start | bytes 2097152 | tf_op jit(solution)/shard_map/all_to_all | solution.py:172
  53.9 32.4 %copy-start.8 = (pred[16,11,16]{2,1,0:T(8,128)(4,1)}, pred[16,11,16]{2,1,0:T(8,128)(4,1)S(1)}, u32[]{:S(2)}) copy-start(pred[16,11,16]{2,1,0:T(8,128)(4,1)S(1)} %compare_reduce_fusion) | copy-start | bytes 8452
  77.7 8.6 %copy-start.18 = (f32[16]{0:T(128)}, f32[16]{0:T(128)S(1)}, u32[]{:S(2)}) copy-start(f32[16]{0:T(128)S(1)} %add_rsqrt_fusion) | copy-start | bytes 196
  86.2 49.4 %all-to-all-start = ((bf16[16,11,2048]{2,1,0:T(8,128)(2,1)}), bf16[16,11,2048]{2,1,0:T(8,128)(2,1)}, u32[]{:S(2)}, u32[]{:S(2)}) async-start(bf16[16,11,2048]{2,1,0:T(8,128)(2,1)} %copy.83), calls=%async_computation.1 | async-start | bytes 2097152 | tf_op jit(solution)/shard_map/all_to_all | solution.py:172
  90.6 64.4 %all-gather.2.cloned.1.call-start = ((), (), s32[]{:S(2)}) async-start(), calls=%async_computation.7 | async-start | bytes 2621440 | tf_op jit(solution)/shard_map/all_gather | solution.py:202
  139.0 3.8 %copy-start.6 = (f32[16,11,768]{2,0,1:T(8,128)}, f32[16,11,768]{2,0,1:T(8,128)S(1)}, u32[]{:S(2)}) copy-start(f32[16,11,768]{2,0,1:T(8,128)S(1)} %fusion.12) | copy-start | bytes 1622020
  139.0 2.5 copy-start.3
  141.5 1.2 copy-start.7
  141.6 2.1 copy-start.2
  146.2 31.3 %all-to-all-start.3 = ((bf16[16,11,2048]{2,1,0:T(8,128)(2,1)}), bf16[16,11,2048]{2,1,0:T(8,128)(2,1)}, u32[]{:S(2)}, u32[]{:S(2)}) async-start(bf16[16,11,2048]{2,1,0:T(8,128)(2,1)} %copy.91), calls=%async_computation.4 | async-start | bytes 2097152 | tf_op jit(solution)/shard_map/all_to_all | solution.py:176
  177.5 57.1 %all-to-all-start.1 = ((bf16[16,11,2048]{2,1,0:T(8,128)(2,1)}), bf16[16,11,2048]{2,1,0:T(8,128)(2,1)}, u32[]{:S(2)}, u32[]{:S(2)}) async-start(bf16[16,11,2048]{2,1,0:T(8,128)(2,1)} %copy.86), calls=%async_computation.2 | async-start | bytes 2097152 | tf_op jit(solution)/shard_map/all_to_all | solution.py:176
  182.1 74.8 %reduce-scatter.5.cloned.1.call-start = ((), (), s32[]{:S(2)}) async-start(), calls=%async_computation.8 | async-start | bytes 655360 | tf_op jit(solution)/shard_map/reduce_scatter | solution.py:168
  183.8 0.6 copy-start.24
  221.8 7.7 %copy-start.29 = (f32[4,4,16]{2,1,0:T(4,128)S(1)}, f32[4,4,16]{2,1,0:T(4,128)}, u32[]{:S(2)}) copy-start(f32[4,4,16]{2,1,0:T(4,128)} %copy-done.28) | copy-start | bytes 3076
  227.7 5.3 %copy-start.1 = (bf16[2048,512]{1,0:T(8,128)(2,1)S(1)}, bf16[2048,512]{1,0:T(8,128)(2,1)}, u32[]{:S(2)}) copy-start(bf16[2048,512]{1,0:T(8,128)(2,1)} %param.26) | copy-start | bytes 6291460
  233.0 23.9 %copy-start.10 = (f32[2048]{0:T(1024)S(1)}, f32[2048]{0:T(1024)}, u32[]{:S(2)}) copy-start(f32[2048]{0:T(1024)} %param.24) | copy-start | bytes 24580
  233.0 23.9 %copy-start.21 = (f32[16]{0:T(128)S(1)}, f32[16]{0:T(128)}, u32[]{:S(2)}) copy-start(f32[16]{0:T(128)} %copy-done.20) | copy-start | bytes 196
  233.0 25.0 %copy-start.19 = (f32[16]{0:T(128)S(1)}, f32[16]{0:T(128)}, u32[]{:S(2)}) copy-start(f32[16]{0:T(128)} %copy-done.18) | copy-start | bytes 196
Sparse Core Ops, SparseCore 0:
  44.5 32.0 reduce-scatter.2
  93.0 59.0 all-gather.1
  234.8 22.0 reduce-scatter.4

commit v5 on v4

--- a/solution.py
+++ b/solution.py
@@ -67,7 +67,6 @@
 def attention_forward(
     row_block,
     query_weights,
-    kv_weights,
     own_kv_weights,
     key_cache,
     prefix_value_cache,
@@ -92,15 +91,6 @@
         axis=1,
     )
     kv_now = kv_first + 0
-    pair_weights = jnp.concatenate(
-        [
-            lax.dynamic_slice_in_dim(kv_weights, kv_now * HEAD_SIZE, HEAD_SIZE, 1),
-            lax.dynamic_slice_in_dim(
-                kv_weights, key_value_width + kv_now * HEAD_SIZE, HEAD_SIZE, 1
-            ),
-        ],
-        axis=1,
-    )
     own_rows = jnp.dot(row_block, own_kv_weights, preferred_element_type=jnp.float32).astype(
         jnp.bfloat16
     )
@@ -127,7 +117,7 @@
         axis=1,
     )
     probabilities, probs_low, attended = attend_forward(queries, key_rows, value_rows, usable)
-    saved = [(queries, key_rows, value_rows, probabilities, probs_low, pair_weights)]
+    saved = [(queries, key_rows, value_rows, probabilities, probs_low)]
     joined = attended.reshape(row_count, heads_here * HEAD_SIZE)
     return (joined, saved)
 
@@ -204,9 +194,11 @@
     first_head = lax.axis_index("head") * heads_here
     gathered_rows = head_rows(attn_rows)
     attended, saved = attention_forward(
-        gathered_rows, w_query, kv_full, key_value_weight, key_cache, prefix_value_cache, cache_lengths, first_head
-    )
-    mixed = head_sums(jnp.dot(attended, w_output, preferred_element_type=jnp.float32))
+        gathered_rows, w_query, key_value_weight, key_cache, prefix_value_cache, cache_lengths, first_head
+    )
+    partial_mixed = jnp.dot(attended, w_output, preferred_element_type=jnp.float32)
+    partial_mixed, kv_full = lax.optimization_barrier((partial_mixed, kv_full))
+    mixed = head_sums(partial_mixed)
     hidden = (hidden_in.astype(jnp.float32) + mixed).astype(jnp.bfloat16)
     normed_two, inverse_two = rms_forward(hidden, moe_gain)
     moe_rows = normed_two.astype(jnp.bfloat16)
@@ -233,6 +225,16 @@
         "dct,tw->dcw", weighting, cotangent, precision=highest_prec
     ).astype(jnp.bfloat16)
     rows_in = to_experts(outgoing)
+    kv_now = first_head // (QUERY_HEADS // KEY_VALUE_HEADS)
+    key_value_width = KEY_VALUE_HEADS * HEAD_SIZE
+    pair_weights = jnp.concatenate(
+        [
+            lax.dynamic_slice_in_dim(kv_full, kv_now * HEAD_SIZE, HEAD_SIZE, 1),
+            lax.dynamic_slice_in_dim(kv_full, key_value_width + kv_now * HEAD_SIZE, HEAD_SIZE, 1),
+        ],
+        axis=1,
+    )
+    saved = [saved[0][:5] + (pair_weights,)]
     grads_in = to_experts(grad_out)
     gate_matrix = w_gate[0]
     up_matrix = w_up[0]

time: 267 us -> 274 us (1.026)
  waiting for transfers between devices: 110 us -> 93.5 us
  blocking collectives: 58.1 us -> 68.7 us
  starting transfers between devices: 18.3 us -> 24.2 us
  local copies, waits for them, and re-layouts: 13.6 us -> 17.2 us
  matrix products: 43.7 us -> 46.5 us
    all_to_all x2, waiting for transfers between devices: 46.6 us -> 29.2 us  [to_experts(): lax.all_to_all(outgoing, ('expert', 'head'), split_axis=0, concat_axis=0,...]
    all_gather x1, blocking collectives: 12.1 us -> 21.1 us  [attention_forward(): kv_rows = lax.all_gather(own_rows, 'head', axis=1, tiled=True)]
    all_to_all x2, starting transfers between devices: 9.31 us -> 15.3 us  [to_experts(): lax.all_to_all(outgoing, ('expert', 'head'), split_axis=0, concat_axis=0,...]
  transfers between devices with their start and end apart: 7 -> 7, of which waited for: 5 -> 5; matrix products, arithmetic and copies ran while one was open for 19% -> 21% of each run, Pallas kernels for 0% -> 0%
where the time goes in v5:
time: 274 us; the launch traced here: 273 us
  waiting for transfers between devices  93.5 us (34%)
  blocking collectives  68.7 us (25%)
  matrix products  46.5 us (17%)
  starting transfers between devices  24.2 us (9%)
  local copies, waits for them, and re-layouts  17.2 us (6%)
  between operations  14.2 us (5%)
  other arithmetic  8.56 us (3%)
    all_gather x2, blocking collectives, head_rows(): return lax.all_gather(row_block, 'head', axis=0, tiled=True)  47.5 us
    reduce_scatter x2, waiting for transfers between devices, head_sums(): lax.psum_scatter(partial_rows, 'head', scatter_dimension=0, tiled=True)  43.1 us
    all_to_all x2, waiting for transfers between devices, to_experts(): lax.all_to_all(outgoing, ('expert', 'head'), split_axis=0, concat_axis=0,...  29.2 us
    all_gather x1, blocking collectives, attention_forward(): kv_rows = lax.all_gather(own_rows, 'head', axis=1, tiled=True)  21.1 us
    all_to_all x2, waiting for transfers between devices, from_experts(): lax.all_to_all(results, ('expert', 'head'), split_axis=0, concat_axis=0,...  20.5 us
    all_to_all x2, starting transfers between devices, to_experts(): lax.all_to_all(outgoing, ('expert', 'head'), split_axis=0, concat_axis=0,...  15.3 us
    all_to_all x2, starting transfers between devices, from_experts(): lax.all_to_all(results, ('expert', 'head'), split_axis=0, concat_axis=0,...  8.86 us
  transfers between devices with their start and end apart: 7, of which 5 were waited for; matrix products, arithmetic and copies ran while one was open for 21% of the time, Pallas kernels for 0%

profile of v5, /device:TPU:0, one launch (start us, length us, event | category | flops | bytes accessed | tf_op | source)
XLA Modules:
  0.0 272.8 jit_solution(3601740604765882717)
XLA Ops:
  8.0 0.9 copy.80
  10.2 1.0 fusion.68
  11.2 0.9 fusion.62
  12.1 17.1 %all_gather.12 = bf16[64,2048]{1,0:T(8,128)(2,1)S(1)} all-gather(bf16[16,2048]{1,0:T(8,128)(2,1)S(1)} %fusion.62), channel_id=1, replica_groups=mesh['groups'=2,'expert'=4,'head'=4] {'head'}, dimensions={0}, use_global_device_ids=true | all-gather | bytes 327680 | tf_op jit(solution)/shard_map/all_gather | solution.py:154
  29.2 2.1 convolution_convert_fusion.5
  31.4 1.3 convolution_convert_fusion.6
  32.7 21.1 %all_gather.13 = bf16[64,512]{1,0:T(8,128)(2,1)S(1)} all-gather(bf16[64,128]{1,0:T(8,128)(2,1)S(1)} %convolution_convert_fusion.6), channel_id=1, replica_groups=mesh['groups'=2,'expert'=4,'head'=4] {'head'}, dimensions={1}, use_global_device_ids=true | all-gather | bytes 81920 | tf_op jit(solution)/shard_map/all_gather | solution.py:97
  56.0 0.9 fusion.120
  56.9 1.2 fusion.34
  58.8 2.9 %fusion.78 = f32[64,2048]{1,0:T(8,128)} fusion(bf16[512,2048]{1,0:T(8,128)(2,1)} %param.28, bf16[8,8,4,128]{3,2,1,0:T(4,128)(2,1)S(1)} %bitcast.105), kind=kOutput, calls=%fused_computation.96 | convolution fusion | flops 134217728 | bytes 2686976 | tf_op jit(solution)/shard_map/dot_general | solution.py:199
  62.3 1.3 convolution_convert_fusion
  63.7 1.4 copy.89
  65.1 10.9 %all-to-all-start.2 = ((bf16[16,11,2048]{2,1,0:T(8,128)(2,1)}), bf16[16,11,2048]{2,1,0:T(8,128)(2,1)}, u32[]{:S(2)}, u32[]{:S(2)}) async-start(bf16[16,11,2048]{2,1,0:T(8,128)(2,1)} %copy.89), calls=%async_computation.3 | async-start | bytes 2097152 | tf_op jit(solution)/shard_map/all_to_all | solution.py:162
  76.3 23.2 %reduce-scatter.3.cloned.1.call-done = f32[16,2048]{1,0:T(8,128)} async-done(((f32[64,2048]{1,0:T(8,128)}), f32[16,2048]{1,0:T(8,128)}) %reduce-scatter.3.cloned.1.call-update) | async-done | bytes 131088 | tf_op jit(solution)/shard_map/reduce_scatter | solution.py:158
  99.6 1.0 fusion.70
  101.0 1.4 copy.83
  102.4 6.7 %all-to-all-done.2 = bf16[16,11,2048]{2,1,0:T(8,128)(2,1)} async-done(((bf16[16,11,2048]{2,1,0:T(8,128)(2,1)}), bf16[16,11,2048]{2,1,0:T(8,128)(2,1)}, u32[]{:S(2)}, u32[]{:S(2)}) %all-to-all-start.2) | async-done | bytes 720928 | tf_op jit(solution)/shard_map/all_to_all | solution.py:162
  109.1 4.3 %all-to-all-start = ((bf16[16,11,2048]{2,1,0:T(8,128)(2,1)}), bf16[16,11,2048]{2,1,0:T(8,128)(2,1)}, u32[]{:S(2)}, u32[]{:S(2)}) async-start(bf16[16,11,2048]{2,1,0:T(8,128)(2,1)} %copy.83), calls=%async_computation.1 | async-start | bytes 2097152 | tf_op jit(solution)/shard_map/all_to_all | solution.py:162
  113.5 4.5 %fusion.2 = f32[16,11,768]{2,0,1:T(8,128)} fusion(bf16[1,768,2048]{2,1,0:T(8,128)(2,1)} %param.31, bf16[16,11,2048]{2,1,0:T(8,128)(2,1)} %all-to-all-done.2), kind=kOutput, calls=%fused_computation.2 | convolution fusion | flops 553648128 | bytes 4407296 | tf_op jit(solution)/shard_map/scw,fw->scf/dot_general | solution.py:249
  118.0 22.5 %all-to-all-done = bf16[16,11,2048]{2,1,0:T(8,128)(2,1)} async-done(((bf16[16,11,2048]{2,1,0:T(8,128)(2,1)}), bf16[16,11,2048]{2,1,0:T(8,128)(2,1)}, u32[]{:S(2)}, u32[]{:S(2)}) %all-to-all-start) | async-done | bytes 720928 | tf_op jit(solution)/shard_map/all_to_all | solution.py:162
  140.5 3.3 %fusion.12 = f32[16,11,768]{2,0,1:T(8,128)S(1)} fusion(bf16[1,2048,768]{2,1,0:T(8,128)(2,1)} %param.29, bf16[16,11,2048]{2,1,0:T(8,128)(2,1)} %all-to-all-done), kind=kOutput, calls=%fused_computation.12 | convolution fusion | flops 553648128 | bytes 4407296 | tf_op jit(solution)/shard_map/scw,wf->scf/dot_general | solution.py:242
  143.8 1.2 fusion.6
  145.0 2.5 fusion.8
  147.5 1.2 fusion.20
  148.7 1.4 copy.91
  150.1 4.3 %all-to-all-start.3 = ((bf16[16,11,2048]{2,1,0:T(8,128)(2,1)}), bf16[16,11,2048]{2,1,0:T(8,128)(2,1)}, u32[]{:S(2)}, u32[]{:S(2)}) async-start(bf16[16,11,2048]{2,1,0:T(8,128)(2,1)} %copy.91), calls=%async_computation.4 | async-start | bytes 2097152 | tf_op jit(solution)/shard_map/all_to_all | solution.py:166
  154.5 2.4 constant_dynamic-slice_fusion
  156.9 2.7 fusion.17
  159.6 1.4 copy.86
  161.0 20.4 %all-to-all-done.3 = bf16[16,11,2048]{2,1,0:T(8,128)(2,1)} async-done(((bf16[16,11,2048]{2,1,0:T(8,128)(2,1)}), bf16[16,11,2048]{2,1,0:T(8,128)(2,1)}, u32[]{:S(2)}, u32[]{:S(2)}) %all-to-all-start.3) | async-done | bytes 720928 | tf_op jit(solution)/shard_map/all_to_all | solution.py:166
  181.4 4.5 %all-to-all-start.1 = ((bf16[16,11,2048]{2,1,0:T(8,128)(2,1)}), bf16[16,11,2048]{2,1,0:T(8,128)(2,1)}, u32[]{:S(2)}, u32[]{:S(2)}) async-start(bf16[16,11,2048]{2,1,0:T(8,128)(2,1)} %copy.86), calls=%async_computation.2 | async-start | bytes 2097152 | tf_op jit(solution)/shard_map/all_to_all | solution.py:166
  186.0 1.6 fusion.58
  188.2 1.0 fusion.118
  189.1 30.4 %all_gather.15 = bf16[64,2048]{1,0:T(8,128)(2,1)S(1)} all-gather(bf16[16,2048]{1,0:T(8,128)(2,1)S(1)} %fusion.118), channel_id=1, replica_groups=mesh['groups'=2,'expert'=4,'head'=4] {'head'}, dimensions={0}, use_global_device_ids=true | all-gather | bytes 327680 | tf_op jit(solution)/shard_map/all_gather | solution.py:154
  219.6 3.0 %convolution_convert_fusion.3 = bf16[64,512]{1,0:T(8,128)(2,1)} fusion(bf16[64,2048]{1,0:T(8,128)(2,1)S(1)} %all_gather.15, bf16[512,2048]{1,0:T(8,128)(2,1)} %param.28), kind=kOutput, calls=%fused_computation.38 | convolution fusion | flops 134250496 | bytes 2424832 | tf_op jit(solution)/shard_map/td,fd->tf/dot_general | solution.py:129
  222.6 1.5 reshape.90
  224.1 1.2 convolution_bitcast_fusion.3
  225.3 1.7 convolution_bitcast_fusion.2
  227.5 3.0 %convolution_bitcast_fusion.4 = f32[4,48,128]{2,1,0:T(8,128)} fusion(f32[4,4,16,48]{3,2,1,0:T(8,128)} %convolution_bitcast_fusion.2, bf16[4,16,4,128]{3,2,1,0:T(4,128)(2,1)} %copy-done.12, f32[4,4,16,48]{3,2,1,0:T(8,128)} %get-tuple-element.13, f32[4,4,16]{2,1,0:T(4,128)} %copy-done.25), kind=kOutput, calls=%fused_computation.37 | convolution fusion | flops 3232047 | bytes 263168 | tf_op jit(solution)/shard_map/shbk,sbhd->skd/dot_general | solution.py:58
  230.5 1.4 slice.8
  231.9 2.9 %fusion.35 = bf16[4,16,4,128]{3,1,2,0:T(8,128)(2,1)} fusion(f32[4,4,16,48]{3,2,1,0:T(8,128)} %convolution_bitcast_fusion.2, bf16[4,16,128]{2,1,0:T(8,128)(2,1)} %bitcast.111, bf16[4,32,128]{2,1,0:T(8,128)(2,1)} %copy-done.14, f32[4,4,16,48]{3,2,1,0:T(8,128)} %get-tuple-element.13, f32[4,4,16]{2,1,0:T(4,128)} %copy-done.25), kind=kOutput, calls=%fused_computation.42 | convolution fusion | flops 3363119 | bytes 214016 | tf_op jit(solution)/shard_map/shbk,skd->sbhd/dot_general | solution.py:55
  234.8 0.9 copy.96
  235.7 2.3 fusion.36
  238.0 3.2 %convolution_add_fusion = f32[64,2048]{1,0:T(8,128)} fusion(f32[64,2048]{1,0:T(8,128)S(1)} %fusion.36, bf16[2048,512]{1,0:T(8,128)(2,1)} %param.26, bf16[8,8,4,128]{3,2,1,0:T(4,128)(2,1)S(1)} %bitcast.104), kind=kOutput, calls=%fused_computation.19 | convolution fusion | flops 134348800 | bytes 3211264 | tf_op jit(solution)/shard_map/tf,df->td/dot_general | solution.py:148
  241.2 2.4 fusion.25
  243.6 19.9 %reduce-scatter.5.cloned.1.call-done = f32[16,2048]{1,0:T(8,128)} async-done(((f32[64,2048]{1,0:T(8,128)}), f32[16,2048]{1,0:T(8,128)}) %reduce-scatter.5.cloned.1.call-update) | async-done | bytes 131088 | tf_op jit(solution)/shard_map/reduce_scatter | solution.py:158
  263.5 1.1 fusion.63
  264.6 1.7 fusion.67
  (84 shorter events, 7.6 us)
Async XLA Ops:
  7.2 136.7 %copy-start = (bf16[1,2048,768]{2,1,0:T(8,128)(2,1)S(1)}, bf16[1,2048,768]{2,1,0:T(8,128)(2,1)}, u32[]{:S(2)}) copy-start(bf16[1,2048,768]{2,1,0:T(8,128)(2,1)} %param.30) | copy-start | bytes 9437188
  7.2 24.2 %copy-start.23 = (s32[4]{0:T(128)S(1)}, s32[4]{0:T(128)}, u32[]{:S(2)}) copy-start(s32[4]{0:T(128)} %param.21) | copy-start | bytes 52
  7.2 54.5 %all-gather.2.cloned.1.call-start = ((), (), s32[]{:S(2)}) async-start(), calls=%async_computation.6 | async-start | bytes 2621440 | tf_op jit(solution)/shard_map/all_gather | solution.py:192
  7.9 91.6 %reduce-scatter.3.cloned.1.call-start = ((), (), s32[]{:S(2)}) async-start(), calls=%async_computation.7 | async-start | bytes 655360 | tf_op jit(solution)/shard_map/reduce_scatter | solution.py:158
  11.2 0.9 copy-start.18
  31.3 30.4 %copy-start.12 = (bf16[4,16,4,128]{3,2,1,0:T(4,128)(2,1)}, bf16[4,16,4,128]{3,2,1,0:T(4,128)(2,1)S(1)}, u32[]{:S(2)}) copy-start(bf16[4,16,4,128]{3,2,1,0:T(4,128)(2,1)S(1)} %reshape.88) | copy-start | bytes 196612
  54.6 7.1 %copy-start.10 = (bf16[4,32,128]{2,1,0:T(8,128)(2,1)}, bf16[4,32,128]{2,1,0:T(8,128)(2,1)S(1)}, u32[]{:S(2)}) copy-start(bf16[4,32,128]{2,1,0:T(8,128)(2,1)S(1)} %constant_dynamic-slice_fusion.5) | copy-start | bytes 98308
  55.4 0.6 copy-start.14
  55.4 0.6 copy-start.15
  56.0 5.8 %copy-start.24 = (s32[16]{0:T(128)S(1)}, s32[16]{0:T(128)}, u32[]{:S(2)}) copy-start(s32[16]{0:T(128)} %param.18) | copy-start | bytes 196
  56.0 5.8 %copy-start.21 = (f32[16,8]{0,1:T(8,128)S(1)}, f32[16,8]{0,1:T(8,128)}, u32[]{:S(2)}) copy-start(f32[16,8]{0,1:T(8,128)} %param.20) | copy-start | bytes 1540
  56.9 4.8 %copy-start.25 = (f32[4,4,16]{2,1,0:T(4,128)}, f32[4,4,16]{2,1,0:T(4,128)S(1)}, u32[]{:S(2)}) copy-start(f32[4,4,16]{2,1,0:T(4,128)S(1)} %get-tuple-element.12) | copy-start | bytes 3076
  56.9 5.4 %copy-start.4 = (bf16[16,2048]{1,0:T(8,128)(2,1)S(1)}, bf16[16,2048]{1,0:T(8,128)(2,1)}, u32[]{:S(2)}) copy-start(bf16[16,2048]{1,0:T(8,128)(2,1)} %param.17) | copy-start | bytes 196612
  61.8 0.5 copy-start.20
  63.6 35.9 %copy-start.3 = (bf16[16,2048]{1,0:T(8,128)(2,1)S(1)}, bf16[16,2048]{1,0:T(8,128)(2,1)}, u32[]{:S(2)}) copy-start(bf16[16,2048]{1,0:T(8,128)(2,1)} %param.16) | copy-start | bytes 196612
  63.6 37.0 %copy-start.13 = (f32[2048]{0:T(1024)S(1)}, f32[2048]{0:T(1024)}, u32[]{:S(2)}) copy-start(f32[2048]{0:T(1024)} %param.25) | copy-start | bytes 24580
  65.1 44.1 %all-to-all-start.2 = ((bf16[16,11,2048]{2,1,0:T(8,128)(2,1)}), bf16[16,11,2048]{2,1,0:T(8,128)(2,1)}, u32[]{:S(2)}, u32[]{:S(2)}) async-start(bf16[16,11,2048]{2,1,0:T(8,128)(2,1)} %copy.89), calls=%async_computation.3 | async-start | bytes 2097152 | tf_op jit(solution)/shard_map/all_to_all | solution.py:162
  76.3 32.8 %copy-start.9 = (pred[16,11,16]{2,1,0:T(8,128)(4,1)}, pred[16,11,16]{2,1,0:T(8,128)(4,1)S(1)}, u32[]{:S(2)}) copy-start(pred[16,11,16]{2,1,0:T(8,128)(4,1)S(1)} %compare_reduce_fusion) | copy-start | bytes 8452
  100.6 8.5 %copy-start.16 = (f32[16]{0:T(128)}, f32[16]{0:T(128)S(1)}, u32[]{:S(2)}) copy-start(f32[16]{0:T(128)S(1)} %add_rsqrt_fusion) | copy-start | bytes 196
  109.1 31.3 %all-to-all-start = ((bf16[16,11,2048]{2,1,0:T(8,128)(2,1)}), bf16[16,11,2048]{2,1,0:T(8,128)(2,1)}, u32[]{:S(2)}, u32[]{:S(2)}) async-start(bf16[16,11,2048]{2,1,0:T(8,128)(2,1)} %copy.83), calls=%async_computation.1 | async-start | bytes 2097152 | tf_op jit(solution)/shard_map/all_to_all | solution.py:162
  140.5 3.4 %copy-start.2 = (f32[16,11,768]{2,0,1:T(8,128)S(1)}, f32[16,11,768]{2,0,1:T(8,128)}, u32[]{:S(2)}) copy-start(f32[16,11,768]{2,0,1:T(8,128)} %fusion.2) | copy-start | bytes 1622020
  143.8 3.7 %copy-start.5 = (f32[16,11,768]{2,0,1:T(8,128)}, f32[16,11,768]{2,0,1:T(8,128)S(1)}, u32[]{:S(2)}) copy-start(f32[16,11,768]{2,0,1:T(8,128)S(1)} %fusion.12) | copy-start | bytes 1622020
  145.0 2.5 copy-start.1
  147.5 1.2 copy-start.7
  150.1 31.3 %all-to-all-start.3 = ((bf16[16,11,2048]{2,1,0:T(8,128)(2,1)}), bf16[16,11,2048]{2,1,0:T(8,128)(2,1)}, u32[]{:S(2)}, u32[]{:S(2)}) async-start(bf16[16,11,2048]{2,1,0:T(8,128)(2,1)} %copy.91), calls=%async_computation.4 | async-start | bytes 2097152 | tf_op jit(solution)/shard_map/all_to_all | solution.py:166
  154.5 2.4 copy-start.6
  154.5 2.4 copy-start.8
  181.4 59.8 %all-to-all-start.1 = ((bf16[16,11,2048]{2,1,0:T(8,128)(2,1)}), bf16[16,11,2048]{2,1,0:T(8,128)(2,1)}, u32[]{:S(2)}, u32[]{:S(2)}) async-start(bf16[16,11,2048]{2,1,0:T(8,128)(2,1)} %copy.86), calls=%async_computation.2 | async-start | bytes 2097152 | tf_op jit(solution)/shard_map/all_to_all | solution.py:166
  186.0 77.5 %reduce-scatter.5.cloned.1.call-start = ((), (), s32[]{:S(2)}) async-start(), calls=%async_computation.8 | async-start | bytes 655360 | tf_op jit(solution)/shard_map/reduce_scatter | solution.py:158
  187.7 0.5 copy-start.22
  238.0 25.5 %copy-start.11 = (f32[2048]{0:T(1024)S(1)}, f32[2048]{0:T(1024)}, u32[]{:S(2)}) copy-start(f32[2048]{0:T(1024)} %param.24) | copy-start | bytes 24580
  238.0 25.5 %copy-start.19 = (f32[16]{0:T(128)S(1)}, f32[16]{0:T(128)}, u32[]{:S(2)}) copy-start(f32[16]{0:T(128)} %copy-done.18) | copy-start | bytes 196
  238.0 26.6 %copy-start.17 = (f32[16]{0:T(128)S(1)}, f32[16]{0:T(128)}, u32[]{:S(2)}) copy-start(f32[16]{0:T(128)} %copy-done.16) | copy-start | bytes 196
Sparse Core Ops, SparseCore 0:
  9.6 51.9 all-gather.1
  63.8 35.6 reduce-scatter.2
  241.3 22.1 reduce-scatter.4

commit v6 on v5

--- a/solution.py
+++ b/solution.py
@@ -122,27 +122,32 @@
     return (joined, saved)
 
 
-def attention_backward(grad_rows, query_weights, output_weights, saved):
+def attention_backward(grad_rows, query_weights, output_weights, own_kv_weights, saved, kv_now):
     heads_here = query_weights.shape[1] // HEAD_SIZE
     row_count = grad_rows.shape[0]
     seq_count = row_count // BLOCK
+    key_value_width = KEY_VALUE_HEADS * HEAD_SIZE
     grad_attn = jnp.einsum(
         "td,fd->tf", grad_rows, output_weights, preferred_element_type=jnp.float32
     ).astype(jnp.bfloat16)
     grad_attn = grad_attn.reshape(seq_count, BLOCK, heads_here, HEAD_SIZE)
-    query_part, key_rows, value_rows, probabilities, probs_low, pair_weights = saved[0]
+    query_part, key_rows, value_rows, probabilities, probs_low = saved[0]
     grad_queries, grad_keys, grad_values = attend_backward(
         query_part, key_rows, value_rows, probabilities, probs_low, grad_attn
     )
-    block_grads = jnp.concatenate(
-        [
-            grad_keys[:, PREFIX_SLOTS:].reshape(row_count, HEAD_SIZE),
-            grad_values[:, PREFIX_SLOTS:].reshape(row_count, HEAD_SIZE),
-        ],
-        axis=1,
-    )
+    placed = jnp.zeros((row_count, 2 * key_value_width), jnp.float32)
+    placed = lax.dynamic_update_slice_in_dim(
+        placed, grad_keys[:, PREFIX_SLOTS:].reshape(row_count, HEAD_SIZE), kv_now * HEAD_SIZE, 1
+    )
+    placed = lax.dynamic_update_slice_in_dim(
+        placed,
+        grad_values[:, PREFIX_SLOTS:].reshape(row_count, HEAD_SIZE),
+        key_value_width + kv_now * HEAD_SIZE,
+        1,
+    )
+    own_grads = lax.psum_scatter(placed, "head", scatter_dimension=1, tiled=True)
     running = jnp.einsum(
-        "tc,dc->td", block_grads, pair_weights.astype(jnp.float32), precision=lax.Precision.HIGHEST
+        "tc,dc->td", own_grads, own_kv_weights.astype(jnp.float32), precision=lax.Precision.HIGHEST
     )
     query_flat = grad_queries.reshape(row_count, heads_here * HEAD_SIZE)
     return running + jnp.einsum(
@@ -189,16 +194,13 @@
     width = hidden_in.shape[1]
     normed_one, inverse_one = rms_forward(hidden_in, attn_gain)
     attn_rows = normed_one.astype(jnp.bfloat16)
-    kv_full = lax.all_gather(key_value_weight, "head", axis=1, tiled=True)
     heads_here = w_query.shape[1] // HEAD_SIZE
     first_head = lax.axis_index("head") * heads_here
     gathered_rows = head_rows(attn_rows)
     attended, saved = attention_forward(
         gathered_rows, w_query, key_value_weight, key_cache, prefix_value_cache, cache_lengths, first_head
     )
-    partial_mixed = jnp.dot(attended, w_output, preferred_element_type=jnp.float32)
-    partial_mixed, kv_full = lax.optimization_barrier((partial_mixed, kv_full))
-    mixed = head_sums(partial_mixed)
+    mixed = head_sums(jnp.dot(attended, w_output, preferred_element_type=jnp.float32))
     hidden = (hidden_in.astype(jnp.float32) + mixed).astype(jnp.bfloat16)
     normed_two, inverse_two = rms_forward(hidden, moe_gain)
     moe_rows = normed_two.astype(jnp.bfloat16)
@@ -225,16 +227,6 @@
         "dct,tw->dcw", weighting, cotangent, precision=highest_prec
     ).astype(jnp.bfloat16)
     rows_in = to_experts(outgoing)
-    kv_now = first_head // (QUERY_HEADS // KEY_VALUE_HEADS)
-    key_value_width = KEY_VALUE_HEADS * HEAD_SIZE
-    pair_weights = jnp.concatenate(
-        [
-            lax.dynamic_slice_in_dim(kv_full, kv_now * HEAD_SIZE, HEAD_SIZE, 1),
-            lax.dynamic_slice_in_dim(kv_full, key_value_width + kv_now * HEAD_SIZE, HEAD_SIZE, 1),
-        ],
-        axis=1,
-    )
-    saved = [saved[0][:5] + (pair_weights,)]
     grads_in = to_experts(grad_out)
     gate_matrix = w_gate[0]
     up_matrix = w_up[0]
@@ -273,7 +265,16 @@
     grad_hidden = cotangent + rms_backward(hidden, moe_gain, inverse_two, grad_moe)
     grad_low = grad_hidden.astype(jnp.bfloat16)
     grad_gathered = head_rows(grad_low)
-    grad_attn_rows = head_sums(attention_backward(grad_gathered, w_query, w_output, saved))
+    grad_attn_rows = head_sums(
+        attention_backward(
+            grad_gathered,
+            w_query,
+            w_output,
+            key_value_weight,
+            saved,
+            first_head // (QUERY_HEADS // KEY_VALUE_HEADS),
+        )
+    )
     input_grad = (
         grad_hidden + rms_backward(hidden_in, attn_gain, inverse_one, grad_attn_rows)
     ).astype(jnp.bfloat16)

time: 274 us -> 244 us (0.89)
  waiting for transfers between devices: 93.5 us -> 77.9 us
  starting transfers between devices: 24.2 us -> 13.8 us
  matrix products: 46.5 us -> 42.6 us
  blocking collectives: 68.7 us -> 72.5 us
  local copies, waits for them, and re-layouts: 17.2 us -> 13.9 us
    all_to_all x0 -> x1, blocking collectives: none -> 30.2 us  [from_experts(): lax.all_to_all(results, ('expert', 'head'), split_axis=0, concat_axis=0,...]
    reduce_scatter x2, waiting for transfers between devices: 43.1 us -> 22.6 us  [head_sums(): lax.psum_scatter(partial_rows, 'head', scatter_dimension=0, tiled=True)]
    all_gather x2, blocking collectives: 47.5 us -> 30.2 us  [head_rows(): return lax.all_gather(row_block, 'head', axis=0, tiled=True)]
    all_gather x1, blocking collectives: 21.1 us -> 12.1 us  [attention_forward(): kv_rows = lax.all_gather(own_rows, 'head', axis=1, tiled=True)]
    all_to_all x2, starting transfers between devices: 15.3 us -> 9.31 us  [to_experts(): lax.all_to_all(outgoing, ('expert', 'head'), split_axis=0, concat_axis=0,...]
    reduce_scatter x0 -> x1, waiting for transfers between devices: none -> 4.74 us  [attention_backward(): lax.psum_scatter(placed, 'head', scatter_dimension=1, tiled=True)]
    all_to_all x2 -> x1, starting transfers between devices: 8.86 us -> 4.35 us  [from_experts(): lax.all_to_all(results, ('expert', 'head'), split_axis=0, concat_axis=0,...]
    all_to_all x2 -> x1, waiting for transfers between devices: 20.5 us -> 21.3 us  [from_experts(): lax.all_to_all(results, ('expert', 'head'), split_axis=0, concat_axis=0,...]
  transfers between devices with their start and end apart: 7 -> 6, of which waited for: 5 -> 5; matrix products, arithmetic and copies ran while one was open for 21% -> 11% of each run, Pallas kernels for 0% -> 0%
where the time goes in v6:
time: 244 us; the launch traced here: 243 us
  waiting for transfers between devices  77.9 us (32%)
  blocking collectives  72.5 us (30%)
  matrix products  42.6 us (17%)
  between operations  14.4 us (6%)
  local copies, waits for them, and re-layouts  13.9 us (6%)
  starting transfers between devices  13.8 us (6%)
  other arithmetic  7.82 us (3%)
    all_gather x2, blocking collectives, head_rows(): return lax.all_gather(row_block, 'head', axis=0, tiled=True)  30.2 us
    all_to_all x1, blocking collectives, from_experts(): lax.all_to_all(results, ('expert', 'head'), split_axis=0, concat_axis=0,...  30.2 us
    all_to_all x2, waiting for transfers between devices, to_experts(): lax.all_to_all(outgoing, ('expert', 'head'), split_axis=0, concat_axis=0,...  29.2 us
    reduce_scatter x2, waiting for transfers between devices, head_sums(): lax.psum_scatter(partial_rows, 'head', scatter_dimension=0, tiled=True)  22.6 us
    all_to_all x1, waiting for transfers between devices, from_experts(): lax.all_to_all(results, ('expert', 'head'), split_axis=0, concat_axis=0,...  21.3 us
    all_gather x1, blocking collectives, attention_forward(): kv_rows = lax.all_gather(own_rows, 'head', axis=1, tiled=True)  12.1 us
    all_to_all x2, starting transfers between devices, to_experts(): lax.all_to_all(outgoing, ('expert', 'head'), split_axis=0, concat_axis=0,...  9.31 us
  transfers between devices with their start and end apart: 6, of which 5 were waited for; matrix products, arithmetic and copies ran while one was open for 11% of the time, Pallas kernels for 0%

profile of v6, /device:TPU:0, one launch (start us, length us, event | category | flops | bytes accessed | tf_op | source)
XLA Modules:
  0.0 242.9 jit_solution(17084259915352963103)
XLA Ops:
  7.3 0.9 iota_compare_fusion.1
  8.1 1.0 fusion.64
  9.1 0.8 constant_dynamic-slice_fusion.1
  9.9 0.8 constant_dynamic-slice_fusion.3
  10.7 0.9 fusion.58
  11.6 15.6 %all_gather.9 = bf16[64,2048]{1,0:T(8,128)(2,1)S(1)} all-gather(bf16[16,2048]{1,0:T(8,128)(2,1)S(1)} %fusion.58), channel_id=1, replica_groups=mesh['groups'=2,'expert'=4,'head'=4] {'head'}, dimensions={0}, use_global_device_ids=true | all-gather | bytes 327680 | tf_op jit(solution)/shard_map/all_gather | solution.py:159
  27.2 1.3 convolution_convert_fusion.6
  28.5 2.1 convolution_convert_fusion.5
  30.6 12.1 %all_gather.10 = bf16[64,512]{1,0:T(8,128)(2,1)S(1)} all-gather(bf16[64,128]{1,0:T(8,128)(2,1)S(1)} %convolution_convert_fusion.6), channel_id=1, replica_groups=mesh['groups'=2,'expert'=4,'head'=4] {'head'}, dimensions={1}, use_global_device_ids=true | all-gather | bytes 81920 | tf_op jit(solution)/shard_map/all_gather | solution.py:97
  43.4 2.9 %fusion.74 = f32[64,2048]{1,0:T(8,128)} fusion(bf16[512,2048]{1,0:T(8,128)(2,1)} %param.28, bf16[8,8,4,128]{3,2,1,0:T(4,128)(2,1)S(1)} %bitcast.107), kind=kOutput, calls=%fused_computation.92 | convolution fusion | flops 134217728 | bytes 2686976 | tf_op jit(solution)/shard_map/dot_general | solution.py:203
  47.7 1.3 convolution_convert_fusion
  49.1 1.5 copy.89
  50.6 5.0 %all-to-all-start.2 = ((bf16[16,11,2048]{2,1,0:T(8,128)(2,1)}), bf16[16,11,2048]{2,1,0:T(8,128)(2,1)}, u32[]{:S(2)}, u32[]{:S(2)}) async-start(bf16[16,11,2048]{2,1,0:T(8,128)(2,1)} %copy.89), calls=%async_computation.3 | async-start | bytes 2097152 | tf_op jit(solution)/shard_map/all_to_all | solution.py:167
  55.9 22.6 %reduce-scatter.4.cloned.1.call-done = f32[16,2048]{1,0:T(8,128)} async-done(((f32[64,2048]{1,0:T(8,128)}), f32[16,2048]{1,0:T(8,128)}) %reduce-scatter.4.cloned.1.call-update) | async-done | bytes 131088 | tf_op jit(solution)/shard_map/reduce_scatter | solution.py:163
  78.5 1.0 fusion.66
  80.0 1.4 copy.83
  81.4 6.7 %all-to-all-done.2 = bf16[16,11,2048]{2,1,0:T(8,128)(2,1)} async-done(((bf16[16,11,2048]{2,1,0:T(8,128)(2,1)}), bf16[16,11,2048]{2,1,0:T(8,128)(2,1)}, u32[]{:S(2)}, u32[]{:S(2)}) %all-to-all-start.2) | async-done | bytes 720928 | tf_op jit(solution)/shard_map/all_to_all | solution.py:167
  88.2 4.3 %all-to-all-start = ((bf16[16,11,2048]{2,1,0:T(8,128)(2,1)}), bf16[16,11,2048]{2,1,0:T(8,128)(2,1)}, u32[]{:S(2)}, u32[]{:S(2)}) async-start(bf16[16,11,2048]{2,1,0:T(8,128)(2,1)} %copy.83), calls=%async_computation.1 | async-start | bytes 2097152 | tf_op jit(solution)/shard_map/all_to_all | solution.py:167
  92.6 4.4 %fusion.2 = f32[16,11,768]{2,0,1:T(8,128)} fusion(bf16[1,768,2048]{2,1,0:T(8,128)(2,1)} %param.31, bf16[16,11,2048]{2,1,0:T(8,128)(2,1)} %all-to-all-done.2), kind=kOutput, calls=%fused_computation.2 | convolution fusion | flops 553648128 | bytes 4407296 | tf_op jit(solution)/shard_map/scw,fw->scf/dot_general | solution.py:241
  97.0 22.5 %all-to-all-done = bf16[16,11,2048]{2,1,0:T(8,128)(2,1)} async-done(((bf16[16,11,2048]{2,1,0:T(8,128)(2,1)}), bf16[16,11,2048]{2,1,0:T(8,128)(2,1)}, u32[]{:S(2)}, u32[]{:S(2)}) %all-to-all-start) | async-done | bytes 720928 | tf_op jit(solution)/shard_map/all_to_all | solution.py:167
  119.5 3.4 %fusion.12 = f32[16,11,768]{2,0,1:T(8,128)S(1)} fusion(bf16[1,2048,768]{2,1,0:T(8,128)(2,1)} %param.29, bf16[16,11,2048]{2,1,0:T(8,128)(2,1)} %all-to-all-done), kind=kOutput, calls=%fused_computation.12 | convolution fusion | flops 553648128 | bytes 4407296 | tf_op jit(solution)/shard_map/scw,wf->scf/dot_general | solution.py:234
  122.9 1.2 fusion.6
  124.1 2.5 %fusion.8 = f32[16,11,768]{2,0,1:T(8,128)S(1)} fusion(bf16[1,2048,768]{2,1,0:T(8,128)(2,1)S(1)} %copy-done, bf16[16,11,2048]{2,1,0:T(8,128)(2,1)} %all-to-all-done), kind=kOutput, calls=%fused_computation.8 | convolution fusion | flops 553648128 | bytes 4407296 | tf_op jit(solution)/shard_map/scw,wf->scf/dot_general | solution.py:235
  126.6 1.2 fusion.20
  128.2 30.2 %all_to_all.20 = bf16[16,11,2048]{2,1,0:T(8,128)(2,1)S(1)} all-to-all(bf16[16,11,2048]{2,1,0:T(8,128)(2,1)S(1)} %copy.91), channel_id=1, replica_groups=mesh['groups'=2,'expert'=4,'head'=4] {'expert','head'}, dimensions={0} | all-to-all | bytes 1441792 | tf_op jit(solution)/shard_map/all_to_all | solution.py:171
  159.4 14.6 %all_gather.11 = bf16[64,2048]{1,0:T(8,128)(2,1)S(1)} all-gather(bf16[16,2048]{1,0:T(8,128)(2,1)S(1)} %fusion.109), channel_id=1, replica_groups=mesh['groups'=2,'expert'=4,'head'=4] {'head'}, dimensions={0}, use_global_device_ids=true | all-gather | bytes 327680 | tf_op jit(solution)/shard_map/all_gather | solution.py:159
  174.0 1.4 convolution_convert_fusion.3
  175.4 1.5 reshape.90
  176.9 1.7 convolution_bitcast_fusion.2
  178.5 1.8 convolution_bitcast_fusion.3
  180.4 3.0 %convolution_bitcast_fusion.4 = f32[4,48,128]{2,1,0:T(8,128)} fusion(f32[4,4,16,48]{3,2,1,0:T(8,128)} %convolution_bitcast_fusion.2, bf16[4,16,4,128]{3,2,1,0:T(4,128)(2,1)} %copy-done.13, f32[4,4,16,48]{3,2,1,0:T(8,128)} %copy-done.30, f32[4,4,16]{2,1,0:T(4,128)} %copy-done.31), kind=kOutput, calls=%fused_computation.37 | convolution fusion | flops 3232047 | bytes 263168 | tf_op jit(solution)/shard_map/shbk,sbhd->skd/dot_general | solution.py:58
  183.4 0.8 slice.9
  184.1 0.8 slice.8
  184.9 0.7 broadcast_in_dim.26
  185.6 0.6 constant_dynamic-update-slice_fusion
  186.2 0.6 constant_dynamic-update-slice_fusion.1
  186.8 3.0 %fusion.17 = bf16[16,11,2048]{2,0,1:T(8,128)(2,1)S(1)} fusion(bf16[1,768,2048]{2,1,0:T(8,128)(2,1)} %param.31, f32[16,11,768]{2,0,1:T(8,128)} %copy-done.8, f32[16,11,768]{2,0,1:T(8,128)} %copy-done.7), kind=kOutput, calls=%fused_computation.15 | convolution fusion | flops 554819584 | bytes 4947968 | tf_op jit(solution)/shard_map/scf,fw->scw/dot_general | solution.py:238
  189.8 1.5 copy.86
  191.3 4.3 %all-to-all-start.1 = ((bf16[16,11,2048]{2,1,0:T(8,128)(2,1)}), bf16[16,11,2048]{2,1,0:T(8,128)(2,1)}, u32[]{:S(2)}, u32[]{:S(2)}) async-start(bf16[16,11,2048]{2,1,0:T(8,128)(2,1)} %copy.86), calls=%async_computation.2 | async-start | bytes 2097152 | tf_op jit(solution)/shard_map/all_to_all | solution.py:171
  195.7 2.9 %fusion.35 = bf16[4,16,4,128]{3,1,2,0:T(8,128)(2,1)} fusion(f32[4,4,16,48]{3,2,1,0:T(8,128)} %convolution_bitcast_fusion.2, bf16[4,16,128]{2,1,0:T(8,128)(2,1)S(1)} %bitcast.113, bf16[4,32,128]{2,1,0:T(8,128)(2,1)} %copy-done.16, f32[4,4,16,48]{3,2,1,0:T(8,128)} %copy-done.30, f32[4,4,16]{2,1,0:T(4,128)} %copy-done.31), kind=kOutput, calls=%fused_computation.42 | convolution fusion | flops 3363119 | bytes 214016 | tf_op jit(solution)/shard_map/shbk,skd->sbhd/dot_general | solution.py:55
  198.6 1.5 copy.96
  200.1 4.7 %reduce-scatter.6.cloned.1.call-done = f32[64,128]{1,0:T(8,128)} async-done(((f32[64,512]{1,0:T(8,128)}), f32[64,128]{1,0:T(8,128)}) %reduce-scatter.6.cloned.1.call-update) | async-done | bytes 32784 | tf_op jit(solution)/shard_map/reduce_scatter | solution.py:148
  204.8 1.7 fusion.114
  206.6 3.2 %convolution_add_fusion = f32[64,2048]{1,0:T(8,128)} fusion(f32[64,2048]{1,0:T(8,128)S(1)} %fusion.114, bf16[2048,512]{1,0:T(8,128)(2,1)} %param.26, bf16[8,8,4,128]{3,2,1,0:T(4,128)(2,1)} %bitcast.106), kind=kOutput, calls=%fused_computation.19 | convolution fusion | flops 134348800 | bytes 3211264 | tf_op jit(solution)/shard_map/tf,df->td/dot_general | solution.py:153
  209.8 21.3 %all-to-all-done.1 = bf16[16,11,2048]{2,1,0:T(8,128)(2,1)} async-done(((bf16[16,11,2048]{2,1,0:T(8,128)(2,1)}), bf16[16,11,2048]{2,1,0:T(8,128)(2,1)}, u32[]{:S(2)}, u32[]{:S(2)}) %all-to-all-start.1) | async-done | bytes 720928 | tf_op jit(solution)/shard_map/all_to_all | solution.py:171
  231.1 2.4 fusion.25
  233.5 1.1 fusion.59
  234.7 1.7 fusion.63
  (97 shorter events, 4.3 us)
Async XLA Ops:
  7.2 115.7 %copy-start = (bf16[1,2048,768]{2,1,0:T(8,128)(2,1)S(1)}, bf16[1,2048,768]{2,1,0:T(8,128)(2,1)}, u32[]{:S(2)}) copy-start(bf16[1,2048,768]{2,1,0:T(8,128)(2,1)} %param.30) | copy-start | bytes 9437188
  7.2 71.4 %reduce-scatter.4.cloned.1.call-start = ((), (), s32[]{:S(2)}) async-start(), calls=%async_computation.7 | async-start | bytes 655360 | tf_op jit(solution)/shard_map/reduce_scatter | solution.py:163
  9.1 2.5 %copy-start.23 = (f32[16]{0:T(128)}, f32[16]{0:T(128)S(1)}, u32[]{:S(2)}) copy-start(f32[16]{0:T(128)S(1)} %add_rsqrt_fusion.1) | copy-start | bytes 196
  9.9 33.2 %copy-start.16 = (bf16[4,32,128]{2,1,0:T(8,128)(2,1)}, bf16[4,32,128]{2,1,0:T(8,128)(2,1)S(1)}, u32[]{:S(2)}) copy-start(bf16[4,32,128]{2,1,0:T(8,128)(2,1)S(1)} %constant_dynamic-slice_fusion.1) | copy-start | bytes 98308
  10.7 32.4 %copy-start.11 = (bf16[4,32,128]{2,1,0:T(8,128)(2,1)}, bf16[4,32,128]{2,1,0:T(8,128)(2,1)S(1)}, u32[]{:S(2)}) copy-start(bf16[4,32,128]{2,1,0:T(8,128)(2,1)S(1)} %constant_dynamic-slice_fusion.3) | copy-start | bytes 98308
  30.6 15.7 %copy-start.13 = (bf16[4,16,4,128]{3,2,1,0:T(4,128)(2,1)}, bf16[4,16,4,128]{3,2,1,0:T(4,128)(2,1)S(1)}, u32[]{:S(2)}) copy-start(bf16[4,16,4,128]{3,2,1,0:T(4,128)(2,1)S(1)} %reshape.88) | copy-start | bytes 196612
  42.7 3.6 %copy-start.18 = (bf16[64,128]{1,0:T(8,128)(2,1)}, bf16[64,128]{1,0:T(8,128)(2,1)S(1)}, u32[]{:S(2)}) copy-start(bf16[64,128]{1,0:T(8,128)(2,1)S(1)} %get-tuple-element.4) | copy-start | bytes 49156
  42.7 3.6 %copy-start.17 = (s32[16,8]{0,1:T(8,128)S(1)}, s32[16,8]{0,1:T(8,128)}, u32[]{:S(2)}) copy-start(s32[16,8]{0,1:T(8,128)} %param.19) | copy-start | bytes 1540
  43.1 3.9 %copy-start.30 = (f32[4,4,16,48]{3,2,1,0:T(8,128)}, f32[4,4,16,48]{3,2,1,0:T(8,128)S(1)}, u32[]{:S(2)}) copy-start(f32[4,4,16,48]{3,2,1,0:T(8,128)S(1)} %get-tuple-element.7) | copy-start | bytes 147460
  43.1 3.9 %copy-start.31 = (f32[4,4,16]{2,1,0:T(4,128)}, f32[4,4,16]{2,1,0:T(4,128)S(1)}, u32[]{:S(2)}) copy-start(f32[4,4,16]{2,1,0:T(4,128)S(1)} %get-tuple-element.6) | copy-start | bytes 3076
  43.1 4.0 %copy-start.29 = (s32[16]{0:T(128)S(1)}, s32[16]{0:T(128)}, u32[]{:S(2)}) copy-start(s32[16]{0:T(128)} %param.18) | copy-start | bytes 196
  43.1 4.0 %copy-start.27 = (f32[16,8]{0,1:T(8,128)S(1)}, f32[16,8]{0,1:T(8,128)}, u32[]{:S(2)}) copy-start(f32[16,8]{0,1:T(8,128)} %param.20) | copy-start | bytes 1540
  43.1 4.6 %copy-start.5 = (bf16[16,2048]{1,0:T(8,128)(2,1)S(1)}, bf16[16,2048]{1,0:T(8,128)(2,1)}, u32[]{:S(2)}) copy-start(bf16[16,2048]{1,0:T(8,128)(2,1)} %param.17) | copy-start | bytes 196612
  47.2 0.6 copy-start.25
  49.1 29.5 %copy-start.4 = (bf16[16,2048]{1,0:T(8,128)(2,1)S(1)}, bf16[16,2048]{1,0:T(8,128)(2,1)}, u32[]{:S(2)}) copy-start(bf16[16,2048]{1,0:T(8,128)(2,1)} %param.16) | copy-start | bytes 196612
  49.1 30.5 %copy-start.14 = (f32[2048]{0:T(1024)S(1)}, f32[2048]{0:T(1024)}, u32[]{:S(2)}) copy-start(f32[2048]{0:T(1024)} %param.25) | copy-start | bytes 24580
  50.6 37.6 %all-to-all-start.2 = ((bf16[16,11,2048]{2,1,0:T(8,128)(2,1)}), bf16[16,11,2048]{2,1,0:T(8,128)(2,1)}, u32[]{:S(2)}, u32[]{:S(2)}) async-start(bf16[16,11,2048]{2,1,0:T(8,128)(2,1)} %copy.89), calls=%async_computation.3 | async-start | bytes 2097152 | tf_op jit(solution)/shard_map/all_to_all | solution.py:167
  55.9 32.3 %copy-start.9 = (pred[16,11,16]{2,1,0:T(8,128)(4,1)}, pred[16,11,16]{2,1,0:T(8,128)(4,1)S(1)}, u32[]{:S(2)}) copy-start(pred[16,11,16]{2,1,0:T(8,128)(4,1)S(1)} %compare_reduce_fusion) | copy-start | bytes 8452
  79.6 8.6 %copy-start.20 = (f32[16]{0:T(128)}, f32[16]{0:T(128)S(1)}, u32[]{:S(2)}) copy-start(f32[16]{0:T(128)S(1)} %add_rsqrt_fusion) | copy-start | bytes 196
  88.2 31.3 %all-to-all-start = ((bf16[16,11,2048]{2,1,0:T(8,128)(2,1)}), bf16[16,11,2048]{2,1,0:T(8,128)(2,1)}, u32[]{:S(2)}, u32[]{:S(2)}) async-start(bf16[16,11,2048]{2,1,0:T(8,128)(2,1)} %copy.83), calls=%async_computation.1 | async-start | bytes 2097152 | tf_op jit(solution)/shard_map/all_to_all | solution.py:167
  92.5 112.3 %reduce-scatter.6.cloned.1.call-start = ((), (), s32[]{:S(2)}) async-start(), calls=%async_computation.8 | async-start | bytes 163840 | tf_op jit(solution)/shard_map/reduce_scatter | solution.py:148
  119.5 3.4 %copy-start.3 = (f32[16,11,768]{2,0,1:T(8,128)S(1)}, f32[16,11,768]{2,0,1:T(8,128)}, u32[]{:S(2)}) copy-start(f32[16,11,768]{2,0,1:T(8,128)} %fusion.2) | copy-start | bytes 1622020
  122.9 3.7 %copy-start.7 = (f32[16,11,768]{2,0,1:T(8,128)}, f32[16,11,768]{2,0,1:T(8,128)S(1)}, u32[]{:S(2)}) copy-start(f32[16,11,768]{2,0,1:T(8,128)S(1)} %fusion.12) | copy-start | bytes 1622020
  124.1 2.5 %copy-start.2 = (bf16[1,2048,768]{2,1,0:T(8,128)(2,1)S(1)}, bf16[1,2048,768]{2,1,0:T(8,128)(2,1)}, u32[]{:S(2)}) copy-start(bf16[1,2048,768]{2,1,0:T(8,128)(2,1)} %param.29) | copy-start | bytes 9437188
  126.5 1.2 copy-start.8
  127.7 30.7 %copy-start.10 = (pred[16,11,16]{2,1,0:T(8,128)(4,1)S(1)}, pred[16,11,16]{2,1,0:T(8,128)(4,1)}, u32[]{:S(2)}) copy-start(pred[16,11,16]{2,1,0:T(8,128)(4,1)} %copy-done.9) | copy-start | bytes 8452
  127.7 30.7 %copy-start.15 = (f32[2048]{0:T(1024)S(1)}, f32[2048]{0:T(1024)}, u32[]{:S(2)}) copy-start(f32[2048]{0:T(1024)} %param.25) | copy-start | bytes 24580
  127.8 30.7 %copy-start.21 = (f32[16]{0:T(128)S(1)}, f32[16]{0:T(128)}, u32[]{:S(2)}) copy-start(f32[16]{0:T(128)} %copy-done.20) | copy-start | bytes 196
  128.2 30.7 %copy-start.6 = (bf16[16,2048]{1,0:T(8,128)(2,1)S(1)}, bf16[16,2048]{1,0:T(8,128)(2,1)}, u32[]{:S(2)}) copy-start(bf16[16,2048]{1,0:T(8,128)(2,1)} %param.17) | copy-start | bytes 196612
  128.2 30.7 %copy-start.26 = (f32[16]{0:T(128)S(1)}, f32[16]{0:T(128)}, u32[]{:S(2)}) copy-start(f32[16]{0:T(128)} %copy-done.25) | copy-start | bytes 196
  128.2 45.8 %copy-start.1 = (bf16[512,2048]{1,0:T(8,128)(2,1)S(1)}, bf16[512,2048]{1,0:T(8,128)(2,1)}, u32[]{:S(2)}) copy-start(bf16[512,2048]{1,0:T(8,128)(2,1)} %param.28) | copy-start | bytes 6291460
  158.8 0.5 copy-start.28
  189.8 5.9 %copy-start.19 = (bf16[64,128]{1,0:T(8,128)(2,1)S(1)}, bf16[64,128]{1,0:T(8,128)(2,1)}, u32[]{:S(2)}) copy-start(bf16[64,128]{1,0:T(8,128)(2,1)} %copy-done.18) | copy-start | bytes 49156
  191.3 39.8 %all-to-all-start.1 = ((bf16[16,11,2048]{2,1,0:T(8,128)(2,1)}), bf16[16,11,2048]{2,1,0:T(8,128)(2,1)}, u32[]{:S(2)}, u32[]{:S(2)}) async-start(bf16[16,11,2048]{2,1,0:T(8,128)(2,1)} %copy.86), calls=%async_computation.2 | async-start | bytes 2097152 | tf_op jit(solution)/shard_map/all_to_all | solution.py:171
  195.6 37.9 %reduce-scatter.8.cloned.1.call-start = ((), (), s32[]{:S(2)}) async-start(), calls=%async_computation.9 | async-start | bytes 655360 | tf_op jit(solution)/shard_map/reduce_scatter | solution.py:163
  206.6 27.0 %copy-start.12 = (f32[2048]{0:T(1024)S(1)}, f32[2048]{0:T(1024)}, u32[]{:S(2)}) copy-start(f32[2048]{0:T(1024)} %param.24) | copy-start | bytes 24580
  206.6 27.0 %copy-start.24 = (f32[16]{0:T(128)S(1)}, f32[16]{0:T(128)}, u32[]{:S(2)}) copy-start(f32[16]{0:T(128)} %copy-done.23) | copy-start | bytes 196
  206.6 28.1 %copy-start.22 = (f32[16]{0:T(128)S(1)}, f32[16]{0:T(128)}, u32[]{:S(2)}) copy-start(f32[16]{0:T(128)} %copy-done.20) | copy-start | bytes 196
Sparse Core Ops, SparseCore 0:
  46.4 32.0 reduce-scatter.3
  186.9 17.8 reduce-scatter.5
  209.9 21.0 reduce-scatter.7

commit v7 on v6

--- a/solution.py
+++ b/solution.py
@@ -252,20 +252,13 @@
     grad_back = grad_back.astype(jnp.bfloat16)
     result_home = from_experts(result)
     grad_home = from_experts(grad_back)
-    moe_sum = jnp.einsum(
-        "dct,dcw->tw",
-        weighting,
-        result_home.astype(jnp.float32),
-        precision=highest_prec,
-    )
-    layer_out = (hidden.astype(jnp.float32) + moe_sum).astype(jnp.bfloat16)
     grad_moe = jnp.einsum(
         "dct,dcw->tw", placement, grad_home, preferred_element_type=jnp.float32
     )
     grad_hidden = cotangent + rms_backward(hidden, moe_gain, inverse_two, grad_moe)
     grad_low = grad_hidden.astype(jnp.bfloat16)
     grad_gathered = head_rows(grad_low)
-    grad_attn_rows = head_sums(
+    grad_partial = (
         attention_backward(
             grad_gathered,
             w_query,
@@ -275,6 +268,16 @@
             first_head // (QUERY_HEADS // KEY_VALUE_HEADS),
         )
     )
+    grad_partial, result_home = lax.optimization_barrier((grad_partial, result_home))
+    grad_attn_rows = head_sums(grad_partial)
+    moe_sum = jnp.einsum(
+        "dct,dcw->tw",
+        weighting,
+        result_home.astype(jnp.float32),
+        precision=highest_prec,
+    )
+    layer_out = (hidden.astype(jnp.float32) + moe_sum).astype(jnp.bfloat16)
+
     input_grad = (
         grad_hidden + rms_backward(hidden_in, attn_gain, inverse_one, grad_attn_rows)
     ).astype(jnp.bfloat16)

time: 244 us -> 266 us (1.090)
  waiting for transfers between devices: 77.9 us -> 107 us
  blocking collectives: 72.5 us -> 57.9 us
  starting transfers between devices: 13.8 us -> 18.3 us
    all_to_all x1 -> x0, blocking collectives: 30.2 us -> none  [from_experts(): lax.all_to_all(results, ('expert', 'head'), split_axis=0, concat_axis=0,...]
    reduce_scatter x2, waiting for transfers between devices: 22.6 us -> 40.3 us  [head_sums(): lax.psum_scatter(partial_rows, 'head', scatter_dimension=0, tiled=True)]
    all_gather x2, blocking collectives: 30.2 us -> 45.8 us  [head_rows(): return lax.all_gather(row_block, 'head', axis=0, tiled=True)]
    reduce_scatter x1, waiting for transfers between devices: 4.74 us -> 15.4 us  [attention_backward(): lax.psum_scatter(placed, 'head', scatter_dimension=1, tiled=True)]
    all_to_all x1 -> x2, starting transfers between devices: 4.35 us -> 8.68 us  [from_experts(): lax.all_to_all(results, ('expert', 'head'), split_axis=0, concat_axis=0,...]
    all_to_all x1 -> x2, waiting for transfers between devices: 21.3 us -> 22.5 us  [from_experts(): lax.all_to_all(results, ('expert', 'head'), split_axis=0, concat_axis=0,...]
  transfers between devices with their start and end apart: 6 -> 7, of which waited for: 5 -> 6; matrix products, arithmetic and copies ran while one was open for 11% -> 17% of each run, Pallas kernels for 0% -> 0%
where the time goes in v7:
time: 266 us; the launch traced here: 265 us
  waiting for transfers between devices  107 us (40%)
  blocking collectives  57.9 us (22%)
  matrix products  43.9 us (17%)
  starting transfers between devices  18.3 us (7%)
  local copies, waits for them, and re-layouts  15 us (6%)
  between operations  14.3 us (5%)
  other arithmetic  8 us (3%)
    all_gather x2, blocking collectives, head_rows(): return lax.all_gather(row_block, 'head', axis=0, tiled=True)  45.8 us
    reduce_scatter x2, waiting for transfers between devices, head_sums(): lax.psum_scatter(partial_rows, 'head', scatter_dimension=0, tiled=True)  40.3 us
    all_to_all x2, waiting for transfers between devices, to_experts(): lax.all_to_all(outgoing, ('expert', 'head'), split_axis=0, concat_axis=0,...  29.3 us
    all_to_all x2, waiting for transfers between devices, from_experts(): lax.all_to_all(results, ('expert', 'head'), split_axis=0, concat_axis=0,...  22.5 us
    reduce_scatter x1, waiting for transfers between devices, attention_backward(): lax.psum_scatter(placed, 'head', scatter_dimension=1, tiled=True)  15.4 us
    all_gather x1, blocking collectives, attention_forward(): kv_rows = lax.all_gather(own_rows, 'head', axis=1, tiled=True)  12.1 us
    all_to_all x2, starting transfers between devices, to_experts(): lax.all_to_all(outgoing, ('expert', 'head'), split_axis=0, concat_axis=0,...  9.31 us
    all_to_all x2, starting transfers between devices, from_experts(): lax.all_to_all(results, ('expert', 'head'), split_axis=0, concat_axis=0,...  8.68 us
  transfers between devices with their start and end apart: 7, of which 6 were waited for; matrix products, arithmetic and copies ran while one was open for 17% of the time, Pallas kernels for 0%

profile of v7, /device:TPU:0, one launch (start us, length us, event | category | flops | bytes accessed | tf_op | source)
XLA Modules:
  0.0 264.9 jit_solution(11613508753461348393)
XLA Ops:
  7.3 1.1 fusion.64
  8.4 0.9 fusion.58
  9.4 15.6 %all_gather.9 = bf16[64,2048]{1,0:T(8,128)(2,1)S(1)} all-gather(bf16[16,2048]{1,0:T(8,128)(2,1)S(1)} %fusion.58), channel_id=1, replica_groups=mesh['groups'=2,'expert'=4,'head'=4] {'head'}, dimensions={0}, use_global_device_ids=true | all-gather | bytes 327680 | tf_op jit(solution)/shard_map/all_gather | solution.py:159
  25.0 1.3 convolution_convert_fusion.6
  26.3 12.1 %all_gather.10 = bf16[64,512]{1,0:T(8,128)(2,1)S(1)} all-gather(bf16[64,128]{1,0:T(8,128)(2,1)S(1)} %convolution_convert_fusion.6), channel_id=1, replica_groups=mesh['groups'=2,'expert'=4,'head'=4] {'head'}, dimensions={1}, use_global_device_ids=true | all-gather | bytes 81920 | tf_op jit(solution)/shard_map/all_gather | solution.py:97
  38.3 2.1 convolution_convert_fusion.5
  41.5 2.9 %fusion.74 = f32[64,2048]{1,0:T(8,128)} fusion(bf16[512,2048]{1,0:T(8,128)(2,1)} %param.28, bf16[8,8,4,128]{3,2,1,0:T(4,128)(2,1)S(1)} %bitcast.107), kind=kOutput, calls=%fused_computation.92 | convolution fusion | flops 134217728 | bytes 2686976 | tf_op jit(solution)/shard_map/dot_general | solution.py:203
  45.8 1.3 convolution_convert_fusion.1
  47.1 1.4 copy.83
  48.6 5.0 %all-to-all-start = ((bf16[16,11,2048]{2,1,0:T(8,128)(2,1)}), bf16[16,11,2048]{2,1,0:T(8,128)(2,1)}, u32[]{:S(2)}, u32[]{:S(2)}) async-start(bf16[16,11,2048]{2,1,0:T(8,128)(2,1)} %copy.83), calls=%async_computation.1 | async-start | bytes 2097152 | tf_op jit(solution)/shard_map/all_to_all | solution.py:167
  53.9 22.7 %reduce-scatter.4.cloned.1.call-done = f32[16,2048]{1,0:T(8,128)} async-done(((f32[64,2048]{1,0:T(8,128)}), f32[16,2048]{1,0:T(8,128)}) %reduce-scatter.4.cloned.1.call-update) | async-done | bytes 131088 | tf_op jit(solution)/shard_map/reduce_scatter | solution.py:163
  76.6 1.0 fusion.66
  78.1 1.4 copy.86
  79.5 6.7 %all-to-all-done = bf16[16,11,2048]{2,1,0:T(8,128)(2,1)} async-done(((bf16[16,11,2048]{2,1,0:T(8,128)(2,1)}), bf16[16,11,2048]{2,1,0:T(8,128)(2,1)}, u32[]{:S(2)}, u32[]{:S(2)}) %all-to-all-start) | async-done | bytes 720928 | tf_op jit(solution)/shard_map/all_to_all | solution.py:167
  86.3 4.3 %all-to-all-start.1 = ((bf16[16,11,2048]{2,1,0:T(8,128)(2,1)}), bf16[16,11,2048]{2,1,0:T(8,128)(2,1)}, u32[]{:S(2)}, u32[]{:S(2)}) async-start(bf16[16,11,2048]{2,1,0:T(8,128)(2,1)} %copy.86), calls=%async_computation.2 | async-start | bytes 2097152 | tf_op jit(solution)/shard_map/all_to_all | solution.py:167
  90.6 4.4 %fusion.12 = f32[16,11,768]{2,0,1:T(8,128)} fusion(bf16[1,768,2048]{2,1,0:T(8,128)(2,1)} %param.31, bf16[16,11,2048]{2,1,0:T(8,128)(2,1)} %all-to-all-done), kind=kOutput, calls=%fused_computation.12 | convolution fusion | flops 553648128 | bytes 4407296 | tf_op jit(solution)/shard_map/scw,fw->scf/dot_general | solution.py:241
  95.0 22.5 %all-to-all-done.1 = bf16[16,11,2048]{2,1,0:T(8,128)(2,1)} async-done(((bf16[16,11,2048]{2,1,0:T(8,128)(2,1)}), bf16[16,11,2048]{2,1,0:T(8,128)(2,1)}, u32[]{:S(2)}, u32[]{:S(2)}) %all-to-all-start.1) | async-done | bytes 720928 | tf_op jit(solution)/shard_map/all_to_all | solution.py:167
  117.6 2.5 fusion.4
  120.1 2.5 fusion.8
  122.6 0.8 copy-done.6
  123.4 1.2 fusion.2
  124.6 1.2 fusion.20
  125.8 1.4 copy.89
  127.2 4.3 %all-to-all-start.2 = ((bf16[16,11,2048]{2,1,0:T(8,128)(2,1)}), bf16[16,11,2048]{2,1,0:T(8,128)(2,1)}, u32[]{:S(2)}, u32[]{:S(2)}) async-start(bf16[16,11,2048]{2,1,0:T(8,128)(2,1)} %copy.89), calls=%async_computation.3 | async-start | bytes 2097152 | tf_op jit(solution)/shard_map/all_to_all | solution.py:171
  131.5 3.0 %fusion.17 = bf16[16,11,2048]{2,0,1:T(8,128)(2,1)S(1)} fusion(bf16[1,768,2048]{2,1,0:T(8,128)(2,1)} %param.31, f32[16,11,768]{2,0,1:T(8,128)} %copy-done.6, f32[16,11,768]{2,0,1:T(8,128)} %copy-done.3), kind=kOutput, calls=%fused_computation.15 | convolution fusion | flops 554819584 | bytes 4947968 | tf_op jit(solution)/shard_map/scf,fw->scw/dot_general | solution.py:238
  134.5 1.5 copy.95
  136.0 22.5 %all-to-all-done.2 = bf16[16,11,2048]{2,1,0:T(8,128)(2,1)} async-done(((bf16[16,11,2048]{2,1,0:T(8,128)(2,1)}), bf16[16,11,2048]{2,1,0:T(8,128)(2,1)}, u32[]{:S(2)}, u32[]{:S(2)}) %all-to-all-start.2) | async-done | bytes 720928 | tf_op jit(solution)/shard_map/all_to_all | solution.py:171
  158.5 4.3 %all-to-all-start.3 = ((bf16[16,11,2048]{2,1,0:T(8,128)(2,1)}), bf16[16,11,2048]{2,1,0:T(8,128)(2,1)}, u32[]{:S(2)}, u32[]{:S(2)}) async-start(bf16[16,11,2048]{2,1,0:T(8,128)(2,1)} %copy.95), calls=%async_computation.5 | async-start | bytes 2097152 | tf_op jit(solution)/shard_map/all_to_all | solution.py:171
  163.1 1.6 fusion.54
  165.3 1.0 fusion.109
  166.3 30.2 %all_gather.11 = bf16[64,2048]{1,0:T(8,128)(2,1)S(1)} all-gather(bf16[16,2048]{1,0:T(8,128)(2,1)S(1)} %fusion.109), channel_id=1, replica_groups=mesh['groups'=2,'expert'=4,'head'=4] {'head'}, dimensions={0}, use_global_device_ids=true | all-gather | bytes 327680 | tf_op jit(solution)/shard_map/all_gather | solution.py:159
  196.4 3.0 %convolution_convert_fusion.3 = bf16[64,512]{1,0:T(8,128)(2,1)} fusion(bf16[64,2048]{1,0:T(8,128)(2,1)S(1)} %all_gather.11, bf16[512,2048]{1,0:T(8,128)(2,1)} %param.28), kind=kOutput, calls=%fused_computation.38 | convolution fusion | flops 134250496 | bytes 2424832 | tf_op jit(solution)/shard_map/td,fd->tf/dot_general | solution.py:130
  199.4 1.5 reshape.90
  200.9 1.2 convolution_bitcast_fusion.3
  202.7 1.7 convolution_bitcast_fusion.2
  204.4 3.0 %convolution_bitcast_fusion.4 = f32[4,48,128]{2,1,0:T(8,128)} fusion(f32[4,4,16,48]{3,2,1,0:T(8,128)} %convolution_bitcast_fusion.2, bf16[4,16,4,128]{3,2,1,0:T(4,128)(2,1)} %copy-done.10, f32[4,4,16,48]{3,2,1,0:T(8,128)} %copy-done.26, f32[4,4,16]{2,1,0:T(4,128)} %copy-done.27), kind=kOutput, calls=%fused_computation.37 | convolution fusion | flops 3232047 | bytes 263168 | tf_op jit(solution)/shard_map/shbk,sbhd->skd/dot_general | solution.py:58
  207.4 0.8 slice.8
  208.2 0.7 broadcast_in_dim.26
  209.4 1.4 constant_dynamic-update-slice_fusion.1
  210.9 2.9 %fusion.35 = bf16[4,16,4,128]{3,1,2,0:T(8,128)(2,1)} fusion(f32[4,4,16,48]{3,2,1,0:T(8,128)} %convolution_bitcast_fusion.2, bf16[4,16,128]{2,1,0:T(8,128)(2,1)} %bitcast.113, bf16[4,32,128]{2,1,0:T(8,128)(2,1)} %copy-done.12, f32[4,4,16,48]{3,2,1,0:T(8,128)} %copy-done.26, f32[4,4,16]{2,1,0:T(4,128)} %copy-done.27), kind=kOutput, calls=%fused_computation.42 | convolution fusion | flops 3363119 | bytes 214016 | tf_op jit(solution)/shard_map/shbk,skd->sbhd/dot_general | solution.py:55
  213.8 1.5 copy.94
  215.3 15.4 %reduce-scatter.6.cloned.1.call-done = f32[64,128]{1,0:T(8,128)} async-done(((f32[64,512]{1,0:T(8,128)}), f32[64,128]{1,0:T(8,128)}) %reduce-scatter.6.cloned.1.call-update) | async-done | bytes 32784 | tf_op jit(solution)/shard_map/reduce_scatter | solution.py:148
  230.6 1.7 fusion.114
  232.4 3.2 %convolution_add_fusion = f32[64,2048]{1,0:T(8,128)} fusion(f32[64,2048]{1,0:T(8,128)S(1)} %fusion.114, bf16[2048,512]{1,0:T(8,128)(2,1)} %param.26, bf16[8,8,4,128]{3,2,1,0:T(4,128)(2,1)} %bitcast.106), kind=kOutput, calls=%fused_computation.19 | convolution fusion | flops 134348800 | bytes 3211264 | tf_op jit(solution)/shard_map/tf,df->td/dot_general | solution.py:153
  235.6 2.4 fusion.25
  238.0 17.6 %reduce-scatter.8.cloned.1.call-done = f32[16,2048]{1,0:T(8,128)} async-done(((f32[64,2048]{1,0:T(8,128)}), f32[16,2048]{1,0:T(8,128)}) %reduce-scatter.8.cloned.1.call-update) | async-done | bytes 131088 | tf_op jit(solution)/shard_map/reduce_scatter | solution.py:163
  255.6 1.1 fusion.59
  256.7 1.7 fusion.63
  (90 shorter events, 5.3 us)
Async XLA Ops:
  7.2 110.4 %copy-start = (bf16[1,2048,768]{2,1,0:T(8,128)(2,1)S(1)}, bf16[1,2048,768]{2,1,0:T(8,128)(2,1)}, u32[]{:S(2)}) copy-start(bf16[1,2048,768]{2,1,0:T(8,128)(2,1)} %param.29) | copy-start | bytes 9437188
  7.2 33.3 %copy-start.24 = (s32[4]{0:T(128)S(1)}, s32[4]{0:T(128)}, u32[]{:S(2)}) copy-start(s32[4]{0:T(128)} %param.21) | copy-start | bytes 52
  7.2 33.3 %copy-start.14 = (bf16[4,32,256]{2,1,0:T(8,128)(2,1)S(1)}, bf16[4,32,256]{2,1,0:T(8,128)(2,1)}, u32[]{:S(2)}) copy-start(bf16[4,32,256]{2,1,0:T(8,128)(2,1)} %param.22) | copy-start | bytes 196612
  7.2 33.3 %copy-start.15 = (bf16[4,32,256]{2,1,0:T(8,128)(2,1)S(1)}, bf16[4,32,256]{2,1,0:T(8,128)(2,1)}, u32[]{:S(2)}) copy-start(bf16[4,32,256]{2,1,0:T(8,128)(2,1)} %param.23) | copy-start | bytes 196612
  7.2 69.4 %reduce-scatter.4.cloned.1.call-start = ((), (), s32[]{:S(2)}) async-start(), calls=%async_computation.7 | async-start | bytes 655360 | tf_op jit(solution)/shard_map/reduce_scatter | solution.py:163
  8.4 17.8 %copy-start.19 = (f32[16]{0:T(128)}, f32[16]{0:T(128)S(1)}, u32[]{:S(2)}) copy-start(f32[16]{0:T(128)S(1)} %add_rsqrt_fusion.1) | copy-start | bytes 196
  40.4 4.0 %copy-start.10 = (bf16[4,16,4,128]{3,2,1,0:T(4,128)(2,1)}, bf16[4,16,4,128]{3,2,1,0:T(4,128)(2,1)S(1)}, u32[]{:S(2)}) copy-start(bf16[4,16,4,128]{3,2,1,0:T(4,128)(2,1)S(1)} %reshape.88) | copy-start | bytes 196612
  40.6 0.6 copy-start.12
  40.6 3.8 %copy-start.8 = (bf16[4,32,128]{2,1,0:T(8,128)(2,1)}, bf16[4,32,128]{2,1,0:T(8,128)(2,1)S(1)}, u32[]{:S(2)}) copy-start(bf16[4,32,128]{2,1,0:T(8,128)(2,1)S(1)} %constant_dynamic-slice_fusion.3) | copy-start | bytes 98308
  40.6 0.6 copy-start.16
  40.7 3.8 %copy-start.13 = (s32[16,8]{0,1:T(8,128)S(1)}, s32[16,8]{0,1:T(8,128)}, u32[]{:S(2)}) copy-start(s32[16,8]{0,1:T(8,128)} %param.19) | copy-start | bytes 1540
  41.0 4.0 %copy-start.26 = (f32[4,4,16,48]{3,2,1,0:T(8,128)}, f32[4,4,16,48]{3,2,1,0:T(8,128)S(1)}, u32[]{:S(2)}) copy-start(f32[4,4,16,48]{3,2,1,0:T(8,128)S(1)} %get-tuple-element.11) | copy-start | bytes 147460
  41.0 4.0 %copy-start.27 = (f32[4,4,16]{2,1,0:T(4,128)}, f32[4,4,16]{2,1,0:T(4,128)S(1)}, u32[]{:S(2)}) copy-start(f32[4,4,16]{2,1,0:T(4,128)S(1)} %get-tuple-element.10) | copy-start | bytes 3076
  41.2 4.0 %copy-start.25 = (s32[16]{0:T(128)S(1)}, s32[16]{0:T(128)}, u32[]{:S(2)}) copy-start(s32[16]{0:T(128)} %param.18) | copy-start | bytes 196
  41.2 4.0 %copy-start.22 = (f32[16,8]{0,1:T(8,128)S(1)}, f32[16,8]{0,1:T(8,128)}, u32[]{:S(2)}) copy-start(f32[16,8]{0,1:T(8,128)} %param.20) | copy-start | bytes 1540
  41.2 4.5 %copy-start.5 = (bf16[16,2048]{1,0:T(8,128)(2,1)S(1)}, bf16[16,2048]{1,0:T(8,128)(2,1)}, u32[]{:S(2)}) copy-start(bf16[16,2048]{1,0:T(8,128)(2,1)} %param.17) | copy-start | bytes 196612
  45.3 0.5 copy-start.21
  47.1 29.5 %copy-start.4 = (bf16[16,2048]{1,0:T(8,128)(2,1)S(1)}, bf16[16,2048]{1,0:T(8,128)(2,1)}, u32[]{:S(2)}) copy-start(bf16[16,2048]{1,0:T(8,128)(2,1)} %param.16) | copy-start | bytes 196612
  47.1 30.6 %copy-start.11 = (f32[2048]{0:T(1024)S(1)}, f32[2048]{0:T(1024)}, u32[]{:S(2)}) copy-start(f32[2048]{0:T(1024)} %param.25) | copy-start | bytes 24580
  48.6 37.7 %all-to-all-start = ((bf16[16,11,2048]{2,1,0:T(8,128)(2,1)}), bf16[16,11,2048]{2,1,0:T(8,128)(2,1)}, u32[]{:S(2)}, u32[]{:S(2)}) async-start(bf16[16,11,2048]{2,1,0:T(8,128)(2,1)} %copy.83), calls=%async_computation.1 | async-start | bytes 2097152 | tf_op jit(solution)/shard_map/all_to_all | solution.py:167
  53.9 32.4 %copy-start.7 = (pred[16,11,16]{2,1,0:T(8,128)(4,1)}, pred[16,11,16]{2,1,0:T(8,128)(4,1)S(1)}, u32[]{:S(2)}) copy-start(pred[16,11,16]{2,1,0:T(8,128)(4,1)S(1)} %compare_reduce_fusion) | copy-start | bytes 8452
  77.7 8.6 %copy-start.17 = (f32[16]{0:T(128)}, f32[16]{0:T(128)S(1)}, u32[]{:S(2)}) copy-start(f32[16]{0:T(128)S(1)} %add_rsqrt_fusion) | copy-start | bytes 196
  86.3 31.3 %all-to-all-start.1 = ((bf16[16,11,2048]{2,1,0:T(8,128)(2,1)}), bf16[16,11,2048]{2,1,0:T(8,128)(2,1)}, u32[]{:S(2)}, u32[]{:S(2)}) async-start(bf16[16,11,2048]{2,1,0:T(8,128)(2,1)} %copy.86), calls=%async_computation.2 | async-start | bytes 2097152 | tf_op jit(solution)/shard_map/all_to_all | solution.py:167
  117.6 2.5 copy-start.2
  120.0 4.5 %copy-start.3 = (f32[16,11,768]{2,0,1:T(8,128)}, f32[16,11,768]{2,0,1:T(8,128)S(1)}, u32[]{:S(2)}) copy-start(f32[16,11,768]{2,0,1:T(8,128)S(1)} %fusion.4) | copy-start | bytes 1622020
  120.0 3.4 %copy-start.1 = (f32[16,11,768]{2,0,1:T(8,128)S(1)}, f32[16,11,768]{2,0,1:T(8,128)}, u32[]{:S(2)}) copy-start(f32[16,11,768]{2,0,1:T(8,128)} %fusion.12) | copy-start | bytes 1622020
  122.6 0.8 copy-start.6
  127.2 31.3 %all-to-all-start.2 = ((bf16[16,11,2048]{2,1,0:T(8,128)(2,1)}), bf16[16,11,2048]{2,1,0:T(8,128)(2,1)}, u32[]{:S(2)}, u32[]{:S(2)}) async-start(bf16[16,11,2048]{2,1,0:T(8,128)(2,1)} %copy.89), calls=%async_computation.3 | async-start | bytes 2097152 | tf_op jit(solution)/shard_map/all_to_all | solution.py:171
  158.5 77.1 %all-to-all-start.3 = ((bf16[16,11,2048]{2,1,0:T(8,128)(2,1)}), bf16[16,11,2048]{2,1,0:T(8,128)(2,1)}, u32[]{:S(2)}, u32[]{:S(2)}) async-start(bf16[16,11,2048]{2,1,0:T(8,128)(2,1)} %copy.95), calls=%async_computation.5 | async-start | bytes 2097152 | tf_op jit(solution)/shard_map/all_to_all | solution.py:171
  162.8 67.8 %reduce-scatter.6.cloned.1.call-start = ((), (), s32[]{:S(2)}) async-start(), calls=%async_computation.8 | async-start | bytes 163840 | tf_op jit(solution)/shard_map/reduce_scatter | solution.py:148
  164.7 0.6 copy-start.23
  210.8 44.8 %reduce-scatter.8.cloned.1.call-start = ((), (), s32[]{:S(2)}) async-start(), calls=%async_computation.9 | async-start | bytes 655360 | tf_op jit(solution)/shard_map/reduce_scatter | solution.py:163
  232.4 23.2 %copy-start.9 = (f32[2048]{0:T(1024)S(1)}, f32[2048]{0:T(1024)}, u32[]{:S(2)}) copy-start(f32[2048]{0:T(1024)} %param.24) | copy-start | bytes 24580
  232.4 23.2 %copy-start.20 = (f32[16]{0:T(128)S(1)}, f32[16]{0:T(128)}, u32[]{:S(2)}) copy-start(f32[16]{0:T(128)} %copy-done.19) | copy-start | bytes 196
  232.4 24.3 %copy-start.18 = (f32[16]{0:T(128)S(1)}, f32[16]{0:T(128)}, u32[]{:S(2)}) copy-start(f32[16]{0:T(128)} %copy-done.17) | copy-start | bytes 196
Sparse Core Ops, SparseCore 0:
  44.5 32.0 reduce-scatter.3
  210.9 19.6 reduce-scatter.5
  235.7 19.8 reduce-scatter.7

commit v8 on v6

--- a/solution.py
+++ b/solution.py
@@ -220,48 +220,60 @@
     placement = jnp.any(matched, axis=3).astype(jnp.bfloat16)
     weighting = jnp.sum(jnp.where(matched, gate_weights[None, None, :, :], 0.0), axis=3)
     cotangent = out_grad.astype(jnp.float32) * loss_mask.astype(jnp.float32)[:, None]
+    lanes = 128
+    pieces = width // lanes
     outgoing = jnp.einsum(
-        "dct,tw->dcw", placement, moe_rows, preferred_element_type=jnp.float32
+        "dct,tkl->dckl",
+        placement,
+        moe_rows.reshape(owned, pieces, lanes),
+        preferred_element_type=jnp.float32,
     ).astype(jnp.bfloat16)
     grad_out = jnp.einsum(
-        "dct,tw->dcw", weighting, cotangent, precision=highest_prec
-    ).astype(jnp.bfloat16)
-    rows_in = to_experts(outgoing)
-    grads_in = to_experts(grad_out)
-    gate_matrix = w_gate[0]
-    up_matrix = w_up[0]
-    down_matrix = w_down[0]
-    gate_pre = jnp.einsum("scw,wf->scf", rows_in, gate_matrix, preferred_element_type=jnp.float32)
-    up_pre = jnp.einsum("scw,wf->scf", rows_in, up_matrix, preferred_element_type=jnp.float32)
+        "dct,tkl->dckl",
+        weighting,
+        cotangent.reshape(owned, pieces, lanes),
+        precision=highest_prec,
+    ).astype(jnp.bfloat16)
+    flat_shape = (device_count, capacity * pieces, lanes)
+    split_shape = (device_count, capacity, pieces, lanes)
+    rows_in = to_experts(outgoing.reshape(flat_shape)).reshape(split_shape)
+    grads_in = to_experts(grad_out.reshape(flat_shape)).reshape(split_shape)
+    gate_matrix = w_gate[0].reshape(pieces, lanes, -1)
+    up_matrix = w_up[0].reshape(pieces, lanes, -1)
+    down_matrix = w_down[0].reshape(-1, pieces, lanes)
+    gate_pre = jnp.einsum(
+        "sckl,klf->scf", rows_in, gate_matrix, preferred_element_type=jnp.float32
+    )
+    up_pre = jnp.einsum("sckl,klf->scf", rows_in, up_matrix, preferred_element_type=jnp.float32)
     sigma = jax.nn.sigmoid(gate_pre)
     activated = (gate_pre * sigma * up_pre).astype(jnp.bfloat16)
     result = jnp.einsum(
-        "scf,fw->scw", activated, down_matrix, preferred_element_type=jnp.float32
+        "scf,fkl->sckl", activated, down_matrix, preferred_element_type=jnp.float32
     ).astype(jnp.bfloat16)
     grad_act = jnp.einsum(
-        "scw,fw->scf", grads_in, down_matrix, preferred_element_type=jnp.float32
+        "sckl,fkl->scf", grads_in, down_matrix, preferred_element_type=jnp.float32
     )
     grad_gate = (grad_act * up_pre * sigma * (1.0 + gate_pre * (1.0 - sigma))).astype(jnp.bfloat16)
     grad_up = (grad_act * gate_pre * sigma).astype(jnp.bfloat16)
     grad_back = jnp.einsum(
-        "scf,wf->scw", grad_gate, gate_matrix, preferred_element_type=jnp.float32
+        "scf,klf->sckl", grad_gate, gate_matrix, preferred_element_type=jnp.float32
     )
     grad_back = grad_back + jnp.einsum(
-        "scf,wf->scw", grad_up, up_matrix, preferred_element_type=jnp.float32
+        "scf,klf->sckl", grad_up, up_matrix, preferred_element_type=jnp.float32
     )
     grad_back = grad_back.astype(jnp.bfloat16)
-    result_home = from_experts(result)
-    grad_home = from_experts(grad_back)
+    result_home = from_experts(result.reshape(flat_shape)).reshape(split_shape)
+    grad_home = from_experts(grad_back.reshape(flat_shape)).reshape(split_shape)
     moe_sum = jnp.einsum(
-        "dct,dcw->tw",
+        "dct,dckl->tkl",
         weighting,
         result_home.astype(jnp.float32),
         precision=highest_prec,
-    )
+    ).reshape(owned, width)
     layer_out = (hidden.astype(jnp.float32) + moe_sum).astype(jnp.bfloat16)
     grad_moe = jnp.einsum(
-        "dct,dcw->tw", placement, grad_home, preferred_element_type=jnp.float32
-    )
+        "dct,dckl->tkl", placement, grad_home, preferred_element_type=jnp.float32
+    ).reshape(owned, width)
     grad_hidden = cotangent + rms_backward(hidden, moe_gain, inverse_two, grad_moe)
     grad_low = grad_hidden.astype(jnp.bfloat16)
     grad_gathered = head_rows(grad_low)

time: 244 us -> 227 us (0.930)
  waiting for transfers between devices: 77.9 us -> 53.9 us
  local copies, waits for them, and re-layouts: 13.9 us -> 27.8 us
  blocking collectives: 72.5 us -> 65.4 us
    all_to_all x1, waiting for transfers between devices: 21.3 us -> 6 us  [from_experts(): lax.all_to_all(results, ('expert', 'head'), split_axis=0, concat_axis=0,...]
    all_to_all x2, waiting for transfers between devices: 29.2 us -> 16.5 us  [to_experts(): lax.all_to_all(outgoing, ('expert', 'head'), split_axis=0, concat_axis=0,...]
    all_to_all x1, blocking collectives: 30.2 us -> 23.1 us  [from_experts(): lax.all_to_all(results, ('expert', 'head'), split_axis=0, concat_axis=0,...]
    reshape x0 -> x6, local copies, waits for them, and re-layouts: none -> 6.51 us  [the longest x2 3.19 us: body(): result_home = from_experts(result.reshape(flat_shape)).reshape(split_shape)]
    unnamed x65 -> x50, local copies, waits for them, and re-layouts: 0.87 us -> 5.72 us
    convert_element_type x4 -> x0, local copies, waits for them, and re-layouts: 4.81 us -> none  [the longest x1 1.48 us: body(): result = jnp.einsum('scf,fw->scw', activated, down_matrix, preferred_elem...]
    dot_general x10, matrix products: 20.1 us -> 15.6 us  [the longest x1 3.08 us: body(): jnp.einsum('scf,fkl->sckl', activated, down_matrix, preferred_element_typ...]
    dot_general x0 -> x2, local copies, waits for them, and re-layouts: none -> 4.26 us  [the longest x1 2.14 us: body(): jnp.einsum('dct,dckl->tkl', placement, grad_home, preferred_element_type=...]
  transfers between devices with their start and end apart: 6 -> 6, of which waited for: 5 -> 6; matrix products, arithmetic and copies ran while one was open for 11% -> 15% of each run, Pallas kernels for 0% -> 0%
where the time goes in v8:
time: 227 us; the launch traced here: 226 us
  blocking collectives  65.4 us (29%)
  waiting for transfers between devices  53.9 us (24%)
  matrix products  41.2 us (18%)
  local copies, waits for them, and re-layouts  27.8 us (12%)
  between operations  14.2 us (6%)
  starting transfers between devices  13.6 us (6%)
  other arithmetic  9.35 us (4%)
    all_gather x2, blocking collectives, head_rows(): return lax.all_gather(row_block, 'head', axis=0, tiled=True)  30.2 us
    reduce_scatter x2, waiting for transfers between devices, head_sums(): lax.psum_scatter(partial_rows, 'head', scatter_dimension=0, tiled=True)  26.3 us
    all_to_all x1, blocking collectives, from_experts(): lax.all_to_all(results, ('expert', 'head'), split_axis=0, concat_axis=0,...  23.1 us
    all_to_all x2, waiting for transfers between devices, to_experts(): lax.all_to_all(outgoing, ('expert', 'head'), split_axis=0, concat_axis=0,...  16.5 us
    all_gather x1, blocking collectives, attention_forward(): kv_rows = lax.all_gather(own_rows, 'head', axis=1, tiled=True)  12.1 us
    all_to_all x2, starting transfers between devices, to_experts(): lax.all_to_all(outgoing, ('expert', 'head'), split_axis=0, concat_axis=0,...  9.24 us
    all_to_all x1, waiting for transfers between devices, from_experts(): lax.all_to_all(results, ('expert', 'head'), split_axis=0, concat_axis=0,...  6 us
    unnamed x50, local copies, waits for them, and re-layouts  5.72 us
  transfers between devices with their start and end apart: 6, of which 6 were waited for; matrix products, arithmetic and copies ran while one was open for 15% of the time, Pallas kernels for 0%

profile of v8, /device:TPU:0, one launch (start us, length us, event | category | flops | bytes accessed | tf_op | source)
XLA Modules:
  0.0 225.5 jit_solution(986717887693939955)
XLA Ops:
  11.6 15.6 %all_gather.9 = bf16[64,2048]{1,0:T(8,128)(2,1)S(1)} all-gather(bf16[16,2048]{1,0:T(8,128)(2,1)S(1)} %fusion.50), channel_id=1, replica_groups=mesh['groups'=2,'expert'=4,'head'=4] {'head'}, dimensions={0}, use_global_device_ids=true | all-gather | bytes 327680 | tf_op jit(solution)/shard_map/all_gather | solution.py:159
  27.2 1.3 convolution_convert_fusion.6
  28.6 2.1 convolution_convert_fusion.5
  30.7 12.1 %all_gather.10 = bf16[64,512]{1,0:T(8,128)(2,1)S(1)} all-gather(bf16[64,128]{1,0:T(8,128)(2,1)S(1)} %convolution_convert_fusion.6), channel_id=1, replica_groups=mesh['groups'=2,'expert'=4,'head'=4] {'head'}, dimensions={1}, use_global_device_ids=true | all-gather | bytes 81920 | tf_op jit(solution)/shard_map/all_gather | solution.py:97
  43.7 1.1 fusion.26
  44.9 2.9 %fusion.66 = f32[64,2048]{1,0:T(8,128)} fusion(bf16[512,2048]{1,0:T(8,128)(2,1)} %param.28, bf16[8,8,4,128]{3,2,1,0:T(4,128)(2,1)S(1)} %bitcast.187), kind=kOutput, calls=%fused_computation.93 | convolution fusion | flops 134217728 | bytes 2686976 | tf_op jit(solution)/shard_map/dot_general | solution.py:203
  49.7 1.3 convolution_convert_fusion
  51.0 1.0 copy.135
  52.0 5.0 %all-to-all-start.2 = ((bf16[16,176,128]{2,1,0:T(8,128)(2,1)}), bf16[16,176,128]{2,1,0:T(8,128)(2,1)}, u32[]{:S(2)}, u32[]{:S(2)}) async-start(bf16[16,176,128]{2,1,0:T(8,128)(2,1)} %copy.135), calls=%async_computation.3 | async-start | bytes 1441792 | tf_op jit(solution)/shard_map/all_to_all | solution.py:167
  57.4 18.7 %reduce-scatter.4.cloned.1.call-done = f32[16,2048]{1,0:T(8,128)} async-done(((f32[64,2048]{1,0:T(8,128)}), f32[16,2048]{1,0:T(8,128)}) %reduce-scatter.4.cloned.1.call-update) | async-done | bytes 131088 | tf_op jit(solution)/shard_map/reduce_scatter | solution.py:163
  76.0 1.0 fusion.58
  77.1 1.1 convolution_convert_fusion.1
  78.2 1.1 copy.126
  79.2 3.4 %all-to-all-done.2 = bf16[16,176,128]{2,1,0:T(8,128)(2,1)} async-done(((bf16[16,176,128]{2,1,0:T(8,128)(2,1)}), bf16[16,176,128]{2,1,0:T(8,128)(2,1)}, u32[]{:S(2)}, u32[]{:S(2)}) %all-to-all-start.2) | async-done | bytes 720928 | tf_op jit(solution)/shard_map/all_to_all | solution.py:167
  82.6 4.3 %all-to-all-start = ((bf16[16,176,128]{2,1,0:T(8,128)(2,1)}), bf16[16,176,128]{2,1,0:T(8,128)(2,1)}, u32[]{:S(2)}, u32[]{:S(2)}) async-start(bf16[16,176,128]{2,1,0:T(8,128)(2,1)} %copy.126), calls=%async_computation.1 | async-start | bytes 1441792 | tf_op jit(solution)/shard_map/all_to_all | solution.py:167
  87.0 2.9 %copy.167 = bf16[96,8,16,128]{3,2,1,0:T(8,128)(2,1)S(1)} copy(bf16[96,8,16,128]{3,1,2,0:T(8,128)(2,1)} %bitcast.174) | data formatting | bytes 6291456
  89.9 1.8 copy.136
  91.7 2.0 fusion.15
  93.7 13.1 %all-to-all-done = bf16[16,176,128]{2,1,0:T(8,128)(2,1)} async-done(((bf16[16,176,128]{2,1,0:T(8,128)(2,1)}), bf16[16,176,128]{2,1,0:T(8,128)(2,1)}, u32[]{:S(2)}, u32[]{:S(2)}) %all-to-all-start) | async-done | bytes 720928 | tf_op jit(solution)/shard_map/all_to_all | solution.py:167
  106.8 1.3 copy.127
  108.9 1.3 copy-done.1
  111.8 1.2 fusion.32
  113.0 1.2 fusion.14
  114.3 23.1 %all_to_all.20 = bf16[16,176,128]{2,1,0:T(8,128)(2,1)S(1)} all-to-all(bf16[16,176,128]{2,1,0:T(8,128)(2,1)S(1)} %copy.138), channel_id=1, replica_groups=mesh['groups'=2,'expert'=4,'head'=4] {'expert','head'}, dimensions={0} | all-to-all | bytes 1441792 | tf_op jit(solution)/shard_map/all_to_all | solution.py:171
  137.4 1.0 copy.223
  138.4 2.1 dot_general.91
  140.6 1.7 fusion.46
  143.8 14.6 %all_gather.11 = bf16[64,2048]{1,0:T(8,128)(2,1)S(1)} all-gather(bf16[16,2048]{1,0:T(8,128)(2,1)S(1)} %fusion.99), channel_id=1, replica_groups=mesh['groups'=2,'expert'=4,'head'=4] {'head'}, dimensions={0}, use_global_device_ids=true | all-gather | bytes 327680 | tf_op jit(solution)/shard_map/all_gather | solution.py:159
  158.4 3.0 %convolution_convert_fusion.3 = bf16[64,512]{1,0:T(8,128)(2,1)} fusion(bf16[64,2048]{1,0:T(8,128)(2,1)S(1)} %all_gather.11, bf16[512,2048]{1,0:T(8,128)(2,1)} %param.28), kind=kOutput, calls=%fused_computation.35 | convolution fusion | flops 134250496 | bytes 2424832 | tf_op jit(solution)/shard_map/td,fd->tf/dot_general | solution.py:130
  161.4 1.5 reshape.134
  162.9 1.7 convolution_bitcast_fusion.4
  164.5 1.8 convolution_bitcast_fusion.5
  166.4 3.0 %convolution_bitcast_fusion.6 = f32[4,48,128]{2,1,0:T(8,128)} fusion(f32[4,4,16,48]{3,2,1,0:T(8,128)} %convolution_bitcast_fusion.4, bf16[4,16,4,128]{3,2,1,0:T(4,128)(2,1)} %copy-done.11, f32[4,4,16,48]{3,2,1,0:T(8,128)} %get-tuple-element.7, f32[4,4,16]{2,1,0:T(4,128)} %copy-done.23), kind=kOutput, calls=%fused_computation.34 | convolution fusion | flops 3232047 | bytes 263168 | tf_op jit(solution)/shard_map/shbk,sbhd->skd/dot_general | solution.py:58
  172.8 3.1 %fusion.11 = bf16[16,11,16,128]{3,0,2,1:T(8,128)(2,1)S(1)} fusion(bf16[768,16,128]{2,1,0:T(8,128)(2,1)} %bitcast.176, f32[16,11,768]{2,0,1:T(8,128)} %copy-done.5, f32[16,11,768]{2,0,1:T(8,128)} %copy-done.2), kind=kOutput, calls=%fused_computation.15 | convolution fusion | flops 554819584 | bytes 4947968 | tf_op jit(solution)/shard_map/scf,fkl->sckl/dot_general | solution.py:250
  175.9 1.1 copy.129
  177.0 4.3 %all-to-all-start.1 = ((bf16[16,176,128]{2,1,0:T(8,128)(2,1)}), bf16[16,176,128]{2,1,0:T(8,128)(2,1)}, u32[]{:S(2)}, u32[]{:S(2)}) async-start(bf16[16,176,128]{2,1,0:T(8,128)(2,1)} %copy.129), calls=%async_computation.2 | async-start | bytes 1441792 | tf_op jit(solution)/shard_map/all_to_all | solution.py:171
  181.3 2.9 %fusion.27 = bf16[4,16,4,128]{3,1,2,0:T(8,128)(2,1)} fusion(f32[4,4,16,48]{3,2,1,0:T(8,128)} %convolution_bitcast_fusion.4, bf16[4,16,128]{2,1,0:T(8,128)(2,1)S(1)} %bitcast.194, bf16[4,32,128]{2,1,0:T(8,128)(2,1)} %copy-done.12, f32[4,4,16,48]{3,2,1,0:T(8,128)} %get-tuple-element.7, f32[4,4,16]{2,1,0:T(4,128)} %copy-done.23), kind=kOutput, calls=%fused_computation.39 | convolution fusion | flops 3363119 | bytes 214016 | tf_op jit(solution)/shard_map/shbk,skd->sbhd/dot_general | solution.py:55
  184.2 1.5 copy.145
  185.7 5.0 %reduce-scatter.6.cloned.1.call-done = f32[64,128]{1,0:T(8,128)} async-done(((f32[64,512]{1,0:T(8,128)}), f32[64,128]{1,0:T(8,128)}) %reduce-scatter.6.cloned.1.call-update) | async-done | bytes 32784 | tf_op jit(solution)/shard_map/reduce_scatter | solution.py:148
  190.7 1.7 fusion.104
  192.5 3.2 %convolution_add_fusion = f32[64,2048]{1,0:T(8,128)} fusion(f32[64,2048]{1,0:T(8,128)S(1)} %fusion.104, bf16[2048,512]{1,0:T(8,128)(2,1)} %param.26, bf16[8,8,4,128]{3,2,1,0:T(4,128)(2,1)} %bitcast.186), kind=kOutput, calls=%fused_computation.8 | convolution fusion | flops 134348800 | bytes 3211264 | tf_op jit(solution)/shard_map/tf,df->td/dot_general | solution.py:153
  195.7 6.0 %all-to-all-done.1 = bf16[16,176,128]{2,1,0:T(8,128)(2,1)} async-done(((bf16[16,176,128]{2,1,0:T(8,128)(2,1)}), bf16[16,176,128]{2,1,0:T(8,128)(2,1)}, u32[]{:S(2)}, u32[]{:S(2)}) %all-to-all-start.1) | async-done | bytes 720928 | tf_op jit(solution)/shard_map/all_to_all | solution.py:171
  201.7 2.1 copy.224
  203.8 2.1 dot_general.84
  205.9 2.6 %fusion.10 = bf16[16,2048]{1,0:T(8,128)(2,1)} fusion(f32[16,11,16]{2,1,0:T(8,128)S(1)} %fusion.30, bf16[2048,11,16]{0,2,1:T(8,128)(2,1)} %dot_general.84, bf16[16,2048]{1,0:T(8,128)(2,1)S(1)} %get-tuple-element.3), kind=kOutput, calls=%fused_computation.13 | convolution fusion | flops 69304320 | bytes 863232 | tf_op jit(solution)/shard_map/dct,dckl->tkl/dot_general | solution.py:267
  208.5 7.7 %reduce-scatter.8.cloned.1.call-done = f32[16,2048]{1,0:T(8,128)} async-done(((f32[64,2048]{1,0:T(8,128)}), f32[16,2048]{1,0:T(8,128)}) %reduce-scatter.8.cloned.1.call-update) | async-done | bytes 131088 | tf_op jit(solution)/shard_map/reduce_scatter | solution.py:163
  216.2 1.1 fusion.51
  217.3 1.7 fusion.55
  (88 shorter events, 15.0 us)
Async XLA Ops:
  7.2 101.0 %copy-start = (bf16[1,2048,768]{2,1,0:T(8,128)(2,1)S(1)}, bf16[1,2048,768]{2,1,0:T(8,128)(2,1)}, u32[]{:S(2)}) copy-start(bf16[1,2048,768]{2,1,0:T(8,128)(2,1)} %param.29) | copy-start | bytes 9437188
  7.2 68.8 %reduce-scatter.4.cloned.1.call-start = ((), (), s32[]{:S(2)}) async-start(), calls=%async_computation.7 | async-start | bytes 655360 | tf_op jit(solution)/shard_map/reduce_scatter | solution.py:163
  9.1 2.5 %copy-start.18 = (f32[16]{0:T(128)}, f32[16]{0:T(128)S(1)}, u32[]{:S(2)}) copy-start(f32[16]{0:T(128)S(1)} %add_rsqrt_fusion.1) | copy-start | bytes 196
  9.9 37.9 %copy-start.12 = (bf16[4,32,128]{2,1,0:T(8,128)(2,1)}, bf16[4,32,128]{2,1,0:T(8,128)(2,1)S(1)}, u32[]{:S(2)}) copy-start(bf16[4,32,128]{2,1,0:T(8,128)(2,1)S(1)} %constant_dynamic-slice_fusion.1) | copy-start | bytes 98308
  10.7 37.1 %copy-start.9 = (bf16[4,32,128]{2,1,0:T(8,128)(2,1)}, bf16[4,32,128]{2,1,0:T(8,128)(2,1)S(1)}, u32[]{:S(2)}) copy-start(bf16[4,32,128]{2,1,0:T(8,128)(2,1)S(1)} %constant_dynamic-slice_fusion.3) | copy-start | bytes 98308
  28.5 19.3 %copy-start.13 = (s32[16,8]{0,1:T(8,128)S(1)}, s32[16,8]{0,1:T(8,128)}, u32[]{:S(2)}) copy-start(s32[16,8]{0,1:T(8,128)} %param.19) | copy-start | bytes 1540
  28.5 20.1 %copy-start.22 = (s32[16]{0:T(128)S(1)}, s32[16]{0:T(128)}, u32[]{:S(2)}) copy-start(s32[16]{0:T(128)} %param.18) | copy-start | bytes 196
  28.5 21.1 %copy-start.7 = (bf16[16,2048]{1,0:T(8,128)(2,1)S(1)}, bf16[16,2048]{1,0:T(8,128)(2,1)}, u32[]{:S(2)}) copy-start(bf16[16,2048]{1,0:T(8,128)(2,1)} %param.17) | copy-start | bytes 196612
  30.7 17.2 %copy-start.11 = (bf16[4,16,4,128]{3,2,1,0:T(4,128)(2,1)}, bf16[4,16,4,128]{3,2,1,0:T(4,128)(2,1)S(1)}, u32[]{:S(2)}) copy-start(bf16[4,16,4,128]{3,2,1,0:T(4,128)(2,1)S(1)} %reshape.122) | copy-start | bytes 196612
  42.8 5.2 %copy-start.14 = (bf16[64,128]{1,0:T(8,128)(2,1)}, bf16[64,128]{1,0:T(8,128)(2,1)S(1)}, u32[]{:S(2)}) copy-start(bf16[64,128]{1,0:T(8,128)(2,1)S(1)} %get-tuple-element.4) | copy-start | bytes 49156
  43.7 4.9 %copy-start.23 = (f32[4,4,16]{2,1,0:T(4,128)}, f32[4,4,16]{2,1,0:T(4,128)S(1)}, u32[]{:S(2)}) copy-start(f32[4,4,16]{2,1,0:T(4,128)S(1)} %get-tuple-element.6) | copy-start | bytes 3076
  44.9 31.1 %copy-start.6 = (bf16[16,2048]{1,0:T(8,128)(2,1)S(1)}, bf16[16,2048]{1,0:T(8,128)(2,1)}, u32[]{:S(2)}) copy-start(bf16[16,2048]{1,0:T(8,128)(2,1)} %param.16) | copy-start | bytes 196612
  48.6 3.4 %copy-start.20 = (f32[16]{0:T(128)}, f32[16]{0:T(128)S(1)}, u32[]{:S(2)}) copy-start(f32[16]{0:T(128)S(1)} %convert_element_type.116) | copy-start | bytes 196
  52.0 30.6 %all-to-all-start.2 = ((bf16[16,176,128]{2,1,0:T(8,128)(2,1)}), bf16[16,176,128]{2,1,0:T(8,128)(2,1)}, u32[]{:S(2)}, u32[]{:S(2)}) async-start(bf16[16,176,128]{2,1,0:T(8,128)(2,1)} %copy.135), calls=%async_computation.3 | async-start | bytes 1441792 | tf_op jit(solution)/shard_map/all_to_all | solution.py:167
  57.4 32.5 %copy-start.8 = (pred[16,11,16]{2,1,0:T(8,128)(4,1)}, pred[16,11,16]{2,1,0:T(8,128)(4,1)S(1)}, u32[]{:S(2)}) copy-start(pred[16,11,16]{2,1,0:T(8,128)(4,1)S(1)} %compare_reduce_fusion) | copy-start | bytes 8452
  77.1 12.8 %copy-start.16 = (f32[16]{0:T(128)}, f32[16]{0:T(128)S(1)}, u32[]{:S(2)}) copy-start(f32[16]{0:T(128)S(1)} %add_rsqrt_fusion) | copy-start | bytes 196
  82.6 24.2 %all-to-all-start = ((bf16[16,176,128]{2,1,0:T(8,128)(2,1)}), bf16[16,176,128]{2,1,0:T(8,128)(2,1)}, u32[]{:S(2)}, u32[]{:S(2)}) async-start(bf16[16,176,128]{2,1,0:T(8,128)(2,1)} %copy.126), calls=%async_computation.1 | async-start | bytes 1441792 | tf_op jit(solution)/shard_map/all_to_all | solution.py:167
  86.9 103.8 %reduce-scatter.6.cloned.1.call-start = ((), (), s32[]{:S(2)}) async-start(), calls=%async_computation.8 | async-start | bytes 163840 | tf_op jit(solution)/shard_map/reduce_scatter | solution.py:148
  89.9 1.8 copy-start.3
  108.1 2.1 copy-start.1
  108.9 4.1 %copy-start.2 = (f32[16,11,768]{2,0,1:T(8,128)}, f32[16,11,768]{2,0,1:T(8,128)S(1)}, u32[]{:S(2)}) copy-start(f32[16,11,768]{2,0,1:T(8,128)S(1)} %convolution_bitcast_fusion.3) | copy-start | bytes 1622020
  110.2 1.6 copy-start.4
  111.0 0.8 copy-start.5
  142.3 0.5 copy-start.21
  172.8 8.5 %copy-start.15 = (bf16[64,128]{1,0:T(8,128)(2,1)S(1)}, bf16[64,128]{1,0:T(8,128)(2,1)}, u32[]{:S(2)}) copy-start(bf16[64,128]{1,0:T(8,128)(2,1)} %copy-done.14) | copy-start | bytes 49156
  177.0 24.7 %all-to-all-start.1 = ((bf16[16,176,128]{2,1,0:T(8,128)(2,1)}), bf16[16,176,128]{2,1,0:T(8,128)(2,1)}, u32[]{:S(2)}, u32[]{:S(2)}) async-start(bf16[16,176,128]{2,1,0:T(8,128)(2,1)} %copy.129), calls=%async_computation.2 | async-start | bytes 1441792 | tf_op jit(solution)/shard_map/all_to_all | solution.py:171
  181.2 35.0 %reduce-scatter.8.cloned.1.call-start = ((), (), s32[]{:S(2)}) async-start(), calls=%async_computation.9 | async-start | bytes 655360 | tf_op jit(solution)/shard_map/reduce_scatter | solution.py:163
  195.6 20.6 %copy-start.10 = (f32[2048]{0:T(1024)S(1)}, f32[2048]{0:T(1024)}, u32[]{:S(2)}) copy-start(f32[2048]{0:T(1024)} %param.24) | copy-start | bytes 24580
  195.6 20.6 %copy-start.19 = (f32[16]{0:T(128)S(1)}, f32[16]{0:T(128)}, u32[]{:S(2)}) copy-start(f32[16]{0:T(128)} %copy-done.18) | copy-start | bytes 196
  195.7 21.7 %copy-start.17 = (f32[16]{0:T(128)S(1)}, f32[16]{0:T(128)}, u32[]{:S(2)}) copy-start(f32[16]{0:T(128)} %copy-done.16) | copy-start | bytes 196
Sparse Core Ops, SparseCore 0:
  47.9 28.0 reduce-scatter.3
  172.9 17.7 reduce-scatter.5
  195.8 20.3 reduce-scatter.7

commit v9 on v8

--- a/solution.py
+++ b/solution.py
@@ -94,7 +94,7 @@
     own_rows = jnp.dot(row_block, own_kv_weights, preferred_element_type=jnp.float32).astype(
         jnp.bfloat16
     )
-    kv_rows = lax.all_gather(own_rows, "head", axis=1, tiled=True)
+    kv_rows = head_gather(own_rows, 1)
     pair_rows = jnp.concatenate(
         [
             lax.dynamic_slice_in_dim(kv_rows, kv_now * HEAD_SIZE, HEAD_SIZE, 1),
@@ -155,8 +155,22 @@
     )
 
 
+def head_gather(block, axis):
+    count = lax.axis_size("head")
+    me = lax.axis_index("head")
+    parts = [block] + [
+        lax.ppermute(block, "head", perm=[(j, (j + shift) % count) for j in range(count)])
+        for shift in range(1, count)
+    ]
+    ordered = jnp.take(jnp.stack(parts), (me - jnp.arange(count)) % count, axis=0)
+    ordered = jnp.moveaxis(ordered, 0, axis)
+    merged = list(block.shape)
+    merged[axis] = count * block.shape[axis]
+    return ordered.reshape(merged)
+
+
 def head_rows(row_block):
-    return lax.all_gather(row_block, "head", axis=0, tiled=True)
+    return head_gather(row_block, 0)
 
 
 def head_sums(partial_rows):

time: 227 us -> 217 us (0.956)
  blocking collectives: 65.4 us -> 23.1 us
  starting transfers between devices: 13.6 us -> 25.6 us
  waiting for transfers between devices: 53.9 us -> 63.4 us
  other arithmetic: 9.35 us -> 15.2 us
  local copies, waits for them, and re-layouts: 27.8 us -> 32.8 us
    all_gather x3 -> x0, blocking collectives: 42.3 us -> none  [the longest x2 30.2 us: head_rows(): return lax.all_gather(row_block, 'head', axis=0, tiled=True)]
    ppermute x0 -> x9, starting transfers between devices: none -> 12.6 us  [head_gather(): lax.ppermute(block, 'head', perm=[(j, (j + shift) % count) for j in range...]
    ppermute x0 -> x9, waiting for transfers between devices: none -> 8.62 us  [head_gather(): lax.ppermute(block, 'head', perm=[(j, (j + shift) % count) for j in range...]
    gather x0 -> x3, local copies, waits for them, and re-layouts: none -> 4.42 us  [head_gather(): jnp.take(jnp.stack(parts), (me - jnp.arange(count)) % count, axis=0)]
    another operation x0 -> x4, other arithmetic: none -> 3.31 us  [head_gather(): jnp.stack(parts)]
    unnamed x50 -> x58, local copies, waits for them, and re-layouts: 5.72 us -> 6.41 us
  transfers between devices with their start and end apart: 6 -> 15, of which waited for: 6 -> 10; matrix products, arithmetic and copies ran while one was open for 15% -> 19% of each run, Pallas kernels for 0% -> 0%
where the time goes in v9:
time: 217 us; the launch traced here: 215 us
  waiting for transfers between devices  63.4 us (29%)
  matrix products  40.5 us (19%)
  local copies, waits for them, and re-layouts  32.8 us (15%)
  starting transfers between devices  25.6 us (12%)
  blocking collectives  23.1 us (11%)
  other arithmetic  15.2 us (7%)
  between operations  14.4 us (7%)
    reduce_scatter x2, waiting for transfers between devices, head_sums(): lax.psum_scatter(partial_rows, 'head', scatter_dimension=0, tiled=True)  26.7 us
    all_to_all x1, blocking collectives, from_experts(): lax.all_to_all(results, ('expert', 'head'), split_axis=0, concat_axis=0,...  23.1 us
    all_to_all x2, waiting for transfers between devices, to_experts(): lax.all_to_all(outgoing, ('expert', 'head'), split_axis=0, concat_axis=0,...  16.9 us
    ppermute x9, starting transfers between devices, head_gather(): lax.ppermute(block, 'head', perm=[(j, (j + shift) % count) for j in range...  12.6 us
    ppermute x9, waiting for transfers between devices, head_gather(): lax.ppermute(block, 'head', perm=[(j, (j + shift) % count) for j in range...  8.62 us
    all_to_all x2, starting transfers between devices, to_experts(): lax.all_to_all(outgoing, ('expert', 'head'), split_axis=0, concat_axis=0,...  8.55 us
    unnamed x58, local copies, waits for them, and re-layouts  6.41 us
    reduce_scatter x1, waiting for transfers between devices, attention_backward(): lax.psum_scatter(placed, 'head', scatter_dimension=1, tiled=True)  5.68 us
  transfers between devices with their start and end apart: 15, of which 10 were waited for; matrix products, arithmetic and copies ran while one was open for 19% of the time, Pallas kernels for 0%

profile of v9, /device:TPU:0, one launch (start us, length us, event | category | flops | bytes accessed | tf_op | source)
XLA Modules:
  0.0 215.0 jit_solution(8757201991441671295)
XLA Ops:
  9.3 4.1 %collective-permute-start.1 = (bf16[16,2048]{1,0:T(8,128)(2,1)S(1)}, bf16[16,2048]{1,0:T(8,128)(2,1)S(1)}, u32[]{:S(2)}, u32[]{:S(2)}) collective-permute-start(bf16[16,2048]{1,0:T(8,128)(2,1)S(1)} %fusion.50), channel_id=1, source_target_pairs={{0,2},{1,3},{2,0},{3,1},{4,6},{5,7},{6,4},{7,5},{8,10},{9,11},{10,... | collective-permute-start | bytes 196616 | tf_op jit(solution)/shard_map/ppermute | solution.py:162
  13.4 1.6 collective-permute-start
  15.0 2.2 %collective-permute-start.2 = (bf16[16,2048]{1,0:T(8,128)(2,1)S(1)}, bf16[16,2048]{1,0:T(8,128)(2,1)}, u32[]{:S(2)}, u32[]{:S(2)}) collective-permute-start(bf16[16,2048]{1,0:T(8,128)(2,1)S(1)} %fusion.50), channel_id=1, source_target_pairs={{0,3},{1,0},{2,1},{3,2},{4,7},{5,4},{6,5},{7,6},{8,11},{9,8},{10,9... | collective-permute-start | bytes 196616 | tf_op jit(solution)/shard_map/ppermute | solution.py:162
  20.4 1.3 multiply_add_fusion.1
  23.1 1.6 pad_maximum_fusion
  24.7 1.5 gather_fusion.1
  26.3 1.3 convolution_convert_fusion.6
  29.7 2.1 convolution_convert_fusion.5
  32.6 1.8 collective-permute-done.3
  37.4 2.9 %fusion.66 = f32[64,2048]{1,0:T(8,128)} fusion(bf16[512,2048]{1,0:T(8,128)(2,1)} %param.30, bf16[8,8,4,128]{3,2,1,0:T(4,128)(2,1)S(1)} %bitcast.214), kind=kOutput, calls=%fused_computation.100 | convolution fusion | flops 134217728 | bytes 2686976 | tf_op jit(solution)/shard_map/dot_general | solution.py:217
  41.4 1.3 convolution_convert_fusion
  43.8 4.3 %all-to-all-start.2 = ((bf16[16,176,128]{2,1,0:T(8,128)(2,1)}), bf16[16,176,128]{2,1,0:T(8,128)(2,1)}, u32[]{:S(2)}, u32[]{:S(2)}) async-start(bf16[16,176,128]{2,1,0:T(8,128)(2,1)} %copy.140), calls=%async_computation.3 | async-start | bytes 1441792 | tf_op jit(solution)/shard_map/all_to_all | solution.py:181
  48.4 18.9 %reduce-scatter.4.cloned.1.call-done = f32[16,2048]{1,0:T(8,128)} async-done(((f32[64,2048]{1,0:T(8,128)}), f32[16,2048]{1,0:T(8,128)}) %reduce-scatter.4.cloned.1.call-update) | async-done | bytes 131088 | tf_op jit(solution)/shard_map/reduce_scatter | solution.py:177
  69.8 3.9 %all-to-all-done.2 = bf16[16,176,128]{2,1,0:T(8,128)(2,1)} async-done(((bf16[16,176,128]{2,1,0:T(8,128)(2,1)}), bf16[16,176,128]{2,1,0:T(8,128)(2,1)}, u32[]{:S(2)}, u32[]{:S(2)}) %all-to-all-start.2) | async-done | bytes 720928 | tf_op jit(solution)/shard_map/all_to_all | solution.py:181
  73.7 4.3 %all-to-all-start = ((bf16[16,176,128]{2,1,0:T(8,128)(2,1)}), bf16[16,176,128]{2,1,0:T(8,128)(2,1)}, u32[]{:S(2)}, u32[]{:S(2)}) async-start(bf16[16,176,128]{2,1,0:T(8,128)(2,1)} %copy.131), calls=%async_computation.1 | async-start | bytes 1441792 | tf_op jit(solution)/shard_map/all_to_all | solution.py:181
  78.0 2.9 %copy.173 = bf16[96,8,16,128]{3,2,1,0:T(8,128)(2,1)S(1)} copy(bf16[96,8,16,128]{3,1,2,0:T(8,128)(2,1)} %bitcast.197) | data formatting | bytes 6291456
  80.9 1.8 copy.141
  82.8 2.0 fusion.15
  84.8 13.1 %all-to-all-done = bf16[16,176,128]{2,1,0:T(8,128)(2,1)} async-done(((bf16[16,176,128]{2,1,0:T(8,128)(2,1)}), bf16[16,176,128]{2,1,0:T(8,128)(2,1)}, u32[]{:S(2)}, u32[]{:S(2)}) %all-to-all-start) | async-done | bytes 720928 | tf_op jit(solution)/shard_map/all_to_all | solution.py:181
  97.9 1.3 copy.132
  99.9 1.3 copy-done.1
  102.8 1.2 fusion.32
  104.0 1.2 fusion.14
  105.4 23.1 %all_to_all.20 = bf16[16,176,128]{2,1,0:T(8,128)(2,1)S(1)} all-to-all(bf16[16,176,128]{2,1,0:T(8,128)(2,1)S(1)} %copy.143), channel_id=1, replica_groups=mesh['groups'=2,'expert'=4,'head'=4] {'expert','head'}, dimensions={0} | all-to-all | bytes 1441792 | tf_op jit(solution)/shard_map/all_to_all | solution.py:185
  129.5 2.1 dot_general.91
  131.6 1.7 fusion.46
  135.7 1.3 collective-permute-start.7
  137.5 1.9 collective-permute-done.8
  139.4 4.1 %collective-permute-done.7 = bf16[16,2048]{1,0:T(8,128)(2,1)S(1)} collective-permute-done((bf16[16,2048]{1,0:T(8,128)(2,1)S(1)}, bf16[16,2048]{1,0:T(8,128)(2,1)S(1)}, u32[]{:S(2)}, u32[]{:S(2)}) %collective-permute-start.7) | collective-permute-done | bytes 65568 | tf_op jit(solution)/shard_map/ppermute | solution.py:162
  144.2 2.3 %gather_fusion.2 = bf16[4,16,2048]{2,1,0:T(8,128)(2,1)} fusion(bf16[4,16,2048]{2,1,0:T(8,128)(2,1)} %pad_maximum_fusion.1, s32[1024]{0:T(1024)} %copy-done.21), kind=kCustom, calls=%fused_computation.1.clone | custom fusion | bytes 524304 | tf_op jit(solution)/shard_map/jit(_take)/gather | solution.py:165
  147.6 3.0 %convolution_convert_fusion.3 = bf16[64,512]{1,0:T(8,128)(2,1)} fusion(bf16[64,2048]{1,0:T(8,128)(2,1)S(1)} %bitcast.208, bf16[512,2048]{1,0:T(8,128)(2,1)} %param.30), kind=kOutput, calls=%fused_computation.38 | convolution fusion | flops 134250496 | bytes 2424832 | tf_op jit(solution)/shard_map/td,fd->tf/dot_general | solution.py:130
  150.6 1.5 reshape.205
  152.1 1.7 convolution_bitcast_fusion.4
  153.7 1.8 convolution_bitcast_fusion.5
  155.6 3.0 %convolution_bitcast_fusion.6 = f32[4,48,128]{2,1,0:T(8,128)} fusion(f32[4,4,16,48]{3,2,1,0:T(8,128)} %convolution_bitcast_fusion.4, bf16[4,16,4,128]{3,2,1,0:T(4,128)(2,1)} %copy-done.11, f32[4,4,16,48]{3,2,1,0:T(8,128)} %get-tuple-element.8, f32[4,4,16]{2,1,0:T(4,128)} %copy-done.27), kind=kOutput, calls=%fused_computation.37 | convolution fusion | flops 3232047 | bytes 263168 | tf_op jit(solution)/shard_map/shbk,sbhd->skd/dot_general | solution.py:58
  162.0 3.1 %fusion.11 = bf16[16,11,16,128]{3,0,2,1:T(8,128)(2,1)S(1)} fusion(bf16[768,16,128]{2,1,0:T(8,128)(2,1)} %bitcast.199, f32[16,11,768]{2,0,1:T(8,128)} %copy-done.6, f32[16,11,768]{2,0,1:T(8,128)} %copy-done.2), kind=kOutput, calls=%fused_computation.18 | convolution fusion | flops 554819584 | bytes 4947968 | tf_op jit(solution)/shard_map/scf,fkl->sckl/dot_general | solution.py:264
  166.2 4.3 %all-to-all-start.1 = ((bf16[16,176,128]{2,1,0:T(8,128)(2,1)}), bf16[16,176,128]{2,1,0:T(8,128)(2,1)}, u32[]{:S(2)}, u32[]{:S(2)}) async-start(bf16[16,176,128]{2,1,0:T(8,128)(2,1)} %copy.134), calls=%async_computation.2 | async-start | bytes 1441792 | tf_op jit(solution)/shard_map/all_to_all | solution.py:185
  170.5 2.9 %fusion.27 = bf16[4,16,4,128]{3,1,2,0:T(8,128)(2,1)} fusion(f32[4,4,16,48]{3,2,1,0:T(8,128)} %convolution_bitcast_fusion.4, bf16[4,16,128]{2,1,0:T(8,128)(2,1)S(1)} %bitcast.226, bf16[4,32,128]{2,1,0:T(8,128)(2,1)} %copy-done.14, f32[4,4,16,48]{3,2,1,0:T(8,128)} %get-tuple-element.8, f32[4,4,16]{2,1,0:T(4,128)} %copy-done.27), kind=kOutput, calls=%fused_computation.42 | convolution fusion | flops 3363119 | bytes 214016 | tf_op jit(solution)/shard_map/shbk,skd->sbhd/dot_general | solution.py:55
  173.4 1.5 copy.150
  174.9 5.7 %reduce-scatter.6.cloned.1.call-done = f32[64,128]{1,0:T(8,128)} async-done(((f32[64,512]{1,0:T(8,128)}), f32[64,128]{1,0:T(8,128)}) %reduce-scatter.6.cloned.1.call-update) | async-done | bytes 32784 | tf_op jit(solution)/shard_map/reduce_scatter | solution.py:148
  180.6 1.7 fusion.107
  182.3 3.2 %convolution_add_fusion = f32[64,2048]{1,0:T(8,128)} fusion(f32[64,2048]{1,0:T(8,128)S(1)} %fusion.107, bf16[2048,512]{1,0:T(8,128)(2,1)} %param.28, bf16[8,8,4,128]{3,2,1,0:T(4,128)(2,1)} %bitcast.212), kind=kOutput, calls=%fused_computation.11 | convolution fusion | flops 134348800 | bytes 3211264 | tf_op jit(solution)/shard_map/tf,df->td/dot_general | solution.py:153
  185.5 5.5 %all-to-all-done.1 = bf16[16,176,128]{2,1,0:T(8,128)(2,1)} async-done(((bf16[16,176,128]{2,1,0:T(8,128)(2,1)}), bf16[16,176,128]{2,1,0:T(8,128)(2,1)}, u32[]{:S(2)}, u32[]{:S(2)}) %all-to-all-start.1) | async-done | bytes 720928 | tf_op jit(solution)/shard_map/all_to_all | solution.py:185
  190.9 2.2 %copy.231 = bf16[16,11,16,128]{3,2,0,1:T(8,128)(2,1)} copy(bf16[16,11,16,128]{3,2,1,0:T(8,128)(2,1)} %bitcast.35) | data formatting | bytes 1441792 | tf_op jit(solution)/shard_map/reshape | solution.py:279
  193.1 2.1 dot_general.84
  195.2 2.6 %fusion.10 = bf16[16,2048]{1,0:T(8,128)(2,1)} fusion(f32[16,11,16]{2,1,0:T(8,128)S(1)} %fusion.30, bf16[2048,11,16]{0,2,1:T(8,128)(2,1)} %dot_general.84, bf16[16,2048]{1,0:T(8,128)(2,1)S(1)} %get-tuple-element.4), kind=kOutput, calls=%fused_computation.16 | convolution fusion | flops 69304320 | bytes 863232 | tf_op jit(solution)/shard_map/dct,dckl->tkl/dot_general | solution.py:281
  197.8 7.8 %reduce-scatter.8.cloned.1.call-done = f32[16,2048]{1,0:T(8,128)} async-done(((f32[64,2048]{1,0:T(8,128)}), f32[16,2048]{1,0:T(8,128)}) %reduce-scatter.8.cloned.1.call-update) | async-done | bytes 131088 | tf_op jit(solution)/shard_map/reduce_scatter | solution.py:177
  206.8 1.7 fusion.55
  (125 shorter events, 31.1 us)
Async XLA Ops:
  7.2 92.0 %copy-start = (bf16[1,2048,768]{2,1,0:T(8,128)(2,1)S(1)}, bf16[1,2048,768]{2,1,0:T(8,128)(2,1)}, u32[]{:S(2)}) copy-start(bf16[1,2048,768]{2,1,0:T(8,128)(2,1)} %param.31) | copy-start | bytes 9437188
  7.2 60.1 %reduce-scatter.4.cloned.1.call-start = ((), (), s32[]{:S(2)}) async-start(), calls=%async_computation.7 | async-start | bytes 655360 | tf_op jit(solution)/shard_map/reduce_scatter | solution.py:177
  8.4 10.6 %copy-start.17 = (f32[16]{0:T(128)}, f32[16]{0:T(128)S(1)}, u32[]{:S(2)}) copy-start(f32[16]{0:T(128)S(1)} %add_rsqrt_fusion.1) | copy-start | bytes 196
  9.3 13.8 %collective-permute-start.1 = (bf16[16,2048]{1,0:T(8,128)(2,1)S(1)}, bf16[16,2048]{1,0:T(8,128)(2,1)S(1)}, u32[]{:S(2)}, u32[]{:S(2)}) collective-permute-start(bf16[16,2048]{1,0:T(8,128)(2,1)S(1)} %fusion.50), channel_id=1, source_target_pairs={{0,2},{1,3},{2,0},{3,1},{4,6},{5,7},{6,4},{7,5},{8,10},{9,11},{10,... | collective-permute-start | bytes 196616 | tf_op jit(solution)/shard_map/ppermute | solution.py:162
  13.4 9.7 %collective-permute-start = (bf16[16,2048]{1,0:T(8,128)(2,1)S(1)}, bf16[16,2048]{1,0:T(8,128)(2,1)}, u32[]{:S(2)}, u32[]{:S(2)}) collective-permute-start(bf16[16,2048]{1,0:T(8,128)(2,1)S(1)} %fusion.50), channel_id=1, source_target_pairs={{0,1},{1,2},{2,3},{3,0},{4,5},{5,6},{6,7},{7,4},{8,9},{9,10},{10,1... | collective-permute-start | bytes 196616 | tf_op jit(solution)/shard_map/ppermute | solution.py:162
  15.0 8.1 %collective-permute-start.2 = (bf16[16,2048]{1,0:T(8,128)(2,1)S(1)}, bf16[16,2048]{1,0:T(8,128)(2,1)}, u32[]{:S(2)}, u32[]{:S(2)}) collective-permute-start(bf16[16,2048]{1,0:T(8,128)(2,1)S(1)} %fusion.50), channel_id=1, source_target_pairs={{0,3},{1,0},{2,1},{3,2},{4,7},{5,4},{6,5},{7,6},{8,11},{9,8},{10,9... | collective-permute-start | bytes 196616 | tf_op jit(solution)/shard_map/ppermute | solution.py:162
  19.0 16.1 %copy-start.21 = (s32[1024]{0:T(1024)}, s32[1024]{0:T(1024)S(1)}, u32[]{:S(2)}) copy-start(s32[1024]{0:T(1024)S(1)} %pad_clamp_fusion.1) | copy-start | bytes 12292
  23.0 14.2 %copy-start.10 = (bf16[4,32,128]{2,1,0:T(8,128)(2,1)}, bf16[4,32,128]{2,1,0:T(8,128)(2,1)S(1)}, u32[]{:S(2)}) copy-start(bf16[4,32,128]{2,1,0:T(8,128)(2,1)S(1)} %get-tuple-element.12) | copy-start | bytes 98308
  23.0 14.2 %copy-start.14 = (bf16[4,32,128]{2,1,0:T(8,128)(2,1)}, bf16[4,32,128]{2,1,0:T(8,128)(2,1)S(1)}, u32[]{:S(2)}) copy-start(bf16[4,32,128]{2,1,0:T(8,128)(2,1)S(1)} %get-tuple-element.11) | copy-start | bytes 98308
  23.1 12.0 %copy-start.23 = (pred[4]{0:T(512)(128)(4,1)}, pred[4]{0:T(512)(128)(4,1)S(1)}, u32[]{:S(2)}) copy-start(pred[4]{0:T(512)(128)(4,1)S(1)} %compare_and_fusion) | copy-start | bytes 16
  24.7 10.5 %copy-start.26 = (pred[4,48]{1,0:T(4,128)(4,1)S(1)}, pred[4,48]{1,0:T(4,128)(4,1)}, u32[]{:S(2)}) copy-start(pred[4,48]{1,0:T(4,128)(4,1)} %concatenate.10) | copy-start | bytes 580
  27.6 12.7 %copy-start.25 = (s32[16]{0:T(128)S(1)}, s32[16]{0:T(128)}, u32[]{:S(2)}) copy-start(s32[16]{0:T(128)} %param.20) | copy-start | bytes 196
  27.6 13.7 %copy-start.7 = (bf16[16,2048]{1,0:T(8,128)(2,1)S(1)}, bf16[16,2048]{1,0:T(8,128)(2,1)}, u32[]{:S(2)}) copy-start(bf16[16,2048]{1,0:T(8,128)(2,1)} %param.19) | copy-start | bytes 196612
  27.6 4.2 %collective-permute-start.5 = (bf16[64,128]{1,0:T(8,128)(2,1)S(1)}, bf16[64,128]{1,0:T(8,128)(2,1)S(1)}, u32[]{:S(2)}, u32[]{:S(2)}) collective-permute-start(bf16[64,128]{1,0:T(8,128)(2,1)S(1)} %convolution_convert_fusion.6), channel_id=1, source_target_pairs={{0,3},{1,0},{2,1},{3,2},{4,7},{5,4},{6,5},{7,6},{8,11},{9,8},{10,9... | collective-permute-start | bytes 49160 | tf_op jit(solution)/shard_map/ppermute | solution.py:162
  28.0 4.6 %collective-permute-start.4 = (bf16[64,128]{1,0:T(8,128)(2,1)S(1)}, bf16[64,128]{1,0:T(8,128)(2,1)S(1)}, u32[]{:S(2)}, u32[]{:S(2)}) collective-permute-start(bf16[64,128]{1,0:T(8,128)(2,1)S(1)} %convolution_convert_fusion.6), channel_id=1, source_target_pairs={{0,2},{1,3},{2,0},{3,1},{4,6},{5,7},{6,4},{7,5},{8,10},{9,11},{10,... | collective-permute-start | bytes 49160 | tf_op jit(solution)/shard_map/ppermute | solution.py:162
  28.9 5.5 %collective-permute-start.3 = (bf16[64,128]{1,0:T(8,128)(2,1)S(1)}, bf16[64,128]{1,0:T(8,128)(2,1)S(1)}, u32[]{:S(2)}, u32[]{:S(2)}) collective-permute-start(bf16[64,128]{1,0:T(8,128)(2,1)S(1)} %convolution_convert_fusion.6), channel_id=1, source_target_pairs={{0,1},{1,2},{2,3},{3,0},{4,5},{5,6},{6,7},{7,4},{8,9},{9,10},{10,1... | collective-permute-start | bytes 49160 | tf_op jit(solution)/shard_map/ppermute | solution.py:162
  31.8 12.0 %copy-start.11 = (bf16[4,16,4,128]{3,2,1,0:T(4,128)(2,1)}, bf16[4,16,4,128]{3,2,1,0:T(4,128)(2,1)S(1)}, u32[]{:S(2)}) copy-start(bf16[4,16,4,128]{3,2,1,0:T(4,128)(2,1)S(1)} %reshape.192) | copy-start | bytes 196612
  35.2 2.1 copy-start.15
  36.1 1.2 copy-start.27
  37.3 10.7 %copy-start.12 = (s32[16,8]{0,1:T(8,128)S(1)}, s32[16,8]{0,1:T(8,128)}, u32[]{:S(2)}) copy-start(s32[16,8]{0,1:T(8,128)} %multiply_add_fusion.1) | copy-start | bytes 1540
  37.3 30.0 %copy-start.4 = (bf16[16,2048]{1,0:T(8,128)(2,1)S(1)}, bf16[16,2048]{1,0:T(8,128)(2,1)}, u32[]{:S(2)}) copy-start(bf16[16,2048]{1,0:T(8,128)(2,1)} %param.18) | copy-start | bytes 196612
  37.3 31.0 %copy-start.13 = (f32[2048]{0:T(1024)S(1)}, f32[2048]{0:T(1024)}, u32[]{:S(2)}) copy-start(f32[2048]{0:T(1024)} %param.27) | copy-start | bytes 24580
  40.3 29.5 %copy-start.22 = (f32[16]{0:T(128)}, f32[16]{0:T(128)S(1)}, u32[]{:S(2)}) copy-start(f32[16]{0:T(128)S(1)} %convert_element_type.116) | copy-start | bytes 196
  43.8 29.9 %all-to-all-start.2 = ((bf16[16,176,128]{2,1,0:T(8,128)(2,1)}), bf16[16,176,128]{2,1,0:T(8,128)(2,1)}, u32[]{:S(2)}, u32[]{:S(2)}) async-start(bf16[16,176,128]{2,1,0:T(8,128)(2,1)} %copy.140), calls=%async_computation.3 | async-start | bytes 1441792 | tf_op jit(solution)/shard_map/all_to_all | solution.py:181
  48.4 32.5 %copy-start.8 = (pred[16,11,16]{2,1,0:T(8,128)(4,1)}, pred[16,11,16]{2,1,0:T(8,128)(4,1)S(1)}, u32[]{:S(2)}) copy-start(pred[16,11,16]{2,1,0:T(8,128)(4,1)S(1)} %compare_reduce_fusion) | copy-start | bytes 8452
  68.3 12.6 %copy-start.19 = (f32[16]{0:T(128)}, f32[16]{0:T(128)S(1)}, u32[]{:S(2)}) copy-start(f32[16]{0:T(128)S(1)} %add_rsqrt_fusion) | copy-start | bytes 196
  73.7 24.2 %all-to-all-start = ((bf16[16,176,128]{2,1,0:T(8,128)(2,1)}), bf16[16,176,128]{2,1,0:T(8,128)(2,1)}, u32[]{:S(2)}, u32[]{:S(2)}) async-start(bf16[16,176,128]{2,1,0:T(8,128)(2,1)} %copy.131), calls=%async_computation.1 | async-start | bytes 1441792 | tf_op jit(solution)/shard_map/all_to_all | solution.py:181
  78.0 102.6 %reduce-scatter.6.cloned.1.call-start = ((), (), s32[]{:S(2)}) async-start(), calls=%async_computation.8 | async-start | bytes 163840 | tf_op jit(solution)/shard_map/reduce_scatter | solution.py:148
  80.9 1.8 copy-start.3
  99.2 2.1 copy-start.1
  99.9 4.1 %copy-start.2 = (f32[16,11,768]{2,0,1:T(8,128)}, f32[16,11,768]{2,0,1:T(8,128)S(1)}, u32[]{:S(2)}) copy-start(f32[16,11,768]{2,0,1:T(8,128)S(1)} %convolution_bitcast_fusion.3) | copy-start | bytes 1622020
  101.3 1.6 copy-start.5
  102.0 0.8 copy-start.6
  133.4 0.5 copy-start.24
  134.8 4.5 %collective-permute-start.8 = (bf16[16,2048]{1,0:T(8,128)(2,1)S(1)}, bf16[16,2048]{1,0:T(8,128)(2,1)S(1)}, u32[]{:S(2)}, u32[]{:S(2)}) collective-permute-start(bf16[16,2048]{1,0:T(8,128)(2,1)S(1)} %fusion.102), channel_id=1, source_target_pairs={{0,3},{1,0},{2,1},{3,2},{4,7},{5,4},{6,5},{7,6},{8,11},{9,8},{10,9... | collective-permute-start | bytes 196616 | tf_op jit(solution)/shard_map/ppermute | solution.py:162
  135.7 7.7 %collective-permute-start.7 = (bf16[16,2048]{1,0:T(8,128)(2,1)S(1)}, bf16[16,2048]{1,0:T(8,128)(2,1)S(1)}, u32[]{:S(2)}, u32[]{:S(2)}) collective-permute-start(bf16[16,2048]{1,0:T(8,128)(2,1)S(1)} %fusion.102), channel_id=1, source_target_pairs={{0,2},{1,3},{2,0},{3,1},{4,6},{5,7},{6,4},{7,5},{8,10},{9,11},{10,... | collective-permute-start | bytes 196616 | tf_op jit(solution)/shard_map/ppermute | solution.py:162
  137.0 6.5 %collective-permute-start.6 = (bf16[16,2048]{1,0:T(8,128)(2,1)S(1)}, bf16[16,2048]{1,0:T(8,128)(2,1)S(1)}, u32[]{:S(2)}, u32[]{:S(2)}) collective-permute-start(bf16[16,2048]{1,0:T(8,128)(2,1)S(1)} %fusion.102), channel_id=1, source_target_pairs={{0,1},{1,2},{2,3},{3,0},{4,5},{5,6},{6,7},{7,4},{8,9},{9,10},{10,1... | collective-permute-start | bytes 196616 | tf_op jit(solution)/shard_map/ppermute | solution.py:162
  162.0 8.5 %copy-start.16 = (bf16[64,128]{1,0:T(8,128)(2,1)S(1)}, bf16[64,128]{1,0:T(8,128)(2,1)}, u32[]{:S(2)}) copy-start(bf16[64,128]{1,0:T(8,128)(2,1)} %copy-done.15) | copy-start | bytes 49156
  166.2 24.8 %all-to-all-start.1 = ((bf16[16,176,128]{2,1,0:T(8,128)(2,1)}), bf16[16,176,128]{2,1,0:T(8,128)(2,1)}, u32[]{:S(2)}, u32[]{:S(2)}) async-start(bf16[16,176,128]{2,1,0:T(8,128)(2,1)} %copy.134), calls=%async_computation.2 | async-start | bytes 1441792 | tf_op jit(solution)/shard_map/all_to_all | solution.py:185
  170.4 35.2 %reduce-scatter.8.cloned.1.call-start = ((), (), s32[]{:S(2)}) async-start(), calls=%async_computation.9 | async-start | bytes 655360 | tf_op jit(solution)/shard_map/reduce_scatter | solution.py:177
  185.4 20.2 %copy-start.9 = (f32[2048]{0:T(1024)S(1)}, f32[2048]{0:T(1024)}, u32[]{:S(2)}) copy-start(f32[2048]{0:T(1024)} %param.26) | copy-start | bytes 24580
  185.5 20.2 %copy-start.18 = (f32[16]{0:T(128)S(1)}, f32[16]{0:T(128)}, u32[]{:S(2)}) copy-start(f32[16]{0:T(128)} %copy-done.17) | copy-start | bytes 196
  185.5 21.3 %copy-start.20 = (f32[16]{0:T(128)S(1)}, f32[16]{0:T(128)}, u32[]{:S(2)}) copy-start(f32[16]{0:T(128)} %copy-done.19) | copy-start | bytes 196
Sparse Core Ops, SparseCore 0:
  40.4 26.8 reduce-scatter.3
  162.1 18.3 reduce-scatter.5
  185.6 20.0 reduce-scatter.7

commit v10 on v9

--- a/solution.py
+++ b/solution.py
@@ -174,7 +174,17 @@
 
 
 def head_sums(partial_rows):
-    return lax.psum_scatter(partial_rows, "head", scatter_dimension=0, tiled=True)
+    count = lax.axis_size("head")
+    me = lax.axis_index("head")
+    chunks = partial_rows.reshape((count, -1) + partial_rows.shape[1:])
+    total = chunks[me]
+    for shift in range(1, count):
+        total = total + lax.ppermute(
+            chunks[(me + shift) % count],
+            "head",
+            perm=[(j, (j + shift) % count) for j in range(count)],
+        )
+    return total
 
 
 def to_experts(outgoing):

time: 217 us -> 209 us (0.963)
  waiting for transfers between devices: 63.4 us -> 49.5 us
  starting transfers between devices: 25.6 us -> 36.6 us
  matrix products: 40.5 us -> 37.2 us
    reduce_scatter x2 -> x0, waiting for transfers between devices: 26.7 us -> none  [head_sums(): lax.psum_scatter(partial_rows, 'head', scatter_dimension=0, tiled=True)]
    ppermute x0 -> x6, waiting for transfers between devices: none -> 17.4 us  [head_sums(): lax.ppermute(chunks[(me + shift) % count], 'head', perm=[(j, (j + shift)...]
    ppermute x0 -> x6, starting transfers between devices: none -> 7.7 us  [head_sums(): lax.ppermute(chunks[(me + shift) % count], 'head', perm=[(j, (j + shift)...]
    all_to_all x2, waiting for transfers between devices: 16.9 us -> 13.1 us  [to_experts(): lax.all_to_all(outgoing, ('expert', 'head'), split_axis=0, concat_axis=0,...]
    ppermute x9, starting transfers between devices: 12.6 us -> 15.2 us  [head_gather(): lax.ppermute(block, 'head', perm=[(j, (j + shift) % count) for j in range...]
    unnamed x58 -> x68, local copies, waits for them, and re-layouts: 6.41 us -> 8.03 us
  transfers between devices with their start and end apart: 15 -> 19, of which waited for: 10 -> 9; matrix products, arithmetic and copies ran while one was open for 19% -> 29% of each run, Pallas kernels for 0% -> 0%
where the time goes in v10:
time: 209 us; the launch traced here: 207 us
  waiting for transfers between devices  49.5 us (24%)
  matrix products  37.2 us (18%)
  starting transfers between devices  36.6 us (18%)
  local copies, waits for them, and re-layouts  32.4 us (16%)
  blocking collectives  23.2 us (11%)
  between operations  14.8 us (7%)
  other arithmetic  13.5 us (6%)
    all_to_all x1, blocking collectives, from_experts(): lax.all_to_all(results, ('expert', 'head'), split_axis=0, concat_axis=0,...  23.2 us
    ppermute x6, waiting for transfers between devices, head_sums(): lax.ppermute(chunks[(me + shift) % count], 'head', perm=[(j, (j + shift)...  17.4 us
    ppermute x9, starting transfers between devices, head_gather(): lax.ppermute(block, 'head', perm=[(j, (j + shift) % count) for j in range...  15.2 us
    all_to_all x2, waiting for transfers between devices, to_experts(): lax.all_to_all(outgoing, ('expert', 'head'), split_axis=0, concat_axis=0,...  13.1 us
    all_to_all x2, starting transfers between devices, to_experts(): lax.all_to_all(outgoing, ('expert', 'head'), split_axis=0, concat_axis=0,...  8.55 us
    unnamed x68, local copies, waits for them, and re-layouts  8.03 us
    ppermute x6, starting transfers between devices, head_sums(): lax.ppermute(chunks[(me + shift) % count], 'head', perm=[(j, (j + shift)...  7.7 us
    ppermute x9, waiting for transfers between devices, head_gather(): lax.ppermute(block, 'head', perm=[(j, (j + shift) % count) for j in range...  7.03 us
  transfers between devices with their start and end apart: 19, of which 9 were waited for; matrix products, arithmetic and copies ran while one was open for 29% of the time, Pallas kernels for 0%

profile of v10, /device:TPU:0, one launch (start us, length us, event | category | flops | bytes accessed | tf_op | source)
XLA Modules:
  0.0 207.1 jit_solution(2678612242105814052)
XLA Ops:
  9.3 4.1 %collective-permute-start.1 = (bf16[16,2048]{1,0:T(8,128)(2,1)S(1)}, bf16[16,2048]{1,0:T(8,128)(2,1)S(1)}, u32[]{:S(2)}, u32[]{:S(2)}) collective-permute-start(bf16[16,2048]{1,0:T(8,128)(2,1)S(1)} %fusion.52), channel_id=1, source_target_pairs={{0,2},{1,3},{2,0},{3,1},{4,6},{5,7},{6,4},{7,5},{8,10},{9,11},{10,... | collective-permute-start | bytes 196616 | tf_op jit(solution)/shard_map/ppermute | solution.py:162
  13.4 1.6 collective-permute-start
  15.0 2.2 %collective-permute-start.2 = (bf16[16,2048]{1,0:T(8,128)(2,1)S(1)}, bf16[16,2048]{1,0:T(8,128)(2,1)}, u32[]{:S(2)}, u32[]{:S(2)}) collective-permute-start(bf16[16,2048]{1,0:T(8,128)(2,1)S(1)} %fusion.52), channel_id=1, source_target_pairs={{0,3},{1,0},{2,1},{3,2},{4,7},{5,4},{6,5},{7,6},{8,11},{9,8},{10,9... | collective-permute-start | bytes 196616 | tf_op jit(solution)/shard_map/ppermute | solution.py:162
  21.7 2.2 %convolution_convert_fusion = bf16[16,11,16,128]{3,0,2,1:T(8,128)(2,1)S(1)} fusion(f32[16,11,16,1]{2,1,0,3:T(8,128)S(1)} %bitcast.243, bf16[16,2048]{1,0:T(8,128)(2,1)} %param.19, f32[16]{0:T(128)S(1)} %convert_element_type.116), kind=kOutput, calls=%fused_computation.21 | convolution fusion | flops 69632000 | bytes 797760 | tf_op jit(solution)/shard_map/dct,tkl->dckl/dot_general | solution.py:255
  24.9 4.3 %all-to-all-start.2 = ((bf16[16,176,128]{2,1,0:T(8,128)(2,1)}), bf16[16,176,128]{2,1,0:T(8,128)(2,1)}, u32[]{:S(2)}, u32[]{:S(2)}) async-start(bf16[16,176,128]{2,1,0:T(8,128)(2,1)} %copy.140), calls=%async_computation.2 | async-start | bytes 1441792 | tf_op jit(solution)/shard_map/all_to_all | solution.py:191
  30.2 1.4 constant_dynamic-slice_fusion.1
  31.6 1.6 pad_maximum_fusion
  33.2 1.5 gather_fusion.1
  34.9 1.3 convolution_convert_fusion.6
  36.2 3.6 %collective-permute-start.5 = (bf16[64,128]{1,0:T(8,128)(2,1)S(1)}, bf16[64,128]{1,0:T(8,128)(2,1)S(1)}, u32[]{:S(2)}, u32[]{:S(2)}) collective-permute-start(bf16[64,128]{1,0:T(8,128)(2,1)S(1)} %convolution_convert_fusion.6), channel_id=1, source_target_pairs={{0,3},{1,0},{2,1},{3,2},{4,7},{5,4},{6,5},{7,6},{8,11},{9,8},{10,9... | collective-permute-start | bytes 49160 | tf_op jit(solution)/shard_map/ppermute | solution.py:162
  40.8 2.1 convolution_convert_fusion.5
  43.0 7.0 %collective-permute-done.4 = bf16[64,128]{1,0:T(8,128)(2,1)S(1)} collective-permute-done((bf16[64,128]{1,0:T(8,128)(2,1)S(1)}, bf16[64,128]{1,0:T(8,128)(2,1)S(1)}, u32[]{:S(2)}, u32[]{:S(2)}) %collective-permute-start.4) | collective-permute-done | bytes 16416 | tf_op jit(solution)/shard_map/ppermute | solution.py:162
  51.4 1.6 fusion.111
  53.9 2.1 %fusion.11 = f32[4,16,2048]{2,1,0:T(8,128)S(1)} fusion(bf16[512,2048]{1,0:T(8,128)(2,1)} %param.30, bf16[4,4,2,8,128]{4,3,2,1,0:T(8,128)(2,1)S(1)} %fusion.28), kind=kOutput, calls=%fused_computation.17 | convolution fusion | flops 134217728 | bytes 2686976 | tf_op jit(solution)/shard_map/dot_general | solution.py:227
  58.0 3.4 %collective-permute-start.8 = (f32[16,2048]{1,0:T(8,128)}, f32[16,2048]{1,0:T(8,128)}, u32[]{:S(2)}, u32[]{:S(2)}) collective-permute-start(f32[16,2048]{1,0:T(8,128)} %get-tuple-element.11), channel_id=1, source_target_pairs={{0,3},{1,0},{2,1},{3,2},{4,7},{5,4},{6,5},{7,6},{8,11},{9,8},{10,9... | collective-permute-start | bytes 393224 | tf_op jit(solution)/shard_map/ppermute | solution.py:182
  61.7 4.2 %collective-permute-done.6 = f32[16,2048]{1,0:T(8,128)S(1)} collective-permute-done((f32[16,2048]{1,0:T(8,128)}, f32[16,2048]{1,0:T(8,128)S(1)}, u32[]{:S(2)}, u32[]{:S(2)}) %collective-permute-start.6) | collective-permute-done | bytes 131104 | tf_op jit(solution)/shard_map/ppermute | solution.py:182
  66.7 5.2 %collective-permute-done.7 = f32[16,2048]{1,0:T(8,128)} collective-permute-done((f32[16,2048]{1,0:T(8,128)}, f32[16,2048]{1,0:T(8,128)}, u32[]{:S(2)}, u32[]{:S(2)}) %collective-permute-start.7) | collective-permute-done | bytes 131104 | tf_op jit(solution)/shard_map/ppermute | solution.py:182
  74.5 4.3 %all-to-all-start = ((bf16[16,176,128]{2,1,0:T(8,128)(2,1)}), bf16[16,176,128]{2,1,0:T(8,128)(2,1)}, u32[]{:S(2)}, u32[]{:S(2)}) async-start(bf16[16,176,128]{2,1,0:T(8,128)(2,1)} %copy.131), calls=%async_computation | async-start | bytes 1441792 | tf_op jit(solution)/shard_map/all_to_all | solution.py:191
  78.8 2.9 %copy.173 = bf16[96,8,16,128]{3,2,1,0:T(8,128)(2,1)S(1)} copy(bf16[96,8,16,128]{3,1,2,0:T(8,128)(2,1)} %bitcast.229) | data formatting | bytes 6291456
  81.7 1.8 copy.141
  83.6 2.0 fusion.17
  85.6 13.1 %all-to-all-done = bf16[16,176,128]{2,1,0:T(8,128)(2,1)} async-done(((bf16[16,176,128]{2,1,0:T(8,128)(2,1)}), bf16[16,176,128]{2,1,0:T(8,128)(2,1)}, u32[]{:S(2)}, u32[]{:S(2)}) %all-to-all-start) | async-done | bytes 720928 | tf_op jit(solution)/shard_map/all_to_all | solution.py:191
  98.7 1.3 copy.132
  100.8 1.3 copy-done.1
  106.2 23.2 %all_to_all.20 = bf16[16,176,128]{2,1,0:T(8,128)(2,1)S(1)} all-to-all(bf16[16,176,128]{2,1,0:T(8,128)(2,1)S(1)} %copy.143), channel_id=1, replica_groups=mesh['groups'=2,'expert'=4,'head'=4] {'expert','head'}, dimensions={0} | all-to-all | bytes 1441792 | tf_op jit(solution)/shard_map/all_to_all | solution.py:195
  130.5 2.1 %dot_general.94 = bf16[2048,11,16]{0,2,1:T(8,128)(2,1)} reshape(bf16[16,128,11,16]{1,0,3,2:T(8,128)(2,1)} %bitcast.234) | data formatting | bytes 1441792 | tf_op jit(solution)/shard_map/dct,dckl->tkl/dot_general | solution.py:298
  132.6 1.7 fusion.48
  136.0 1.3 collective-permute-start.10
  137.8 3.1 %fusion.13 = bf16[16,11,16,128]{3,0,2,1:T(8,128)(2,1)S(1)} fusion(bf16[768,16,128]{2,1,0:T(8,128)(2,1)} %bitcast.231, f32[16,11,768]{2,0,1:T(8,128)} %copy-done.7, f32[16,11,768]{2,0,1:T(8,128)} %copy-done.2), kind=kOutput, calls=%fused_computation.20 | convolution fusion | flops 554819584 | bytes 4947968 | tf_op jit(solution)/shard_map/scf,fkl->sckl/dot_general | solution.py:274
  142.0 5.0 %all-to-all-start.1 = ((bf16[16,176,128]{2,1,0:T(8,128)(2,1)}), bf16[16,176,128]{2,1,0:T(8,128)(2,1)}, u32[]{:S(2)}, u32[]{:S(2)}) async-start(bf16[16,176,128]{2,1,0:T(8,128)(2,1)} %copy.134), calls=%async_computation.1 | async-start | bytes 1441792 | tf_op jit(solution)/shard_map/all_to_all | solution.py:195
  147.1 1.6 pad_maximum_fusion.1
  148.7 2.4 %gather_fusion.2 = bf16[4,16,2048]{2,1,0:T(8,128)(2,1)} fusion(bf16[4,16,2048]{2,1,0:T(8,128)(2,1)} %pad_maximum_fusion.1, s32[1024]{0:T(1024)} %copy-done.26), kind=kCustom, calls=%fused_computation.1.clone | custom fusion | bytes 524304 | tf_op jit(solution)/shard_map/jit(_take)/gather | solution.py:165
  152.1 2.4 %convolution_convert_fusion.3 = bf16[64,512]{1,0:T(8,128)(2,1)S(1)} fusion(bf16[64,2048]{1,0:T(8,128)(2,1)S(1)} %bitcast.242, bf16[512,2048]{1,0:T(8,128)(2,1)} %param.30), kind=kOutput, calls=%fused_computation.40 | convolution fusion | flops 134250496 | bytes 2424832 | tf_op jit(solution)/shard_map/td,fd->tf/dot_general | solution.py:130
  154.5 1.2 convolution_bitcast_fusion.5
  156.3 1.6 convolution_bitcast_fusion.4
  157.9 2.4 %convolution_bitcast_fusion.6 = f32[4,48,128]{2,1,0:T(8,128)S(1)} fusion(f32[4,4,16,48]{3,2,1,0:T(8,128)} %convolution_bitcast_fusion.4, bf16[4,16,4,128]{3,2,1,0:T(4,128)(2,1)} %copy-done.16, f32[4,4,16,48]{3,2,1,0:T(8,128)} %copy-done.32, f32[4,4,16]{2,1,0:T(4,128)} %get-tuple-element.15), kind=kOutput, calls=%fused_computation.39 | convolution fusion | flops 3232047 | bytes 263168 | tf_op jit(solution)/shard_map/shbk,sbhd->skd/dot_general | solution.py:58
  161.7 5.3 %all-to-all-done.1 = bf16[16,176,128]{2,1,0:T(8,128)(2,1)} async-done(((bf16[16,176,128]{2,1,0:T(8,128)(2,1)}), bf16[16,176,128]{2,1,0:T(8,128)(2,1)}, u32[]{:S(2)}, u32[]{:S(2)}) %all-to-all-start.1) | async-done | bytes 720928 | tf_op jit(solution)/shard_map/all_to_all | solution.py:195
  167.0 2.2 %copy.231 = bf16[16,11,16,128]{3,2,0,1:T(8,128)(2,1)} copy(bf16[16,11,16,128]{3,2,1,0:T(8,128)(2,1)} %bitcast.40) | data formatting | bytes 1441792 | tf_op jit(solution)/shard_map/reshape | solution.py:289
  169.1 2.1 %dot_general.87 = bf16[2048,11,16]{0,2,1:T(8,128)(2,1)} reshape(bf16[16,128,11,16]{1,0,3,2:T(8,128)(2,1)} %bitcast.235) | data formatting | bytes 1441792 | tf_op jit(solution)/shard_map/dct,dckl->tkl/dot_general | solution.py:291
  171.3 2.9 %fusion.29 = bf16[4,16,4,128]{3,1,2,0:T(8,128)(2,1)} fusion(f32[4,4,16,48]{3,2,1,0:T(8,128)} %convolution_bitcast_fusion.4, bf16[4,16,128]{2,1,0:T(8,128)(2,1)} %bitcast.257, bf16[4,32,128]{2,1,0:T(8,128)(2,1)} %get-tuple-element.19, f32[4,4,16,48]{3,2,1,0:T(8,128)} %copy-done.32, f32[4,4,16]{2,1,0:T(4,128)} %get-tuple-element.15), kind=kOutput, calls=%fused_computation.44 | convolution fusion | flops 3363119 | bytes 214016 | tf_op jit(solution)/shard_map/shbk,skd->sbhd/dot_general | solution.py:55
  174.2 1.5 copy.150
  175.7 6.6 %reduce-scatter.2.cloned.1.call-done = f32[64,128]{1,0:T(8,128)} async-done(((f32[64,512]{1,0:T(8,128)}), f32[64,128]{1,0:T(8,128)}) %reduce-scatter.2.cloned.1.call-update) | async-done | bytes 32784 | tf_op jit(solution)/shard_map/reduce_scatter | solution.py:148
  182.4 1.8 fusion.114
  184.2 2.4 %convolution_add_fusion = f32[64,2048]{1,0:T(8,128)S(1)} fusion(f32[64,2048]{1,0:T(8,128)S(1)} %fusion.114, bf16[2048,512]{1,0:T(8,128)(2,1)} %param.28, bf16[8,8,4,128]{3,2,1,0:T(4,128)(2,1)} %bitcast.246), kind=kOutput, calls=%fused_computation.11 | convolution fusion | flops 134348800 | bytes 3211264 | tf_op jit(solution)/shard_map/tf,df->td/dot_general | solution.py:153
  186.7 3.8 %collective-permute-start.14 = (f32[16,2048]{1,0:T(8,128)S(1)}, f32[16,2048]{1,0:T(8,128)S(1)}, u32[]{:S(2)}, u32[]{:S(2)}) collective-permute-start(f32[16,2048]{1,0:T(8,128)S(1)} %get-tuple-element.8), channel_id=1, source_target_pairs={{0,3},{1,0},{2,1},{3,2},{4,7},{5,4},{6,5},{7,6},{8,11},{9,8},{10,9... | collective-permute-start | bytes 393224 | tf_op jit(solution)/shard_map/ppermute | solution.py:182
  190.5 1.5 fusion.10
  192.0 2.4 %collective-permute-done.12 = f32[16,2048]{1,0:T(8,128)S(1)} collective-permute-done((f32[16,2048]{1,0:T(8,128)S(1)}, f32[16,2048]{1,0:T(8,128)S(1)}, u32[]{:S(2)}, u32[]{:S(2)}) %collective-permute-start.12) | collective-permute-done | bytes 131104 | tf_op jit(solution)/shard_map/ppermute | solution.py:182
  194.4 4.9 %collective-permute-done.13 = f32[16,2048]{1,0:T(8,128)S(1)} collective-permute-done((f32[16,2048]{1,0:T(8,128)S(1)}, f32[16,2048]{1,0:T(8,128)S(1)}, u32[]{:S(2)}, u32[]{:S(2)}) %collective-permute-start.13) | collective-permute-done | bytes 131104 | tf_op jit(solution)/shard_map/ppermute | solution.py:182
  (142 shorter events, 31.0 us)
Async XLA Ops:
  7.2 92.8 %copy-start = (bf16[1,2048,768]{2,1,0:T(8,128)(2,1)S(1)}, bf16[1,2048,768]{2,1,0:T(8,128)(2,1)}, u32[]{:S(2)}) copy-start(bf16[1,2048,768]{2,1,0:T(8,128)(2,1)} %param.31) | copy-start | bytes 9437188
  7.2 22.1 %copy-start.5 = (bf16[16,2048]{1,0:T(8,128)(2,1)S(1)}, bf16[16,2048]{1,0:T(8,128)(2,1)}, u32[]{:S(2)}) copy-start(bf16[16,2048]{1,0:T(8,128)(2,1)} %param.18) | copy-start | bytes 196612
  7.2 22.1 %copy-start.15 = (f32[2048]{0:T(1024)S(1)}, f32[2048]{0:T(1024)}, u32[]{:S(2)}) copy-start(f32[2048]{0:T(1024)} %param.26) | copy-start | bytes 24580
  7.2 22.2 %copy-start.31 = (s32[4]{0:T(128)S(1)}, s32[4]{0:T(128)}, u32[]{:S(2)}) copy-start(s32[4]{0:T(128)} %param.23) | copy-start | bytes 52
  8.3 26.5 %copy-start.22 = (f32[16]{0:T(128)}, f32[16]{0:T(128)S(1)}, u32[]{:S(2)}) copy-start(f32[16]{0:T(128)S(1)} %add_rsqrt_fusion.1) | copy-start | bytes 196
  9.3 22.3 %collective-permute-start.1 = (bf16[16,2048]{1,0:T(8,128)(2,1)S(1)}, bf16[16,2048]{1,0:T(8,128)(2,1)S(1)}, u32[]{:S(2)}, u32[]{:S(2)}) collective-permute-start(bf16[16,2048]{1,0:T(8,128)(2,1)S(1)} %fusion.52), channel_id=1, source_target_pairs={{0,2},{1,3},{2,0},{3,1},{4,6},{5,7},{6,4},{7,5},{8,10},{9,11},{10,... | collective-permute-start | bytes 196616 | tf_op jit(solution)/shard_map/ppermute | solution.py:162
  13.4 18.2 %collective-permute-start = (bf16[16,2048]{1,0:T(8,128)(2,1)S(1)}, bf16[16,2048]{1,0:T(8,128)(2,1)}, u32[]{:S(2)}, u32[]{:S(2)}) collective-permute-start(bf16[16,2048]{1,0:T(8,128)(2,1)S(1)} %fusion.52), channel_id=1, source_target_pairs={{0,1},{1,2},{2,3},{3,0},{4,5},{5,6},{6,7},{7,4},{8,9},{9,10},{10,1... | collective-permute-start | bytes 196616 | tf_op jit(solution)/shard_map/ppermute | solution.py:162
  15.0 16.6 %collective-permute-start.2 = (bf16[16,2048]{1,0:T(8,128)(2,1)S(1)}, bf16[16,2048]{1,0:T(8,128)(2,1)}, u32[]{:S(2)}, u32[]{:S(2)}) collective-permute-start(bf16[16,2048]{1,0:T(8,128)(2,1)S(1)} %fusion.52), channel_id=1, source_target_pairs={{0,3},{1,0},{2,1},{3,2},{4,7},{5,4},{6,5},{7,6},{8,11},{9,8},{10,9... | collective-permute-start | bytes 196616 | tf_op jit(solution)/shard_map/ppermute | solution.py:162
  17.9 11.6 %copy-start.27 = (f32[16]{0:T(128)}, f32[16]{0:T(128)S(1)}, u32[]{:S(2)}) copy-start(f32[16]{0:T(128)S(1)} %convert_element_type.116) | copy-start | bytes 196
  19.0 11.2 %copy-start.20 = (bf16[4,32,256]{2,1,0:T(8,128)(2,1)S(1)}, bf16[4,32,256]{2,1,0:T(8,128)(2,1)}, u32[]{:S(2)}) copy-start(bf16[4,32,256]{2,1,0:T(8,128)(2,1)} %param.24) | copy-start | bytes 196612
  24.9 49.6 %all-to-all-start.2 = ((bf16[16,176,128]{2,1,0:T(8,128)(2,1)}), bf16[16,176,128]{2,1,0:T(8,128)(2,1)}, u32[]{:S(2)}, u32[]{:S(2)}) async-start(bf16[16,176,128]{2,1,0:T(8,128)(2,1)} %copy.140), calls=%async_computation.2 | async-start | bytes 1441792 | tf_op jit(solution)/shard_map/all_to_all | solution.py:191
  29.5 5.3 %copy-start.26 = (s32[1024]{0:T(1024)}, s32[1024]{0:T(1024)S(1)}, u32[]{:S(2)}) copy-start(s32[1024]{0:T(1024)S(1)} %pad_clamp_fusion.1) | copy-start | bytes 12292
  31.5 22.4 %copy-start.14 = (bf16[4,32,128]{2,1,0:T(8,128)(2,1)}, bf16[4,32,128]{2,1,0:T(8,128)(2,1)S(1)}, u32[]{:S(2)}) copy-start(bf16[4,32,128]{2,1,0:T(8,128)(2,1)S(1)} %get-tuple-element.20) | copy-start | bytes 98308
  31.6 3.3 %copy-start.29 = (pred[4]{0:T(512)(128)(4,1)}, pred[4]{0:T(512)(128)(4,1)S(1)}, u32[]{:S(2)}) copy-start(pred[4]{0:T(512)(128)(4,1)S(1)} %compare_and_fusion) | copy-start | bytes 16
  34.9 16.5 %copy-start.19 = (bf16[4,32,128]{2,1,0:T(8,128)(2,1)S(1)}, bf16[4,32,128]{2,1,0:T(8,128)(2,1)}, u32[]{:S(2)}) copy-start(bf16[4,32,128]{2,1,0:T(8,128)(2,1)} %get-tuple-element.19) | copy-start | bytes 98308
  36.2 6.8 %collective-permute-start.5 = (bf16[64,128]{1,0:T(8,128)(2,1)S(1)}, bf16[64,128]{1,0:T(8,128)(2,1)S(1)}, u32[]{:S(2)}, u32[]{:S(2)}) collective-permute-start(bf16[64,128]{1,0:T(8,128)(2,1)S(1)} %convolution_convert_fusion.6), channel_id=1, source_target_pairs={{0,3},{1,0},{2,1},{3,2},{4,7},{5,4},{6,5},{7,6},{8,11},{9,8},{10,9... | collective-permute-start | bytes 49160 | tf_op jit(solution)/shard_map/ppermute | solution.py:162
  39.7 10.3 %collective-permute-start.4 = (bf16[64,128]{1,0:T(8,128)(2,1)S(1)}, bf16[64,128]{1,0:T(8,128)(2,1)S(1)}, u32[]{:S(2)}, u32[]{:S(2)}) collective-permute-start(bf16[64,128]{1,0:T(8,128)(2,1)S(1)} %convolution_convert_fusion.6), channel_id=1, source_target_pairs={{0,2},{1,3},{2,0},{3,1},{4,6},{5,7},{6,4},{7,5},{8,10},{9,11},{10,... | collective-permute-start | bytes 49160 | tf_op jit(solution)/shard_map/ppermute | solution.py:162
  39.7 10.3 %collective-permute-start.3 = (bf16[64,128]{1,0:T(8,128)(2,1)S(1)}, bf16[64,128]{1,0:T(8,128)(2,1)S(1)}, u32[]{:S(2)}, u32[]{:S(2)}) collective-permute-start(bf16[64,128]{1,0:T(8,128)(2,1)S(1)} %convolution_convert_fusion.6), channel_id=1, source_target_pairs={{0,1},{1,2},{2,3},{3,0},{4,5},{5,6},{6,7},{7,4},{8,9},{9,10},{10,1... | collective-permute-start | bytes 49160 | tf_op jit(solution)/shard_map/ppermute | solution.py:162
  42.9 30.1 %copy-start.18 = (f32[2048]{0:T(1024)S(1)}, f32[2048]{0:T(1024)}, u32[]{:S(2)}) copy-start(f32[2048]{0:T(1024)} %param.27) | copy-start | bytes 24580
  43.0 14.6 %copy-start.16 = (bf16[4,16,4,128]{3,2,1,0:T(4,128)(2,1)}, bf16[4,16,4,128]{3,2,1,0:T(4,128)(2,1)S(1)}, u32[]{:S(2)}) copy-start(bf16[4,16,4,128]{3,2,1,0:T(4,128)(2,1)S(1)} %reshape.196) | copy-start | bytes 196612
  51.3 1.6 copy-start.21
  51.4 23.2 %copy-start.17 = (bf16[64,128]{1,0:T(8,128)(2,1)}, bf16[64,128]{1,0:T(8,128)(2,1)S(1)}, u32[]{:S(2)}) copy-start(bf16[64,128]{1,0:T(8,128)(2,1)S(1)} %get-tuple-element.14) | copy-start | bytes 49156
  53.0 4.6 %copy-start.32 = (f32[4,4,16,48]{3,2,1,0:T(8,128)}, f32[4,4,16,48]{3,2,1,0:T(8,128)S(1)}, u32[]{:S(2)}) copy-start(f32[4,4,16,48]{3,2,1,0:T(8,128)S(1)} %get-tuple-element.16) | copy-start | bytes 147460
  57.6 8.4 %collective-permute-start.6 = (f32[16,2048]{1,0:T(8,128)}, f32[16,2048]{1,0:T(8,128)S(1)}, u32[]{:S(2)}, u32[]{:S(2)}) collective-permute-start(f32[16,2048]{1,0:T(8,128)} %get-tuple-element.10), channel_id=1, source_target_pairs={{0,1},{1,2},{2,3},{3,0},{4,5},{5,6},{6,7},{7,4},{8,9},{9,10},{10,1... | collective-permute-start | bytes 393224 | tf_op jit(solution)/shard_map/ppermute | solution.py:182
  58.0 8.7 %collective-permute-start.8 = (f32[16,2048]{1,0:T(8,128)}, f32[16,2048]{1,0:T(8,128)}, u32[]{:S(2)}, u32[]{:S(2)}) collective-permute-start(f32[16,2048]{1,0:T(8,128)} %get-tuple-element.11), channel_id=1, source_target_pairs={{0,3},{1,0},{2,1},{3,2},{4,7},{5,4},{6,5},{7,6},{8,11},{9,8},{10,9... | collective-permute-start | bytes 393224 | tf_op jit(solution)/shard_map/ppermute | solution.py:182
  61.4 10.5 %collective-permute-start.7 = (f32[16,2048]{1,0:T(8,128)}, f32[16,2048]{1,0:T(8,128)}, u32[]{:S(2)}, u32[]{:S(2)}) collective-permute-start(f32[16,2048]{1,0:T(8,128)} %get-tuple-element.12), channel_id=1, source_target_pairs={{0,2},{1,3},{2,0},{3,1},{4,6},{5,7},{6,4},{7,5},{8,10},{9,11},{10,... | collective-permute-start | bytes 393224 | tf_op jit(solution)/shard_map/ppermute | solution.py:182
  73.0 59.6 %copy-start.24 = (f32[16]{0:T(128)}, f32[16]{0:T(128)S(1)}, u32[]{:S(2)}) copy-start(f32[16]{0:T(128)S(1)} %add_rsqrt_fusion) | copy-start | bytes 196
  74.5 24.2 %all-to-all-start = ((bf16[16,176,128]{2,1,0:T(8,128)(2,1)}), bf16[16,176,128]{2,1,0:T(8,128)(2,1)}, u32[]{:S(2)}, u32[]{:S(2)}) async-start(bf16[16,176,128]{2,1,0:T(8,128)(2,1)} %copy.131), calls=%async_computation | async-start | bytes 1441792 | tf_op jit(solution)/shard_map/all_to_all | solution.py:191
  81.7 1.8 copy-start.4
  100.0 2.1 %copy-start.1 = (bf16[1,2048,768]{2,1,0:T(8,128)(2,1)S(1)}, bf16[1,2048,768]{2,1,0:T(8,128)(2,1)}, u32[]{:S(2)}) copy-start(bf16[1,2048,768]{2,1,0:T(8,128)(2,1)} %param.32) | copy-start | bytes 9437188
  100.8 4.1 %copy-start.2 = (f32[16,11,768]{2,0,1:T(8,128)}, f32[16,11,768]{2,0,1:T(8,128)S(1)}, u32[]{:S(2)}) copy-start(f32[16,11,768]{2,0,1:T(8,128)S(1)} %convolution_bitcast_fusion.3) | copy-start | bytes 1622020
  102.1 1.6 copy-start.6
  106.2 28.1 %copy-start.11 = (bf16[16,2048]{1,0:T(8,128)(2,1)S(1)}, bf16[16,2048]{1,0:T(8,128)(2,1)}, u32[]{:S(2)}) copy-start(bf16[16,2048]{1,0:T(8,128)(2,1)} %param.19) | copy-start | bytes 196612
  135.1 11.9 %collective-permute-start.11 = (bf16[16,2048]{1,0:T(8,128)(2,1)S(1)}, bf16[16,2048]{1,0:T(8,128)(2,1)S(1)}, u32[]{:S(2)}, u32[]{:S(2)}) collective-permute-start(bf16[16,2048]{1,0:T(8,128)(2,1)S(1)} %fusion.108), channel_id=1, source_target_pairs={{0,3},{1,0},{2,1},{3,2},{4,7},{5,4},{6,5},{7,6},{8,11},{9,8},{10,9... | collective-permute-start | bytes 196616 | tf_op jit(solution)/shard_map/ppermute | solution.py:162
  136.0 11.0 %collective-permute-start.10 = (bf16[16,2048]{1,0:T(8,128)(2,1)S(1)}, bf16[16,2048]{1,0:T(8,128)(2,1)}, u32[]{:S(2)}, u32[]{:S(2)}) collective-permute-start(bf16[16,2048]{1,0:T(8,128)(2,1)S(1)} %fusion.108), channel_id=1, source_target_pairs={{0,2},{1,3},{2,0},{3,1},{4,6},{5,7},{6,4},{7,5},{8,10},{9,11},{10,... | collective-permute-start | bytes 196616 | tf_op jit(solution)/shard_map/ppermute | solution.py:162
  137.3 9.8 %collective-permute-start.9 = (bf16[16,2048]{1,0:T(8,128)(2,1)S(1)}, bf16[16,2048]{1,0:T(8,128)(2,1)}, u32[]{:S(2)}, u32[]{:S(2)}) collective-permute-start(bf16[16,2048]{1,0:T(8,128)(2,1)S(1)} %fusion.108), channel_id=1, source_target_pairs={{0,1},{1,2},{2,3},{3,0},{4,5},{5,6},{6,7},{7,4},{8,9},{9,10},{10,1... | collective-permute-start | bytes 196616 | tf_op jit(solution)/shard_map/ppermute | solution.py:162
  140.9 10.2 %copy-start.30 = (pred[4]{0:T(512)(128)(4,1)S(1)}, pred[4]{0:T(512)(128)(4,1)}, u32[]{:S(2)}) copy-start(pred[4]{0:T(512)(128)(4,1)} %copy-done.29) | copy-start | bytes 16
  142.0 25.0 %all-to-all-start.1 = ((bf16[16,176,128]{2,1,0:T(8,128)(2,1)}), bf16[16,176,128]{2,1,0:T(8,128)(2,1)}, u32[]{:S(2)}, u32[]{:S(2)}) async-start(bf16[16,176,128]{2,1,0:T(8,128)(2,1)} %copy.134), calls=%async_computation.1 | async-start | bytes 1441792 | tf_op jit(solution)/shard_map/all_to_all | solution.py:195
  147.0 35.4 %reduce-scatter.2.cloned.1.call-start = ((), (), s32[]{:S(2)}) async-start(), calls=%async_computation.5 | async-start | bytes 163840 | tf_op jit(solution)/shard_map/reduce_scatter | solution.py:148
  171.3 19.2 %copy-start.10 = (f32[16,11,16]{2,1,0:T(8,128)S(1)}, f32[16,11,16]{2,1,0:T(8,128)}, u32[]{:S(2)}) copy-start(f32[16,11,16]{2,1,0:T(8,128)} %copy-done.9) | copy-start | bytes 33796
  175.7 23.5 %copy-start.23 = (f32[16]{0:T(128)S(1)}, f32[16]{0:T(128)}, u32[]{:S(2)}) copy-start(f32[16]{0:T(128)} %copy-done.22) | copy-start | bytes 196
  182.4 8.1 %copy-start.3 = (bf16[2048,11,16]{0,2,1:T(8,128)(2,1)S(1)}, bf16[2048,11,16]{0,2,1:T(8,128)(2,1)}, u32[]{:S(2)}) copy-start(bf16[2048,11,16]{0,2,1:T(8,128)(2,1)} %dot_general.87) | copy-start | bytes 2162692
  184.2 15.3 %copy-start.12 = (bf16[16,2048]{1,0:T(8,128)(2,1)S(1)}, bf16[16,2048]{1,0:T(8,128)(2,1)}, u32[]{:S(2)}) copy-start(bf16[16,2048]{1,0:T(8,128)(2,1)} %param.19) | copy-start | bytes 196612
  184.2 15.3 %copy-start.25 = (f32[16]{0:T(128)S(1)}, f32[16]{0:T(128)}, u32[]{:S(2)}) copy-start(f32[16]{0:T(128)} %copy-done.24) | copy-start | bytes 196
  184.2 15.3 %copy-start.28 = (f32[16]{0:T(128)S(1)}, f32[16]{0:T(128)}, u32[]{:S(2)}) copy-start(f32[16]{0:T(128)} %copy-done.27) | copy-start | bytes 196
  186.6 7.8 %collective-permute-start.12 = (f32[16,2048]{1,0:T(8,128)S(1)}, f32[16,2048]{1,0:T(8,128)S(1)}, u32[]{:S(2)}, u32[]{:S(2)}) collective-permute-start(f32[16,2048]{1,0:T(8,128)S(1)} %get-tuple-element.7), channel_id=1, source_target_pairs={{0,1},{1,2},{2,3},{3,0},{4,5},{5,6},{6,7},{7,4},{8,9},{9,10},{10,1... | collective-permute-start | bytes 393224 | tf_op jit(solution)/shard_map/ppermute | solution.py:182
  186.7 7.7 %collective-permute-start.14 = (f32[16,2048]{1,0:T(8,128)S(1)}, f32[16,2048]{1,0:T(8,128)S(1)}, u32[]{:S(2)}, u32[]{:S(2)}) collective-permute-start(f32[16,2048]{1,0:T(8,128)S(1)} %get-tuple-element.8), channel_id=1, source_target_pairs={{0,3},{1,0},{2,1},{3,2},{4,7},{5,4},{6,5},{7,6},{8,11},{9,8},{10,9... | collective-permute-start | bytes 393224 | tf_op jit(solution)/shard_map/ppermute | solution.py:182
  190.5 8.8 %collective-permute-start.13 = (f32[16,2048]{1,0:T(8,128)S(1)}, f32[16,2048]{1,0:T(8,128)S(1)}, u32[]{:S(2)}, u32[]{:S(2)}) collective-permute-start(f32[16,2048]{1,0:T(8,128)S(1)} %get-tuple-element.9), channel_id=1, source_target_pairs={{0,2},{1,3},{2,0},{3,1},{4,6},{5,7},{6,4},{7,5},{8,10},{9,11},{10,... | collective-permute-start | bytes 393224 | tf_op jit(solution)/shard_map/ppermute | solution.py:182
  (4 other events, 2.9 us)
Sparse Core Ops, SparseCore 0:
  161.8 20.4 reduce-scatter.1

commit v11 on v10

--- a/solution.py
+++ b/solution.py
@@ -162,7 +162,9 @@
         lax.ppermute(block, "head", perm=[(j, (j + shift) % count) for j in range(count)])
         for shift in range(1, count)
     ]
-    ordered = jnp.take(jnp.stack(parts), (me - jnp.arange(count)) % count, axis=0)
+    reversed_parts = parts[::-1]
+    doubled = jnp.stack(reversed_parts + reversed_parts)
+    ordered = lax.dynamic_slice_in_dim(doubled, count - 1 - me, count, 0)
     ordered = jnp.moveaxis(ordered, 0, axis)
     merged = list(block.shape)
     merged[axis] = count * block.shape[axis]
@@ -264,7 +266,7 @@
     grads_in = to_experts(grad_out.reshape(flat_shape)).reshape(split_shape)
     gate_matrix = w_gate[0].reshape(pieces, lanes, -1)
     up_matrix = w_up[0].reshape(pieces, lanes, -1)
-    down_matrix = w_down[0].reshape(-1, pieces, lanes)
+    down_matrix = w_down[0]
     gate_pre = jnp.einsum(
         "sckl,klf->scf", rows_in, gate_matrix, preferred_element_type=jnp.float32
     )
@@ -272,10 +274,13 @@
     sigma = jax.nn.sigmoid(gate_pre)
     activated = (gate_pre * sigma * up_pre).astype(jnp.bfloat16)
     result = jnp.einsum(
-        "scf,fkl->sckl", activated, down_matrix, preferred_element_type=jnp.float32
+        "scf,fw->scw", activated, down_matrix, preferred_element_type=jnp.float32
     ).astype(jnp.bfloat16)
     grad_act = jnp.einsum(
-        "sckl,fkl->scf", grads_in, down_matrix, preferred_element_type=jnp.float32
+        "scw,fw->scf",
+        grads_in.reshape(device_count, capacity, width),
+        down_matrix,
+        preferred_element_type=jnp.float32,
     )
     grad_gate = (grad_act * up_pre * sigma * (1.0 + gate_pre * (1.0 - sigma))).astype(jnp.bfloat16)
     grad_up = (grad_act * gate_pre * sigma).astype(jnp.bfloat16)

time: 209 us -> 236 us (1.13)
  waiting for transfers between devices: 49.5 us -> 68.2 us
  local copies, waits for them, and re-layouts: 32.4 us -> 36.8 us
  matrix products: 37.2 us -> 39.9 us
    ppermute x9, waiting for transfers between devices: 7.03 us -> 25.4 us  [head_gather(): lax.ppermute(block, 'head', perm=[(j, (j + shift) % count) for j in range...]
    all_to_all x1, waiting for transfers between devices: 5.27 us -> 0.01 us  [from_experts(): lax.all_to_all(results, ('expert', 'head'), split_axis=0, concat_axis=0,...]
    reduce_scatter x1, waiting for transfers between devices: 6.65 us -> 11.8 us  [attention_backward(): lax.psum_scatter(placed, 'head', scatter_dimension=1, tiled=True)]
    gather x3 -> x0, local copies, waits for them, and re-layouts: 4.43 us -> none  [head_gather(): jnp.take(jnp.stack(parts), (me - jnp.arange(count)) % count, axis=0)]
    another operation x0 -> x3, local copies, waits for them, and re-layouts: none -> 3.15 us  [the longest x1 2.29 us: body(): grads_in.reshape(device_count, capacity, width)]
    another operation x4 -> x1, other arithmetic: 3.31 us -> 0.69 us  [head_gather(): doubled = jnp.stack(reversed_parts + reversed_parts)]
    unnamed x68 -> x71, local copies, waits for them, and re-layouts: 8.03 us -> 9.88 us
  transfers between devices with their start and end apart: 19 -> 19, of which waited for: 9 -> 10; matrix products, arithmetic and copies ran while one was open for 29% -> 28% of each run, Pallas kernels for 0% -> 0%
where the time goes in v11:
time: 236 us; the launch traced here: 234 us
  waiting for transfers between devices  68.2 us (29%)
  matrix products  39.9 us (17%)
  starting transfers between devices  38.1 us (16%)
  local copies, waits for them, and re-layouts  36.8 us (16%)
  blocking collectives  23.1 us (10%)
  between operations  14.7 us (6%)
  other arithmetic  12.9 us (5%)
    ppermute x9, waiting for transfers between devices, head_gather(): lax.ppermute(block, 'head', perm=[(j, (j + shift) % count) for j in range...  25.4 us
    all_to_all x1, blocking collectives, from_experts(): lax.all_to_all(results, ('expert', 'head'), split_axis=0, concat_axis=0,...  23.1 us
    ppermute x6, waiting for transfers between devices, head_sums(): lax.ppermute(chunks[(me + shift) % count], 'head', perm=[(j, (j + shift)...  17.8 us
    ppermute x9, starting transfers between devices, head_gather(): lax.ppermute(block, 'head', perm=[(j, (j + shift) % count) for j in range...  17.5 us
    all_to_all x2, waiting for transfers between devices, to_experts(): lax.all_to_all(outgoing, ('expert', 'head'), split_axis=0, concat_axis=0,...  13.2 us
    reduce_scatter x1, waiting for transfers between devices, attention_backward(): lax.psum_scatter(placed, 'head', scatter_dimension=1, tiled=True)  11.8 us
    unnamed x71, local copies, waits for them, and re-layouts  9.88 us
    all_to_all x2, starting transfers between devices, to_experts(): lax.all_to_all(outgoing, ('expert', 'head'), split_axis=0, concat_axis=0,...  8.55 us
  transfers between devices with their start and end apart: 19, of which 10 were waited for; matrix products, arithmetic and copies ran while one was open for 28% of the time, Pallas kernels for 0%

profile of v11, /device:TPU:0, one launch (start us, length us, event | category | flops | bytes accessed | tf_op | source)
XLA Modules:
  0.0 233.6 jit_solution(15150255296068720430)
XLA Ops:
  8.3 1.6 fusion.47
  9.9 3.0 %collective-permute-start.2 = (bf16[16,2048]{1,0:T(8,128)(2,1)}, bf16[16,2048]{1,0:T(8,128)(2,1)S(1)}, u32[]{:S(2)}, u32[]{:S(2)}) collective-permute-start(bf16[16,2048]{1,0:T(8,128)(2,1)} %fusion.47), channel_id=1, source_target_pairs={{0,1},{1,2},{2,3},{3,0},{4,5},{5,6},{6,7},{7,4},{8,9},{9,10},{10,1... | collective-permute-start | bytes 196616 | tf_op jit(solution)/shard_map/ppermute | solution.py:162
  12.9 2.6 %collective-permute-start.1 = (bf16[16,2048]{1,0:T(8,128)(2,1)}, bf16[16,2048]{1,0:T(8,128)(2,1)S(1)}, u32[]{:S(2)}, u32[]{:S(2)}) collective-permute-start(bf16[16,2048]{1,0:T(8,128)(2,1)} %fusion.47), channel_id=1, source_target_pairs={{0,2},{1,3},{2,0},{3,1},{4,6},{5,7},{6,4},{7,5},{8,10},{9,11},{10,... | collective-permute-start | bytes 196616 | tf_op jit(solution)/shard_map/ppermute | solution.py:162
  15.5 1.3 collective-permute-start
  21.3 2.2 convolution_convert_fusion
  24.6 4.3 %all-to-all-start.2 = ((bf16[16,176,128]{2,1,0:T(8,128)(2,1)}), bf16[16,176,128]{2,1,0:T(8,128)(2,1)}, u32[]{:S(2)}, u32[]{:S(2)}) async-start(bf16[16,176,128]{2,1,0:T(8,128)(2,1)} %copy.131), calls=%async_computation.2 | async-start | bytes 1441792 | tf_op jit(solution)/shard_map/all_to_all | solution.py:193
  30.2 1.3 concatenate.10
  31.6 1.4 constant_dynamic-slice_fusion.2
  35.8 1.7 collective-permute-start.5
  37.5 2.4 %collective-permute-start.4 = (bf16[64,128]{1,0:T(8,128)(2,1)S(1)}, bf16[64,128]{1,0:T(8,128)(2,1)}, u32[]{:S(2)}, u32[]{:S(2)}) collective-permute-start(bf16[64,128]{1,0:T(8,128)(2,1)S(1)} %convolution_convert_fusion.6), channel_id=1, source_target_pairs={{0,2},{1,3},{2,0},{3,1},{4,6},{5,7},{6,4},{7,5},{8,10},{9,11},{10,... | collective-permute-start | bytes 49160 | tf_op jit(solution)/shard_map/ppermute | solution.py:162
  39.9 1.5 collective-permute-start.3
  41.9 2.0 collective-permute-done.3
  44.6 4.9 %collective-permute-done.4 = bf16[64,128]{1,0:T(8,128)(2,1)} collective-permute-done((bf16[64,128]{1,0:T(8,128)(2,1)S(1)}, bf16[64,128]{1,0:T(8,128)(2,1)}, u32[]{:S(2)}, u32[]{:S(2)}) %collective-permute-start.4) | collective-permute-done | bytes 16416 | tf_op jit(solution)/shard_map/ppermute | solution.py:162
  52.4 2.3 fusion.103
  55.8 2.1 fusion.12
  59.4 1.5 collective-permute-start.6
  60.9 2.4 %collective-permute-start.8 = (f32[16,2048]{1,0:T(8,128)}, f32[16,2048]{1,0:T(8,128)}, u32[]{:S(2)}, u32[]{:S(2)}) collective-permute-start(f32[16,2048]{1,0:T(8,128)} %get-tuple-element.10), channel_id=1, source_target_pairs={{0,3},{1,0},{2,1},{3,2},{4,7},{5,4},{6,5},{7,6},{8,11},{9,8},{10,9... | collective-permute-start | bytes 393224 | tf_op jit(solution)/shard_map/ppermute | solution.py:184
  63.6 4.4 %collective-permute-done.6 = f32[16,2048]{1,0:T(8,128)} collective-permute-done((f32[16,2048]{1,0:T(8,128)}, f32[16,2048]{1,0:T(8,128)}, u32[]{:S(2)}, u32[]{:S(2)}) %collective-permute-start.6) | collective-permute-done | bytes 131104 | tf_op jit(solution)/shard_map/ppermute | solution.py:184
  69.1 4.7 %collective-permute-done.7 = f32[16,2048]{1,0:T(8,128)} collective-permute-done((f32[16,2048]{1,0:T(8,128)}, f32[16,2048]{1,0:T(8,128)}, u32[]{:S(2)}, u32[]{:S(2)}) %collective-permute-start.7) | collective-permute-done | bytes 131104 | tf_op jit(solution)/shard_map/ppermute | solution.py:184
  76.6 4.3 %all-to-all-start = ((bf16[16,176,128]{2,1,0:T(8,128)(2,1)}), bf16[16,176,128]{2,1,0:T(8,128)(2,1)}, u32[]{:S(2)}, u32[]{:S(2)}) async-start(bf16[16,176,128]{2,1,0:T(8,128)(2,1)} %copy.123), calls=%async_computation | async-start | bytes 1441792 | tf_op jit(solution)/shard_map/all_to_all | solution.py:193
  80.9 2.3 reshape_reshape.3
  83.2 4.4 %fusion.2 = f32[16,11,768]{2,0,1:T(8,128)} fusion(bf16[1,768,2048]{2,1,0:T(8,128)(2,1)} %param.31, bf16[16,11,2048]{2,1,0:T(8,128)(2,1)} %reshape_reshape.3), kind=kOutput, calls=%fused_computation.2 | convolution fusion | flops 553648128 | bytes 4407296 | tf_op jit(solution)/shard_map/scw,fw->scf/dot_general | solution.py:279
  87.6 13.2 %all-to-all-done = bf16[16,176,128]{2,1,0:T(8,128)(2,1)} async-done(((bf16[16,176,128]{2,1,0:T(8,128)(2,1)}), bf16[16,176,128]{2,1,0:T(8,128)(2,1)}, u32[]{:S(2)}, u32[]{:S(2)}) %all-to-all-start) | async-done | bytes 720928 | tf_op jit(solution)/shard_map/all_to_all | solution.py:193
  108.3 23.1 %all_to_all.20 = bf16[16,176,128]{2,1,0:T(8,128)(2,1)S(1)} all-to-all(bf16[16,176,128]{2,1,0:T(8,128)(2,1)S(1)} %copy.133), channel_id=1, replica_groups=mesh['groups'=2,'expert'=4,'head'=4] {'expert','head'}, dimensions={0} | all-to-all | bytes 1441792 | tf_op jit(solution)/shard_map/all_to_all | solution.py:197
  132.4 2.2 dot_general.94
  134.6 1.7 fusion.43
  136.4 1.6 fusion.100
  138.8 3.0 %fusion.6 = bf16[16,11,2048]{2,0,1:T(8,128)(2,1)S(1)} fusion(bf16[1,768,2048]{2,1,0:T(8,128)(2,1)} %param.31, f32[16,11,768]{2,0,1:T(8,128)} %copy-done.7, f32[16,11,768]{2,0,1:T(8,128)} %copy-done.4), kind=kOutput, calls=%fused_computation.6 | convolution fusion | flops 554819584 | bytes 4947968 | tf_op jit(solution)/shard_map/scf,fw->scw/dot_general | solution.py:276
  141.8 1.4 copy.125
  143.2 2.3 %reshape.138 = bf16[16,176,128]{2,1,0:T(8,128)(2,1)} reshape(bf16[16,11,2048]{2,1,0:T(8,128)(2,1)} %copy.125) | data formatting | bytes 1441792 | tf_op jit(solution)/shard_map/reshape | solution.py:294
  145.5 4.3 %all-to-all-start.1 = ((bf16[16,176,128]{2,1,0:T(8,128)(2,1)}), bf16[16,176,128]{2,1,0:T(8,128)(2,1)}, u32[]{:S(2)}, u32[]{:S(2)}) async-start(bf16[16,176,128]{2,1,0:T(8,128)(2,1)} %reshape.138), calls=%async_computation.1 | async-start | bytes 1441792 | tf_op jit(solution)/shard_map/all_to_all | solution.py:197
  149.9 1.8 collective-permute-start.11
  151.7 2.4 %collective-permute-start.10 = (bf16[16,2048]{1,0:T(8,128)(2,1)}, bf16[16,2048]{1,0:T(8,128)(2,1)S(1)}, u32[]{:S(2)}, u32[]{:S(2)}) collective-permute-start(bf16[16,2048]{1,0:T(8,128)(2,1)} %fusion.100), channel_id=1, source_target_pairs={{0,2},{1,3},{2,0},{3,1},{4,6},{5,7},{6,4},{7,5},{8,10},{9,11},{10,... | collective-permute-start | bytes 196616 | tf_op jit(solution)/shard_map/ppermute | solution.py:162
  154.9 18.5 %collective-permute-done.10 = bf16[16,2048]{1,0:T(8,128)(2,1)S(1)} collective-permute-done((bf16[16,2048]{1,0:T(8,128)(2,1)}, bf16[16,2048]{1,0:T(8,128)(2,1)S(1)}, u32[]{:S(2)}, u32[]{:S(2)}) %collective-permute-start.10) | collective-permute-done | bytes 65568 | tf_op jit(solution)/shard_map/ppermute | solution.py:162
  176.0 3.0 %convolution_convert_fusion.3 = bf16[64,512]{1,0:T(8,128)(2,1)} fusion(bf16[64,2048]{1,0:T(8,128)(2,1)S(1)} %bitcast.243, bf16[512,2048]{1,0:T(8,128)(2,1)} %param.28), kind=kOutput, calls=%fused_computation.34 | convolution fusion | flops 134250496 | bytes 2424832 | tf_op jit(solution)/shard_map/td,fd->tf/dot_general | solution.py:130
  178.9 1.5 reshape.145
  182.3 1.7 convolution_bitcast_fusion.4
  183.9 3.0 %convolution_bitcast_fusion.6 = f32[4,48,128]{2,1,0:T(8,128)} fusion(f32[4,4,16,48]{3,2,1,0:T(8,128)} %convolution_bitcast_fusion.4, bf16[4,16,4,128]{3,2,1,0:T(4,128)(2,1)} %copy-done.13, f32[4,4,16,48]{3,2,1,0:T(8,128)} %get-tuple-element.15, f32[4,4,16]{2,1,0:T(4,128)} %get-tuple-element.14), kind=kOutput, calls=%fused_computation.33 | convolution fusion | flops 3232047 | bytes 263168 | tf_op jit(solution)/shard_map/shbk,sbhd->skd/dot_general | solution.py:58
  189.0 1.4 constant_dynamic-update-slice_fusion.8
  190.4 2.3 reshape.168
  192.7 2.9 %fusion.24 = bf16[4,16,4,128]{3,1,2,0:T(8,128)(2,1)} fusion(f32[4,4,16,48]{3,2,1,0:T(8,128)} %convolution_bitcast_fusion.4, bf16[4,16,128]{2,1,0:T(8,128)(2,1)} %bitcast.252, bf16[4,32,128]{2,1,0:T(8,128)(2,1)} %get-tuple-element.18, f32[4,4,16,48]{3,2,1,0:T(8,128)} %get-tuple-element.15, f32[4,4,16]{2,1,0:T(4,128)} %get-tuple-element.14), kind=kOutput, calls=%fused_computation.38 | convolution fusion | flops 3363119 | bytes 214016 | tf_op jit(solution)/shard_map/shbk,skd->sbhd/dot_general | solution.py:55
  195.6 1.5 copy.140
  197.1 11.8 %reduce-scatter.2.cloned.1.call-done = f32[64,128]{1,0:T(8,128)} async-done(((f32[64,512]{1,0:T(8,128)}), f32[64,128]{1,0:T(8,128)}) %reduce-scatter.2.cloned.1.call-update) | async-done | bytes 32784 | tf_op jit(solution)/shard_map/reduce_scatter | solution.py:148
  208.9 1.7 fusion.106
  210.6 2.5 %convolution_add_fusion = f32[64,2048]{1,0:T(8,128)S(1)} fusion(f32[64,2048]{1,0:T(8,128)S(1)} %fusion.106, bf16[2048,512]{1,0:T(8,128)(2,1)} %param.26, bf16[8,8,4,128]{3,2,1,0:T(4,128)(2,1)} %bitcast.245), kind=kOutput, calls=%fused_computation.7 | convolution fusion | flops 134348800 | bytes 3211264 | tf_op jit(solution)/shard_map/tf,df->td/dot_general | solution.py:153
  213.2 3.8 %collective-permute-start.14 = (f32[16,2048]{1,0:T(8,128)S(1)}, f32[16,2048]{1,0:T(8,128)S(1)}, u32[]{:S(2)}, u32[]{:S(2)}) collective-permute-start(f32[16,2048]{1,0:T(8,128)S(1)} %get-tuple-element.7), channel_id=1, source_target_pairs={{0,3},{1,0},{2,1},{3,2},{4,7},{5,4},{6,5},{7,6},{8,11},{9,8},{10,9... | collective-permute-start | bytes 393224 | tf_op jit(solution)/shard_map/ppermute | solution.py:184
  218.3 2.6 %collective-permute-done.12 = f32[16,2048]{1,0:T(8,128)S(1)} collective-permute-done((f32[16,2048]{1,0:T(8,128)S(1)}, f32[16,2048]{1,0:T(8,128)S(1)}, u32[]{:S(2)}, u32[]{:S(2)}) %collective-permute-start.12) | collective-permute-done | bytes 131104 | tf_op jit(solution)/shard_map/ppermute | solution.py:184
  220.9 4.9 %collective-permute-done.13 = f32[16,2048]{1,0:T(8,128)S(1)} collective-permute-done((f32[16,2048]{1,0:T(8,128)S(1)}, f32[16,2048]{1,0:T(8,128)S(1)}, u32[]{:S(2)}, u32[]{:S(2)}) %collective-permute-start.13) | collective-permute-done | bytes 131104 | tf_op jit(solution)/shard_map/ppermute | solution.py:184
  (137 shorter events, 40.6 us)
Async XLA Ops:
  7.2 94.9 %copy-start = (bf16[1,2048,768]{2,1,0:T(8,128)(2,1)S(1)}, bf16[1,2048,768]{2,1,0:T(8,128)(2,1)}, u32[]{:S(2)}) copy-start(bf16[1,2048,768]{2,1,0:T(8,128)(2,1)} %param.29) | copy-start | bytes 9437188
  8.3 8.5 %copy-start.20 = (f32[16]{0:T(128)}, f32[16]{0:T(128)S(1)}, u32[]{:S(2)}) copy-start(f32[16]{0:T(128)S(1)} %add_rsqrt_fusion.1) | copy-start | bytes 196
  9.9 23.1 %collective-permute-start.2 = (bf16[16,2048]{1,0:T(8,128)(2,1)}, bf16[16,2048]{1,0:T(8,128)(2,1)S(1)}, u32[]{:S(2)}, u32[]{:S(2)}) collective-permute-start(bf16[16,2048]{1,0:T(8,128)(2,1)} %fusion.47), channel_id=1, source_target_pairs={{0,1},{1,2},{2,3},{3,0},{4,5},{5,6},{6,7},{7,4},{8,9},{9,10},{10,1... | collective-permute-start | bytes 196616 | tf_op jit(solution)/shard_map/ppermute | solution.py:162
  12.9 20.1 %collective-permute-start.1 = (bf16[16,2048]{1,0:T(8,128)(2,1)}, bf16[16,2048]{1,0:T(8,128)(2,1)S(1)}, u32[]{:S(2)}, u32[]{:S(2)}) collective-permute-start(bf16[16,2048]{1,0:T(8,128)(2,1)} %fusion.47), channel_id=1, source_target_pairs={{0,2},{1,3},{2,0},{3,1},{4,6},{5,7},{6,4},{7,5},{8,10},{9,11},{10,... | collective-permute-start | bytes 196616 | tf_op jit(solution)/shard_map/ppermute | solution.py:162
  15.5 17.5 %collective-permute-start = (bf16[16,2048]{1,0:T(8,128)(2,1)}, bf16[16,2048]{1,0:T(8,128)(2,1)S(1)}, u32[]{:S(2)}, u32[]{:S(2)}) collective-permute-start(bf16[16,2048]{1,0:T(8,128)(2,1)} %fusion.47), channel_id=1, source_target_pairs={{0,3},{1,0},{2,1},{3,2},{4,7},{5,4},{6,5},{7,6},{8,11},{9,8},{10,9... | collective-permute-start | bytes 196616 | tf_op jit(solution)/shard_map/ppermute | solution.py:162
  20.2 1.0 copy-start.15
  21.3 11.8 %copy-start.6 = (bf16[16,2048]{1,0:T(8,128)(2,1)S(1)}, bf16[16,2048]{1,0:T(8,128)(2,1)}, u32[]{:S(2)}) copy-start(bf16[16,2048]{1,0:T(8,128)(2,1)} %param.16) | copy-start | bytes 196612
  21.3 11.8 %copy-start.11 = (f32[2048]{0:T(1024)S(1)}, f32[2048]{0:T(1024)}, u32[]{:S(2)}) copy-start(f32[2048]{0:T(1024)} %param.24) | copy-start | bytes 24580
  24.6 52.0 %all-to-all-start.2 = ((bf16[16,176,128]{2,1,0:T(8,128)(2,1)}), bf16[16,176,128]{2,1,0:T(8,128)(2,1)}, u32[]{:S(2)}, u32[]{:S(2)}) async-start(bf16[16,176,128]{2,1,0:T(8,128)(2,1)} %copy.131), calls=%async_computation.2 | async-start | bytes 1441792 | tf_op jit(solution)/shard_map/all_to_all | solution.py:193
  30.2 11.1 %copy-start.2 = (bf16[2048,512]{1,0:T(8,128)(2,1)S(1)}, bf16[2048,512]{1,0:T(8,128)(2,1)}, u32[]{:S(2)}) copy-start(bf16[2048,512]{1,0:T(8,128)(2,1)} %param.26) | copy-start | bytes 6291460
  34.5 20.1 %copy-start.12 = (bf16[4,32,128]{2,1,0:T(8,128)(2,1)S(1)}, bf16[4,32,128]{2,1,0:T(8,128)(2,1)}, u32[]{:S(2)}) copy-start(bf16[4,32,128]{2,1,0:T(8,128)(2,1)} %get-tuple-element.19) | copy-start | bytes 98308
  35.8 14.4 %collective-permute-start.5 = (bf16[64,128]{1,0:T(8,128)(2,1)S(1)}, bf16[64,128]{1,0:T(8,128)(2,1)S(1)}, u32[]{:S(2)}, u32[]{:S(2)}) collective-permute-start(bf16[64,128]{1,0:T(8,128)(2,1)S(1)} %convolution_convert_fusion.6), channel_id=1, source_target_pairs={{0,1},{1,2},{2,3},{3,0},{4,5},{5,6},{6,7},{7,4},{8,9},{9,10},{10,1... | collective-permute-start | bytes 49160 | tf_op jit(solution)/shard_map/ppermute | solution.py:162
  37.5 12.0 %collective-permute-start.4 = (bf16[64,128]{1,0:T(8,128)(2,1)S(1)}, bf16[64,128]{1,0:T(8,128)(2,1)}, u32[]{:S(2)}, u32[]{:S(2)}) collective-permute-start(bf16[64,128]{1,0:T(8,128)(2,1)S(1)} %convolution_convert_fusion.6), channel_id=1, source_target_pairs={{0,2},{1,3},{2,0},{3,1},{4,6},{5,7},{6,4},{7,5},{8,10},{9,11},{10,... | collective-permute-start | bytes 49160 | tf_op jit(solution)/shard_map/ppermute | solution.py:162
  39.9 4.0 %collective-permute-start.3 = (bf16[64,128]{1,0:T(8,128)(2,1)S(1)}, bf16[64,128]{1,0:T(8,128)(2,1)}, u32[]{:S(2)}, u32[]{:S(2)}) collective-permute-start(bf16[64,128]{1,0:T(8,128)(2,1)S(1)} %convolution_convert_fusion.6), channel_id=1, source_target_pairs={{0,3},{1,0},{2,1},{3,2},{4,7},{5,4},{6,5},{7,6},{8,11},{9,8},{10,9... | collective-permute-start | bytes 49160 | tf_op jit(solution)/shard_map/ppermute | solution.py:162
  41.9 17.5 %copy-start.13 = (bf16[4,16,4,128]{3,2,1,0:T(4,128)(2,1)}, bf16[4,16,4,128]{3,2,1,0:T(4,128)(2,1)S(1)}, u32[]{:S(2)}) copy-start(bf16[4,16,4,128]{3,2,1,0:T(4,128)(2,1)S(1)} %reshape.134) | copy-start | bytes 196612
  51.8 0.6 copy-start.19
  51.8 7.7 %copy-start.14 = (bf16[64,128]{1,0:T(8,128)(2,1)}, bf16[64,128]{1,0:T(8,128)(2,1)S(1)}, u32[]{:S(2)}) copy-start(bf16[64,128]{1,0:T(8,128)(2,1)S(1)} %get-tuple-element.13) | copy-start | bytes 49156
  54.6 8.6 %copy-start.16 = (s32[16,8]{0,1:T(8,128)S(1)}, s32[16,8]{0,1:T(8,128)}, u32[]{:S(2)}) copy-start(s32[16,8]{0,1:T(8,128)} %copy-done.15) | copy-start | bytes 1540
  55.8 19.4 %copy-start.17 = (f32[2048]{0:T(1024)S(1)}, f32[2048]{0:T(1024)}, u32[]{:S(2)}) copy-start(f32[2048]{0:T(1024)} %param.25) | copy-start | bytes 24580
  57.9 0.8 copy-start.8
  59.4 8.6 %collective-permute-start.6 = (f32[16,2048]{1,0:T(8,128)}, f32[16,2048]{1,0:T(8,128)}, u32[]{:S(2)}, u32[]{:S(2)}) collective-permute-start(f32[16,2048]{1,0:T(8,128)} %get-tuple-element.9), channel_id=1, source_target_pairs={{0,1},{1,2},{2,3},{3,0},{4,5},{5,6},{6,7},{7,4},{8,9},{9,10},{10,1... | collective-permute-start | bytes 393224 | tf_op jit(solution)/shard_map/ppermute | solution.py:184
  60.9 8.2 %collective-permute-start.8 = (f32[16,2048]{1,0:T(8,128)}, f32[16,2048]{1,0:T(8,128)}, u32[]{:S(2)}, u32[]{:S(2)}) collective-permute-start(f32[16,2048]{1,0:T(8,128)} %get-tuple-element.10), channel_id=1, source_target_pairs={{0,3},{1,0},{2,1},{3,2},{4,7},{5,4},{6,5},{7,6},{8,11},{9,8},{10,9... | collective-permute-start | bytes 393224 | tf_op jit(solution)/shard_map/ppermute | solution.py:184
  63.2 10.6 %collective-permute-start.7 = (f32[16,2048]{1,0:T(8,128)}, f32[16,2048]{1,0:T(8,128)}, u32[]{:S(2)}, u32[]{:S(2)}) collective-permute-start(f32[16,2048]{1,0:T(8,128)} %get-tuple-element.11), channel_id=1, source_target_pairs={{0,2},{1,3},{2,0},{3,1},{4,6},{5,7},{6,4},{7,5},{8,10},{9,11},{10,... | collective-permute-start | bytes 393224 | tf_op jit(solution)/shard_map/ppermute | solution.py:184
  63.6 13.0 %copy-start.10 = (pred[16,11,16]{2,1,0:T(8,128)(4,1)}, pred[16,11,16]{2,1,0:T(8,128)(4,1)S(1)}, u32[]{:S(2)}) copy-start(pred[16,11,16]{2,1,0:T(8,128)(4,1)S(1)} %compare_reduce_fusion) | copy-start | bytes 8452
  75.1 8.1 %copy-start.22 = (f32[16]{0:T(128)}, f32[16]{0:T(128)S(1)}, u32[]{:S(2)}) copy-start(f32[16]{0:T(128)S(1)} %add_rsqrt_fusion) | copy-start | bytes 196
  76.6 24.2 %all-to-all-start = ((bf16[16,176,128]{2,1,0:T(8,128)(2,1)}), bf16[16,176,128]{2,1,0:T(8,128)(2,1)}, u32[]{:S(2)}, u32[]{:S(2)}) async-start(bf16[16,176,128]{2,1,0:T(8,128)(2,1)} %copy.123), calls=%async_computation | async-start | bytes 1441792 | tf_op jit(solution)/shard_map/all_to_all | solution.py:193
  102.1 2.1 copy-start.1
  102.8 4.1 %copy-start.4 = (f32[16,11,768]{2,0,1:T(8,128)}, f32[16,11,768]{2,0,1:T(8,128)S(1)}, u32[]{:S(2)}) copy-start(f32[16,11,768]{2,0,1:T(8,128)S(1)} %convolution_bitcast_fusion.3) | copy-start | bytes 1622020
  104.2 1.6 copy-start.3
  104.9 0.8 copy-start.7
  108.3 26.3 %copy-start.18 = (f32[2048]{0:T(1024)S(1)}, f32[2048]{0:T(1024)}, u32[]{:S(2)}) copy-start(f32[2048]{0:T(1024)} %param.25) | copy-start | bytes 24580
  137.9 16.1 %collective-permute-start.9 = (bf16[16,2048]{1,0:T(8,128)(2,1)}, bf16[16,2048]{1,0:T(8,128)(2,1)}, u32[]{:S(2)}, u32[]{:S(2)}) collective-permute-start(bf16[16,2048]{1,0:T(8,128)(2,1)} %fusion.100), channel_id=1, source_target_pairs={{0,3},{1,0},{2,1},{3,2},{4,7},{5,4},{6,5},{7,6},{8,11},{9,8},{10,9... | collective-permute-start | bytes 196616 | tf_op jit(solution)/shard_map/ppermute | solution.py:162
  145.5 44.8 %all-to-all-start.1 = ((bf16[16,176,128]{2,1,0:T(8,128)(2,1)}), bf16[16,176,128]{2,1,0:T(8,128)(2,1)}, u32[]{:S(2)}, u32[]{:S(2)}) async-start(bf16[16,176,128]{2,1,0:T(8,128)(2,1)} %reshape.138), calls=%async_computation.1 | async-start | bytes 1441792 | tf_op jit(solution)/shard_map/all_to_all | solution.py:197
  149.8 59.1 %reduce-scatter.2.cloned.1.call-start = ((), (), s32[]{:S(2)}) async-start(), calls=%async_computation.5 | async-start | bytes 163840 | tf_op jit(solution)/shard_map/reduce_scatter | solution.py:148
  149.9 23.5 %collective-permute-start.11 = (bf16[16,2048]{1,0:T(8,128)(2,1)}, bf16[16,2048]{1,0:T(8,128)(2,1)S(1)}, u32[]{:S(2)}, u32[]{:S(2)}) collective-permute-start(bf16[16,2048]{1,0:T(8,128)(2,1)} %fusion.100), channel_id=1, source_target_pairs={{0,1},{1,2},{2,3},{3,0},{4,5},{5,6},{6,7},{7,4},{8,9},{9,10},{10,1... | collective-permute-start | bytes 196616 | tf_op jit(solution)/shard_map/ppermute | solution.py:162
  151.7 21.7 %collective-permute-start.10 = (bf16[16,2048]{1,0:T(8,128)(2,1)}, bf16[16,2048]{1,0:T(8,128)(2,1)S(1)}, u32[]{:S(2)}, u32[]{:S(2)}) collective-permute-start(bf16[16,2048]{1,0:T(8,128)(2,1)} %fusion.100), channel_id=1, source_target_pairs={{0,2},{1,3},{2,0},{3,1},{4,6},{5,7},{6,4},{7,5},{8,10},{9,11},{10,... | collective-permute-start | bytes 196616 | tf_op jit(solution)/shard_map/ppermute | solution.py:162
  210.6 6.4 %copy-start.5 = (bf16[2048,11,16]{0,1,2:T(8,128)(2,1)S(1)}, bf16[2048,11,16]{0,1,2:T(8,128)(2,1)}, u32[]{:S(2)}) copy-start(bf16[2048,11,16]{0,1,2:T(8,128)(2,1)} %reshape.168) | copy-start | bytes 2162692
  210.6 15.2 %copy-start.21 = (f32[16]{0:T(128)S(1)}, f32[16]{0:T(128)}, u32[]{:S(2)}) copy-start(f32[16]{0:T(128)} %copy-done.20) | copy-start | bytes 196
  213.1 12.9 %copy-start.9 = (bf16[16,2048]{1,0:T(8,128)(2,1)S(1)}, bf16[16,2048]{1,0:T(8,128)(2,1)}, u32[]{:S(2)}) copy-start(bf16[16,2048]{1,0:T(8,128)(2,1)} %param.17) | copy-start | bytes 196612
  213.1 12.9 %copy-start.23 = (f32[16]{0:T(128)S(1)}, f32[16]{0:T(128)}, u32[]{:S(2)}) copy-start(f32[16]{0:T(128)} %copy-done.22) | copy-start | bytes 196
  213.1 12.9 %copy-start.24 = (f32[16]{0:T(128)S(1)}, f32[16]{0:T(128)}, u32[]{:S(2)}) copy-start(f32[16]{0:T(128)} %convert_element_type.116) | copy-start | bytes 196
  213.2 7.7 %collective-permute-start.12 = (f32[16,2048]{1,0:T(8,128)S(1)}, f32[16,2048]{1,0:T(8,128)S(1)}, u32[]{:S(2)}, u32[]{:S(2)}) collective-permute-start(f32[16,2048]{1,0:T(8,128)S(1)} %get-tuple-element.6), channel_id=1, source_target_pairs={{0,1},{1,2},{2,3},{3,0},{4,5},{5,6},{6,7},{7,4},{8,9},{9,10},{10,1... | collective-permute-start | bytes 393224 | tf_op jit(solution)/shard_map/ppermute | solution.py:184
  213.2 7.6 %collective-permute-start.14 = (f32[16,2048]{1,0:T(8,128)S(1)}, f32[16,2048]{1,0:T(8,128)S(1)}, u32[]{:S(2)}, u32[]{:S(2)}) collective-permute-start(f32[16,2048]{1,0:T(8,128)S(1)} %get-tuple-element.7), channel_id=1, source_target_pairs={{0,3},{1,0},{2,1},{3,2},{4,7},{5,4},{6,5},{7,6},{8,11},{9,8},{10,9... | collective-permute-start | bytes 393224 | tf_op jit(solution)/shard_map/ppermute | solution.py:184
  217.0 8.8 %collective-permute-start.13 = (f32[16,2048]{1,0:T(8,128)S(1)}, f32[16,2048]{1,0:T(8,128)S(1)}, u32[]{:S(2)}, u32[]{:S(2)}) collective-permute-start(f32[16,2048]{1,0:T(8,128)S(1)} %get-tuple-element.8), channel_id=1, source_target_pairs={{0,2},{1,3},{2,0},{3,1},{4,6},{5,7},{6,4},{7,5},{8,10},{9,11},{10,... | collective-permute-start | bytes 393224 | tf_op jit(solution)/shard_map/ppermute | solution.py:184
Sparse Core Ops, SparseCore 0:
  190.5 18.3 reduce-scatter.1

commit v12 on v10

--- a/solution.py
+++ b/solution.py
@@ -122,7 +122,9 @@
     return (joined, saved)
 
 
-def attention_backward(grad_rows, query_weights, output_weights, own_kv_weights, saved, kv_now):
+def attention_backward(
+    grad_rows, query_weights, output_weights, own_kv_weights, saved, kv_now, carried
+):
     heads_here = query_weights.shape[1] // HEAD_SIZE
     row_count = grad_rows.shape[0]
     seq_count = row_count // BLOCK
@@ -145,14 +147,16 @@
         key_value_width + kv_now * HEAD_SIZE,
         1,
     )
+    placed, carried = lax.optimization_barrier((placed, carried))
     own_grads = lax.psum_scatter(placed, "head", scatter_dimension=1, tiled=True)
     running = jnp.einsum(
         "tc,dc->td", own_grads, own_kv_weights.astype(jnp.float32), precision=lax.Precision.HIGHEST
     )
     query_flat = grad_queries.reshape(row_count, heads_here * HEAD_SIZE)
-    return running + jnp.einsum(
+    total = running + jnp.einsum(
         "tf,df->td", query_flat, query_weights, preferred_element_type=jnp.float32
     )
+    return (total, carried)
 
 
 def head_gather(block, axis):
@@ -162,7 +166,9 @@
         lax.ppermute(block, "head", perm=[(j, (j + shift) % count) for j in range(count)])
         for shift in range(1, count)
     ]
-    ordered = jnp.take(jnp.stack(parts), (me - jnp.arange(count)) % count, axis=0)
+    reversed_parts = parts[::-1]
+    doubled = jnp.stack(reversed_parts + reversed_parts)
+    ordered = lax.dynamic_slice_in_dim(doubled, count - 1 - me, count, 0)
     ordered = jnp.moveaxis(ordered, 0, axis)
     merged = list(block.shape)
     merged[axis] = count * block.shape[axis]
@@ -286,8 +292,28 @@
         "scf,klf->sckl", grad_up, up_matrix, preferred_element_type=jnp.float32
     )
     grad_back = grad_back.astype(jnp.bfloat16)
+    grad_home = from_experts(grad_back.reshape(flat_shape)).reshape(split_shape)
+    grad_moe = jnp.einsum(
+        "dct,dckl->tkl", placement, grad_home, preferred_element_type=jnp.float32
+    ).reshape(owned, width)
+    grad_hidden = cotangent + rms_backward(hidden, moe_gain, inverse_two, grad_moe)
+    grad_low = grad_hidden.astype(jnp.bfloat16)
+    grad_gathered = head_rows(grad_low)
+    result, grad_gathered = lax.optimization_barrier((result, grad_gathered))
     result_home = from_experts(result.reshape(flat_shape)).reshape(split_shape)
-    grad_home = from_experts(grad_back.reshape(flat_shape)).reshape(split_shape)
+    grad_partial, result_home = attention_backward(
+        grad_gathered,
+        w_query,
+        w_output,
+        key_value_weight,
+        saved,
+        first_head // (QUERY_HEADS // KEY_VALUE_HEADS),
+        result_home,
+    )
+    grad_attn_rows = head_sums(grad_partial)
+    input_grad = (
+        grad_hidden + rms_backward(hidden_in, attn_gain, inverse_one, grad_attn_rows)
+    ).astype(jnp.bfloat16)
     moe_sum = jnp.einsum(
         "dct,dckl->tkl",
         weighting,
@@ -295,25 +321,6 @@
         precision=highest_prec,
     ).reshape(owned, width)
     layer_out = (hidden.astype(jnp.float32) + moe_sum).astype(jnp.bfloat16)
-    grad_moe = jnp.einsum(
-        "dct,dckl->tkl", placement, grad_home, preferred_element_type=jnp.float32
-    ).reshape(owned, width)
-    grad_hidden = cotangent + rms_backward(hidden, moe_gain, inverse_two, grad_moe)
-    grad_low = grad_hidden.astype(jnp.bfloat16)
-    grad_gathered = head_rows(grad_low)
-    grad_attn_rows = head_sums(
-        attention_backward(
-            grad_gathered,
-            w_query,
-            w_output,
-            key_value_weight,
-            saved,
-            first_head // (QUERY_HEADS // KEY_VALUE_HEADS),
-        )
-    )
-    input_grad = (
-        grad_hidden + rms_backward(hidden_in, attn_gain, inverse_one, grad_attn_rows)
-    ).astype(jnp.bfloat16)
     return (layer_out, input_grad)
 
 

time: 209 us -> 218 us (1.043)
  waiting for transfers between devices: 49.5 us -> 56.7 us
    ppermute x9, waiting for transfers between devices: 7.03 us -> 11.6 us  [head_gather(): lax.ppermute(block, 'head', perm=[(j, (j + shift) % count) for j in range...]
    gather x3 -> x0, local copies, waits for them, and re-layouts: 4.43 us -> none  [head_gather(): jnp.take(jnp.stack(parts), (me - jnp.arange(count)) % count, axis=0)]
    reduce_scatter x1, waiting for transfers between devices: 6.65 us -> 9.32 us  [attention_backward(): lax.psum_scatter(placed, 'head', scatter_dimension=1, tiled=True)]
    another operation x4 -> x1, other arithmetic: 3.31 us -> 0.75 us  [head_gather(): doubled = jnp.stack(reversed_parts + reversed_parts)]
    unnamed x68 -> x76, local copies, waits for them, and re-layouts: 8.03 us -> 7.93 us
  transfers between devices with their start and end apart: 19 -> 19, of which waited for: 9 -> 10; matrix products, arithmetic and copies ran while one was open for 29% -> 28% of each run, Pallas kernels for 0% -> 0%
where the time goes in v12:
time: 218 us; the launch traced here: 217 us
  waiting for transfers between devices  56.7 us (26%)
  matrix products  39 us (18%)
  starting transfers between devices  36 us (17%)
  local copies, waits for them, and re-layouts  34 us (16%)
  blocking collectives  23.1 us (11%)
  between operations  14.7 us (7%)
  other arithmetic  12.9 us (6%)
    all_to_all x1, blocking collectives, from_experts(): lax.all_to_all(results, ('expert', 'head'), split_axis=0, concat_axis=0,...  23.1 us
    ppermute x6, waiting for transfers between devices, head_sums(): lax.ppermute(chunks[(me + shift) % count], 'head', perm=[(j, (j + shift)...  17.3 us
    ppermute x9, starting transfers between devices, head_gather(): lax.ppermute(block, 'head', perm=[(j, (j + shift) % count) for j in range...  15.4 us
    all_to_all x2, waiting for transfers between devices, to_experts(): lax.all_to_all(outgoing, ('expert', 'head'), split_axis=0, concat_axis=0,...  13.1 us
    ppermute x9, waiting for transfers between devices, head_gather(): lax.ppermute(block, 'head', perm=[(j, (j + shift) % count) for j in range...  11.6 us
    reduce_scatter x1, waiting for transfers between devices, attention_backward(): lax.psum_scatter(placed, 'head', scatter_dimension=1, tiled=True)  9.32 us
    all_to_all x2, starting transfers between devices, to_experts(): lax.all_to_all(outgoing, ('expert', 'head'), split_axis=0, concat_axis=0,...  8.57 us
    unnamed x76, local copies, waits for them, and re-layouts  7.93 us
  transfers between devices with their start and end apart: 19, of which 10 were waited for; matrix products, arithmetic and copies ran while one was open for 28% of the time, Pallas kernels for 0%

profile of v12, /device:TPU:0, one launch (start us, length us, event | category | flops | bytes accessed | tf_op | source)
XLA Modules:
  0.0 216.5 jit_solution(2984756836008335793)
XLA Ops:
  8.9 1.6 fusion.52
  10.5 3.0 %collective-permute-start.2 = (bf16[16,2048]{1,0:T(8,128)(2,1)}, bf16[16,2048]{1,0:T(8,128)(2,1)S(1)}, u32[]{:S(2)}, u32[]{:S(2)}) collective-permute-start(bf16[16,2048]{1,0:T(8,128)(2,1)} %fusion.52), channel_id=1, source_target_pairs={{0,1},{1,2},{2,3},{3,0},{4,5},{5,6},{6,7},{7,4},{8,9},{9,10},{10,1... | collective-permute-start | bytes 196616 | tf_op jit(solution)/shard_map/ppermute | solution.py:166
  13.5 2.6 %collective-permute-start.1 = (bf16[16,2048]{1,0:T(8,128)(2,1)}, bf16[16,2048]{1,0:T(8,128)(2,1)S(1)}, u32[]{:S(2)}, u32[]{:S(2)}) collective-permute-start(bf16[16,2048]{1,0:T(8,128)(2,1)} %fusion.52), channel_id=1, source_target_pairs={{0,2},{1,3},{2,0},{3,1},{4,6},{5,7},{6,4},{7,5},{8,10},{9,11},{10,... | collective-permute-start | bytes 196616 | tf_op jit(solution)/shard_map/ppermute | solution.py:166
  16.1 1.3 collective-permute-start
  23.0 2.2 convolution_convert_fusion
  26.2 4.3 %all-to-all-start.1 = ((bf16[16,176,128]{2,1,0:T(8,128)(2,1)}), bf16[16,176,128]{2,1,0:T(8,128)(2,1)}, u32[]{:S(2)}, u32[]{:S(2)}) async-start(bf16[16,176,128]{2,1,0:T(8,128)(2,1)} %copy.136), calls=%async_computation.1 | async-start | bytes 1441792 | tf_op jit(solution)/shard_map/all_to_all | solution.py:197
  33.0 1.4 constant_dynamic-slice_fusion.2
  36.1 1.3 convolution_convert_fusion.6
  37.4 1.7 collective-permute-start.5
  39.1 2.4 %collective-permute-start.4 = (bf16[64,128]{1,0:T(8,128)(2,1)S(1)}, bf16[64,128]{1,0:T(8,128)(2,1)S(1)}, u32[]{:S(2)}, u32[]{:S(2)}) collective-permute-start(bf16[64,128]{1,0:T(8,128)(2,1)S(1)} %convolution_convert_fusion.6), channel_id=1, source_target_pairs={{0,2},{1,3},{2,0},{3,1},{4,6},{5,7},{6,4},{7,5},{8,10},{9,11},{10,... | collective-permute-start | bytes 49160 | tf_op jit(solution)/shard_map/ppermute | solution.py:166
  41.5 1.5 collective-permute-start.3
  43.0 2.1 convolution_convert_fusion.5
  45.7 5.3 %collective-permute-done.4 = bf16[64,128]{1,0:T(8,128)(2,1)S(1)} collective-permute-done((bf16[64,128]{1,0:T(8,128)(2,1)S(1)}, bf16[64,128]{1,0:T(8,128)(2,1)S(1)}, u32[]{:S(2)}, u32[]{:S(2)}) %collective-permute-start.4) | collective-permute-done | bytes 16416 | tf_op jit(solution)/shard_map/ppermute | solution.py:166
  51.2 1.8 fusion.108
  54.1 2.1 fusion.11
  58.5 3.1 %collective-permute-start.8 = (f32[16,2048]{1,0:T(8,128)}, f32[16,2048]{1,0:T(8,128)}, u32[]{:S(2)}, u32[]{:S(2)}) collective-permute-start(f32[16,2048]{1,0:T(8,128)} %get-tuple-element.18), channel_id=1, source_target_pairs={{0,3},{1,0},{2,1},{3,2},{4,7},{5,4},{6,5},{7,6},{8,11},{9,8},{10,9... | collective-permute-start | bytes 393224 | tf_op jit(solution)/shard_map/ppermute | solution.py:188
  61.9 4.4 %collective-permute-done.6 = f32[16,2048]{1,0:T(8,128)} collective-permute-done((f32[16,2048]{1,0:T(8,128)}, f32[16,2048]{1,0:T(8,128)}, u32[]{:S(2)}, u32[]{:S(2)}) %collective-permute-start.6) | collective-permute-done | bytes 131104 | tf_op jit(solution)/shard_map/ppermute | solution.py:188
  67.0 5.0 %collective-permute-done.7 = f32[16,2048]{1,0:T(8,128)} collective-permute-done((f32[16,2048]{1,0:T(8,128)}, f32[16,2048]{1,0:T(8,128)}, u32[]{:S(2)}, u32[]{:S(2)}) %collective-permute-start.7) | collective-permute-done | bytes 131104 | tf_op jit(solution)/shard_map/ppermute | solution.py:188
  74.7 4.3 %all-to-all-start = ((bf16[16,176,128]{2,1,0:T(8,128)(2,1)}), bf16[16,176,128]{2,1,0:T(8,128)(2,1)}, u32[]{:S(2)}, u32[]{:S(2)}) async-start(bf16[16,176,128]{2,1,0:T(8,128)(2,1)} %copy.131), calls=%async_computation | async-start | bytes 1441792 | tf_op jit(solution)/shard_map/all_to_all | solution.py:197
  79.0 2.9 %copy.173 = bf16[96,8,16,128]{3,2,1,0:T(8,128)(2,1)S(1)} copy(bf16[96,8,16,128]{3,1,2,0:T(8,128)(2,1)} %bitcast.250) | data formatting | bytes 6291456
  82.0 1.8 copy.137
  83.8 2.0 fusion.17
  85.8 13.1 %all-to-all-done = bf16[16,176,128]{2,1,0:T(8,128)(2,1)} async-done(((bf16[16,176,128]{2,1,0:T(8,128)(2,1)}), bf16[16,176,128]{2,1,0:T(8,128)(2,1)}, u32[]{:S(2)}, u32[]{:S(2)}) %all-to-all-start) | async-done | bytes 720928 | tf_op jit(solution)/shard_map/all_to_all | solution.py:197
  98.9 1.3 copy.132
  101.0 1.3 copy-done.1
  106.4 23.1 %all_to_all.20 = bf16[16,176,128]{2,1,0:T(8,128)(2,1)S(1)} all-to-all(bf16[16,176,128]{2,1,0:T(8,128)(2,1)S(1)} %copy.139), channel_id=1, replica_groups=mesh['groups'=2,'expert'=4,'head'=4] {'expert','head'}, dimensions={0} | all-to-all | bytes 1441792 | tf_op jit(solution)/shard_map/all_to_all | solution.py:201
  130.6 2.1 dot_general.91
  132.7 1.7 fusion.48
  136.5 3.1 %fusion.13 = bf16[16,11,16,128]{3,0,2,1:T(8,128)(2,1)S(1)} fusion(bf16[768,16,128]{2,1,0:T(8,128)(2,1)} %bitcast.252, f32[16,11,768]{2,0,1:T(8,128)} %copy-done.7, f32[16,11,768]{2,0,1:T(8,128)} %copy-done.2), kind=kOutput, calls=%fused_computation.17 | convolution fusion | flops 554819584 | bytes 4947968 | tf_op jit(solution)/shard_map/scf,fkl->sckl/dot_general | solution.py:280
  141.4 6.3 %collective-permute-done.10 = bf16[16,2048]{1,0:T(8,128)(2,1)S(1)} collective-permute-done((bf16[16,2048]{1,0:T(8,128)(2,1)S(1)}, bf16[16,2048]{1,0:T(8,128)(2,1)S(1)}, u32[]{:S(2)}, u32[]{:S(2)}) %collective-permute-start.10) | collective-permute-done | bytes 65568 | tf_op jit(solution)/shard_map/ppermute | solution.py:166
  149.5 4.3 %all-to-all-start.3 = ((bf16[16,176,128]{2,1,0:T(8,128)(2,1)}), bf16[16,176,128]{2,1,0:T(8,128)(2,1)}, u32[]{:S(2)}, u32[]{:S(2)}) async-start(bf16[16,176,128]{2,1,0:T(8,128)(2,1)} %copy.146), calls=%async_computation.3 | async-start | bytes 1441792 | tf_op jit(solution)/shard_map/all_to_all | solution.py:201
  153.9 3.1 %convolution_convert_fusion.3 = bf16[64,512]{1,0:T(8,128)(2,1)} fusion(bf16[64,2048]{1,0:T(8,128)(2,1)} %bitcast.263, bf16[512,2048]{1,0:T(8,128)(2,1)} %param.28), kind=kOutput, calls=%fused_computation.37 | convolution fusion | flops 134250496 | bytes 2424832 | tf_op jit(solution)/shard_map/td,fd->tf/dot_general | solution.py:132
  156.9 1.5 reshape.147
  160.3 1.7 convolution_bitcast_fusion.4
  161.9 3.0 %convolution_bitcast_fusion.6 = f32[4,48,128]{2,1,0:T(8,128)} fusion(f32[4,4,16,48]{3,2,1,0:T(8,128)} %convolution_bitcast_fusion.4, bf16[4,16,4,128]{3,2,1,0:T(4,128)(2,1)} %reshape.137, f32[4,4,16,48]{3,2,1,0:T(8,128)} %get-tuple-element.23, f32[4,4,16]{2,1,0:T(4,128)} %copy-done.26), kind=kOutput, calls=%fused_computation.36 | convolution fusion | flops 3232047 | bytes 263168 | tf_op jit(solution)/shard_map/shbk,sbhd->skd/dot_general | solution.py:58
  167.0 1.4 constant_dynamic-update-slice_fusion.8
  168.4 5.3 %all-to-all-done.3 = bf16[16,176,128]{2,1,0:T(8,128)(2,1)} async-done(((bf16[16,176,128]{2,1,0:T(8,128)(2,1)}), bf16[16,176,128]{2,1,0:T(8,128)(2,1)}, u32[]{:S(2)}, u32[]{:S(2)}) %all-to-all-start.3) | async-done | bytes 720928 | tf_op jit(solution)/shard_map/all_to_all | solution.py:201
  173.7 2.9 %fusion.29 = bf16[4,16,4,128]{3,1,2,0:T(8,128)(2,1)} fusion(f32[4,4,16,48]{3,2,1,0:T(8,128)} %convolution_bitcast_fusion.4, bf16[4,16,128]{2,1,0:T(8,128)(2,1)} %bitcast.274, bf16[4,32,128]{2,1,0:T(8,128)(2,1)} %get-tuple-element.26, f32[4,4,16,48]{3,2,1,0:T(8,128)} %get-tuple-element.23, f32[4,4,16]{2,1,0:T(4,128)} %copy-done.26), kind=kOutput, calls=%fused_computation.41 | convolution fusion | flops 3363119 | bytes 214016 | tf_op jit(solution)/shard_map/shbk,skd->sbhd/dot_general | solution.py:55
  176.6 1.5 copy.150
  178.1 2.2 copy.230
  180.3 2.2 dot_general.98
  182.5 9.3 %reduce-scatter.2.cloned.1.call-done = f32[64,128]{1,0:T(8,128)} async-done(((f32[64,512]{1,0:T(8,128)}), f32[64,128]{1,0:T(8,128)}) %reduce-scatter.2.cloned.1.call-update) | async-done | bytes 32784 | tf_op jit(solution)/shard_map/reduce_scatter | solution.py:151
  191.8 1.8 fusion.111
  193.6 2.4 %convolution_add_fusion = f32[64,2048]{1,0:T(8,128)S(1)} fusion(f32[64,2048]{1,0:T(8,128)S(1)} %fusion.111, bf16[2048,512]{1,0:T(8,128)(2,1)} %param.26, bf16[8,8,4,128]{3,2,1,0:T(4,128)(2,1)} %bitcast.267), kind=kOutput, calls=%fused_computation.8 | convolution fusion | flops 134348800 | bytes 3211264 | tf_op jit(solution)/shard_map/tf,df->td/dot_general | solution.py:156
  196.1 3.8 %collective-permute-start.14 = (f32[16,2048]{1,0:T(8,128)S(1)}, f32[16,2048]{1,0:T(8,128)S(1)}, u32[]{:S(2)}, u32[]{:S(2)}) collective-permute-start(f32[16,2048]{1,0:T(8,128)S(1)} %get-tuple-element.15), channel_id=1, source_target_pairs={{0,3},{1,0},{2,1},{3,2},{4,7},{5,4},{6,5},{7,6},{8,11},{9,8},{10,9... | collective-permute-start | bytes 393224 | tf_op jit(solution)/shard_map/ppermute | solution.py:188
  199.9 1.5 fusion.10
  201.4 2.3 %collective-permute-done.12 = f32[16,2048]{1,0:T(8,128)S(1)} collective-permute-done((f32[16,2048]{1,0:T(8,128)S(1)}, f32[16,2048]{1,0:T(8,128)S(1)}, u32[]{:S(2)}, u32[]{:S(2)}) %collective-permute-start.12) | collective-permute-done | bytes 131104 | tf_op jit(solution)/shard_map/ppermute | solution.py:188
  203.7 4.9 %collective-permute-done.13 = f32[16,2048]{1,0:T(8,128)S(1)} collective-permute-done((f32[16,2048]{1,0:T(8,128)S(1)}, f32[16,2048]{1,0:T(8,128)S(1)}, u32[]{:S(2)}, u32[]{:S(2)}) %collective-permute-start.13) | collective-permute-done | bytes 131104 | tf_op jit(solution)/shard_map/ppermute | solution.py:188
  (142 shorter events, 36.8 us)
Async XLA Ops:
  7.2 93.1 %copy-start = (bf16[1,2048,768]{2,1,0:T(8,128)(2,1)S(1)}, bf16[1,2048,768]{2,1,0:T(8,128)(2,1)}, u32[]{:S(2)}) copy-start(bf16[1,2048,768]{2,1,0:T(8,128)(2,1)} %param.29) | copy-start | bytes 9437188
  7.2 27.3 %copy-start.4 = (bf16[16,2048]{1,0:T(8,128)(2,1)S(1)}, bf16[16,2048]{1,0:T(8,128)(2,1)}, u32[]{:S(2)}) copy-start(bf16[16,2048]{1,0:T(8,128)(2,1)} %param.16) | copy-start | bytes 196612
  7.2 27.3 %copy-start.11 = (f32[2048]{0:T(1024)S(1)}, f32[2048]{0:T(1024)}, u32[]{:S(2)}) copy-start(f32[2048]{0:T(1024)} %param.24) | copy-start | bytes 24580
  8.3 0.6 copy-start.19
  10.5 24.0 %collective-permute-start.2 = (bf16[16,2048]{1,0:T(8,128)(2,1)}, bf16[16,2048]{1,0:T(8,128)(2,1)S(1)}, u32[]{:S(2)}, u32[]{:S(2)}) collective-permute-start(bf16[16,2048]{1,0:T(8,128)(2,1)} %fusion.52), channel_id=1, source_target_pairs={{0,1},{1,2},{2,3},{3,0},{4,5},{5,6},{6,7},{7,4},{8,9},{9,10},{10,1... | collective-permute-start | bytes 196616 | tf_op jit(solution)/shard_map/ppermute | solution.py:166
  13.5 21.0 %collective-permute-start.1 = (bf16[16,2048]{1,0:T(8,128)(2,1)}, bf16[16,2048]{1,0:T(8,128)(2,1)S(1)}, u32[]{:S(2)}, u32[]{:S(2)}) collective-permute-start(bf16[16,2048]{1,0:T(8,128)(2,1)} %fusion.52), channel_id=1, source_target_pairs={{0,2},{1,3},{2,0},{3,1},{4,6},{5,7},{6,4},{7,5},{8,10},{9,11},{10,... | collective-permute-start | bytes 196616 | tf_op jit(solution)/shard_map/ppermute | solution.py:166
  16.1 18.4 %collective-permute-start = (bf16[16,2048]{1,0:T(8,128)(2,1)}, bf16[16,2048]{1,0:T(8,128)(2,1)S(1)}, u32[]{:S(2)}, u32[]{:S(2)}) collective-permute-start(bf16[16,2048]{1,0:T(8,128)(2,1)} %fusion.52), channel_id=1, source_target_pairs={{0,3},{1,0},{2,1},{3,2},{4,7},{5,4},{6,5},{7,6},{8,11},{9,8},{10,9... | collective-permute-start | bytes 196616 | tf_op jit(solution)/shard_map/ppermute | solution.py:166
  19.5 0.5 copy-start.24
  21.9 1.0 copy-start.14
  26.2 48.5 %all-to-all-start.1 = ((bf16[16,176,128]{2,1,0:T(8,128)(2,1)}), bf16[16,176,128]{2,1,0:T(8,128)(2,1)}, u32[]{:S(2)}, u32[]{:S(2)}) async-start(bf16[16,176,128]{2,1,0:T(8,128)(2,1)} %copy.136), calls=%async_computation.1 | async-start | bytes 1441792 | tf_op jit(solution)/shard_map/all_to_all | solution.py:197
  35.3 17.7 %copy-start.12 = (bf16[4,32,128]{2,1,0:T(8,128)(2,1)S(1)}, bf16[4,32,128]{2,1,0:T(8,128)(2,1)}, u32[]{:S(2)}) copy-start(bf16[4,32,128]{2,1,0:T(8,128)(2,1)} %get-tuple-element.27) | copy-start | bytes 98308
  35.3 15.9 %copy-start.25 = (pred[4,48]{1,0:T(4,128)(4,1)S(1)}, pred[4,48]{1,0:T(4,128)(4,1)}, u32[]{:S(2)}) copy-start(pred[4,48]{1,0:T(4,128)(4,1)} %concatenate.10) | copy-start | bytes 580
  37.4 24.2 %copy-start.15 = (s32[16,8]{0,1:T(8,128)S(1)}, s32[16,8]{0,1:T(8,128)}, u32[]{:S(2)}) copy-start(s32[16,8]{0,1:T(8,128)} %copy-done.14) | copy-start | bytes 1540
  37.4 13.6 %collective-permute-start.5 = (bf16[64,128]{1,0:T(8,128)(2,1)S(1)}, bf16[64,128]{1,0:T(8,128)(2,1)S(1)}, u32[]{:S(2)}, u32[]{:S(2)}) collective-permute-start(bf16[64,128]{1,0:T(8,128)(2,1)S(1)} %convolution_convert_fusion.6), channel_id=1, source_target_pairs={{0,1},{1,2},{2,3},{3,0},{4,5},{5,6},{6,7},{7,4},{8,9},{9,10},{10,1... | collective-permute-start | bytes 49160 | tf_op jit(solution)/shard_map/ppermute | solution.py:166
  39.1 11.9 %collective-permute-start.4 = (bf16[64,128]{1,0:T(8,128)(2,1)S(1)}, bf16[64,128]{1,0:T(8,128)(2,1)S(1)}, u32[]{:S(2)}, u32[]{:S(2)}) collective-permute-start(bf16[64,128]{1,0:T(8,128)(2,1)S(1)} %convolution_convert_fusion.6), channel_id=1, source_target_pairs={{0,2},{1,3},{2,0},{3,1},{4,6},{5,7},{6,4},{7,5},{8,10},{9,11},{10,... | collective-permute-start | bytes 49160 | tf_op jit(solution)/shard_map/ppermute | solution.py:166
  41.5 4.2 %collective-permute-start.3 = (bf16[64,128]{1,0:T(8,128)(2,1)S(1)}, bf16[64,128]{1,0:T(8,128)(2,1)S(1)}, u32[]{:S(2)}, u32[]{:S(2)}) collective-permute-start(bf16[64,128]{1,0:T(8,128)(2,1)S(1)} %convolution_convert_fusion.6), channel_id=1, source_target_pairs={{0,3},{1,0},{2,1},{3,2},{4,7},{5,4},{6,5},{7,6},{8,11},{9,8},{10,9... | collective-permute-start | bytes 49160 | tf_op jit(solution)/shard_map/ppermute | solution.py:166
  45.0 28.2 %copy-start.16 = (f32[2048]{0:T(1024)S(1)}, f32[2048]{0:T(1024)}, u32[]{:S(2)}) copy-start(f32[2048]{0:T(1024)} %param.25) | copy-start | bytes 24580
  51.2 23.5 %copy-start.13 = (bf16[64,128]{1,0:T(8,128)(2,1)}, bf16[64,128]{1,0:T(8,128)(2,1)S(1)}, u32[]{:S(2)}) copy-start(bf16[64,128]{1,0:T(8,128)(2,1)S(1)} %get-tuple-element.21) | copy-start | bytes 49156
  51.2 23.5 %copy-start.18 = (bf16[64,128]{1,0:T(8,128)(2,1)}, bf16[64,128]{1,0:T(8,128)(2,1)S(1)}, u32[]{:S(2)}) copy-start(bf16[64,128]{1,0:T(8,128)(2,1)S(1)} %get-tuple-element.20) | copy-start | bytes 49156
  53.0 21.7 %copy-start.26 = (f32[4,4,16]{2,1,0:T(4,128)}, f32[4,4,16]{2,1,0:T(4,128)S(1)}, u32[]{:S(2)}) copy-start(f32[4,4,16]{2,1,0:T(4,128)S(1)} %get-tuple-element.22) | copy-start | bytes 3076
  56.2 0.8 copy-start.8
  57.8 8.5 %collective-permute-start.6 = (f32[16,2048]{1,0:T(8,128)}, f32[16,2048]{1,0:T(8,128)}, u32[]{:S(2)}, u32[]{:S(2)}) collective-permute-start(f32[16,2048]{1,0:T(8,128)} %get-tuple-element.17), channel_id=1, source_target_pairs={{0,1},{1,2},{2,3},{3,0},{4,5},{5,6},{6,7},{7,4},{8,9},{9,10},{10,1... | collective-permute-start | bytes 393224 | tf_op jit(solution)/shard_map/ppermute | solution.py:188
  58.5 8.4 %collective-permute-start.8 = (f32[16,2048]{1,0:T(8,128)}, f32[16,2048]{1,0:T(8,128)}, u32[]{:S(2)}, u32[]{:S(2)}) collective-permute-start(f32[16,2048]{1,0:T(8,128)} %get-tuple-element.18), channel_id=1, source_target_pairs={{0,3},{1,0},{2,1},{3,2},{4,7},{5,4},{6,5},{7,6},{8,11},{9,8},{10,9... | collective-permute-start | bytes 393224 | tf_op jit(solution)/shard_map/ppermute | solution.py:188
  61.6 10.4 %collective-permute-start.7 = (f32[16,2048]{1,0:T(8,128)}, f32[16,2048]{1,0:T(8,128)}, u32[]{:S(2)}, u32[]{:S(2)}) collective-permute-start(f32[16,2048]{1,0:T(8,128)} %get-tuple-element.19), channel_id=1, source_target_pairs={{0,2},{1,3},{2,0},{3,1},{4,6},{5,7},{6,4},{7,5},{8,10},{9,11},{10,... | collective-permute-start | bytes 393224 | tf_op jit(solution)/shard_map/ppermute | solution.py:188
  61.9 20.0 %copy-start.10 = (pred[16,11,16]{2,1,0:T(8,128)(4,1)}, pred[16,11,16]{2,1,0:T(8,128)(4,1)S(1)}, u32[]{:S(2)}) copy-start(pred[16,11,16]{2,1,0:T(8,128)(4,1)S(1)} %compare_reduce_fusion) | copy-start | bytes 8452
  73.2 8.7 %copy-start.21 = (f32[16]{0:T(128)}, f32[16]{0:T(128)S(1)}, u32[]{:S(2)}) copy-start(f32[16]{0:T(128)S(1)} %add_rsqrt_fusion) | copy-start | bytes 196
  74.7 24.2 %all-to-all-start = ((bf16[16,176,128]{2,1,0:T(8,128)(2,1)}), bf16[16,176,128]{2,1,0:T(8,128)(2,1)}, u32[]{:S(2)}, u32[]{:S(2)}) async-start(bf16[16,176,128]{2,1,0:T(8,128)(2,1)} %copy.131), calls=%async_computation | async-start | bytes 1441792 | tf_op jit(solution)/shard_map/all_to_all | solution.py:197
  82.0 1.8 copy-start.5
  100.2 2.1 copy-start.1
  101.0 4.1 %copy-start.2 = (f32[16,11,768]{2,0,1:T(8,128)}, f32[16,11,768]{2,0,1:T(8,128)S(1)}, u32[]{:S(2)}) copy-start(f32[16,11,768]{2,0,1:T(8,128)S(1)} %convolution_bitcast_fusion.3) | copy-start | bytes 1622020
  102.3 1.6 copy-start.6
  103.1 0.8 copy-start.7
  106.2 26.5 %copy-start.17 = (f32[2048]{0:T(1024)S(1)}, f32[2048]{0:T(1024)}, u32[]{:S(2)}) copy-start(f32[2048]{0:T(1024)} %param.25) | copy-start | bytes 24580
  135.4 6.0 %collective-permute-start.9 = (bf16[16,2048]{1,0:T(8,128)(2,1)S(1)}, bf16[16,2048]{1,0:T(8,128)(2,1)S(1)}, u32[]{:S(2)}, u32[]{:S(2)}) collective-permute-start(bf16[16,2048]{1,0:T(8,128)(2,1)S(1)} %fusion.105), channel_id=1, source_target_pairs={{0,3},{1,0},{2,1},{3,2},{4,7},{5,4},{6,5},{7,6},{8,11},{9,8},{10,9... | collective-permute-start | bytes 196616 | tf_op jit(solution)/shard_map/ppermute | solution.py:166
  139.5 8.1 %collective-permute-start.11 = (bf16[16,2048]{1,0:T(8,128)(2,1)S(1)}, bf16[16,2048]{1,0:T(8,128)(2,1)S(1)}, u32[]{:S(2)}, u32[]{:S(2)}) collective-permute-start(bf16[16,2048]{1,0:T(8,128)(2,1)S(1)} %fusion.105), channel_id=1, source_target_pairs={{0,1},{1,2},{2,3},{3,0},{4,5},{5,6},{6,7},{7,4},{8,9},{9,10},{10,1... | collective-permute-start | bytes 196616 | tf_op jit(solution)/shard_map/ppermute | solution.py:166
  140.8 6.8 %collective-permute-start.10 = (bf16[16,2048]{1,0:T(8,128)(2,1)S(1)}, bf16[16,2048]{1,0:T(8,128)(2,1)S(1)}, u32[]{:S(2)}, u32[]{:S(2)}) collective-permute-start(bf16[16,2048]{1,0:T(8,128)(2,1)S(1)} %fusion.105), channel_id=1, source_target_pairs={{0,2},{1,3},{2,0},{3,1},{4,6},{5,7},{6,4},{7,5},{8,10},{9,11},{10,... | collective-permute-start | bytes 196616 | tf_op jit(solution)/shard_map/ppermute | solution.py:166
  149.5 24.2 %all-to-all-start.3 = ((bf16[16,176,128]{2,1,0:T(8,128)(2,1)}), bf16[16,176,128]{2,1,0:T(8,128)(2,1)}, u32[]{:S(2)}, u32[]{:S(2)}) async-start(bf16[16,176,128]{2,1,0:T(8,128)(2,1)} %copy.146), calls=%async_computation.3 | async-start | bytes 1441792 | tf_op jit(solution)/shard_map/all_to_all | solution.py:201
  153.8 38.0 %reduce-scatter.2.cloned.1.call-start = ((), (), s32[]{:S(2)}) async-start(), calls=%async_computation.5 | async-start | bytes 163840 | tf_op jit(solution)/shard_map/reduce_scatter | solution.py:151
  182.5 26.2 %copy-start.20 = (f32[16]{0:T(128)S(1)}, f32[16]{0:T(128)}, u32[]{:S(2)}) copy-start(f32[16]{0:T(128)} %copy-done.19) | copy-start | bytes 196
  191.8 8.1 %copy-start.3 = (bf16[2048,11,16]{0,2,1:T(8,128)(2,1)S(1)}, bf16[2048,11,16]{0,2,1:T(8,128)(2,1)}, u32[]{:S(2)}) copy-start(bf16[2048,11,16]{0,2,1:T(8,128)(2,1)} %dot_general.98) | copy-start | bytes 2162692
  193.6 15.3 %copy-start.9 = (bf16[16,2048]{1,0:T(8,128)(2,1)S(1)}, bf16[16,2048]{1,0:T(8,128)(2,1)}, u32[]{:S(2)}) copy-start(bf16[16,2048]{1,0:T(8,128)(2,1)} %param.17) | copy-start | bytes 196612
  193.6 15.3 %copy-start.22 = (f32[16]{0:T(128)S(1)}, f32[16]{0:T(128)}, u32[]{:S(2)}) copy-start(f32[16]{0:T(128)} %copy-done.21) | copy-start | bytes 196
  193.6 15.3 %copy-start.23 = (f32[16]{0:T(128)S(1)}, f32[16]{0:T(128)}, u32[]{:S(2)}) copy-start(f32[16]{0:T(128)} %convert_element_type.115) | copy-start | bytes 196
  196.0 7.7 %collective-permute-start.12 = (f32[16,2048]{1,0:T(8,128)S(1)}, f32[16,2048]{1,0:T(8,128)S(1)}, u32[]{:S(2)}, u32[]{:S(2)}) collective-permute-start(f32[16,2048]{1,0:T(8,128)S(1)} %get-tuple-element.14), channel_id=1, source_target_pairs={{0,1},{1,2},{2,3},{3,0},{4,5},{5,6},{6,7},{7,4},{8,9},{9,10},{10,1... | collective-permute-start | bytes 393224 | tf_op jit(solution)/shard_map/ppermute | solution.py:188
  196.1 7.6 %collective-permute-start.14 = (f32[16,2048]{1,0:T(8,128)S(1)}, f32[16,2048]{1,0:T(8,128)S(1)}, u32[]{:S(2)}, u32[]{:S(2)}) collective-permute-start(f32[16,2048]{1,0:T(8,128)S(1)} %get-tuple-element.15), channel_id=1, source_target_pairs={{0,3},{1,0},{2,1},{3,2},{4,7},{5,4},{6,5},{7,6},{8,11},{9,8},{10,9... | collective-permute-start | bytes 393224 | tf_op jit(solution)/shard_map/ppermute | solution.py:188
  199.9 8.8 %collective-permute-start.13 = (f32[16,2048]{1,0:T(8,128)S(1)}, f32[16,2048]{1,0:T(8,128)S(1)}, u32[]{:S(2)}, u32[]{:S(2)}) collective-permute-start(f32[16,2048]{1,0:T(8,128)S(1)} %get-tuple-element.16), channel_id=1, source_target_pairs={{0,2},{1,3},{2,0},{3,1},{4,6},{5,7},{6,4},{7,5},{8,10},{9,11},{10,... | collective-permute-start | bytes 393224 | tf_op jit(solution)/shard_map/ppermute | solution.py:188
Sparse Core Ops, SparseCore 0:
  173.9 17.8 reduce-scatter.1

commit v13 on v10

--- a/solution.py
+++ b/solution.py
@@ -162,7 +162,9 @@
         lax.ppermute(block, "head", perm=[(j, (j + shift) % count) for j in range(count)])
         for shift in range(1, count)
     ]
-    ordered = jnp.take(jnp.stack(parts), (me - jnp.arange(count)) % count, axis=0)
+    reversed_parts = parts[::-1]
+    doubled = jnp.stack(reversed_parts + reversed_parts)
+    ordered = lax.dynamic_slice_in_dim(doubled, count - 1 - me, count, 0)
     ordered = jnp.moveaxis(ordered, 0, axis)
     merged = list(block.shape)
     merged[axis] = count * block.shape[axis]

time: 209 us -> 231 us (1.11)
  waiting for transfers between devices: 49.5 us -> 64.1 us
  local copies, waits for them, and re-layouts: 32.4 us -> 36.7 us
    ppermute x9, waiting for transfers between devices: 7.03 us -> 23.8 us  [head_gather(): lax.ppermute(block, 'head', perm=[(j, (j + shift) % count) for j in range...]
    all_to_all x1, waiting for transfers between devices: 5.27 us -> 0.01 us  [from_experts(): lax.all_to_all(results, ('expert', 'head'), split_axis=0, concat_axis=0,...]
    gather x3 -> x0, local copies, waits for them, and re-layouts: 4.43 us -> none  [head_gather(): jnp.take(jnp.stack(parts), (me - jnp.arange(count)) % count, axis=0)]
    reduce_scatter x1, waiting for transfers between devices: 6.65 us -> 9.83 us  [attention_backward(): lax.psum_scatter(placed, 'head', scatter_dimension=1, tiled=True)]
    another operation x4 -> x1, other arithmetic: 3.31 us -> 0.75 us  [head_gather(): doubled = jnp.stack(reversed_parts + reversed_parts)]
    unnamed x68 -> x76, local copies, waits for them, and re-layouts: 8.03 us -> 10.4 us
where the time goes in v13:
time: 231 us; the launch traced here: 229 us
  waiting for transfers between devices  64.1 us (28%)
  matrix products  38.9 us (17%)
  starting transfers between devices  38.1 us (16%)
  local copies, waits for them, and re-layouts  36.7 us (16%)
  blocking collectives  23.1 us (10%)
  between operations  14.7 us (6%)
  other arithmetic  13.6 us (6%)
    ppermute x9, waiting for transfers between devices, head_gather(): lax.ppermute(block, 'head', perm=[(j, (j + shift) % count) for j in range...  23.8 us
    all_to_all x1, blocking collectives, from_experts(): lax.all_to_all(results, ('expert', 'head'), split_axis=0, concat_axis=0,...  23.1 us
    ppermute x9, starting transfers between devices, head_gather(): lax.ppermute(block, 'head', perm=[(j, (j + shift) % count) for j in range...  17.5 us
    ppermute x6, waiting for transfers between devices, head_sums(): lax.ppermute(chunks[(me + shift) % count], 'head', perm=[(j, (j + shift)...  17.3 us
    all_to_all x2, waiting for transfers between devices, to_experts(): lax.all_to_all(outgoing, ('expert', 'head'), split_axis=0, concat_axis=0,...  13.1 us
    unnamed x76, local copies, waits for them, and re-layouts  10.4 us
    reduce_scatter x1, waiting for transfers between devices, attention_backward(): lax.psum_scatter(placed, 'head', scatter_dimension=1, tiled=True)  9.83 us
    all_to_all x2, starting transfers between devices, to_experts(): lax.all_to_all(outgoing, ('expert', 'head'), split_axis=0, concat_axis=0,...  8.57 us
  transfers between devices with their start and end apart: 19, of which 9 were waited for; matrix products, arithmetic and copies ran while one was open for 29% of the time, Pallas kernels for 0%

profile of v13, /device:TPU:0, one launch (start us, length us, event | category | flops | bytes accessed | tf_op | source)
XLA Modules:
  0.0 229.2 jit_solution(16325036548045310389)
XLA Ops:
  8.9 1.6 fusion.52
  10.5 3.0 %collective-permute-start.2 = (bf16[16,2048]{1,0:T(8,128)(2,1)}, bf16[16,2048]{1,0:T(8,128)(2,1)S(1)}, u32[]{:S(2)}, u32[]{:S(2)}) collective-permute-start(bf16[16,2048]{1,0:T(8,128)(2,1)} %fusion.52), channel_id=1, source_target_pairs={{0,1},{1,2},{2,3},{3,0},{4,5},{5,6},{6,7},{7,4},{8,9},{9,10},{10,1... | collective-permute-start | bytes 196616 | tf_op jit(solution)/shard_map/ppermute | solution.py:162
  13.5 2.6 %collective-permute-start.1 = (bf16[16,2048]{1,0:T(8,128)(2,1)}, bf16[16,2048]{1,0:T(8,128)(2,1)S(1)}, u32[]{:S(2)}, u32[]{:S(2)}) collective-permute-start(bf16[16,2048]{1,0:T(8,128)(2,1)} %fusion.52), channel_id=1, source_target_pairs={{0,2},{1,3},{2,0},{3,1},{4,6},{5,7},{6,4},{7,5},{8,10},{9,11},{10,... | collective-permute-start | bytes 196616 | tf_op jit(solution)/shard_map/ppermute | solution.py:162
  16.1 1.3 collective-permute-start
  23.0 2.2 convolution_convert_fusion
  26.2 4.3 %all-to-all-start.2 = ((bf16[16,176,128]{2,1,0:T(8,128)(2,1)}), bf16[16,176,128]{2,1,0:T(8,128)(2,1)}, u32[]{:S(2)}, u32[]{:S(2)}) async-start(bf16[16,176,128]{2,1,0:T(8,128)(2,1)} %copy.140), calls=%async_computation.2 | async-start | bytes 1441792 | tf_op jit(solution)/shard_map/all_to_all | solution.py:193
  33.0 1.4 constant_dynamic-slice_fusion.2
  37.4 1.7 collective-permute-start.5
  39.1 2.4 %collective-permute-start.4 = (bf16[64,128]{1,0:T(8,128)(2,1)S(1)}, bf16[64,128]{1,0:T(8,128)(2,1)S(1)}, u32[]{:S(2)}, u32[]{:S(2)}) collective-permute-start(bf16[64,128]{1,0:T(8,128)(2,1)S(1)} %convolution_convert_fusion.6), channel_id=1, source_target_pairs={{0,2},{1,3},{2,0},{3,1},{4,6},{5,7},{6,4},{7,5},{8,10},{9,11},{10,... | collective-permute-start | bytes 49160 | tf_op jit(solution)/shard_map/ppermute | solution.py:162
  41.5 1.5 collective-permute-start.3
  43.0 2.1 convolution_convert_fusion.5
  45.7 5.3 %collective-permute-done.4 = bf16[64,128]{1,0:T(8,128)(2,1)S(1)} collective-permute-done((bf16[64,128]{1,0:T(8,128)(2,1)S(1)}, bf16[64,128]{1,0:T(8,128)(2,1)S(1)}, u32[]{:S(2)}, u32[]{:S(2)}) %collective-permute-start.4) | collective-permute-done | bytes 16416 | tf_op jit(solution)/shard_map/ppermute | solution.py:162
  51.2 1.8 fusion.108
  54.1 2.1 fusion.11
  58.5 3.1 %collective-permute-start.8 = (f32[16,2048]{1,0:T(8,128)}, f32[16,2048]{1,0:T(8,128)}, u32[]{:S(2)}, u32[]{:S(2)}) collective-permute-start(f32[16,2048]{1,0:T(8,128)} %get-tuple-element.10), channel_id=1, source_target_pairs={{0,3},{1,0},{2,1},{3,2},{4,7},{5,4},{6,5},{7,6},{8,11},{9,8},{10,9... | collective-permute-start | bytes 393224 | tf_op jit(solution)/shard_map/ppermute | solution.py:184
  61.9 4.4 %collective-permute-done.6 = f32[16,2048]{1,0:T(8,128)} collective-permute-done((f32[16,2048]{1,0:T(8,128)}, f32[16,2048]{1,0:T(8,128)}, u32[]{:S(2)}, u32[]{:S(2)}) %collective-permute-start.6) | collective-permute-done | bytes 131104 | tf_op jit(solution)/shard_map/ppermute | solution.py:184
  67.0 5.0 %collective-permute-done.7 = f32[16,2048]{1,0:T(8,128)} collective-permute-done((f32[16,2048]{1,0:T(8,128)}, f32[16,2048]{1,0:T(8,128)}, u32[]{:S(2)}, u32[]{:S(2)}) %collective-permute-start.7) | collective-permute-done | bytes 131104 | tf_op jit(solution)/shard_map/ppermute | solution.py:184
  74.7 4.3 %all-to-all-start = ((bf16[16,176,128]{2,1,0:T(8,128)(2,1)}), bf16[16,176,128]{2,1,0:T(8,128)(2,1)}, u32[]{:S(2)}, u32[]{:S(2)}) async-start(bf16[16,176,128]{2,1,0:T(8,128)(2,1)} %copy.131), calls=%async_computation | async-start | bytes 1441792 | tf_op jit(solution)/shard_map/all_to_all | solution.py:193
  79.0 2.9 %copy.173 = bf16[96,8,16,128]{3,2,1,0:T(8,128)(2,1)S(1)} copy(bf16[96,8,16,128]{3,1,2,0:T(8,128)(2,1)} %bitcast.250) | data formatting | bytes 6291456
  82.0 1.8 copy.141
  83.8 2.0 fusion.17
  85.8 13.1 %all-to-all-done = bf16[16,176,128]{2,1,0:T(8,128)(2,1)} async-done(((bf16[16,176,128]{2,1,0:T(8,128)(2,1)}), bf16[16,176,128]{2,1,0:T(8,128)(2,1)}, u32[]{:S(2)}, u32[]{:S(2)}) %all-to-all-start) | async-done | bytes 720928 | tf_op jit(solution)/shard_map/all_to_all | solution.py:193
  101.0 1.3 copy-done.1
  106.4 23.1 %all_to_all.20 = bf16[16,176,128]{2,1,0:T(8,128)(2,1)S(1)} all-to-all(bf16[16,176,128]{2,1,0:T(8,128)(2,1)S(1)} %copy.143), channel_id=1, replica_groups=mesh['groups'=2,'expert'=4,'head'=4] {'expert','head'}, dimensions={0} | all-to-all | bytes 1441792 | tf_op jit(solution)/shard_map/all_to_all | solution.py:197
  130.6 2.1 dot_general.94
  132.7 1.7 fusion.48
  134.4 1.6 fusion.105
  136.9 3.1 %fusion.13 = bf16[16,11,16,128]{3,0,2,1:T(8,128)(2,1)S(1)} fusion(bf16[768,16,128]{2,1,0:T(8,128)(2,1)} %bitcast.252, f32[16,11,768]{2,0,1:T(8,128)} %copy-done.7, f32[16,11,768]{2,0,1:T(8,128)} %copy-done.2), kind=kOutput, calls=%fused_computation.17 | convolution fusion | flops 554819584 | bytes 4947968 | tf_op jit(solution)/shard_map/scf,fkl->sckl/dot_general | solution.py:276
  141.0 4.3 %all-to-all-start.1 = ((bf16[16,176,128]{2,1,0:T(8,128)(2,1)}), bf16[16,176,128]{2,1,0:T(8,128)(2,1)}, u32[]{:S(2)}, u32[]{:S(2)}) async-start(bf16[16,176,128]{2,1,0:T(8,128)(2,1)} %copy.134), calls=%async_computation.1 | async-start | bytes 1441792 | tf_op jit(solution)/shard_map/all_to_all | solution.py:197
  145.3 1.8 collective-permute-start.11
  147.1 2.4 %collective-permute-start.10 = (bf16[16,2048]{1,0:T(8,128)(2,1)}, bf16[16,2048]{1,0:T(8,128)(2,1)S(1)}, u32[]{:S(2)}, u32[]{:S(2)}) collective-permute-start(bf16[16,2048]{1,0:T(8,128)(2,1)} %fusion.105), channel_id=1, source_target_pairs={{0,2},{1,3},{2,0},{3,1},{4,6},{5,7},{6,4},{7,5},{8,10},{9,11},{10,... | collective-permute-start | bytes 196616 | tf_op jit(solution)/shard_map/ppermute | solution.py:162
  150.4 18.5 %collective-permute-done.10 = bf16[16,2048]{1,0:T(8,128)(2,1)S(1)} collective-permute-done((bf16[16,2048]{1,0:T(8,128)(2,1)}, bf16[16,2048]{1,0:T(8,128)(2,1)S(1)}, u32[]{:S(2)}, u32[]{:S(2)}) %collective-permute-start.10) | collective-permute-done | bytes 65568 | tf_op jit(solution)/shard_map/ppermute | solution.py:162
  171.4 3.0 %convolution_convert_fusion.3 = bf16[64,512]{1,0:T(8,128)(2,1)} fusion(bf16[64,2048]{1,0:T(8,128)(2,1)S(1)} %bitcast.263, bf16[512,2048]{1,0:T(8,128)(2,1)} %param.28), kind=kOutput, calls=%fused_computation.37 | convolution fusion | flops 134250496 | bytes 2424832 | tf_op jit(solution)/shard_map/td,fd->tf/dot_general | solution.py:130
  174.4 1.5 reshape.149
  177.7 1.7 convolution_bitcast_fusion.4
  179.4 3.0 %convolution_bitcast_fusion.6 = f32[4,48,128]{2,1,0:T(8,128)} fusion(f32[4,4,16,48]{3,2,1,0:T(8,128)} %convolution_bitcast_fusion.4, bf16[4,16,4,128]{3,2,1,0:T(4,128)(2,1)} %reshape.137, f32[4,4,16,48]{3,2,1,0:T(8,128)} %get-tuple-element.15, f32[4,4,16]{2,1,0:T(4,128)} %copy-done.26), kind=kOutput, calls=%fused_computation.36 | convolution fusion | flops 3232047 | bytes 263168 | tf_op jit(solution)/shard_map/shbk,sbhd->skd/dot_general | solution.py:58
  184.5 1.4 constant_dynamic-update-slice_fusion.8
  185.9 2.2 copy.231
  188.0 2.2 dot_general.87
  190.2 2.9 %fusion.29 = bf16[4,16,4,128]{3,1,2,0:T(8,128)(2,1)} fusion(f32[4,4,16,48]{3,2,1,0:T(8,128)} %convolution_bitcast_fusion.4, bf16[4,16,128]{2,1,0:T(8,128)(2,1)} %bitcast.274, bf16[4,32,128]{2,1,0:T(8,128)(2,1)} %get-tuple-element.18, f32[4,4,16,48]{3,2,1,0:T(8,128)} %get-tuple-element.15, f32[4,4,16]{2,1,0:T(4,128)} %copy-done.26), kind=kOutput, calls=%fused_computation.41 | convolution fusion | flops 3363119 | bytes 214016 | tf_op jit(solution)/shard_map/shbk,skd->sbhd/dot_general | solution.py:55
  193.1 1.5 copy.150
  194.6 9.8 %reduce-scatter.2.cloned.1.call-done = f32[64,128]{1,0:T(8,128)} async-done(((f32[64,512]{1,0:T(8,128)}), f32[64,128]{1,0:T(8,128)}) %reduce-scatter.2.cloned.1.call-update) | async-done | bytes 32784 | tf_op jit(solution)/shard_map/reduce_scatter | solution.py:148
  204.4 1.8 fusion.111
  206.3 2.4 %convolution_add_fusion = f32[64,2048]{1,0:T(8,128)S(1)} fusion(f32[64,2048]{1,0:T(8,128)S(1)} %fusion.111, bf16[2048,512]{1,0:T(8,128)(2,1)} %param.26, bf16[8,8,4,128]{3,2,1,0:T(4,128)(2,1)} %bitcast.267), kind=kOutput, calls=%fused_computation.8 | convolution fusion | flops 134348800 | bytes 3211264 | tf_op jit(solution)/shard_map/tf,df->td/dot_general | solution.py:153
  208.8 3.8 %collective-permute-start.14 = (f32[16,2048]{1,0:T(8,128)S(1)}, f32[16,2048]{1,0:T(8,128)S(1)}, u32[]{:S(2)}, u32[]{:S(2)}) collective-permute-start(f32[16,2048]{1,0:T(8,128)S(1)} %get-tuple-element.7), channel_id=1, source_target_pairs={{0,3},{1,0},{2,1},{3,2},{4,7},{5,4},{6,5},{7,6},{8,11},{9,8},{10,9... | collective-permute-start | bytes 393224 | tf_op jit(solution)/shard_map/ppermute | solution.py:184
  212.6 1.5 fusion.10
  214.1 2.3 %collective-permute-done.12 = f32[16,2048]{1,0:T(8,128)S(1)} collective-permute-done((f32[16,2048]{1,0:T(8,128)S(1)}, f32[16,2048]{1,0:T(8,128)S(1)}, u32[]{:S(2)}, u32[]{:S(2)}) %collective-permute-start.12) | collective-permute-done | bytes 131104 | tf_op jit(solution)/shard_map/ppermute | solution.py:184
  216.4 5.0 %collective-permute-done.13 = f32[16,2048]{1,0:T(8,128)S(1)} collective-permute-done((f32[16,2048]{1,0:T(8,128)S(1)}, f32[16,2048]{1,0:T(8,128)S(1)}, u32[]{:S(2)}, u32[]{:S(2)}) %collective-permute-start.13) | collective-permute-done | bytes 131104 | tf_op jit(solution)/shard_map/ppermute | solution.py:184
  (142 shorter events, 39.0 us)
Async XLA Ops:
  7.2 93.1 %copy-start = (bf16[1,2048,768]{2,1,0:T(8,128)(2,1)S(1)}, bf16[1,2048,768]{2,1,0:T(8,128)(2,1)}, u32[]{:S(2)}) copy-start(bf16[1,2048,768]{2,1,0:T(8,128)(2,1)} %param.29) | copy-start | bytes 9437188
  7.2 27.3 %copy-start.4 = (bf16[16,2048]{1,0:T(8,128)(2,1)S(1)}, bf16[16,2048]{1,0:T(8,128)(2,1)}, u32[]{:S(2)}) copy-start(bf16[16,2048]{1,0:T(8,128)(2,1)} %param.16) | copy-start | bytes 196612
  7.2 27.3 %copy-start.11 = (f32[2048]{0:T(1024)S(1)}, f32[2048]{0:T(1024)}, u32[]{:S(2)}) copy-start(f32[2048]{0:T(1024)} %param.24) | copy-start | bytes 24580
  8.3 0.6 copy-start.19
  10.5 24.0 %collective-permute-start.2 = (bf16[16,2048]{1,0:T(8,128)(2,1)}, bf16[16,2048]{1,0:T(8,128)(2,1)S(1)}, u32[]{:S(2)}, u32[]{:S(2)}) collective-permute-start(bf16[16,2048]{1,0:T(8,128)(2,1)} %fusion.52), channel_id=1, source_target_pairs={{0,1},{1,2},{2,3},{3,0},{4,5},{5,6},{6,7},{7,4},{8,9},{9,10},{10,1... | collective-permute-start | bytes 196616 | tf_op jit(solution)/shard_map/ppermute | solution.py:162
  13.5 21.0 %collective-permute-start.1 = (bf16[16,2048]{1,0:T(8,128)(2,1)}, bf16[16,2048]{1,0:T(8,128)(2,1)S(1)}, u32[]{:S(2)}, u32[]{:S(2)}) collective-permute-start(bf16[16,2048]{1,0:T(8,128)(2,1)} %fusion.52), channel_id=1, source_target_pairs={{0,2},{1,3},{2,0},{3,1},{4,6},{5,7},{6,4},{7,5},{8,10},{9,11},{10,... | collective-permute-start | bytes 196616 | tf_op jit(solution)/shard_map/ppermute | solution.py:162
  16.1 18.4 %collective-permute-start = (bf16[16,2048]{1,0:T(8,128)(2,1)}, bf16[16,2048]{1,0:T(8,128)(2,1)S(1)}, u32[]{:S(2)}, u32[]{:S(2)}) collective-permute-start(bf16[16,2048]{1,0:T(8,128)(2,1)} %fusion.52), channel_id=1, source_target_pairs={{0,3},{1,0},{2,1},{3,2},{4,7},{5,4},{6,5},{7,6},{8,11},{9,8},{10,9... | collective-permute-start | bytes 196616 | tf_op jit(solution)/shard_map/ppermute | solution.py:162
  19.5 0.5 copy-start.24
  21.9 1.0 copy-start.14
  26.2 48.5 %all-to-all-start.2 = ((bf16[16,176,128]{2,1,0:T(8,128)(2,1)}), bf16[16,176,128]{2,1,0:T(8,128)(2,1)}, u32[]{:S(2)}, u32[]{:S(2)}) async-start(bf16[16,176,128]{2,1,0:T(8,128)(2,1)} %copy.140), calls=%async_computation.2 | async-start | bytes 1441792 | tf_op jit(solution)/shard_map/all_to_all | solution.py:193
  35.3 17.7 %copy-start.12 = (bf16[4,32,128]{2,1,0:T(8,128)(2,1)S(1)}, bf16[4,32,128]{2,1,0:T(8,128)(2,1)}, u32[]{:S(2)}) copy-start(bf16[4,32,128]{2,1,0:T(8,128)(2,1)} %get-tuple-element.19) | copy-start | bytes 98308
  35.3 15.9 %copy-start.25 = (pred[4,48]{1,0:T(4,128)(4,1)S(1)}, pred[4,48]{1,0:T(4,128)(4,1)}, u32[]{:S(2)}) copy-start(pred[4,48]{1,0:T(4,128)(4,1)} %concatenate.10) | copy-start | bytes 580
  37.4 24.2 %copy-start.15 = (s32[16,8]{0,1:T(8,128)S(1)}, s32[16,8]{0,1:T(8,128)}, u32[]{:S(2)}) copy-start(s32[16,8]{0,1:T(8,128)} %copy-done.14) | copy-start | bytes 1540
  37.4 13.6 %collective-permute-start.5 = (bf16[64,128]{1,0:T(8,128)(2,1)S(1)}, bf16[64,128]{1,0:T(8,128)(2,1)S(1)}, u32[]{:S(2)}, u32[]{:S(2)}) collective-permute-start(bf16[64,128]{1,0:T(8,128)(2,1)S(1)} %convolution_convert_fusion.6), channel_id=1, source_target_pairs={{0,1},{1,2},{2,3},{3,0},{4,5},{5,6},{6,7},{7,4},{8,9},{9,10},{10,1... | collective-permute-start | bytes 49160 | tf_op jit(solution)/shard_map/ppermute | solution.py:162
  39.1 11.9 %collective-permute-start.4 = (bf16[64,128]{1,0:T(8,128)(2,1)S(1)}, bf16[64,128]{1,0:T(8,128)(2,1)S(1)}, u32[]{:S(2)}, u32[]{:S(2)}) collective-permute-start(bf16[64,128]{1,0:T(8,128)(2,1)S(1)} %convolution_convert_fusion.6), channel_id=1, source_target_pairs={{0,2},{1,3},{2,0},{3,1},{4,6},{5,7},{6,4},{7,5},{8,10},{9,11},{10,... | collective-permute-start | bytes 49160 | tf_op jit(solution)/shard_map/ppermute | solution.py:162
  41.5 4.2 %collective-permute-start.3 = (bf16[64,128]{1,0:T(8,128)(2,1)S(1)}, bf16[64,128]{1,0:T(8,128)(2,1)S(1)}, u32[]{:S(2)}, u32[]{:S(2)}) collective-permute-start(bf16[64,128]{1,0:T(8,128)(2,1)S(1)} %convolution_convert_fusion.6), channel_id=1, source_target_pairs={{0,3},{1,0},{2,1},{3,2},{4,7},{5,4},{6,5},{7,6},{8,11},{9,8},{10,9... | collective-permute-start | bytes 49160 | tf_op jit(solution)/shard_map/ppermute | solution.py:162
  45.0 28.2 %copy-start.16 = (f32[2048]{0:T(1024)S(1)}, f32[2048]{0:T(1024)}, u32[]{:S(2)}) copy-start(f32[2048]{0:T(1024)} %param.25) | copy-start | bytes 24580
  51.2 23.5 %copy-start.13 = (bf16[64,128]{1,0:T(8,128)(2,1)}, bf16[64,128]{1,0:T(8,128)(2,1)S(1)}, u32[]{:S(2)}) copy-start(bf16[64,128]{1,0:T(8,128)(2,1)S(1)} %get-tuple-element.13) | copy-start | bytes 49156
  51.2 23.5 %copy-start.18 = (bf16[64,128]{1,0:T(8,128)(2,1)}, bf16[64,128]{1,0:T(8,128)(2,1)S(1)}, u32[]{:S(2)}) copy-start(bf16[64,128]{1,0:T(8,128)(2,1)S(1)} %get-tuple-element.12) | copy-start | bytes 49156
  53.0 21.7 %copy-start.26 = (f32[4,4,16]{2,1,0:T(4,128)}, f32[4,4,16]{2,1,0:T(4,128)S(1)}, u32[]{:S(2)}) copy-start(f32[4,4,16]{2,1,0:T(4,128)S(1)} %get-tuple-element.14) | copy-start | bytes 3076
  56.2 0.8 copy-start.8
  57.8 8.5 %collective-permute-start.6 = (f32[16,2048]{1,0:T(8,128)}, f32[16,2048]{1,0:T(8,128)}, u32[]{:S(2)}, u32[]{:S(2)}) collective-permute-start(f32[16,2048]{1,0:T(8,128)} %get-tuple-element.9), channel_id=1, source_target_pairs={{0,1},{1,2},{2,3},{3,0},{4,5},{5,6},{6,7},{7,4},{8,9},{9,10},{10,1... | collective-permute-start | bytes 393224 | tf_op jit(solution)/shard_map/ppermute | solution.py:184
  58.5 8.4 %collective-permute-start.8 = (f32[16,2048]{1,0:T(8,128)}, f32[16,2048]{1,0:T(8,128)}, u32[]{:S(2)}, u32[]{:S(2)}) collective-permute-start(f32[16,2048]{1,0:T(8,128)} %get-tuple-element.10), channel_id=1, source_target_pairs={{0,3},{1,0},{2,1},{3,2},{4,7},{5,4},{6,5},{7,6},{8,11},{9,8},{10,9... | collective-permute-start | bytes 393224 | tf_op jit(solution)/shard_map/ppermute | solution.py:184
  61.6 10.4 %collective-permute-start.7 = (f32[16,2048]{1,0:T(8,128)}, f32[16,2048]{1,0:T(8,128)}, u32[]{:S(2)}, u32[]{:S(2)}) collective-permute-start(f32[16,2048]{1,0:T(8,128)} %get-tuple-element.11), channel_id=1, source_target_pairs={{0,2},{1,3},{2,0},{3,1},{4,6},{5,7},{6,4},{7,5},{8,10},{9,11},{10,... | collective-permute-start | bytes 393224 | tf_op jit(solution)/shard_map/ppermute | solution.py:184
  61.9 20.0 %copy-start.10 = (pred[16,11,16]{2,1,0:T(8,128)(4,1)}, pred[16,11,16]{2,1,0:T(8,128)(4,1)S(1)}, u32[]{:S(2)}) copy-start(pred[16,11,16]{2,1,0:T(8,128)(4,1)S(1)} %compare_reduce_fusion) | copy-start | bytes 8452
  73.2 8.7 %copy-start.21 = (f32[16]{0:T(128)}, f32[16]{0:T(128)S(1)}, u32[]{:S(2)}) copy-start(f32[16]{0:T(128)S(1)} %add_rsqrt_fusion) | copy-start | bytes 196
  74.7 24.2 %all-to-all-start = ((bf16[16,176,128]{2,1,0:T(8,128)(2,1)}), bf16[16,176,128]{2,1,0:T(8,128)(2,1)}, u32[]{:S(2)}, u32[]{:S(2)}) async-start(bf16[16,176,128]{2,1,0:T(8,128)(2,1)} %copy.131), calls=%async_computation | async-start | bytes 1441792 | tf_op jit(solution)/shard_map/all_to_all | solution.py:193
  82.0 1.8 copy-start.5
  100.2 2.1 copy-start.1
  101.0 4.1 %copy-start.2 = (f32[16,11,768]{2,0,1:T(8,128)}, f32[16,11,768]{2,0,1:T(8,128)S(1)}, u32[]{:S(2)}) copy-start(f32[16,11,768]{2,0,1:T(8,128)S(1)} %convolution_bitcast_fusion.3) | copy-start | bytes 1622020
  102.3 1.6 copy-start.6
  103.1 0.8 copy-start.7
  106.2 26.5 %copy-start.17 = (f32[2048]{0:T(1024)S(1)}, f32[2048]{0:T(1024)}, u32[]{:S(2)}) copy-start(f32[2048]{0:T(1024)} %param.25) | copy-start | bytes 24580
  136.0 13.5 %collective-permute-start.9 = (bf16[16,2048]{1,0:T(8,128)(2,1)}, bf16[16,2048]{1,0:T(8,128)(2,1)}, u32[]{:S(2)}, u32[]{:S(2)}) collective-permute-start(bf16[16,2048]{1,0:T(8,128)(2,1)} %fusion.105), channel_id=1, source_target_pairs={{0,3},{1,0},{2,1},{3,2},{4,7},{5,4},{6,5},{7,6},{8,11},{9,8},{10,9... | collective-permute-start | bytes 196616 | tf_op jit(solution)/shard_map/ppermute | solution.py:162
  141.0 44.9 %all-to-all-start.1 = ((bf16[16,176,128]{2,1,0:T(8,128)(2,1)}), bf16[16,176,128]{2,1,0:T(8,128)(2,1)}, u32[]{:S(2)}, u32[]{:S(2)}) async-start(bf16[16,176,128]{2,1,0:T(8,128)(2,1)} %copy.134), calls=%async_computation.1 | async-start | bytes 1441792 | tf_op jit(solution)/shard_map/all_to_all | solution.py:197
  145.3 59.2 %reduce-scatter.2.cloned.1.call-start = ((), (), s32[]{:S(2)}) async-start(), calls=%async_computation.5 | async-start | bytes 163840 | tf_op jit(solution)/shard_map/reduce_scatter | solution.py:148
  145.3 23.5 %collective-permute-start.11 = (bf16[16,2048]{1,0:T(8,128)(2,1)}, bf16[16,2048]{1,0:T(8,128)(2,1)S(1)}, u32[]{:S(2)}, u32[]{:S(2)}) collective-permute-start(bf16[16,2048]{1,0:T(8,128)(2,1)} %fusion.105), channel_id=1, source_target_pairs={{0,1},{1,2},{2,3},{3,0},{4,5},{5,6},{6,7},{7,4},{8,9},{9,10},{10,1... | collective-permute-start | bytes 196616 | tf_op jit(solution)/shard_map/ppermute | solution.py:162
  147.1 21.7 %collective-permute-start.10 = (bf16[16,2048]{1,0:T(8,128)(2,1)}, bf16[16,2048]{1,0:T(8,128)(2,1)S(1)}, u32[]{:S(2)}, u32[]{:S(2)}) collective-permute-start(bf16[16,2048]{1,0:T(8,128)(2,1)} %fusion.105), channel_id=1, source_target_pairs={{0,2},{1,3},{2,0},{3,1},{4,6},{5,7},{6,4},{7,5},{8,10},{9,11},{10,... | collective-permute-start | bytes 196616 | tf_op jit(solution)/shard_map/ppermute | solution.py:162
  194.6 26.7 %copy-start.20 = (f32[16]{0:T(128)S(1)}, f32[16]{0:T(128)}, u32[]{:S(2)}) copy-start(f32[16]{0:T(128)} %copy-done.19) | copy-start | bytes 196
  204.4 8.1 %copy-start.3 = (bf16[2048,11,16]{0,2,1:T(8,128)(2,1)S(1)}, bf16[2048,11,16]{0,2,1:T(8,128)(2,1)}, u32[]{:S(2)}) copy-start(bf16[2048,11,16]{0,2,1:T(8,128)(2,1)} %dot_general.87) | copy-start | bytes 2162692
  206.2 15.3 %copy-start.9 = (bf16[16,2048]{1,0:T(8,128)(2,1)S(1)}, bf16[16,2048]{1,0:T(8,128)(2,1)}, u32[]{:S(2)}) copy-start(bf16[16,2048]{1,0:T(8,128)(2,1)} %param.17) | copy-start | bytes 196612
  206.2 15.3 %copy-start.22 = (f32[16]{0:T(128)S(1)}, f32[16]{0:T(128)}, u32[]{:S(2)}) copy-start(f32[16]{0:T(128)} %copy-done.21) | copy-start | bytes 196
  206.3 15.3 %copy-start.23 = (f32[16]{0:T(128)S(1)}, f32[16]{0:T(128)}, u32[]{:S(2)}) copy-start(f32[16]{0:T(128)} %convert_element_type.116) | copy-start | bytes 196
  208.7 7.7 %collective-permute-start.12 = (f32[16,2048]{1,0:T(8,128)S(1)}, f32[16,2048]{1,0:T(8,128)S(1)}, u32[]{:S(2)}, u32[]{:S(2)}) collective-permute-start(f32[16,2048]{1,0:T(8,128)S(1)} %get-tuple-element.6), channel_id=1, source_target_pairs={{0,1},{1,2},{2,3},{3,0},{4,5},{5,6},{6,7},{7,4},{8,9},{9,10},{10,1... | collective-permute-start | bytes 393224 | tf_op jit(solution)/shard_map/ppermute | solution.py:184
  208.8 7.6 %collective-permute-start.14 = (f32[16,2048]{1,0:T(8,128)S(1)}, f32[16,2048]{1,0:T(8,128)S(1)}, u32[]{:S(2)}, u32[]{:S(2)}) collective-permute-start(f32[16,2048]{1,0:T(8,128)S(1)} %get-tuple-element.7), channel_id=1, source_target_pairs={{0,3},{1,0},{2,1},{3,2},{4,7},{5,4},{6,5},{7,6},{8,11},{9,8},{10,9... | collective-permute-start | bytes 393224 | tf_op jit(solution)/shard_map/ppermute | solution.py:184
  212.6 8.8 %collective-permute-start.13 = (f32[16,2048]{1,0:T(8,128)S(1)}, f32[16,2048]{1,0:T(8,128)S(1)}, u32[]{:S(2)}, u32[]{:S(2)}) collective-permute-start(f32[16,2048]{1,0:T(8,128)S(1)} %get-tuple-element.8), channel_id=1, source_target_pairs={{0,2},{1,3},{2,0},{3,1},{4,6},{5,7},{6,4},{7,5},{8,10},{9,11},{10,... | collective-permute-start | bytes 393224 | tf_op jit(solution)/shard_map/ppermute | solution.py:184
Sparse Core Ops, SparseCore 0:
  186.0 18.3 reduce-scatter.1

commit v14 on v10

--- a/solution.py
+++ b/solution.py
@@ -145,7 +145,7 @@
         key_value_width + kv_now * HEAD_SIZE,
         1,
     )
-    own_grads = lax.psum_scatter(placed, "head", scatter_dimension=1, tiled=True)
+    own_grads = head_sums(placed, axis=1)
     running = jnp.einsum(
         "tc,dc->td", own_grads, own_kv_weights.astype(jnp.float32), precision=lax.Precision.HIGHEST
     )
@@ -162,6 +162,13 @@
         lax.ppermute(block, "head", perm=[(j, (j + shift) % count) for j in range(count)])
         for shift in range(1, count)
     ]
+    return head_order(parts, axis)
+
+
+def head_order(parts, axis):
+    count = lax.axis_size("head")
+    me = lax.axis_index("head")
+    block = parts[0]
     ordered = jnp.take(jnp.stack(parts), (me - jnp.arange(count)) % count, axis=0)
     ordered = jnp.moveaxis(ordered, 0, axis)
     merged = list(block.shape)
@@ -173,14 +180,24 @@
     return head_gather(row_block, 0)
 
 
-def head_sums(partial_rows):
+def after_first_hop(block, waiting):
+    count = lax.axis_size("head")
+    first = lax.ppermute(block, "head", perm=[(j, (j + 1) % count) for j in range(count)])
+    return lax.optimization_barrier((waiting, first))
+
+
+def head_sums(partial_rows, axis=0):
     count = lax.axis_size("head")
     me = lax.axis_index("head")
-    chunks = partial_rows.reshape((count, -1) + partial_rows.shape[1:])
-    total = chunks[me]
+    size = partial_rows.shape[axis] // count
+
+    def chunk(index):
+        return lax.dynamic_slice_in_dim(partial_rows, index * size, size, axis)
+
+    total = chunk(me)
     for shift in range(1, count):
         total = total + lax.ppermute(
-            chunks[(me + shift) % count],
+            chunk((me + shift) % count),
             "head",
             perm=[(j, (j + shift) % count) for j in range(count)],
         )
@@ -286,21 +303,20 @@
         "scf,klf->sckl", grad_up, up_matrix, preferred_element_type=jnp.float32
     )
     grad_back = grad_back.astype(jnp.bfloat16)
-    result_home = from_experts(result.reshape(flat_shape)).reshape(split_shape)
     grad_home = from_experts(grad_back.reshape(flat_shape)).reshape(split_shape)
-    moe_sum = jnp.einsum(
-        "dct,dckl->tkl",
-        weighting,
-        result_home.astype(jnp.float32),
-        precision=highest_prec,
-    ).reshape(owned, width)
-    layer_out = (hidden.astype(jnp.float32) + moe_sum).astype(jnp.bfloat16)
     grad_moe = jnp.einsum(
         "dct,dckl->tkl", placement, grad_home, preferred_element_type=jnp.float32
     ).reshape(owned, width)
     grad_hidden = cotangent + rms_backward(hidden, moe_gain, inverse_two, grad_moe)
     grad_low = grad_hidden.astype(jnp.bfloat16)
-    grad_gathered = head_rows(grad_low)
+    count = lax.axis_size("head")
+    (result, first_hop) = after_first_hop(grad_low, result)
+    grad_parts = [grad_low, first_hop] + [
+        lax.ppermute(grad_low, "head", perm=[(j, (j + shift) % count) for j in range(count)])
+        for shift in range(2, count)
+    ]
+    grad_gathered = head_order(grad_parts, 0)
+    result_home = from_experts(result.reshape(flat_shape)).reshape(split_shape)
     grad_attn_rows = head_sums(
         attention_backward(
             grad_gathered,
@@ -314,6 +330,13 @@
     input_grad = (
         grad_hidden + rms_backward(hidden_in, attn_gain, inverse_one, grad_attn_rows)
     ).astype(jnp.bfloat16)
+    moe_sum = jnp.einsum(
+        "dct,dckl->tkl",
+        weighting,
+        result_home.astype(jnp.float32),
+        precision=highest_prec,
+    ).reshape(owned, width)
+    layer_out = (hidden.astype(jnp.float32) + moe_sum).astype(jnp.bfloat16)
     return (layer_out, input_grad)
 
 

time: 209 us -> 208 us (level)
  waiting for transfers between devices: 49.5 us -> 76.4 us
  blocking collectives: 23.2 us -> 0 us
  between operations: 14.8 us -> 1.46 us
  starting transfers between devices: 36.6 us -> 44.3 us
    all_to_all x1 -> x0, blocking collectives: 23.2 us -> none  [from_experts(): lax.all_to_all(results, ('expert', 'head'), split_axis=0, concat_axis=0,...]
    ppermute x6 -> x12, waiting for transfers between devices: 17.4 us -> 36.3 us  [the longest x9 34 us: head_sums(): lax.ppermute(chunk((me + shift) % count), 'head', perm=[(j, (j + shift) %...]
    all_to_all x1 -> x2, waiting for transfers between devices: 5.27 us -> 19.9 us  [from_experts(): lax.all_to_all(results, ('expert', 'head'), split_axis=0, concat_axis=0,...]
    ppermute x6 -> x12, starting transfers between devices: 7.7 us -> 14.5 us  [the longest x9 12.4 us: head_sums(): lax.ppermute(chunk((me + shift) % count), 'head', perm=[(j, (j + shift) %...]
    reduce_scatter x1 -> x0, waiting for transfers between devices: 6.65 us -> none  [attention_backward(): lax.psum_scatter(placed, 'head', scatter_dimension=1, tiled=True)]
    all_to_all x1 -> x2, starting transfers between devices: 5.04 us -> 8.68 us  [from_experts(): lax.all_to_all(results, ('expert', 'head'), split_axis=0, concat_axis=0,...]
    ppermute x9 -> x6, starting transfers between devices: 15.2 us -> 12.6 us  [head_gather(): lax.ppermute(block, 'head', perm=[(j, (j + shift) % count) for j in range...]
    ppermute x9 -> x6, waiting for transfers between devices: 7.03 us -> 7.06 us  [head_gather(): lax.ppermute(block, 'head', perm=[(j, (j + shift) % count) for j in range...]
  transfers between devices with their start and end apart: 19 -> 22, of which waited for: 9 -> 13; matrix products, arithmetic and copies ran while one was open for 29% -> 20% of each run, Pallas kernels for 0% -> 0%
where the time goes in v14:
time: 208 us; the launch traced here: 206 us
  waiting for transfers between devices  76.4 us (37%)
  starting transfers between devices  44.3 us (21%)
  matrix products  39.2 us (19%)
  local copies, waits for them, and re-layouts  32.9 us (16%)
  other arithmetic  11.9 us (6%)
    ppermute x9, waiting for transfers between devices, head_sums(): lax.ppermute(chunk((me + shift) % count), 'head', perm=[(j, (j + shift) %...  34 us
    all_to_all x2, waiting for transfers between devices, from_experts(): lax.all_to_all(results, ('expert', 'head'), split_axis=0, concat_axis=0,...  19.9 us
    all_to_all x2, waiting for transfers between devices, to_experts(): lax.all_to_all(outgoing, ('expert', 'head'), split_axis=0, concat_axis=0,...  13.1 us
    ppermute x6, starting transfers between devices, head_gather(): lax.ppermute(block, 'head', perm=[(j, (j + shift) % count) for j in range...  12.6 us
    ppermute x9, starting transfers between devices, head_sums(): lax.ppermute(chunk((me + shift) % count), 'head', perm=[(j, (j + shift) %...  12.4 us
    all_to_all x2, starting transfers between devices, from_experts(): lax.all_to_all(results, ('expert', 'head'), split_axis=0, concat_axis=0,...  8.68 us
    all_to_all x2, starting transfers between devices, to_experts(): lax.all_to_all(outgoing, ('expert', 'head'), split_axis=0, concat_axis=0,...  8.54 us
    unnamed x68, local copies, waits for them, and re-layouts  7.4 us
  transfers between devices with their start and end apart: 22, of which 13 were waited for; matrix products, arithmetic and copies ran while one was open for 20% of the time, Pallas kernels for 0%

profile of v14, /device:TPU:0, one launch (start us, length us, event | category | flops | bytes accessed | tf_op | source)
XLA Modules:
  0.0 206.3 jit_solution(2484371156545639679)
XLA Ops:
  2.7 4.1 %collective-permute-start.1 = (bf16[16,2048]{1,0:T(8,128)(2,1)S(1)}, bf16[16,2048]{1,0:T(8,128)(2,1)S(1)}, u32[]{:S(2)}, u32[]{:S(2)}) collective-permute-start(bf16[16,2048]{1,0:T(8,128)(2,1)S(1)} %fusion.50), channel_id=1, source_target_pairs={{0,2},{1,3},{2,0},{3,1},{4,6},{5,7},{6,4},{7,5},{8,10},{9,11},{10,... | collective-permute-start | bytes 196616 | tf_op jit(solution)/shard_map/ppermute | solution.py:162
  6.8 1.6 collective-permute-start
  8.4 2.2 %collective-permute-start.2 = (bf16[16,2048]{1,0:T(8,128)(2,1)S(1)}, bf16[16,2048]{1,0:T(8,128)(2,1)}, u32[]{:S(2)}, u32[]{:S(2)}) collective-permute-start(bf16[16,2048]{1,0:T(8,128)(2,1)S(1)} %fusion.50), channel_id=1, source_target_pairs={{0,3},{1,0},{2,1},{3,2},{4,7},{5,4},{6,5},{7,6},{8,11},{9,8},{10,9... | collective-permute-start | bytes 196616 | tf_op jit(solution)/shard_map/ppermute | solution.py:162
  15.2 2.2 %convolution_convert_fusion = bf16[16,11,16,128]{3,0,2,1:T(8,128)(2,1)S(1)} fusion(f32[16,11,16,1]{2,1,0,3:T(8,128)S(1)} %bitcast.207, bf16[16,2048]{1,0:T(8,128)(2,1)} %param.19, f32[16]{0:T(128)S(1)} %convert_element_type.115), kind=kOutput, calls=%fused_computation.19 | convolution fusion | flops 69632000 | bytes 797760 | tf_op jit(solution)/shard_map/dct,tkl->dckl/dot_general | solution.py:272
  18.4 4.3 %all-to-all-start.1 = ((bf16[16,176,128]{2,1,0:T(8,128)(2,1)}), bf16[16,176,128]{2,1,0:T(8,128)(2,1)}, u32[]{:S(2)}, u32[]{:S(2)}) async-start(bf16[16,176,128]{2,1,0:T(8,128)(2,1)} %copy.136), calls=%async_computation.1 | async-start | bytes 1441792 | tf_op jit(solution)/shard_map/all_to_all | solution.py:208
  23.6 1.4 constant_dynamic-slice_fusion.10
  25.0 1.6 pad_maximum_fusion
  26.6 1.5 gather_fusion.1
  29.6 3.6 %collective-permute-start.5 = (bf16[64,128]{1,0:T(8,128)(2,1)S(1)}, bf16[64,128]{1,0:T(8,128)(2,1)S(1)}, u32[]{:S(2)}, u32[]{:S(2)}) collective-permute-start(bf16[64,128]{1,0:T(8,128)(2,1)S(1)} %convolution_convert_fusion.6), channel_id=1, source_target_pairs={{0,3},{1,0},{2,1},{3,2},{4,7},{5,4},{6,5},{7,6},{8,11},{9,8},{10,9... | collective-permute-start | bytes 49160 | tf_op jit(solution)/shard_map/ppermute | solution.py:162
  34.2 2.1 %convolution_convert_fusion.5 = bf16[64,512]{1,0:T(8,128)(2,1)S(1)} fusion(bf16[64,2048]{1,0:T(8,128)(2,1)S(1)} %bitcast.205, bf16[2048,512]{1,0:T(8,128)(2,1)} %param.28), kind=kOutput, calls=%fused_computation.40 | convolution fusion | flops 134250496 | bytes 2424832 | tf_op jit(solution)/shard_map/dot_general | solution.py:82
  36.4 7.0 %collective-permute-done.4 = bf16[64,128]{1,0:T(8,128)(2,1)S(1)} collective-permute-done((bf16[64,128]{1,0:T(8,128)(2,1)S(1)}, bf16[64,128]{1,0:T(8,128)(2,1)S(1)}, u32[]{:S(2)}, u32[]{:S(2)}) %collective-permute-start.4) | collective-permute-done | bytes 16416 | tf_op jit(solution)/shard_map/ppermute | solution.py:162
  44.8 1.5 fusion.110
  47.3 2.1 %fusion.67 = f32[64,2048]{1,0:T(8,128)S(1)} fusion(bf16[512,2048]{1,0:T(8,128)(2,1)} %param.30, bf16[8,8,4,128]{3,2,1,0:T(4,128)(2,1)S(1)} %bitcast.212), kind=kOutput, calls=%fused_computation.102 | convolution fusion | flops 134217728 | bytes 2686976 | tf_op jit(solution)/shard_map/dot_general | solution.py:244
  51.4 3.4 %collective-permute-start.8 = (f32[16,2048]{1,0:T(8,128)}, f32[16,2048]{1,0:T(8,128)}, u32[]{:S(2)}, u32[]{:S(2)}) collective-permute-start(f32[16,2048]{1,0:T(8,128)} %get-tuple-element.15), channel_id=1, source_target_pairs={{0,3},{1,0},{2,1},{3,2},{4,7},{5,4},{6,5},{7,6},{8,11},{9,8},{10,9... | collective-permute-start | bytes 393224 | tf_op jit(solution)/shard_map/ppermute | solution.py:199
  55.2 4.2 %collective-permute-done.6 = f32[16,2048]{1,0:T(8,128)S(1)} collective-permute-done((f32[16,2048]{1,0:T(8,128)}, f32[16,2048]{1,0:T(8,128)S(1)}, u32[]{:S(2)}, u32[]{:S(2)}) %collective-permute-start.6) | collective-permute-done | bytes 131104 | tf_op jit(solution)/shard_map/ppermute | solution.py:199
  60.1 5.2 %collective-permute-done.7 = f32[16,2048]{1,0:T(8,128)} collective-permute-done((f32[16,2048]{1,0:T(8,128)}, f32[16,2048]{1,0:T(8,128)}, u32[]{:S(2)}, u32[]{:S(2)}) %collective-permute-start.7) | collective-permute-done | bytes 131104 | tf_op jit(solution)/shard_map/ppermute | solution.py:199
  68.0 4.3 %all-to-all-start = ((bf16[16,176,128]{2,1,0:T(8,128)(2,1)}), bf16[16,176,128]{2,1,0:T(8,128)(2,1)}, u32[]{:S(2)}, u32[]{:S(2)}) async-start(bf16[16,176,128]{2,1,0:T(8,128)(2,1)} %copy.131), calls=%async_computation | async-start | bytes 1441792 | tf_op jit(solution)/shard_map/all_to_all | solution.py:208
  72.3 2.9 %copy.173 = bf16[96,8,16,128]{3,2,1,0:T(8,128)(2,1)S(1)} copy(bf16[96,8,16,128]{3,1,2,0:T(8,128)(2,1)} %bitcast.196) | data formatting | bytes 6291456
  75.2 1.8 copy.137
  77.0 2.0 fusion.15
  79.0 13.1 %all-to-all-done = bf16[16,176,128]{2,1,0:T(8,128)(2,1)} async-done(((bf16[16,176,128]{2,1,0:T(8,128)(2,1)}), bf16[16,176,128]{2,1,0:T(8,128)(2,1)}, u32[]{:S(2)}, u32[]{:S(2)}) %all-to-all-start) | async-done | bytes 720928 | tf_op jit(solution)/shard_map/all_to_all | solution.py:208
  94.2 1.3 copy-done.1
  100.5 4.4 %all-to-all-start.2 = ((bf16[16,176,128]{2,1,0:T(8,128)(2,1)}), bf16[16,176,128]{2,1,0:T(8,128)(2,1)}, u32[]{:S(2)}, u32[]{:S(2)}) async-start(bf16[16,176,128]{2,1,0:T(8,128)(2,1)} %copy.139), calls=%async_computation.2 | async-start | bytes 1441792 | tf_op jit(solution)/shard_map/all_to_all | solution.py:212
  105.0 19.9 %all-to-all-done.2 = bf16[16,176,128]{2,1,0:T(8,128)(2,1)} async-done(((bf16[16,176,128]{2,1,0:T(8,128)(2,1)}), bf16[16,176,128]{2,1,0:T(8,128)(2,1)}, u32[]{:S(2)}, u32[]{:S(2)}) %all-to-all-start.2) | async-done | bytes 720928 | tf_op jit(solution)/shard_map/all_to_all | solution.py:212
  124.9 2.1 %copy.231 = bf16[16,11,16,128]{3,2,0,1:T(8,128)(2,1)} copy(bf16[16,11,16,128]{3,2,1,0:T(8,128)(2,1)} %bitcast.48) | data formatting | bytes 1441792 | tf_op jit(solution)/shard_map/reshape | solution.py:306
  127.0 2.1 %dot_general.88 = bf16[2048,11,16]{0,2,1:T(8,128)(2,1)} reshape(bf16[16,128,11,16]{1,0,3,2:T(8,128)(2,1)} %bitcast.200) | data formatting | bytes 1441792 | tf_op jit(solution)/shard_map/dct,dckl->tkl/dot_general | solution.py:307
  129.1 1.7 fusion.46
  133.1 3.9 %fusion.11 = bf16[16,11,16,128]{3,0,2,1:T(8,128)(2,1)} fusion(bf16[768,16,128]{2,1,0:T(8,128)(2,1)} %bitcast.198, f32[16,11,768]{2,0,1:T(8,128)} %copy-done.6, f32[16,11,768]{2,0,1:T(8,128)} %copy-done.2), kind=kOutput, calls=%fused_computation.18 | convolution fusion | flops 554819584 | bytes 4947968 | tf_op jit(solution)/shard_map/scf,fkl->sckl/dot_general | solution.py:291
  137.1 1.4 collective-permute-done.9
  140.1 2.3 %gather_fusion.2 = bf16[4,16,2048]{2,1,0:T(8,128)(2,1)} fusion(bf16[4,16,2048]{2,1,0:T(8,128)(2,1)} %pad_maximum_fusion.1, s32[1024]{0:T(1024)} %copy-done.25), kind=kCustom, calls=%fused_computation.1.clone | custom fusion | bytes 524304 | tf_op jit(solution)/shard_map/jit(_take)/gather | solution.py:172
  143.5 2.4 %convolution_convert_fusion.3 = bf16[64,512]{1,0:T(8,128)(2,1)S(1)} fusion(bf16[64,2048]{1,0:T(8,128)(2,1)S(1)} %bitcast.206, bf16[512,2048]{1,0:T(8,128)(2,1)} %param.30), kind=kOutput, calls=%fused_computation.38 | convolution fusion | flops 134250496 | bytes 2424832 | tf_op jit(solution)/shard_map/td,fd->tf/dot_general | solution.py:130
  145.9 1.6 convolution_bitcast_fusion.4
  147.5 2.9 %fusion.27 = bf16[4,16,4,128]{3,1,2,0:T(8,128)(2,1)} fusion(f32[4,4,16,48]{3,2,1,0:T(8,128)} %convolution_bitcast_fusion.4, bf16[4,16,128]{2,1,0:T(8,128)(2,1)} %bitcast.224, bf16[4,32,128]{2,1,0:T(8,128)(2,1)} %get-tuple-element.26, f32[4,4,16,48]{3,2,1,0:T(8,128)} %copy-done.32, f32[4,4,16]{2,1,0:T(4,128)} %get-tuple-element.22), kind=kOutput, calls=%fused_computation.42 | convolution fusion | flops 3363119 | bytes 214016 | tf_op jit(solution)/shard_map/shbk,skd->sbhd/dot_general | solution.py:55
  150.4 3.0 %convolution_bitcast_fusion.6 = f32[4,48,128]{2,1,0:T(8,128)} fusion(f32[4,4,16,48]{3,2,1,0:T(8,128)} %convolution_bitcast_fusion.4, bf16[4,16,4,128]{3,2,1,0:T(4,128)(2,1)} %copy-done.15, f32[4,4,16,48]{3,2,1,0:T(8,128)} %copy-done.32, f32[4,4,16]{2,1,0:T(4,128)} %get-tuple-element.22), kind=kOutput, calls=%fused_computation.37 | convolution fusion | flops 3232047 | bytes 263168 | tf_op jit(solution)/shard_map/shbk,sbhd->skd/dot_general | solution.py:58
  153.4 1.8 convolution_bitcast_fusion.5
  155.2 2.2 %copy.143 = bf16[16,176,128]{2,1,0:T(8,128)(2,1)} copy(bf16[16,176,128]{2,0,1:T(8,128)(2,1)} %bitcast.208) | data formatting | bytes 1441792 | tf_op jit(solution)/shard_map/reshape | solution.py:319
  157.4 4.3 %all-to-all-start.3 = ((bf16[16,176,128]{2,1,0:T(8,128)(2,1)}), bf16[16,176,128]{2,1,0:T(8,128)(2,1)}, u32[]{:S(2)}, u32[]{:S(2)}) async-start(bf16[16,176,128]{2,1,0:T(8,128)(2,1)} %copy.143), calls=%async_computation.3 | async-start | bytes 1441792 | tf_op jit(solution)/shard_map/all_to_all | solution.py:212
  162.8 1.8 collective-permute-start.12
  164.6 2.1 %collective-permute-start.14 = (f32[64,128]{1,0:T(8,128)S(1)}, f32[64,128]{1,0:T(8,128)S(1)}, u32[]{:S(2)}, u32[]{:S(2)}) collective-permute-start(f32[64,128]{1,0:T(8,128)S(1)} %get-tuple-element.18), channel_id=1, source_target_pairs={{0,3},{1,0},{2,1},{3,2},{4,7},{5,4},{6,5},{7,6},{8,11},{9,8},{10,9... | collective-permute-start | bytes 98312 | tf_op jit(solution)/shard_map/ppermute | solution.py:199
  167.6 2.3 %fusion.64 = f32[64,2048]{1,0:T(8,128)S(1)} fusion(bf16[2048,512]{1,0:T(8,128)(2,1)} %param.28, bf16[8,8,4,128]{3,2,1,0:T(4,128)(2,1)S(1)} %bitcast.211), kind=kOutput, calls=%fused_computation.99 | convolution fusion | flops 134217728 | bytes 2686976 | tf_op jit(solution)/shard_map/tf,df->td/dot_general | solution.py:153
  169.9 9.4 %collective-permute-done.12 = f32[64,128]{1,0:T(8,128)S(1)} collective-permute-done((f32[64,128]{1,0:T(8,128)S(1)}, f32[64,128]{1,0:T(8,128)S(1)}, u32[]{:S(2)}, u32[]{:S(2)}) %collective-permute-start.12) | collective-permute-done | bytes 32800 | tf_op jit(solution)/shard_map/ppermute | solution.py:199
  179.3 4.6 %collective-permute-done.13 = f32[64,128]{1,0:T(8,128)S(1)} collective-permute-done((f32[64,128]{1,0:T(8,128)S(1)}, f32[64,128]{1,0:T(8,128)S(1)}, u32[]{:S(2)}, u32[]{:S(2)}) %collective-permute-start.13) | collective-permute-done | bytes 32800 | tf_op jit(solution)/shard_map/ppermute | solution.py:199
  184.9 3.6 %collective-permute-start.17 = (f32[16,2048]{1,0:T(8,128)S(1)}, f32[16,2048]{1,0:T(8,128)S(1)}, u32[]{:S(2)}, u32[]{:S(2)}) collective-permute-start(f32[16,2048]{1,0:T(8,128)S(1)} %get-tuple-element.12), channel_id=1, source_target_pairs={{0,3},{1,0},{2,1},{3,2},{4,7},{5,4},{6,5},{7,6},{8,11},{9,8},{10,9... | collective-permute-start | bytes 393224 | tf_op jit(solution)/shard_map/ppermute | solution.py:199
  188.5 4.4 %collective-permute-done.15 = f32[16,2048]{1,0:T(8,128)S(1)} collective-permute-done((f32[16,2048]{1,0:T(8,128)S(1)}, f32[16,2048]{1,0:T(8,128)S(1)}, u32[]{:S(2)}, u32[]{:S(2)}) %collective-permute-start.15) | collective-permute-done | bytes 131104 | tf_op jit(solution)/shard_map/ppermute | solution.py:199
  193.1 5.3 %collective-permute-done.16 = f32[16,2048]{1,0:T(8,128)S(1)} collective-permute-done((f32[16,2048]{1,0:T(8,128)S(1)}, f32[16,2048]{1,0:T(8,128)S(1)}, u32[]{:S(2)}, u32[]{:S(2)}) %collective-permute-start.16) | collective-permute-done | bytes 131104 | tf_op jit(solution)/shard_map/ppermute | solution.py:199
  199.4 2.2 %copy.230 = bf16[16,11,16,128]{3,2,0,1:T(8,128)(2,1)} copy(bf16[16,11,16,128]{3,2,1,0:T(8,128)(2,1)} %bitcast.52) | data formatting | bytes 1441792 | tf_op jit(solution)/shard_map/reshape | solution.py:319
  201.5 2.1 %dot_general.91 = bf16[2048,11,16]{0,2,1:T(8,128)(2,1)} reshape(bf16[16,128,11,16]{1,0,3,2:T(8,128)(2,1)} %bitcast.201) | data formatting | bytes 1441792 | tf_op jit(solution)/shard_map/dct,dckl->tkl/dot_general | solution.py:333
  203.7 2.6 %fusion.10 = bf16[16,2048]{1,0:T(8,128)(2,1)} fusion(f32[16,11,16]{2,1,0:T(8,128)S(1)} %copy-done.10, bf16[2048,11,16]{0,2,1:T(8,128)(2,1)} %dot_general.91, bf16[16,2048]{1,0:T(8,128)(2,1)S(1)} %get-tuple-element.10), kind=kOutput, calls=%fused_computation.16 | convolution fusion | flops 69304320 | bytes 863232 | tf_op jit(solution)/shard_map/dct,dckl->tkl/dot_general | solution.py:333
  (150 shorter events, 34.9 us)
Async XLA Ops:
  0.6 92.8 %copy-start = (bf16[1,2048,768]{2,1,0:T(8,128)(2,1)S(1)}, bf16[1,2048,768]{2,1,0:T(8,128)(2,1)}, u32[]{:S(2)}) copy-start(bf16[1,2048,768]{2,1,0:T(8,128)(2,1)} %param.31) | copy-start | bytes 9437188
  0.6 22.1 %copy-start.4 = (bf16[16,2048]{1,0:T(8,128)(2,1)S(1)}, bf16[16,2048]{1,0:T(8,128)(2,1)}, u32[]{:S(2)}) copy-start(bf16[16,2048]{1,0:T(8,128)(2,1)} %param.18) | copy-start | bytes 196612
  0.7 22.1 %copy-start.14 = (f32[2048]{0:T(1024)S(1)}, f32[2048]{0:T(1024)}, u32[]{:S(2)}) copy-start(f32[2048]{0:T(1024)} %param.26) | copy-start | bytes 24580
  0.7 22.2 %copy-start.31 = (s32[4]{0:T(128)S(1)}, s32[4]{0:T(128)}, u32[]{:S(2)}) copy-start(s32[4]{0:T(128)} %param.23) | copy-start | bytes 52
  1.8 26.4 %copy-start.21 = (f32[16]{0:T(128)}, f32[16]{0:T(128)S(1)}, u32[]{:S(2)}) copy-start(f32[16]{0:T(128)S(1)} %add_rsqrt_fusion.1) | copy-start | bytes 196
  2.7 22.2 %collective-permute-start.1 = (bf16[16,2048]{1,0:T(8,128)(2,1)S(1)}, bf16[16,2048]{1,0:T(8,128)(2,1)S(1)}, u32[]{:S(2)}, u32[]{:S(2)}) collective-permute-start(bf16[16,2048]{1,0:T(8,128)(2,1)S(1)} %fusion.50), channel_id=1, source_target_pairs={{0,2},{1,3},{2,0},{3,1},{4,6},{5,7},{6,4},{7,5},{8,10},{9,11},{10,... | collective-permute-start | bytes 196616 | tf_op jit(solution)/shard_map/ppermute | solution.py:162
  6.8 18.1 %collective-permute-start = (bf16[16,2048]{1,0:T(8,128)(2,1)S(1)}, bf16[16,2048]{1,0:T(8,128)(2,1)}, u32[]{:S(2)}, u32[]{:S(2)}) collective-permute-start(bf16[16,2048]{1,0:T(8,128)(2,1)S(1)} %fusion.50), channel_id=1, source_target_pairs={{0,1},{1,2},{2,3},{3,0},{4,5},{5,6},{6,7},{7,4},{8,9},{9,10},{10,1... | collective-permute-start | bytes 196616 | tf_op jit(solution)/shard_map/ppermute | solution.py:162
  8.4 16.6 %collective-permute-start.2 = (bf16[16,2048]{1,0:T(8,128)(2,1)S(1)}, bf16[16,2048]{1,0:T(8,128)(2,1)}, u32[]{:S(2)}, u32[]{:S(2)}) collective-permute-start(bf16[16,2048]{1,0:T(8,128)(2,1)S(1)} %fusion.50), channel_id=1, source_target_pairs={{0,3},{1,0},{2,1},{3,2},{4,7},{5,4},{6,5},{7,6},{8,11},{9,8},{10,9... | collective-permute-start | bytes 196616 | tf_op jit(solution)/shard_map/ppermute | solution.py:162
  11.3 11.5 %copy-start.26 = (f32[16]{0:T(128)}, f32[16]{0:T(128)S(1)}, u32[]{:S(2)}) copy-start(f32[16]{0:T(128)S(1)} %convert_element_type.115) | copy-start | bytes 196
  12.5 11.1 %copy-start.19 = (bf16[4,32,256]{2,1,0:T(8,128)(2,1)S(1)}, bf16[4,32,256]{2,1,0:T(8,128)(2,1)}, u32[]{:S(2)}) copy-start(bf16[4,32,256]{2,1,0:T(8,128)(2,1)} %param.24) | copy-start | bytes 196612
  18.4 49.6 %all-to-all-start.1 = ((bf16[16,176,128]{2,1,0:T(8,128)(2,1)}), bf16[16,176,128]{2,1,0:T(8,128)(2,1)}, u32[]{:S(2)}, u32[]{:S(2)}) async-start(bf16[16,176,128]{2,1,0:T(8,128)(2,1)} %copy.136), calls=%async_computation.1 | async-start | bytes 1441792 | tf_op jit(solution)/shard_map/all_to_all | solution.py:208
  23.0 5.3 %copy-start.25 = (s32[1024]{0:T(1024)}, s32[1024]{0:T(1024)S(1)}, u32[]{:S(2)}) copy-start(s32[1024]{0:T(1024)S(1)} %pad_clamp_fusion.1) | copy-start | bytes 12292
  24.9 22.3 %copy-start.13 = (bf16[4,32,128]{2,1,0:T(8,128)(2,1)}, bf16[4,32,128]{2,1,0:T(8,128)(2,1)S(1)}, u32[]{:S(2)}) copy-start(bf16[4,32,128]{2,1,0:T(8,128)(2,1)S(1)} %get-tuple-element.27) | copy-start | bytes 98308
  28.3 16.5 %copy-start.18 = (bf16[4,32,128]{2,1,0:T(8,128)(2,1)S(1)}, bf16[4,32,128]{2,1,0:T(8,128)(2,1)}, u32[]{:S(2)}) copy-start(bf16[4,32,128]{2,1,0:T(8,128)(2,1)} %get-tuple-element.26) | copy-start | bytes 98308
  29.6 6.8 %collective-permute-start.5 = (bf16[64,128]{1,0:T(8,128)(2,1)S(1)}, bf16[64,128]{1,0:T(8,128)(2,1)S(1)}, u32[]{:S(2)}, u32[]{:S(2)}) collective-permute-start(bf16[64,128]{1,0:T(8,128)(2,1)S(1)} %convolution_convert_fusion.6), channel_id=1, source_target_pairs={{0,3},{1,0},{2,1},{3,2},{4,7},{5,4},{6,5},{7,6},{8,11},{9,8},{10,9... | collective-permute-start | bytes 49160 | tf_op jit(solution)/shard_map/ppermute | solution.py:162
  33.1 10.3 %collective-permute-start.4 = (bf16[64,128]{1,0:T(8,128)(2,1)S(1)}, bf16[64,128]{1,0:T(8,128)(2,1)S(1)}, u32[]{:S(2)}, u32[]{:S(2)}) collective-permute-start(bf16[64,128]{1,0:T(8,128)(2,1)S(1)} %convolution_convert_fusion.6), channel_id=1, source_target_pairs={{0,2},{1,3},{2,0},{3,1},{4,6},{5,7},{6,4},{7,5},{8,10},{9,11},{10,... | collective-permute-start | bytes 49160 | tf_op jit(solution)/shard_map/ppermute | solution.py:162
  33.1 10.3 %collective-permute-start.3 = (bf16[64,128]{1,0:T(8,128)(2,1)S(1)}, bf16[64,128]{1,0:T(8,128)(2,1)S(1)}, u32[]{:S(2)}, u32[]{:S(2)}) collective-permute-start(bf16[64,128]{1,0:T(8,128)(2,1)S(1)} %convolution_convert_fusion.6), channel_id=1, source_target_pairs={{0,1},{1,2},{2,3},{3,0},{4,5},{5,6},{6,7},{7,4},{8,9},{9,10},{10,1... | collective-permute-start | bytes 49160 | tf_op jit(solution)/shard_map/ppermute | solution.py:162
  36.3 30.2 %copy-start.17 = (f32[2048]{0:T(1024)S(1)}, f32[2048]{0:T(1024)}, u32[]{:S(2)}) copy-start(f32[2048]{0:T(1024)} %param.27) | copy-start | bytes 24580
  36.4 14.7 %copy-start.15 = (bf16[4,16,4,128]{3,2,1,0:T(4,128)(2,1)}, bf16[4,16,4,128]{3,2,1,0:T(4,128)(2,1)S(1)}, u32[]{:S(2)}) copy-start(bf16[4,16,4,128]{3,2,1,0:T(4,128)(2,1)S(1)} %reshape.192) | copy-start | bytes 196612
  44.8 23.2 %copy-start.16 = (bf16[64,128]{1,0:T(8,128)(2,1)}, bf16[64,128]{1,0:T(8,128)(2,1)S(1)}, u32[]{:S(2)}) copy-start(bf16[64,128]{1,0:T(8,128)(2,1)S(1)} %get-tuple-element.21) | copy-start | bytes 49156
  46.3 4.7 %copy-start.32 = (f32[4,4,16,48]{3,2,1,0:T(8,128)}, f32[4,4,16,48]{3,2,1,0:T(8,128)S(1)}, u32[]{:S(2)}) copy-start(f32[4,4,16,48]{3,2,1,0:T(8,128)S(1)} %get-tuple-element.23) | copy-start | bytes 147460
  51.0 8.4 %collective-permute-start.6 = (f32[16,2048]{1,0:T(8,128)}, f32[16,2048]{1,0:T(8,128)S(1)}, u32[]{:S(2)}, u32[]{:S(2)}) collective-permute-start(f32[16,2048]{1,0:T(8,128)} %get-tuple-element.14), channel_id=1, source_target_pairs={{0,1},{1,2},{2,3},{3,0},{4,5},{5,6},{6,7},{7,4},{8,9},{9,10},{10,1... | collective-permute-start | bytes 393224 | tf_op jit(solution)/shard_map/ppermute | solution.py:199
  51.4 8.7 %collective-permute-start.8 = (f32[16,2048]{1,0:T(8,128)}, f32[16,2048]{1,0:T(8,128)}, u32[]{:S(2)}, u32[]{:S(2)}) collective-permute-start(f32[16,2048]{1,0:T(8,128)} %get-tuple-element.15), channel_id=1, source_target_pairs={{0,3},{1,0},{2,1},{3,2},{4,7},{5,4},{6,5},{7,6},{8,11},{9,8},{10,9... | collective-permute-start | bytes 393224 | tf_op jit(solution)/shard_map/ppermute | solution.py:199
  54.8 10.5 %collective-permute-start.7 = (f32[16,2048]{1,0:T(8,128)}, f32[16,2048]{1,0:T(8,128)}, u32[]{:S(2)}, u32[]{:S(2)}) collective-permute-start(f32[16,2048]{1,0:T(8,128)} %get-tuple-element.16), channel_id=1, source_target_pairs={{0,2},{1,3},{2,0},{3,1},{4,6},{5,7},{6,4},{7,5},{8,10},{9,11},{10,... | collective-permute-start | bytes 393224 | tf_op jit(solution)/shard_map/ppermute | solution.py:199
  66.5 64.4 %copy-start.23 = (f32[16]{0:T(128)}, f32[16]{0:T(128)S(1)}, u32[]{:S(2)}) copy-start(f32[16]{0:T(128)S(1)} %add_rsqrt_fusion) | copy-start | bytes 196
  68.0 24.2 %all-to-all-start = ((bf16[16,176,128]{2,1,0:T(8,128)(2,1)}), bf16[16,176,128]{2,1,0:T(8,128)(2,1)}, u32[]{:S(2)}, u32[]{:S(2)}) async-start(bf16[16,176,128]{2,1,0:T(8,128)(2,1)} %copy.131), calls=%async_computation | async-start | bytes 1441792 | tf_op jit(solution)/shard_map/all_to_all | solution.py:208
  100.5 30.4 %copy-start.11 = (bf16[16,2048]{1,0:T(8,128)(2,1)S(1)}, bf16[16,2048]{1,0:T(8,128)(2,1)}, u32[]{:S(2)}) copy-start(bf16[16,2048]{1,0:T(8,128)(2,1)} %param.19) | copy-start | bytes 196612
  100.5 30.4 %copy-start.27 = (f32[16]{0:T(128)S(1)}, f32[16]{0:T(128)}, u32[]{:S(2)}) copy-start(f32[16]{0:T(128)} %copy-done.26) | copy-start | bytes 196
  100.5 24.3 %all-to-all-start.2 = ((bf16[16,176,128]{2,1,0:T(8,128)(2,1)}), bf16[16,176,128]{2,1,0:T(8,128)(2,1)}, u32[]{:S(2)}, u32[]{:S(2)}) async-start(bf16[16,176,128]{2,1,0:T(8,128)(2,1)} %copy.139), calls=%async_computation.2 | async-start | bytes 1441792 | tf_op jit(solution)/shard_map/all_to_all | solution.py:212
  131.0 11.4 %copy-start.30 = (pred[4]{0:T(512)(128)(4,1)S(1)}, pred[4]{0:T(512)(128)(4,1)}, u32[]{:S(2)}) copy-start(pred[4]{0:T(512)(128)(4,1)} %copy-done.29) | copy-start | bytes 16
  131.0 7.4 %collective-permute-start.11 = (bf16[16,2048]{1,0:T(8,128)(2,1)S(1)}, bf16[16,2048]{1,0:T(8,128)(2,1)S(1)}, u32[]{:S(2)}, u32[]{:S(2)}) collective-permute-start(bf16[16,2048]{1,0:T(8,128)(2,1)S(1)} %fusion.108), channel_id=1, source_target_pairs={{0,3},{1,0},{2,1},{3,2},{4,7},{5,4},{6,5},{7,6},{8,11},{9,8},{10,9... | collective-permute-start | bytes 196616 | tf_op jit(solution)/shard_map/ppermute | solution.py:315
  131.9 7.5 %collective-permute-start.10 = (bf16[16,2048]{1,0:T(8,128)(2,1)S(1)}, bf16[16,2048]{1,0:T(8,128)(2,1)S(1)}, u32[]{:S(2)}, u32[]{:S(2)}) collective-permute-start(bf16[16,2048]{1,0:T(8,128)(2,1)S(1)} %fusion.108), channel_id=1, source_target_pairs={{0,2},{1,3},{2,0},{3,1},{4,6},{5,7},{6,4},{7,5},{8,10},{9,11},{10,... | collective-permute-start | bytes 196616 | tf_op jit(solution)/shard_map/ppermute | solution.py:315
  132.1 6.3 %collective-permute-start.9 = (bf16[16,2048]{1,0:T(8,128)(2,1)S(1)}, bf16[16,2048]{1,0:T(8,128)(2,1)S(1)}, u32[]{:S(2)}, u32[]{:S(2)}) collective-permute-start(bf16[16,2048]{1,0:T(8,128)(2,1)S(1)} %fusion.108), channel_id=1, source_target_pairs={{0,1},{1,2},{2,3},{3,0},{4,5},{5,6},{6,7},{7,4},{8,9},{9,10},{10,1... | collective-permute-start | bytes 196616 | tf_op jit(solution)/shard_map/ppermute | solution.py:185
  153.4 9.3 %slice-start.1 = ((f32[4,48,128]{2,1,0:T(8,128)}), f32[4,16,128]{2,1,0:T(8,128)S(1)}, s32[]{:S(2)}) async-start(f32[4,48,128]{2,1,0:T(8,128)} %convolution_bitcast_fusion.6), calls=%async_computation.5 | async-start | bytes 65536 | tf_op jit(solution)/shard_map/slice | solution.py:140
  155.2 7.5 %slice-start = ((f32[4,48,128]{2,1,0:T(8,128)}), f32[4,16,128]{2,1,0:T(8,128)S(1)}, s32[]{:S(2)}) async-start(f32[4,48,128]{2,1,0:T(8,128)} %convolution_bitcast_fusion.5), calls=%async_computation.4 | async-start | bytes 65536 | tf_op jit(solution)/shard_map/slice | solution.py:144
  157.4 41.9 %all-to-all-start.3 = ((bf16[16,176,128]{2,1,0:T(8,128)(2,1)}), bf16[16,176,128]{2,1,0:T(8,128)(2,1)}, u32[]{:S(2)}, u32[]{:S(2)}) async-start(bf16[16,176,128]{2,1,0:T(8,128)(2,1)} %copy.143), calls=%async_computation.3 | async-start | bytes 1441792 | tf_op jit(solution)/shard_map/all_to_all | solution.py:212
  161.7 22.2 %copy-start.7 = (bf16[2048,128]{1,0:T(8,128)(2,1)S(1)}, bf16[2048,128]{1,0:T(8,128)(2,1)}, u32[]{:S(2)}) copy-start(bf16[2048,128]{1,0:T(8,128)(2,1)} %param.29) | copy-start | bytes 1572868
  161.7 36.6 %copy-start.22 = (f32[16]{0:T(128)S(1)}, f32[16]{0:T(128)}, u32[]{:S(2)}) copy-start(f32[16]{0:T(128)} %copy-done.21) | copy-start | bytes 196
  162.7 35.9 %copy-start.12 = (bf16[16,2048]{1,0:T(8,128)(2,1)S(1)}, bf16[16,2048]{1,0:T(8,128)(2,1)}, u32[]{:S(2)}) copy-start(bf16[16,2048]{1,0:T(8,128)(2,1)} %param.19) | copy-start | bytes 196612
  162.7 35.9 %copy-start.24 = (f32[16]{0:T(128)S(1)}, f32[16]{0:T(128)}, u32[]{:S(2)}) copy-start(f32[16]{0:T(128)} %copy-done.23) | copy-start | bytes 196
  162.7 35.9 %copy-start.28 = (f32[16]{0:T(128)S(1)}, f32[16]{0:T(128)}, u32[]{:S(2)}) copy-start(f32[16]{0:T(128)} %copy-done.26) | copy-start | bytes 196
  162.8 16.5 %collective-permute-start.12 = (f32[64,128]{1,0:T(8,128)S(1)}, f32[64,128]{1,0:T(8,128)S(1)}, u32[]{:S(2)}, u32[]{:S(2)}) collective-permute-start(f32[64,128]{1,0:T(8,128)S(1)} %get-tuple-element.17), channel_id=1, source_target_pairs={{0,1},{1,2},{2,3},{3,0},{4,5},{5,6},{6,7},{7,4},{8,9},{9,10},{10,1... | collective-permute-start | bytes 98312 | tf_op jit(solution)/shard_map/ppermute | solution.py:199
  164.6 14.7 %collective-permute-start.14 = (f32[64,128]{1,0:T(8,128)S(1)}, f32[64,128]{1,0:T(8,128)S(1)}, u32[]{:S(2)}, u32[]{:S(2)}) collective-permute-start(f32[64,128]{1,0:T(8,128)S(1)} %get-tuple-element.18), channel_id=1, source_target_pairs={{0,3},{1,0},{2,1},{3,2},{4,7},{5,4},{6,5},{7,6},{8,11},{9,8},{10,9... | collective-permute-start | bytes 98312 | tf_op jit(solution)/shard_map/ppermute | solution.py:199
  166.7 17.2 %collective-permute-start.13 = (f32[64,128]{1,0:T(8,128)S(1)}, f32[64,128]{1,0:T(8,128)S(1)}, u32[]{:S(2)}, u32[]{:S(2)}) collective-permute-start(f32[64,128]{1,0:T(8,128)S(1)} %get-tuple-element.19), channel_id=1, source_target_pairs={{0,2},{1,3},{2,0},{3,1},{4,6},{5,7},{6,4},{7,5},{8,10},{9,11},{10,... | collective-permute-start | bytes 98312 | tf_op jit(solution)/shard_map/ppermute | solution.py:199
  169.9 33.8 %copy-start.10 = (f32[16,11,16]{2,1,0:T(8,128)S(1)}, f32[16,11,16]{2,1,0:T(8,128)}, u32[]{:S(2)}) copy-start(f32[16,11,16]{2,1,0:T(8,128)} %copy-done.9) | copy-start | bytes 33796
  184.6 8.3 %collective-permute-start.15 = (f32[16,2048]{1,0:T(8,128)S(1)}, f32[16,2048]{1,0:T(8,128)S(1)}, u32[]{:S(2)}, u32[]{:S(2)}) collective-permute-start(f32[16,2048]{1,0:T(8,128)S(1)} %get-tuple-element.11), channel_id=1, source_target_pairs={{0,1},{1,2},{2,3},{3,0},{4,5},{5,6},{6,7},{7,4},{8,9},{9,10},{10,1... | collective-permute-start | bytes 393224 | tf_op jit(solution)/shard_map/ppermute | solution.py:199
  184.9 8.2 %collective-permute-start.17 = (f32[16,2048]{1,0:T(8,128)S(1)}, f32[16,2048]{1,0:T(8,128)S(1)}, u32[]{:S(2)}, u32[]{:S(2)}) collective-permute-start(f32[16,2048]{1,0:T(8,128)S(1)} %get-tuple-element.12), channel_id=1, source_target_pairs={{0,3},{1,0},{2,1},{3,2},{4,7},{5,4},{6,5},{7,6},{8,11},{9,8},{10,9... | collective-permute-start | bytes 393224 | tf_op jit(solution)/shard_map/ppermute | solution.py:199
  188.5 9.9 %collective-permute-start.16 = (f32[16,2048]{1,0:T(8,128)S(1)}, f32[16,2048]{1,0:T(8,128)S(1)}, u32[]{:S(2)}, u32[]{:S(2)}) collective-permute-start(f32[16,2048]{1,0:T(8,128)S(1)} %get-tuple-element.13), channel_id=1, source_target_pairs={{0,2},{1,3},{2,0},{3,1},{4,6},{5,7},{6,4},{7,5},{8,10},{9,11},{10,... | collective-permute-start | bytes 393224 | tf_op jit(solution)/shard_map/ppermute | solution.py:199
  (9 other events, 16.7 us)

commit v15 on v14

--- a/solution.py
+++ b/solution.py
@@ -122,7 +122,9 @@
     return (joined, saved)
 
 
-def attention_backward(grad_rows, query_weights, output_weights, own_kv_weights, saved, kv_now):
+def attention_backward(
+    grad_rows, query_weights, output_weights, own_kv_weights, saved, kv_now, carried
+):
     heads_here = query_weights.shape[1] // HEAD_SIZE
     row_count = grad_rows.shape[0]
     seq_count = row_count // BLOCK
@@ -145,14 +147,16 @@
         key_value_width + kv_now * HEAD_SIZE,
         1,
     )
+    placed, carried = lax.optimization_barrier((placed, carried))
     own_grads = head_sums(placed, axis=1)
     running = jnp.einsum(
         "tc,dc->td", own_grads, own_kv_weights.astype(jnp.float32), precision=lax.Precision.HIGHEST
     )
     query_flat = grad_queries.reshape(row_count, heads_here * HEAD_SIZE)
-    return running + jnp.einsum(
+    total = running + jnp.einsum(
         "tf,df->td", query_flat, query_weights, preferred_element_type=jnp.float32
     )
+    return (total, carried)
 
 
 def head_gather(block, axis):
@@ -310,23 +314,24 @@
     grad_hidden = cotangent + rms_backward(hidden, moe_gain, inverse_two, grad_moe)
     grad_low = grad_hidden.astype(jnp.bfloat16)
     count = lax.axis_size("head")
-    (result, first_hop) = after_first_hop(grad_low, result)
-    grad_parts = [grad_low, first_hop] + [
+    grad_low, result = lax.optimization_barrier((grad_low, result))
+    grad_parts = [grad_low] + [
         lax.ppermute(grad_low, "head", perm=[(j, (j + shift) % count) for j in range(count)])
-        for shift in range(2, count)
+        for shift in range(1, count)
     ]
+    result_home = from_experts(result.reshape(flat_shape)).reshape(split_shape)
+    grad_parts = list(lax.optimization_barrier(tuple(grad_parts)))
     grad_gathered = head_order(grad_parts, 0)
-    result_home = from_experts(result.reshape(flat_shape)).reshape(split_shape)
-    grad_attn_rows = head_sums(
-        attention_backward(
-            grad_gathered,
-            w_query,
-            w_output,
-            key_value_weight,
-            saved,
-            first_head // (QUERY_HEADS // KEY_VALUE_HEADS),
-        )
-    )
+    grad_partial, result_home = attention_backward(
+        grad_gathered,
+        w_query,
+        w_output,
+        key_value_weight,
+        saved,
+        first_head // (QUERY_HEADS // KEY_VALUE_HEADS),
+        result_home,
+    )
+    grad_attn_rows = head_sums(grad_partial)
     input_grad = (
         grad_hidden + rms_backward(hidden_in, attn_gain, inverse_one, grad_attn_rows)
     ).astype(jnp.bfloat16)

time: 208 us -> 193 us (0.928)
  waiting for transfers between devices: 76.4 us -> 55.1 us
  local copies, waits for them, and re-layouts: 32.9 us -> 36 us
  other arithmetic: 11.9 us -> 14 us
    ppermute x9, waiting for transfers between devices: 34 us -> 17.4 us  [head_sums(): lax.ppermute(chunk((me + shift) % count), 'head', perm=[(j, (j + shift) %...]
    all_to_all x2, waiting for transfers between devices: 19.9 us -> 17.5 us  [from_experts(): lax.all_to_all(results, ('expert', 'head'), split_axis=0, concat_axis=0,...]
    optimization_barrier x0 -> x1, local copies, waits for them, and re-layouts: none -> 2.19 us  [attention_backward(): placed, carried = lax.optimization_barrier((placed, carried))]
    reshape x2 -> x1, local copies, waits for them, and re-layouts: 4.37 us -> 2.18 us  [body(): result_home = from_experts(result.reshape(flat_shape)).reshape(split_shape)]
  transfers between devices with their start and end apart: 22 -> 22, of which waited for: 13 -> 10; matrix products, arithmetic and copies ran while one was open for 20% -> 35% of each run, Pallas kernels for 0% -> 0%
where the time goes in v15:
time: 193 us; the launch traced here: 191 us
  waiting for transfers between devices  55.1 us (29%)
  starting transfers between devices  45.6 us (24%)
  matrix products  39.2 us (20%)
  local copies, waits for them, and re-layouts  36 us (19%)
  other arithmetic  14 us (7%)
    all_to_all x2, waiting for transfers between devices, from_experts(): lax.all_to_all(results, ('expert', 'head'), split_axis=0, concat_axis=0,...  17.5 us
    ppermute x9, waiting for transfers between devices, head_sums(): lax.ppermute(chunk((me + shift) % count), 'head', perm=[(j, (j + shift) %...  17.4 us
    all_to_all x2, waiting for transfers between devices, to_experts(): lax.all_to_all(outgoing, ('expert', 'head'), split_axis=0, concat_axis=0,...  13.1 us
    ppermute x9, starting transfers between devices, head_sums(): lax.ppermute(chunk((me + shift) % count), 'head', perm=[(j, (j + shift) %...  12.7 us
    ppermute x6, starting transfers between devices, head_gather(): lax.ppermute(block, 'head', perm=[(j, (j + shift) % count) for j in range...  12.6 us
    all_to_all x2, starting transfers between devices, from_experts(): lax.all_to_all(results, ('expert', 'head'), split_axis=0, concat_axis=0,...  9.67 us
    all_to_all x2, starting transfers between devices, to_experts(): lax.all_to_all(outgoing, ('expert', 'head'), split_axis=0, concat_axis=0,...  8.56 us
    unnamed x68, local copies, waits for them, and re-layouts  7.37 us
  transfers between devices with their start and end apart: 22, of which 10 were waited for; matrix products, arithmetic and copies ran while one was open for 35% of the time, Pallas kernels for 0%

profile of v15, /device:TPU:0, one launch (start us, length us, event | category | flops | bytes accessed | tf_op | source)
XLA Modules:
  0.0 191.4 jit_solution(10554667164996656802)
XLA Ops:
  2.7 4.1 %collective-permute-start.1 = (bf16[16,2048]{1,0:T(8,128)(2,1)S(1)}, bf16[16,2048]{1,0:T(8,128)(2,1)S(1)}, u32[]{:S(2)}, u32[]{:S(2)}) collective-permute-start(bf16[16,2048]{1,0:T(8,128)(2,1)S(1)} %fusion.50), channel_id=1, source_target_pairs={{0,2},{1,3},{2,0},{3,1},{4,6},{5,7},{6,4},{7,5},{8,10},{9,11},{10,... | collective-permute-start | bytes 196616 | tf_op jit(solution)/shard_map/ppermute | solution.py:166
  6.8 1.6 collective-permute-start
  8.4 2.2 %collective-permute-start.2 = (bf16[16,2048]{1,0:T(8,128)(2,1)S(1)}, bf16[16,2048]{1,0:T(8,128)(2,1)}, u32[]{:S(2)}, u32[]{:S(2)}) collective-permute-start(bf16[16,2048]{1,0:T(8,128)(2,1)S(1)} %fusion.50), channel_id=1, source_target_pairs={{0,3},{1,0},{2,1},{3,2},{4,7},{5,4},{6,5},{7,6},{8,11},{9,8},{10,9... | collective-permute-start | bytes 196616 | tf_op jit(solution)/shard_map/ppermute | solution.py:166
  15.2 2.2 %convolution_convert_fusion = bf16[16,11,16,128]{3,0,2,1:T(8,128)(2,1)S(1)} fusion(f32[16,11,16,1]{2,1,0,3:T(8,128)S(1)} %bitcast.207, bf16[16,2048]{1,0:T(8,128)(2,1)} %param.19, f32[16]{0:T(128)S(1)} %convert_element_type.111), kind=kOutput, calls=%fused_computation.19 | convolution fusion | flops 69632000 | bytes 797760 | tf_op jit(solution)/shard_map/dct,tkl->dckl/dot_general | solution.py:276
  18.4 4.3 %all-to-all-start = ((bf16[16,176,128]{2,1,0:T(8,128)(2,1)}), bf16[16,176,128]{2,1,0:T(8,128)(2,1)}, u32[]{:S(2)}, u32[]{:S(2)}) async-start(bf16[16,176,128]{2,1,0:T(8,128)(2,1)} %copy.131), calls=%async_computation | async-start | bytes 1441792 | tf_op jit(solution)/shard_map/all_to_all | solution.py:212
  23.5 1.4 constant_dynamic-slice_fusion.10
  25.0 1.6 pad_maximum_fusion
  26.6 1.5 gather_fusion.1
  28.3 1.3 convolution_convert_fusion.6
  29.5 3.6 %collective-permute-start.5 = (bf16[64,128]{1,0:T(8,128)(2,1)S(1)}, bf16[64,128]{1,0:T(8,128)(2,1)S(1)}, u32[]{:S(2)}, u32[]{:S(2)}) collective-permute-start(bf16[64,128]{1,0:T(8,128)(2,1)S(1)} %convolution_convert_fusion.6), channel_id=1, source_target_pairs={{0,3},{1,0},{2,1},{3,2},{4,7},{5,4},{6,5},{7,6},{8,11},{9,8},{10,9... | collective-permute-start | bytes 49160 | tf_op jit(solution)/shard_map/ppermute | solution.py:166
  34.2 2.1 %convolution_convert_fusion.5 = bf16[64,512]{1,0:T(8,128)(2,1)S(1)} fusion(bf16[64,2048]{1,0:T(8,128)(2,1)S(1)} %bitcast.205, bf16[2048,512]{1,0:T(8,128)(2,1)} %param.28), kind=kOutput, calls=%fused_computation.40 | convolution fusion | flops 134250496 | bytes 2424832 | tf_op jit(solution)/shard_map/dot_general | solution.py:82
  36.4 7.1 %collective-permute-done.4 = bf16[64,128]{1,0:T(8,128)(2,1)S(1)} collective-permute-done((bf16[64,128]{1,0:T(8,128)(2,1)S(1)}, bf16[64,128]{1,0:T(8,128)(2,1)S(1)}, u32[]{:S(2)}, u32[]{:S(2)}) %collective-permute-start.4) | collective-permute-done | bytes 16416 | tf_op jit(solution)/shard_map/ppermute | solution.py:166
  44.9 1.5 fusion.110
  47.3 2.1 %fusion.67 = f32[64,2048]{1,0:T(8,128)S(1)} fusion(bf16[512,2048]{1,0:T(8,128)(2,1)} %param.30, bf16[8,8,4,128]{3,2,1,0:T(4,128)(2,1)S(1)} %bitcast.212), kind=kOutput, calls=%fused_computation.102 | convolution fusion | flops 134217728 | bytes 2686976 | tf_op jit(solution)/shard_map/dot_general | solution.py:248
  51.4 3.4 %collective-permute-start.8 = (f32[16,2048]{1,0:T(8,128)}, f32[16,2048]{1,0:T(8,128)}, u32[]{:S(2)}, u32[]{:S(2)}) collective-permute-start(f32[16,2048]{1,0:T(8,128)} %get-tuple-element.27), channel_id=1, source_target_pairs={{0,3},{1,0},{2,1},{3,2},{4,7},{5,4},{6,5},{7,6},{8,11},{9,8},{10,9... | collective-permute-start | bytes 393224 | tf_op jit(solution)/shard_map/ppermute | solution.py:203
  55.2 4.2 %collective-permute-done.6 = f32[16,2048]{1,0:T(8,128)S(1)} collective-permute-done((f32[16,2048]{1,0:T(8,128)}, f32[16,2048]{1,0:T(8,128)S(1)}, u32[]{:S(2)}, u32[]{:S(2)}) %collective-permute-start.6) | collective-permute-done | bytes 131104 | tf_op jit(solution)/shard_map/ppermute | solution.py:203
  60.1 5.2 %collective-permute-done.7 = f32[16,2048]{1,0:T(8,128)} collective-permute-done((f32[16,2048]{1,0:T(8,128)}, f32[16,2048]{1,0:T(8,128)}, u32[]{:S(2)}, u32[]{:S(2)}) %collective-permute-start.7) | collective-permute-done | bytes 131104 | tf_op jit(solution)/shard_map/ppermute | solution.py:203
  68.0 4.3 %all-to-all-start.1 = ((bf16[16,176,128]{2,1,0:T(8,128)(2,1)}), bf16[16,176,128]{2,1,0:T(8,128)(2,1)}, u32[]{:S(2)}, u32[]{:S(2)}) async-start(bf16[16,176,128]{2,1,0:T(8,128)(2,1)} %copy.136), calls=%async_computation.1 | async-start | bytes 1441792 | tf_op jit(solution)/shard_map/all_to_all | solution.py:212
  72.3 2.9 %copy.173 = bf16[96,8,16,128]{3,2,1,0:T(8,128)(2,1)S(1)} copy(bf16[96,8,16,128]{3,1,2,0:T(8,128)(2,1)} %bitcast.196) | data formatting | bytes 6291456
  75.2 1.8 copy.132
  77.0 2.0 %fusion.15 = f32[16,11,768]{2,0,1:T(8,128)} fusion(bf16[16,11,16,128]{3,0,2,1:T(8,128)(2,1)S(1)} %bitcast.209, bf16[768,16,128]{2,1,0:T(8,128)(2,1)S(1)} %bitcast.197), kind=kOutput, calls=%fused_computation.22 | convolution fusion | flops 553648128 | bytes 4407296 | tf_op jit(solution)/shard_map/sckl,fkl->scf/dot_general | solution.py:298
  79.0 13.1 %all-to-all-done.1 = bf16[16,176,128]{2,1,0:T(8,128)(2,1)} async-done(((bf16[16,176,128]{2,1,0:T(8,128)(2,1)}), bf16[16,176,128]{2,1,0:T(8,128)(2,1)}, u32[]{:S(2)}, u32[]{:S(2)}) %all-to-all-start.1) | async-done | bytes 720928 | tf_op jit(solution)/shard_map/all_to_all | solution.py:212
  92.2 1.3 copy.137
  94.2 1.3 copy-done.1
  100.5 4.5 %all-to-all-start.2 = ((bf16[16,176,128]{2,1,0:T(8,128)(2,1)}), bf16[16,176,128]{2,1,0:T(8,128)(2,1)}, u32[]{:S(2)}, u32[]{:S(2)}) async-start(bf16[16,176,128]{2,1,0:T(8,128)(2,1)} %copy.138), calls=%async_computation.2 | async-start | bytes 1441792 | tf_op jit(solution)/shard_map/all_to_all | solution.py:216
  105.0 3.9 %fusion.11 = bf16[16,11,16,128]{3,0,2,1:T(8,128)(2,1)} fusion(bf16[768,16,128]{2,1,0:T(8,128)(2,1)} %bitcast.198, f32[16,11,768]{2,0,1:T(8,128)} %copy-done.6, f32[16,11,768]{2,0,1:T(8,128)} %copy-done.2), kind=kOutput, calls=%fused_computation.18 | convolution fusion | flops 554819584 | bytes 4947968 | tf_op jit(solution)/shard_map/scf,fkl->sckl/dot_general | solution.py:295
  108.9 15.8 %all-to-all-done.2 = bf16[16,176,128]{2,1,0:T(8,128)(2,1)} async-done(((bf16[16,176,128]{2,1,0:T(8,128)(2,1)}), bf16[16,176,128]{2,1,0:T(8,128)(2,1)}, u32[]{:S(2)}, u32[]{:S(2)}) %all-to-all-start.2) | async-done | bytes 720928 | tf_op jit(solution)/shard_map/all_to_all | solution.py:216
  124.7 2.2 %copy.231 = bf16[16,11,16,128]{3,2,0,1:T(8,128)(2,1)} copy(bf16[16,11,16,128]{3,2,1,0:T(8,128)(2,1)} %bitcast.45) | data formatting | bytes 1441792 | tf_op jit(solution)/shard_map/reshape | solution.py:310
  126.9 2.2 %dot_general.87 = bf16[2048,11,16]{0,2,1:T(8,128)(2,1)} reshape(bf16[16,128,11,16]{1,0,3,2:T(8,128)(2,1)} %bitcast.200) | data formatting | bytes 1441792 | tf_op jit(solution)/shard_map/dct,dckl->tkl/dot_general | solution.py:311
  129.0 1.7 fusion.46
  133.6 2.2 %copy.146 = bf16[16,176,128]{2,1,0:T(8,128)(2,1)} copy(bf16[16,176,128]{2,0,1:T(8,128)(2,1)} %bitcast.208) | data formatting | bytes 1441792 | tf_op jit(solution)/shard_map/reshape | solution.py:322
  135.8 5.2 %all-to-all-start.3 = ((bf16[16,176,128]{2,1,0:T(8,128)(2,1)}), bf16[16,176,128]{2,1,0:T(8,128)(2,1)}, u32[]{:S(2)}, u32[]{:S(2)}) async-start(bf16[16,176,128]{2,1,0:T(8,128)(2,1)} %copy.146), calls=%async_computation.3 | async-start | bytes 1441792 | tf_op jit(solution)/shard_map/all_to_all | solution.py:216
  141.1 1.6 pad_maximum_fusion.1
  142.7 2.3 %gather_fusion.2 = bf16[4,16,2048]{2,1,0:T(8,128)(2,1)} fusion(bf16[4,16,2048]{2,1,0:T(8,128)(2,1)} %pad_maximum_fusion.1, s32[1024]{0:T(1024)} %copy-done.25), kind=kCustom, calls=%fused_computation.1.clone | custom fusion | bytes 524304 | tf_op jit(solution)/shard_map/jit(_take)/gather | solution.py:176
  146.1 2.4 %convolution_convert_fusion.3 = bf16[64,512]{1,0:T(8,128)(2,1)S(1)} fusion(bf16[64,2048]{1,0:T(8,128)(2,1)S(1)} %bitcast.206, bf16[512,2048]{1,0:T(8,128)(2,1)} %param.30), kind=kOutput, calls=%fused_computation.38 | convolution fusion | flops 134250496 | bytes 2424832 | tf_op jit(solution)/shard_map/td,fd->tf/dot_general | solution.py:132
  150.3 1.6 convolution_bitcast_fusion.4
  151.9 2.3 %convolution_bitcast_fusion.6 = f32[4,48,128]{2,1,0:T(8,128)S(1)} fusion(f32[4,4,16,48]{3,2,1,0:T(8,128)} %convolution_bitcast_fusion.4, bf16[4,16,4,128]{3,2,1,0:T(4,128)(2,1)} %copy-done.15, f32[4,4,16,48]{3,2,1,0:T(8,128)} %copy-done.31, f32[4,4,16]{2,1,0:T(4,128)S(1)} %copy-done.32), kind=kOutput, calls=%fused_computation.37 | convolution fusion | flops 3232047 | bytes 263168 | tf_op jit(solution)/shard_map/shbk,sbhd->skd/dot_general | solution.py:58
  154.8 2.2 %fusion.27 = bf16[4,16,4,128]{3,1,2,0:T(8,128)(2,1)S(1)} fusion(f32[4,4,16,48]{3,2,1,0:T(8,128)} %convolution_bitcast_fusion.4, bf16[4,16,128]{2,1,0:T(8,128)(2,1)} %bitcast.222, bf16[4,32,128]{2,1,0:T(8,128)(2,1)} %get-tuple-element.38, f32[4,4,16,48]{3,2,1,0:T(8,128)} %copy-done.31, f32[4,4,16]{2,1,0:T(4,128)S(1)} %copy-done.32), kind=kOutput, calls=%fused_computation.42 | convolution fusion | flops 3363119 | bytes 214016 | tf_op jit(solution)/shard_map/shbk,skd->sbhd/dot_general | solution.py:55
  159.3 1.7 all-to-all-done.3
  161.8 3.7 %collective-permute-start.14 = (f32[64,128]{1,0:T(8,128)}, f32[64,128]{1,0:T(8,128)}, u32[]{:S(2)}, u32[]{:S(2)}) collective-permute-start(f32[64,128]{1,0:T(8,128)} %get-tuple-element.30), channel_id=1, source_target_pairs={{0,3},{1,0},{2,1},{3,2},{4,7},{5,4},{6,5},{7,6},{8,11},{9,8},{10,9... | collective-permute-start | bytes 98312 | tf_op jit(solution)/shard_map/ppermute | solution.py:203
  165.5 3.2 %fusion.64 = f32[64,2048]{1,0:T(8,128)} fusion(bf16[2048,512]{1,0:T(8,128)(2,1)} %param.28, bf16[8,8,4,128]{3,2,1,0:T(4,128)(2,1)} %bitcast.211), kind=kOutput, calls=%fused_computation.99 | convolution fusion | flops 134217728 | bytes 2686976 | tf_op jit(solution)/shard_map/tf,df->td/dot_general | solution.py:156
  168.7 2.2 %copy.230 = bf16[16,11,16,128]{3,2,0,1:T(8,128)(2,1)} copy(bf16[16,11,16,128]{3,2,1,0:T(8,128)(2,1)} %bitcast.64) | data formatting | bytes 1441792 | tf_op jit(solution)/shard_map/optimization_barrier | solution.py:150
  170.8 2.2 %dot_general.95 = bf16[2048,11,16]{0,2,1:T(8,128)(2,1)} reshape(bf16[16,128,11,16]{1,0,3,2:T(8,128)(2,1)} %bitcast.201) | data formatting | bytes 1441792 | tf_op jit(solution)/shard_map/dct,dckl->tkl/dot_general | solution.py:338
  173.0 1.9 %convolution_add_fusion = f32[64,2048]{1,0:T(8,128)S(1)} fusion(f32[64,2048]{1,0:T(8,128)} %fusion.64, bf16[2048,128]{1,0:T(8,128)(2,1)} %param.29, f32[64,128]{1,0:T(8,128)} %collective-permute-done.14, f32[64,128]{1,0:T(8,128)} %collective-permute-done.13, f32[64,128]{1,0:T(8,128)} %collective-permute-done.12, f32[64,512]{1,0:T(8,128)} %copy-done.12, ...), kind=kOutput, calls=%fused_computation.11 | convolution fusion | flops 201482240 | bytes 1703940 | tf_op jit(solution)/shard_map/tc,dc->td/dot_general | solution.py:152
  175.8 3.1 %collective-permute-start.17 = (f32[16,2048]{1,0:T(8,128)S(1)}, f32[16,2048]{1,0:T(8,128)S(1)}, u32[]{:S(2)}, u32[]{:S(2)}) collective-permute-start(f32[16,2048]{1,0:T(8,128)S(1)} %get-tuple-element.24), channel_id=1, source_target_pairs={{0,3},{1,0},{2,1},{3,2},{4,7},{5,4},{6,5},{7,6},{8,11},{9,8},{10,9... | collective-permute-start | bytes 393224 | tf_op jit(solution)/shard_map/ppermute | solution.py:203
  180.0 2.6 %fusion.10 = bf16[16,2048]{1,0:T(8,128)(2,1)} fusion(f32[16,11,16]{2,1,0:T(8,128)S(1)} %copy-done.9, bf16[2048,11,16]{0,2,1:T(8,128)(2,1)} %dot_general.95, bf16[16,2048]{1,0:T(8,128)(2,1)S(1)} %get-tuple-element.22), kind=kOutput, calls=%fused_computation.16 | convolution fusion | flops 69304320 | bytes 863232 | tf_op jit(solution)/shard_map/dct,dckl->tkl/dot_general | solution.py:338
  183.6 6.2 %collective-permute-done.16 = f32[16,2048]{1,0:T(8,128)S(1)} collective-permute-done((f32[16,2048]{1,0:T(8,128)S(1)}, f32[16,2048]{1,0:T(8,128)S(1)}, u32[]{:S(2)}, u32[]{:S(2)}) %collective-permute-start.16) | collective-permute-done | bytes 131104 | tf_op jit(solution)/shard_map/ppermute | solution.py:203
  190.1 1.4 fusion.55
  (148 shorter events, 35.8 us)
Async XLA Ops:
  0.6 92.8 %copy-start = (bf16[1,2048,768]{2,1,0:T(8,128)(2,1)S(1)}, bf16[1,2048,768]{2,1,0:T(8,128)(2,1)}, u32[]{:S(2)}) copy-start(bf16[1,2048,768]{2,1,0:T(8,128)(2,1)} %param.31) | copy-start | bytes 9437188
  0.6 22.1 %copy-start.4 = (bf16[16,2048]{1,0:T(8,128)(2,1)S(1)}, bf16[16,2048]{1,0:T(8,128)(2,1)}, u32[]{:S(2)}) copy-start(bf16[16,2048]{1,0:T(8,128)(2,1)} %param.18) | copy-start | bytes 196612
  0.7 22.1 %copy-start.14 = (f32[2048]{0:T(1024)S(1)}, f32[2048]{0:T(1024)}, u32[]{:S(2)}) copy-start(f32[2048]{0:T(1024)} %param.26) | copy-start | bytes 24580
  0.7 22.2 %copy-start.30 = (s32[4]{0:T(128)S(1)}, s32[4]{0:T(128)}, u32[]{:S(2)}) copy-start(s32[4]{0:T(128)} %param.23) | copy-start | bytes 52
  1.8 26.4 %copy-start.21 = (f32[16]{0:T(128)}, f32[16]{0:T(128)S(1)}, u32[]{:S(2)}) copy-start(f32[16]{0:T(128)S(1)} %add_rsqrt_fusion.1) | copy-start | bytes 196
  2.7 22.2 %collective-permute-start.1 = (bf16[16,2048]{1,0:T(8,128)(2,1)S(1)}, bf16[16,2048]{1,0:T(8,128)(2,1)S(1)}, u32[]{:S(2)}, u32[]{:S(2)}) collective-permute-start(bf16[16,2048]{1,0:T(8,128)(2,1)S(1)} %fusion.50), channel_id=1, source_target_pairs={{0,2},{1,3},{2,0},{3,1},{4,6},{5,7},{6,4},{7,5},{8,10},{9,11},{10,... | collective-permute-start | bytes 196616 | tf_op jit(solution)/shard_map/ppermute | solution.py:166
  6.8 18.1 %collective-permute-start = (bf16[16,2048]{1,0:T(8,128)(2,1)S(1)}, bf16[16,2048]{1,0:T(8,128)(2,1)}, u32[]{:S(2)}, u32[]{:S(2)}) collective-permute-start(bf16[16,2048]{1,0:T(8,128)(2,1)S(1)} %fusion.50), channel_id=1, source_target_pairs={{0,1},{1,2},{2,3},{3,0},{4,5},{5,6},{6,7},{7,4},{8,9},{9,10},{10,1... | collective-permute-start | bytes 196616 | tf_op jit(solution)/shard_map/ppermute | solution.py:166
  8.4 16.5 %collective-permute-start.2 = (bf16[16,2048]{1,0:T(8,128)(2,1)S(1)}, bf16[16,2048]{1,0:T(8,128)(2,1)}, u32[]{:S(2)}, u32[]{:S(2)}) collective-permute-start(bf16[16,2048]{1,0:T(8,128)(2,1)S(1)} %fusion.50), channel_id=1, source_target_pairs={{0,3},{1,0},{2,1},{3,2},{4,7},{5,4},{6,5},{7,6},{8,11},{9,8},{10,9... | collective-permute-start | bytes 196616 | tf_op jit(solution)/shard_map/ppermute | solution.py:166
  11.3 11.6 %copy-start.26 = (f32[16]{0:T(128)}, f32[16]{0:T(128)S(1)}, u32[]{:S(2)}) copy-start(f32[16]{0:T(128)S(1)} %convert_element_type.111) | copy-start | bytes 196
  12.5 11.1 %copy-start.19 = (bf16[4,32,256]{2,1,0:T(8,128)(2,1)S(1)}, bf16[4,32,256]{2,1,0:T(8,128)(2,1)}, u32[]{:S(2)}) copy-start(bf16[4,32,256]{2,1,0:T(8,128)(2,1)} %param.24) | copy-start | bytes 196612
  18.4 49.6 %all-to-all-start = ((bf16[16,176,128]{2,1,0:T(8,128)(2,1)}), bf16[16,176,128]{2,1,0:T(8,128)(2,1)}, u32[]{:S(2)}, u32[]{:S(2)}) async-start(bf16[16,176,128]{2,1,0:T(8,128)(2,1)} %copy.131), calls=%async_computation | async-start | bytes 1441792 | tf_op jit(solution)/shard_map/all_to_all | solution.py:212
  23.0 5.2 %copy-start.25 = (s32[1024]{0:T(1024)}, s32[1024]{0:T(1024)S(1)}, u32[]{:S(2)}) copy-start(s32[1024]{0:T(1024)S(1)} %pad_clamp_fusion.1) | copy-start | bytes 12292
  24.9 22.4 %copy-start.13 = (bf16[4,32,128]{2,1,0:T(8,128)(2,1)}, bf16[4,32,128]{2,1,0:T(8,128)(2,1)S(1)}, u32[]{:S(2)}) copy-start(bf16[4,32,128]{2,1,0:T(8,128)(2,1)S(1)} %get-tuple-element.39) | copy-start | bytes 98308
  24.9 3.3 %copy-start.27 = (pred[4]{0:T(512)(128)(4,1)}, pred[4]{0:T(512)(128)(4,1)S(1)}, u32[]{:S(2)}) copy-start(pred[4]{0:T(512)(128)(4,1)S(1)} %compare_and_fusion) | copy-start | bytes 16
  28.2 16.6 %copy-start.18 = (bf16[4,32,128]{2,1,0:T(8,128)(2,1)S(1)}, bf16[4,32,128]{2,1,0:T(8,128)(2,1)}, u32[]{:S(2)}) copy-start(bf16[4,32,128]{2,1,0:T(8,128)(2,1)} %get-tuple-element.38) | copy-start | bytes 98308
  29.5 6.8 %collective-permute-start.5 = (bf16[64,128]{1,0:T(8,128)(2,1)S(1)}, bf16[64,128]{1,0:T(8,128)(2,1)S(1)}, u32[]{:S(2)}, u32[]{:S(2)}) collective-permute-start(bf16[64,128]{1,0:T(8,128)(2,1)S(1)} %convolution_convert_fusion.6), channel_id=1, source_target_pairs={{0,3},{1,0},{2,1},{3,2},{4,7},{5,4},{6,5},{7,6},{8,11},{9,8},{10,9... | collective-permute-start | bytes 49160 | tf_op jit(solution)/shard_map/ppermute | solution.py:166
  33.1 10.3 %collective-permute-start.4 = (bf16[64,128]{1,0:T(8,128)(2,1)S(1)}, bf16[64,128]{1,0:T(8,128)(2,1)S(1)}, u32[]{:S(2)}, u32[]{:S(2)}) collective-permute-start(bf16[64,128]{1,0:T(8,128)(2,1)S(1)} %convolution_convert_fusion.6), channel_id=1, source_target_pairs={{0,2},{1,3},{2,0},{3,1},{4,6},{5,7},{6,4},{7,5},{8,10},{9,11},{10,... | collective-permute-start | bytes 49160 | tf_op jit(solution)/shard_map/ppermute | solution.py:166
  33.1 10.3 %collective-permute-start.3 = (bf16[64,128]{1,0:T(8,128)(2,1)S(1)}, bf16[64,128]{1,0:T(8,128)(2,1)S(1)}, u32[]{:S(2)}, u32[]{:S(2)}) collective-permute-start(bf16[64,128]{1,0:T(8,128)(2,1)S(1)} %convolution_convert_fusion.6), channel_id=1, source_target_pairs={{0,1},{1,2},{2,3},{3,0},{4,5},{5,6},{6,7},{7,4},{8,9},{9,10},{10,1... | collective-permute-start | bytes 49160 | tf_op jit(solution)/shard_map/ppermute | solution.py:166
  36.3 30.2 %copy-start.17 = (f32[2048]{0:T(1024)S(1)}, f32[2048]{0:T(1024)}, u32[]{:S(2)}) copy-start(f32[2048]{0:T(1024)} %param.27) | copy-start | bytes 24580
  36.3 14.7 %copy-start.15 = (bf16[4,16,4,128]{3,2,1,0:T(4,128)(2,1)}, bf16[4,16,4,128]{3,2,1,0:T(4,128)(2,1)S(1)}, u32[]{:S(2)}) copy-start(bf16[4,16,4,128]{3,2,1,0:T(4,128)(2,1)S(1)} %reshape.192) | copy-start | bytes 196612
  44.8 23.1 %copy-start.16 = (bf16[64,128]{1,0:T(8,128)(2,1)}, bf16[64,128]{1,0:T(8,128)(2,1)S(1)}, u32[]{:S(2)}) copy-start(bf16[64,128]{1,0:T(8,128)(2,1)S(1)} %get-tuple-element.33) | copy-start | bytes 49156
  46.4 4.7 %copy-start.31 = (f32[4,4,16,48]{3,2,1,0:T(8,128)}, f32[4,4,16,48]{3,2,1,0:T(8,128)S(1)}, u32[]{:S(2)}) copy-start(f32[4,4,16,48]{3,2,1,0:T(8,128)S(1)} %get-tuple-element.35) | copy-start | bytes 147460
  51.0 8.4 %collective-permute-start.6 = (f32[16,2048]{1,0:T(8,128)}, f32[16,2048]{1,0:T(8,128)S(1)}, u32[]{:S(2)}, u32[]{:S(2)}) collective-permute-start(f32[16,2048]{1,0:T(8,128)} %get-tuple-element.26), channel_id=1, source_target_pairs={{0,1},{1,2},{2,3},{3,0},{4,5},{5,6},{6,7},{7,4},{8,9},{9,10},{10,1... | collective-permute-start | bytes 393224 | tf_op jit(solution)/shard_map/ppermute | solution.py:203
  51.4 8.7 %collective-permute-start.8 = (f32[16,2048]{1,0:T(8,128)}, f32[16,2048]{1,0:T(8,128)}, u32[]{:S(2)}, u32[]{:S(2)}) collective-permute-start(f32[16,2048]{1,0:T(8,128)} %get-tuple-element.27), channel_id=1, source_target_pairs={{0,3},{1,0},{2,1},{3,2},{4,7},{5,4},{6,5},{7,6},{8,11},{9,8},{10,9... | collective-permute-start | bytes 393224 | tf_op jit(solution)/shard_map/ppermute | solution.py:203
  54.8 10.5 %collective-permute-start.7 = (f32[16,2048]{1,0:T(8,128)}, f32[16,2048]{1,0:T(8,128)}, u32[]{:S(2)}, u32[]{:S(2)}) collective-permute-start(f32[16,2048]{1,0:T(8,128)} %get-tuple-element.28), channel_id=1, source_target_pairs={{0,2},{1,3},{2,0},{3,1},{4,6},{5,7},{6,4},{7,5},{8,10},{9,11},{10,... | collective-permute-start | bytes 393224 | tf_op jit(solution)/shard_map/ppermute | solution.py:203
  66.5 62.5 %copy-start.23 = (f32[16]{0:T(128)}, f32[16]{0:T(128)S(1)}, u32[]{:S(2)}) copy-start(f32[16]{0:T(128)S(1)} %add_rsqrt_fusion) | copy-start | bytes 196
  68.0 24.2 %all-to-all-start.1 = ((bf16[16,176,128]{2,1,0:T(8,128)(2,1)}), bf16[16,176,128]{2,1,0:T(8,128)(2,1)}, u32[]{:S(2)}, u32[]{:S(2)}) async-start(bf16[16,176,128]{2,1,0:T(8,128)(2,1)} %copy.136), calls=%async_computation.1 | async-start | bytes 1441792 | tf_op jit(solution)/shard_map/all_to_all | solution.py:212
  93.5 2.1 %copy-start.1 = (bf16[1,2048,768]{2,1,0:T(8,128)(2,1)S(1)}, bf16[1,2048,768]{2,1,0:T(8,128)(2,1)}, u32[]{:S(2)}) copy-start(bf16[1,2048,768]{2,1,0:T(8,128)(2,1)} %param.32) | copy-start | bytes 9437188
  94.2 4.1 %copy-start.2 = (f32[16,11,768]{2,0,1:T(8,128)}, f32[16,11,768]{2,0,1:T(8,128)S(1)}, u32[]{:S(2)}) copy-start(f32[16,11,768]{2,0,1:T(8,128)S(1)} %convolution_bitcast_fusion.2) | copy-start | bytes 1622020
  100.5 24.2 %all-to-all-start.2 = ((bf16[16,176,128]{2,1,0:T(8,128)(2,1)}), bf16[16,176,128]{2,1,0:T(8,128)(2,1)}, u32[]{:S(2)}, u32[]{:S(2)}) async-start(bf16[16,176,128]{2,1,0:T(8,128)(2,1)} %copy.138), calls=%async_computation.2 | async-start | bytes 1441792 | tf_op jit(solution)/shard_map/all_to_all | solution.py:216
  108.9 21.9 %copy-start.10 = (bf16[16,2048]{1,0:T(8,128)(2,1)S(1)}, bf16[16,2048]{1,0:T(8,128)(2,1)}, u32[]{:S(2)}) copy-start(bf16[16,2048]{1,0:T(8,128)(2,1)} %param.19) | copy-start | bytes 196612
  130.8 14.2 %copy-start.28 = (pred[4]{0:T(512)(128)(4,1)S(1)}, pred[4]{0:T(512)(128)(4,1)}, u32[]{:S(2)}) copy-start(pred[4]{0:T(512)(128)(4,1)} %copy-done.27) | copy-start | bytes 16
  131.5 9.5 %collective-permute-start.11 = (bf16[16,2048]{1,0:T(8,128)(2,1)S(1)}, bf16[16,2048]{1,0:T(8,128)(2,1)S(1)}, u32[]{:S(2)}, u32[]{:S(2)}) collective-permute-start(bf16[16,2048]{1,0:T(8,128)(2,1)S(1)} %fusion.108), channel_id=1, source_target_pairs={{0,3},{1,0},{2,1},{3,2},{4,7},{5,4},{6,5},{7,6},{8,11},{9,8},{10,9... | collective-permute-start | bytes 196616 | tf_op jit(solution)/shard_map/ppermute | solution.py:319
  132.4 8.6 %collective-permute-start.10 = (bf16[16,2048]{1,0:T(8,128)(2,1)S(1)}, bf16[16,2048]{1,0:T(8,128)(2,1)}, u32[]{:S(2)}, u32[]{:S(2)}) collective-permute-start(bf16[16,2048]{1,0:T(8,128)(2,1)S(1)} %fusion.108), channel_id=1, source_target_pairs={{0,2},{1,3},{2,0},{3,1},{4,6},{5,7},{6,4},{7,5},{8,10},{9,11},{10,... | collective-permute-start | bytes 196616 | tf_op jit(solution)/shard_map/ppermute | solution.py:319
  132.6 8.4 %collective-permute-start.9 = (bf16[16,2048]{1,0:T(8,128)(2,1)S(1)}, bf16[16,2048]{1,0:T(8,128)(2,1)}, u32[]{:S(2)}, u32[]{:S(2)}) collective-permute-start(bf16[16,2048]{1,0:T(8,128)(2,1)S(1)} %fusion.108), channel_id=1, source_target_pairs={{0,1},{1,2},{2,3},{3,0},{4,5},{5,6},{6,7},{7,4},{8,9},{9,10},{10,1... | collective-permute-start | bytes 196616 | tf_op jit(solution)/shard_map/ppermute | solution.py:319
  135.8 25.2 %all-to-all-start.3 = ((bf16[16,176,128]{2,1,0:T(8,128)(2,1)}), bf16[16,176,128]{2,1,0:T(8,128)(2,1)}, u32[]{:S(2)}, u32[]{:S(2)}) async-start(bf16[16,176,128]{2,1,0:T(8,128)(2,1)} %copy.146), calls=%async_computation.3 | async-start | bytes 1441792 | tf_op jit(solution)/shard_map/all_to_all | solution.py:216
  146.1 5.8 %copy-start.32 = (f32[4,4,16]{2,1,0:T(4,128)S(1)}, f32[4,4,16]{2,1,0:T(4,128)}, u32[]{:S(2)}) copy-start(f32[4,4,16]{2,1,0:T(4,128)} %get-tuple-element.34) | copy-start | bytes 3076
  159.3 6.2 %copy-start.12 = (f32[64,512]{1,0:T(8,128)}, f32[64,512]{1,0:T(8,128)S(1)}, u32[]{:S(2)}) copy-start(f32[64,512]{1,0:T(8,128)S(1)} %constant_dynamic-update-slice_fusion) | copy-start | bytes 393220
  161.6 11.4 %collective-permute-start.12 = (f32[64,128]{1,0:T(8,128)}, f32[64,128]{1,0:T(8,128)}, u32[]{:S(2)}, u32[]{:S(2)}) collective-permute-start(f32[64,128]{1,0:T(8,128)} %get-tuple-element.29), channel_id=1, source_target_pairs={{0,1},{1,2},{2,3},{3,0},{4,5},{5,6},{6,7},{7,4},{8,9},{9,10},{10,1... | collective-permute-start | bytes 98312 | tf_op jit(solution)/shard_map/ppermute | solution.py:203
  161.8 11.2 %collective-permute-start.14 = (f32[64,128]{1,0:T(8,128)}, f32[64,128]{1,0:T(8,128)}, u32[]{:S(2)}, u32[]{:S(2)}) collective-permute-start(f32[64,128]{1,0:T(8,128)} %get-tuple-element.30), channel_id=1, source_target_pairs={{0,3},{1,0},{2,1},{3,2},{4,7},{5,4},{6,5},{7,6},{8,11},{9,8},{10,9... | collective-permute-start | bytes 98312 | tf_op jit(solution)/shard_map/ppermute | solution.py:203
  165.5 7.6 %collective-permute-start.13 = (f32[64,128]{1,0:T(8,128)}, f32[64,128]{1,0:T(8,128)}, u32[]{:S(2)}, u32[]{:S(2)}) collective-permute-start(f32[64,128]{1,0:T(8,128)} %get-tuple-element.31), channel_id=1, source_target_pairs={{0,2},{1,3},{2,0},{3,1},{4,6},{5,7},{6,4},{7,5},{8,10},{9,11},{10,... | collective-permute-start | bytes 98312 | tf_op jit(solution)/shard_map/ppermute | solution.py:203
  168.7 11.4 %copy-start.9 = (f32[16,11,16]{2,1,0:T(8,128)S(1)}, f32[16,11,16]{2,1,0:T(8,128)}, u32[]{:S(2)}) copy-start(f32[16,11,16]{2,1,0:T(8,128)} %copy-done.8) | copy-start | bytes 33796
  168.7 21.2 %copy-start.22 = (f32[16]{0:T(128)S(1)}, f32[16]{0:T(128)}, u32[]{:S(2)}) copy-start(f32[16]{0:T(128)} %copy-done.21) | copy-start | bytes 196
  170.8 19.2 %copy-start.24 = (f32[16]{0:T(128)S(1)}, f32[16]{0:T(128)}, u32[]{:S(2)}) copy-start(f32[16]{0:T(128)} %copy-done.23) | copy-start | bytes 196
  173.0 17.0 %copy-start.11 = (bf16[16,2048]{1,0:T(8,128)(2,1)S(1)}, bf16[16,2048]{1,0:T(8,128)(2,1)}, u32[]{:S(2)}) copy-start(bf16[16,2048]{1,0:T(8,128)(2,1)} %param.19) | copy-start | bytes 196612
  175.0 8.3 %collective-permute-start.15 = (f32[16,2048]{1,0:T(8,128)S(1)}, f32[16,2048]{1,0:T(8,128)S(1)}, u32[]{:S(2)}, u32[]{:S(2)}) collective-permute-start(f32[16,2048]{1,0:T(8,128)S(1)} %get-tuple-element.23), channel_id=1, source_target_pairs={{0,1},{1,2},{2,3},{3,0},{4,5},{5,6},{6,7},{7,4},{8,9},{9,10},{10,1... | collective-permute-start | bytes 393224 | tf_op jit(solution)/shard_map/ppermute | solution.py:203
  175.8 7.8 %collective-permute-start.17 = (f32[16,2048]{1,0:T(8,128)S(1)}, f32[16,2048]{1,0:T(8,128)S(1)}, u32[]{:S(2)}, u32[]{:S(2)}) collective-permute-start(f32[16,2048]{1,0:T(8,128)S(1)} %get-tuple-element.24), channel_id=1, source_target_pairs={{0,3},{1,0},{2,1},{3,2},{4,7},{5,4},{6,5},{7,6},{8,11},{9,8},{10,9... | collective-permute-start | bytes 393224 | tf_op jit(solution)/shard_map/ppermute | solution.py:203
  178.9 10.9 %collective-permute-start.16 = (f32[16,2048]{1,0:T(8,128)S(1)}, f32[16,2048]{1,0:T(8,128)S(1)}, u32[]{:S(2)}, u32[]{:S(2)}) collective-permute-start(f32[16,2048]{1,0:T(8,128)S(1)} %get-tuple-element.25), channel_id=1, source_target_pairs={{0,2},{1,3},{2,0},{3,1},{4,6},{5,7},{6,4},{7,5},{8,10},{9,11},{10,... | collective-permute-start | bytes 393224 | tf_op jit(solution)/shard_map/ppermute | solution.py:203
  (7 other events, 8.8 us)

commit v16 on v15

--- a/solution.py
+++ b/solution.py
@@ -245,10 +245,6 @@
     attended, saved = attention_forward(
         gathered_rows, w_query, key_value_weight, key_cache, prefix_value_cache, cache_lengths, first_head
     )
-    mixed = head_sums(jnp.dot(attended, w_output, preferred_element_type=jnp.float32))
-    hidden = (hidden_in.astype(jnp.float32) + mixed).astype(jnp.bfloat16)
-    normed_two, inverse_two = rms_forward(hidden, moe_gain)
-    moe_rows = normed_two.astype(jnp.bfloat16)
     device_count = lax.axis_size("expert") * lax.axis_size("head")
     capacity = (owned * TOP * 4 + 3 * device_count - 1) // (3 * device_count)
     slot_total = device_count * capacity
@@ -267,17 +263,23 @@
     cotangent = out_grad.astype(jnp.float32) * loss_mask.astype(jnp.float32)[:, None]
     lanes = 128
     pieces = width // lanes
+    grad_out = jnp.einsum(
+        "dct,tkl->dckl",
+        weighting,
+        cotangent.reshape(owned, pieces, lanes),
+        precision=highest_prec,
+    ).astype(jnp.bfloat16)
+    partial_mixed = jnp.dot(attended, w_output, preferred_element_type=jnp.float32)
+    partial_mixed, grad_out = lax.optimization_barrier((partial_mixed, grad_out))
+    mixed = head_sums(partial_mixed)
+    hidden = (hidden_in.astype(jnp.float32) + mixed).astype(jnp.bfloat16)
+    normed_two, inverse_two = rms_forward(hidden, moe_gain)
+    moe_rows = normed_two.astype(jnp.bfloat16)
     outgoing = jnp.einsum(
         "dct,tkl->dckl",
         placement,
         moe_rows.reshape(owned, pieces, lanes),
         preferred_element_type=jnp.float32,
-    ).astype(jnp.bfloat16)
-    grad_out = jnp.einsum(
-        "dct,tkl->dckl",
-        weighting,
-        cotangent.reshape(owned, pieces, lanes),
-        precision=highest_prec,
     ).astype(jnp.bfloat16)
     flat_shape = (device_count, capacity * pieces, lanes)
     split_shape = (device_count, capacity, pieces, lanes)

time: 193 us -> 215 us (1.11)
  waiting for transfers between devices: 55.1 us -> 63.2 us
  local copies, waits for them, and re-layouts: 36 us -> 42.8 us
  other arithmetic: 14 us -> 18.8 us
  matrix products: 39.2 us -> 43.4 us
    ppermute x9, waiting for transfers between devices: 17.4 us -> 32.2 us  [head_sums(): lax.ppermute(chunk((me + shift) % count), 'head', perm=[(j, (j + shift) %...]
    ppermute x6, waiting for transfers between devices: 7.11 us -> 2.02 us  [head_gather(): lax.ppermute(block, 'head', perm=[(j, (j + shift) % count) for j in range...]
    ppermute x6, starting transfers between devices: 12.6 us -> 10 us  [head_gather(): lax.ppermute(block, 'head', perm=[(j, (j + shift) % count) for j in range...]
    unnamed x68 -> x52, local copies, waits for them, and re-layouts: 7.37 us -> 6.56 us
  transfers between devices with their start and end apart: 22 -> 22, of which waited for: 10 -> 8; matrix products, arithmetic and copies ran while one was open for 35% -> 32% of each run, Pallas kernels for 0% -> 0%
where the time goes in v16:
time: 215 us; the launch traced here: 213 us
  waiting for transfers between devices  63.2 us (29%)
  starting transfers between devices  43.8 us (20%)
  matrix products  43.4 us (20%)
  local copies, waits for them, and re-layouts  42.8 us (20%)
  other arithmetic  18.8 us (9%)
    ppermute x9, waiting for transfers between devices, head_sums(): lax.ppermute(chunk((me + shift) % count), 'head', perm=[(j, (j + shift) %...  32.2 us
    all_to_all x2, waiting for transfers between devices, from_experts(): lax.all_to_all(results, ('expert', 'head'), split_axis=0, concat_axis=0,...  15.8 us
    ppermute x9, starting transfers between devices, head_sums(): lax.ppermute(chunk((me + shift) % count), 'head', perm=[(j, (j + shift) %...  13.5 us
    all_to_all x2, waiting for transfers between devices, to_experts(): lax.all_to_all(outgoing, ('expert', 'head'), split_axis=0, concat_axis=0,...  13.1 us
    ppermute x6, starting transfers between devices, head_gather(): lax.ppermute(block, 'head', perm=[(j, (j + shift) % count) for j in range...  10 us
    all_to_all x2, starting transfers between devices, from_experts(): lax.all_to_all(results, ('expert', 'head'), split_axis=0, concat_axis=0,...  9.8 us
    all_to_all x2, starting transfers between devices, to_experts(): lax.all_to_all(outgoing, ('expert', 'head'), split_axis=0, concat_axis=0,...  8.55 us
    unnamed x52, local copies, waits for them, and re-layouts  6.56 us
  transfers between devices with their start and end apart: 22, of which 8 were waited for; matrix products, arithmetic and copies ran while one was open for 32% of the time, Pallas kernels for 0%

profile of v16, /device:TPU:0, one launch (start us, length us, event | category | flops | bytes accessed | tf_op | source)
XLA Modules:
  0.0 213.2 jit_solution(496787431717097122)
XLA Ops:
  2.7 4.1 %collective-permute-start.1 = (bf16[16,2048]{1,0:T(8,128)(2,1)S(1)}, bf16[16,2048]{1,0:T(8,128)(2,1)}, u32[]{:S(2)}, u32[]{:S(2)}) collective-permute-start(bf16[16,2048]{1,0:T(8,128)(2,1)S(1)} %fusion.50), channel_id=1, source_target_pairs={{0,2},{1,3},{2,0},{3,1},{4,6},{5,7},{6,4},{7,5},{8,10},{9,11},{10,... | collective-permute-start | bytes 196616 | tf_op jit(solution)/shard_map/ppermute | solution.py:166
  6.8 1.6 collective-permute-start
  8.4 2.2 %collective-permute-start.2 = (bf16[16,2048]{1,0:T(8,128)(2,1)S(1)}, bf16[16,2048]{1,0:T(8,128)(2,1)}, u32[]{:S(2)}, u32[]{:S(2)}) collective-permute-start(bf16[16,2048]{1,0:T(8,128)(2,1)S(1)} %fusion.50), channel_id=1, source_target_pairs={{0,3},{1,0},{2,1},{3,2},{4,7},{5,4},{6,5},{7,6},{8,11},{9,8},{10,9... | collective-permute-start | bytes 196616 | tf_op jit(solution)/shard_map/ppermute | solution.py:166
  19.3 3.0 %convolution_convert_fusion = bf16[16,11,16,128]{3,0,2,1:T(8,128)(2,1)} fusion(f32[16,11,16,1]{2,1,0,3:T(8,128)S(1)} %bitcast.207, bf16[16,2048]{1,0:T(8,128)(2,1)} %param.19, f32[16]{0:T(128)} %convert_element_type.109), kind=kOutput, calls=%fused_computation.19 | convolution fusion | flops 69632000 | bytes 797760 | tf_op jit(solution)/shard_map/dct,tkl->dckl/dot_general | solution.py:266
  22.9 1.6 pad_maximum_fusion
  24.5 1.5 gather_fusion.1
  30.1 2.1 convolution_convert_fusion.5
  32.9 2.0 collective-permute-done.3
  36.3 1.8 fusion.110
  39.7 2.9 %fusion.67 = f32[64,2048]{1,0:T(8,128)} fusion(bf16[512,2048]{1,0:T(8,128)(2,1)} %param.30, bf16[8,8,4,128]{3,2,1,0:T(4,128)(2,1)S(1)} %bitcast.211), kind=kOutput, calls=%fused_computation.102 | convolution fusion | flops 134217728 | bytes 2686976 | tf_op jit(solution)/shard_map/dot_general | solution.py:272
  43.7 4.3 %all-to-all-start = ((bf16[16,176,128]{2,1,0:T(8,128)(2,1)}), bf16[16,176,128]{2,1,0:T(8,128)(2,1)}, u32[]{:S(2)}, u32[]{:S(2)}) async-start(bf16[16,176,128]{2,1,0:T(8,128)(2,1)} %copy.131), calls=%async_computation | async-start | bytes 1441792 | tf_op jit(solution)/shard_map/all_to_all | solution.py:212
  48.0 1.8 constant_dynamic-slice_fusion.7
  49.9 1.7 collective-permute-start.6
  51.6 2.1 collective-permute-start.8
  54.9 12.9 %collective-permute-done.6 = f32[16,2048]{1,0:T(8,128)} collective-permute-done((f32[16,2048]{1,0:T(8,128)}, f32[16,2048]{1,0:T(8,128)}, u32[]{:S(2)}, u32[]{:S(2)}) %collective-permute-start.6) | collective-permute-done | bytes 131104 | tf_op jit(solution)/shard_map/ppermute | solution.py:203
  67.8 10.9 %collective-permute-done.7 = f32[16,2048]{1,0:T(8,128)} collective-permute-done((f32[16,2048]{1,0:T(8,128)}, f32[16,2048]{1,0:T(8,128)}, u32[]{:S(2)}, u32[]{:S(2)}) %collective-permute-start.7) | collective-permute-done | bytes 131104 | tf_op jit(solution)/shard_map/ppermute | solution.py:203
  81.4 4.3 %all-to-all-start.1 = ((bf16[16,176,128]{2,1,0:T(8,128)(2,1)}), bf16[16,176,128]{2,1,0:T(8,128)(2,1)}, u32[]{:S(2)}, u32[]{:S(2)}) async-start(bf16[16,176,128]{2,1,0:T(8,128)(2,1)} %copy.136), calls=%async_computation.1 | async-start | bytes 1441792 | tf_op jit(solution)/shard_map/all_to_all | solution.py:212
  85.7 2.9 %copy.173 = bf16[96,8,16,128]{3,2,1,0:T(8,128)(2,1)S(1)} copy(bf16[96,8,16,128]{3,1,2,0:T(8,128)(2,1)} %bitcast.196) | data formatting | bytes 6291456
  88.6 1.8 copy.132
  90.5 2.0 fusion.15
  92.5 13.1 %all-to-all-done.1 = bf16[16,176,128]{2,1,0:T(8,128)(2,1)} async-done(((bf16[16,176,128]{2,1,0:T(8,128)(2,1)}), bf16[16,176,128]{2,1,0:T(8,128)(2,1)}, u32[]{:S(2)}, u32[]{:S(2)}) %all-to-all-start.1) | async-done | bytes 720928 | tf_op jit(solution)/shard_map/all_to_all | solution.py:212
  114.0 4.5 %all-to-all-start.2 = ((bf16[16,176,128]{2,1,0:T(8,128)(2,1)}), bf16[16,176,128]{2,1,0:T(8,128)(2,1)}, u32[]{:S(2)}, u32[]{:S(2)}) async-start(bf16[16,176,128]{2,1,0:T(8,128)(2,1)} %copy.138), calls=%async_computation.2 | async-start | bytes 1441792 | tf_op jit(solution)/shard_map/all_to_all | solution.py:216
  118.5 3.9 %fusion.11 = bf16[16,11,16,128]{3,0,2,1:T(8,128)(2,1)} fusion(bf16[768,16,128]{2,1,0:T(8,128)(2,1)} %bitcast.198, f32[16,11,768]{2,0,1:T(8,128)} %copy-done.7, f32[16,11,768]{2,0,1:T(8,128)} %copy-done.2), kind=kOutput, calls=%fused_computation.18 | convolution fusion | flops 554819584 | bytes 4947968 | tf_op jit(solution)/shard_map/scf,fkl->sckl/dot_general | solution.py:297
  122.4 15.8 %all-to-all-done.2 = bf16[16,176,128]{2,1,0:T(8,128)(2,1)} async-done(((bf16[16,176,128]{2,1,0:T(8,128)(2,1)}), bf16[16,176,128]{2,1,0:T(8,128)(2,1)}, u32[]{:S(2)}, u32[]{:S(2)}) %all-to-all-start.2) | async-done | bytes 720928 | tf_op jit(solution)/shard_map/all_to_all | solution.py:216
  138.2 2.1 %copy.231 = bf16[16,11,16,128]{3,2,0,1:T(8,128)(2,1)} copy(bf16[16,11,16,128]{3,2,1,0:T(8,128)(2,1)} %bitcast.45) | data formatting | bytes 1441792 | tf_op jit(solution)/shard_map/reshape | solution.py:312
  140.3 2.2 %dot_general.87 = bf16[2048,11,16]{0,2,1:T(8,128)(2,1)} reshape(bf16[16,128,11,16]{1,0,3,2:T(8,128)(2,1)} %bitcast.201) | data formatting | bytes 1441792 | tf_op jit(solution)/shard_map/dct,dckl->tkl/dot_general | solution.py:313
  142.5 1.8 fusion.46
  144.3 1.6 fusion.108
  147.9 2.2 %copy.146 = bf16[16,176,128]{2,1,0:T(8,128)(2,1)} copy(bf16[16,176,128]{2,0,1:T(8,128)(2,1)} %bitcast.208) | data formatting | bytes 1441792 | tf_op jit(solution)/shard_map/reshape | solution.py:324
  150.1 5.4 %all-to-all-start.3 = ((bf16[16,176,128]{2,1,0:T(8,128)(2,1)}), bf16[16,176,128]{2,1,0:T(8,128)(2,1)}, u32[]{:S(2)}, u32[]{:S(2)}) async-start(bf16[16,176,128]{2,1,0:T(8,128)(2,1)} %copy.146), calls=%async_computation.3 | async-start | bytes 1441792 | tf_op jit(solution)/shard_map/all_to_all | solution.py:216
  155.5 1.7 pad_maximum_fusion.1
  157.2 2.4 %gather_fusion.2 = bf16[4,16,2048]{2,1,0:T(8,128)(2,1)} fusion(bf16[4,16,2048]{2,1,0:T(8,128)(2,1)} %pad_maximum_fusion.1, s32[1024]{0:T(1024)} %copy-done.21), kind=kCustom, calls=%fused_computation.1.clone | custom fusion | bytes 524304 | tf_op jit(solution)/shard_map/jit(_take)/gather | solution.py:176
  160.6 3.0 %convolution_convert_fusion.3 = bf16[64,512]{1,0:T(8,128)(2,1)} fusion(bf16[64,2048]{1,0:T(8,128)(2,1)S(1)} %bitcast.206, bf16[512,2048]{1,0:T(8,128)(2,1)} %param.30), kind=kOutput, calls=%fused_computation.38 | convolution fusion | flops 134250496 | bytes 2424832 | tf_op jit(solution)/shard_map/td,fd->tf/dot_general | solution.py:132
  166.9 1.7 convolution_bitcast_fusion.4
  168.6 3.0 %convolution_bitcast_fusion.6 = f32[4,48,128]{2,1,0:T(8,128)} fusion(f32[4,4,16,48]{3,2,1,0:T(8,128)} %convolution_bitcast_fusion.4, bf16[4,16,4,128]{3,2,1,0:T(4,128)(2,1)} %reshape.192, f32[4,4,16,48]{3,2,1,0:T(8,128)} %copy-done.24, f32[4,4,16]{2,1,0:T(4,128)} %get-tuple-element.38), kind=kOutput, calls=%fused_computation.37 | convolution fusion | flops 3232047 | bytes 263168 | tf_op jit(solution)/shard_map/shbk,sbhd->skd/dot_general | solution.py:58
  172.9 2.9 %fusion.27 = bf16[4,16,4,128]{3,1,2,0:T(8,128)(2,1)} fusion(f32[4,4,16,48]{3,2,1,0:T(8,128)} %convolution_bitcast_fusion.4, bf16[4,16,128]{2,1,0:T(8,128)(2,1)} %bitcast.219, bf16[4,32,128]{2,1,0:T(8,128)(2,1)} %get-tuple-element.42, f32[4,4,16,48]{3,2,1,0:T(8,128)} %copy-done.24, f32[4,4,16]{2,1,0:T(4,128)} %get-tuple-element.38), kind=kOutput, calls=%fused_computation.42 | convolution fusion | flops 3363119 | bytes 214016 | tf_op jit(solution)/shard_map/shbk,skd->sbhd/dot_general | solution.py:55
  175.8 1.5 copy.150
  182.2 1.9 collective-permute-start.12
  184.0 2.0 collective-permute-start.14
  187.0 3.2 %fusion.64 = f32[64,2048]{1,0:T(8,128)} fusion(bf16[2048,512]{1,0:T(8,128)(2,1)} %param.28, bf16[8,8,4,128]{3,2,1,0:T(4,128)(2,1)} %bitcast.210), kind=kOutput, calls=%fused_computation.99 | convolution fusion | flops 134217728 | bytes 2686976 | tf_op jit(solution)/shard_map/tf,df->td/dot_general | solution.py:156
  190.2 2.2 %copy.230 = bf16[16,11,16,128]{3,2,0,1:T(8,128)(2,1)} copy(bf16[16,11,16,128]{3,2,1,0:T(8,128)(2,1)} %bitcast.64) | data formatting | bytes 1441792 | tf_op jit(solution)/shard_map/optimization_barrier | solution.py:150
  192.4 2.1 %dot_general.95 = bf16[2048,11,16]{0,2,1:T(8,128)(2,1)} reshape(bf16[16,128,11,16]{1,0,3,2:T(8,128)(2,1)} %bitcast.202) | data formatting | bytes 1441792 | tf_op jit(solution)/shard_map/dct,dckl->tkl/dot_general | solution.py:340
  194.5 1.9 convolution_add_fusion
  196.5 1.5 collective-permute-start.15
  198.0 2.4 %collective-permute-start.17 = (f32[16,2048]{1,0:T(8,128)S(1)}, f32[16,2048]{1,0:T(8,128)S(1)}, u32[]{:S(2)}, u32[]{:S(2)}) collective-permute-start(f32[16,2048]{1,0:T(8,128)S(1)} %get-tuple-element.28), channel_id=1, source_target_pairs={{0,3},{1,0},{2,1},{3,2},{4,7},{5,4},{6,5},{7,6},{8,11},{9,8},{10,9... | collective-permute-start | bytes 393224 | tf_op jit(solution)/shard_map/ppermute | solution.py:203
  200.6 2.6 %fusion.10 = bf16[16,2048]{1,0:T(8,128)(2,1)} fusion(f32[16,11,16]{2,1,0:T(8,128)S(1)} %fusion.30, bf16[2048,11,16]{0,2,1:T(8,128)(2,1)} %dot_general.95, bf16[16,2048]{1,0:T(8,128)(2,1)S(1)} %get-tuple-element.26), kind=kOutput, calls=%fused_computation.16 | convolution fusion | flops 69304320 | bytes 863232 | tf_op jit(solution)/shard_map/dct,dckl->tkl/dot_general | solution.py:340
  203.1 1.7 collective-permute-done.15
  205.3 6.2 %collective-permute-done.16 = f32[16,2048]{1,0:T(8,128)S(1)} collective-permute-done((f32[16,2048]{1,0:T(8,128)S(1)}, f32[16,2048]{1,0:T(8,128)S(1)}, u32[]{:S(2)}, u32[]{:S(2)}) %collective-permute-start.16) | collective-permute-done | bytes 131104 | tf_op jit(solution)/shard_map/ppermute | solution.py:203
  (132 shorter events, 48.0 us)
Async XLA Ops:
  0.6 106.3 %copy-start = (bf16[1,2048,768]{2,1,0:T(8,128)(2,1)S(1)}, bf16[1,2048,768]{2,1,0:T(8,128)(2,1)}, u32[]{:S(2)}) copy-start(bf16[1,2048,768]{2,1,0:T(8,128)(2,1)} %param.31) | copy-start | bytes 9437188
  1.8 11.8 %copy-start.17 = (f32[16]{0:T(128)}, f32[16]{0:T(128)S(1)}, u32[]{:S(2)}) copy-start(f32[16]{0:T(128)S(1)} %add_rsqrt_fusion.1) | copy-start | bytes 196
  2.7 20.2 %collective-permute-start.1 = (bf16[16,2048]{1,0:T(8,128)(2,1)S(1)}, bf16[16,2048]{1,0:T(8,128)(2,1)}, u32[]{:S(2)}, u32[]{:S(2)}) collective-permute-start(bf16[16,2048]{1,0:T(8,128)(2,1)S(1)} %fusion.50), channel_id=1, source_target_pairs={{0,2},{1,3},{2,0},{3,1},{4,6},{5,7},{6,4},{7,5},{8,10},{9,11},{10,... | collective-permute-start | bytes 196616 | tf_op jit(solution)/shard_map/ppermute | solution.py:166
  6.8 16.1 %collective-permute-start = (bf16[16,2048]{1,0:T(8,128)(2,1)S(1)}, bf16[16,2048]{1,0:T(8,128)(2,1)}, u32[]{:S(2)}, u32[]{:S(2)}) collective-permute-start(bf16[16,2048]{1,0:T(8,128)(2,1)S(1)} %fusion.50), channel_id=1, source_target_pairs={{0,1},{1,2},{2,3},{3,0},{4,5},{5,6},{6,7},{7,4},{8,9},{9,10},{10,1... | collective-permute-start | bytes 196616 | tf_op jit(solution)/shard_map/ppermute | solution.py:166
  8.4 14.5 %collective-permute-start.2 = (bf16[16,2048]{1,0:T(8,128)(2,1)S(1)}, bf16[16,2048]{1,0:T(8,128)(2,1)}, u32[]{:S(2)}, u32[]{:S(2)}) collective-permute-start(bf16[16,2048]{1,0:T(8,128)(2,1)S(1)} %fusion.50), channel_id=1, source_target_pairs={{0,3},{1,0},{2,1},{3,2},{4,7},{5,4},{6,5},{7,6},{8,11},{9,8},{10,9... | collective-permute-start | bytes 196616 | tf_op jit(solution)/shard_map/ppermute | solution.py:166
  13.6 18.6 %copy-start.21 = (s32[1024]{0:T(1024)}, s32[1024]{0:T(1024)S(1)}, u32[]{:S(2)}) copy-start(s32[1024]{0:T(1024)S(1)} %pad_clamp_fusion.1) | copy-start | bytes 12292
  26.7 12.0 %copy-start.10 = (bf16[4,32,128]{2,1,0:T(8,128)(2,1)S(1)}, bf16[4,32,128]{2,1,0:T(8,128)(2,1)}, u32[]{:S(2)}) copy-start(bf16[4,32,128]{2,1,0:T(8,128)(2,1)} %get-tuple-element.43) | copy-start | bytes 98308
  28.0 4.8 %collective-permute-start.5 = (bf16[64,128]{1,0:T(8,128)(2,1)S(1)}, bf16[64,128]{1,0:T(8,128)(2,1)S(1)}, u32[]{:S(2)}, u32[]{:S(2)}) collective-permute-start(bf16[64,128]{1,0:T(8,128)(2,1)S(1)} %convolution_convert_fusion.6), channel_id=1, source_target_pairs={{0,3},{1,0},{2,1},{3,2},{4,7},{5,4},{6,5},{7,6},{8,11},{9,8},{10,9... | collective-permute-start | bytes 49160 | tf_op jit(solution)/shard_map/ppermute | solution.py:166
  28.1 4.8 %collective-permute-start.4 = (bf16[64,128]{1,0:T(8,128)(2,1)S(1)}, bf16[64,128]{1,0:T(8,128)(2,1)S(1)}, u32[]{:S(2)}, u32[]{:S(2)}) collective-permute-start(bf16[64,128]{1,0:T(8,128)(2,1)S(1)} %convolution_convert_fusion.6), channel_id=1, source_target_pairs={{0,2},{1,3},{2,0},{3,1},{4,6},{5,7},{6,4},{7,5},{8,10},{9,11},{10,... | collective-permute-start | bytes 49160 | tf_op jit(solution)/shard_map/ppermute | solution.py:166
  29.3 5.5 %collective-permute-start.3 = (bf16[64,128]{1,0:T(8,128)(2,1)S(1)}, bf16[64,128]{1,0:T(8,128)(2,1)S(1)}, u32[]{:S(2)}, u32[]{:S(2)}) collective-permute-start(bf16[64,128]{1,0:T(8,128)(2,1)S(1)} %convolution_convert_fusion.6), channel_id=1, source_target_pairs={{0,1},{1,2},{2,3},{3,0},{4,5},{5,6},{6,7},{7,4},{8,9},{9,10},{10,1... | collective-permute-start | bytes 49160 | tf_op jit(solution)/shard_map/ppermute | solution.py:166
  36.3 3.4 %copy-start.16 = (bf16[64,128]{1,0:T(8,128)(2,1)}, bf16[64,128]{1,0:T(8,128)(2,1)S(1)}, u32[]{:S(2)}) copy-start(bf16[64,128]{1,0:T(8,128)(2,1)S(1)} %get-tuple-element.36) | copy-start | bytes 49156
  36.3 7.4 %copy-start.12 = (bf16[64,128]{1,0:T(8,128)(2,1)}, bf16[64,128]{1,0:T(8,128)(2,1)S(1)}, u32[]{:S(2)}) copy-start(bf16[64,128]{1,0:T(8,128)(2,1)S(1)} %get-tuple-element.37) | copy-start | bytes 49156
  38.1 0.7 copy-start.24
  38.1 4.6 %copy-start.4 = (bf16[16,11,16,128]{3,0,2,1:T(8,128)(2,1)S(1)}, bf16[16,11,16,128]{3,0,2,1:T(8,128)(2,1)}, u32[]{:S(2)}) copy-start(bf16[16,11,16,128]{3,0,2,1:T(8,128)(2,1)} %convolution_convert_fusion) | copy-start | bytes 2162692
  39.7 39.0 %copy-start.5 = (bf16[16,2048]{1,0:T(8,128)(2,1)S(1)}, bf16[16,2048]{1,0:T(8,128)(2,1)}, u32[]{:S(2)}) copy-start(bf16[16,2048]{1,0:T(8,128)(2,1)} %param.18) | copy-start | bytes 196612
  39.7 40.2 %copy-start.14 = (f32[2048]{0:T(1024)S(1)}, f32[2048]{0:T(1024)}, u32[]{:S(2)}) copy-start(f32[2048]{0:T(1024)} %param.27) | copy-start | bytes 24580
  43.7 37.7 %all-to-all-start = ((bf16[16,176,128]{2,1,0:T(8,128)(2,1)}), bf16[16,176,128]{2,1,0:T(8,128)(2,1)}, u32[]{:S(2)}, u32[]{:S(2)}) async-start(bf16[16,176,128]{2,1,0:T(8,128)(2,1)} %copy.131), calls=%async_computation | async-start | bytes 1441792 | tf_op jit(solution)/shard_map/all_to_all | solution.py:212
  49.9 17.9 %collective-permute-start.6 = (f32[16,2048]{1,0:T(8,128)}, f32[16,2048]{1,0:T(8,128)}, u32[]{:S(2)}, u32[]{:S(2)}) collective-permute-start(f32[16,2048]{1,0:T(8,128)} %get-tuple-element.30), channel_id=1, source_target_pairs={{0,1},{1,2},{2,3},{3,0},{4,5},{5,6},{6,7},{7,4},{8,9},{9,10},{10,1... | collective-permute-start | bytes 393224 | tf_op jit(solution)/shard_map/ppermute | solution.py:203
  51.6 16.2 %collective-permute-start.8 = (f32[16,2048]{1,0:T(8,128)}, f32[16,2048]{1,0:T(8,128)}, u32[]{:S(2)}, u32[]{:S(2)}) collective-permute-start(f32[16,2048]{1,0:T(8,128)} %get-tuple-element.31), channel_id=1, source_target_pairs={{0,3},{1,0},{2,1},{3,2},{4,7},{5,4},{6,5},{7,6},{8,11},{9,8},{10,9... | collective-permute-start | bytes 393224 | tf_op jit(solution)/shard_map/ppermute | solution.py:203
  53.7 25.0 %collective-permute-start.7 = (f32[16,2048]{1,0:T(8,128)}, f32[16,2048]{1,0:T(8,128)}, u32[]{:S(2)}, u32[]{:S(2)}) collective-permute-start(f32[16,2048]{1,0:T(8,128)} %get-tuple-element.32), channel_id=1, source_target_pairs={{0,2},{1,3},{2,0},{3,1},{4,6},{5,7},{6,4},{7,5},{8,10},{9,11},{10,... | collective-permute-start | bytes 393224 | tf_op jit(solution)/shard_map/ppermute | solution.py:203
  54.8 33.8 %copy-start.9 = (pred[16,11,16]{2,1,0:T(8,128)(4,1)}, pred[16,11,16]{2,1,0:T(8,128)(4,1)S(1)}, u32[]{:S(2)}) copy-start(pred[16,11,16]{2,1,0:T(8,128)(4,1)S(1)} %compare_reduce_fusion) | copy-start | bytes 8452
  79.9 64.3 %copy-start.19 = (f32[16]{0:T(128)}, f32[16]{0:T(128)S(1)}, u32[]{:S(2)}) copy-start(f32[16]{0:T(128)S(1)} %add_rsqrt_fusion) | copy-start | bytes 196
  81.4 24.2 %all-to-all-start.1 = ((bf16[16,176,128]{2,1,0:T(8,128)(2,1)}), bf16[16,176,128]{2,1,0:T(8,128)(2,1)}, u32[]{:S(2)}, u32[]{:S(2)}) async-start(bf16[16,176,128]{2,1,0:T(8,128)(2,1)} %copy.136), calls=%async_computation.1 | async-start | bytes 1441792 | tf_op jit(solution)/shard_map/all_to_all | solution.py:212
  88.6 1.8 copy-start.3
  106.9 2.1 copy-start.1
  107.7 4.1 %copy-start.2 = (f32[16,11,768]{2,0,1:T(8,128)}, f32[16,11,768]{2,0,1:T(8,128)S(1)}, u32[]{:S(2)}) copy-start(f32[16,11,768]{2,0,1:T(8,128)S(1)} %convolution_bitcast_fusion.2) | copy-start | bytes 1622020
  109.0 1.6 copy-start.6
  109.8 0.8 copy-start.7
  114.0 24.2 %all-to-all-start.2 = ((bf16[16,176,128]{2,1,0:T(8,128)(2,1)}), bf16[16,176,128]{2,1,0:T(8,128)(2,1)}, u32[]{:S(2)}, u32[]{:S(2)}) async-start(bf16[16,176,128]{2,1,0:T(8,128)(2,1)} %copy.138), calls=%async_computation.2 | async-start | bytes 1441792 | tf_op jit(solution)/shard_map/all_to_all | solution.py:216
  118.5 24.0 %copy-start.15 = (f32[2048]{0:T(1024)S(1)}, f32[2048]{0:T(1024)}, u32[]{:S(2)}) copy-start(f32[2048]{0:T(1024)} %param.27) | copy-start | bytes 24580
  122.4 21.9 %copy-start.22 = (f32[16]{0:T(128)S(1)}, f32[16]{0:T(128)}, u32[]{:S(2)}) copy-start(f32[16]{0:T(128)} %convert_element_type.109) | copy-start | bytes 196
  144.3 3.6 %copy-start.23 = (f32[16]{0:T(128)}, f32[16]{0:T(128)S(1)}, u32[]{:S(2)}) copy-start(f32[16]{0:T(128)S(1)} %broadcast_multiply_fusion.1) | copy-start | bytes 196
  145.9 9.6 %collective-permute-start.11 = (bf16[16,2048]{1,0:T(8,128)(2,1)}, bf16[16,2048]{1,0:T(8,128)(2,1)}, u32[]{:S(2)}, u32[]{:S(2)}) collective-permute-start(bf16[16,2048]{1,0:T(8,128)(2,1)} %fusion.108), channel_id=1, source_target_pairs={{0,3},{1,0},{2,1},{3,2},{4,7},{5,4},{6,5},{7,6},{8,11},{9,8},{10,9... | collective-permute-start | bytes 196616 | tf_op jit(solution)/shard_map/ppermute | solution.py:321
  146.7 8.8 %collective-permute-start.10 = (bf16[16,2048]{1,0:T(8,128)(2,1)}, bf16[16,2048]{1,0:T(8,128)(2,1)}, u32[]{:S(2)}, u32[]{:S(2)}) collective-permute-start(bf16[16,2048]{1,0:T(8,128)(2,1)} %fusion.108), channel_id=1, source_target_pairs={{0,2},{1,3},{2,0},{3,1},{4,6},{5,7},{6,4},{7,5},{8,10},{9,11},{10,... | collective-permute-start | bytes 196616 | tf_op jit(solution)/shard_map/ppermute | solution.py:321
  146.9 8.6 %collective-permute-start.9 = (bf16[16,2048]{1,0:T(8,128)(2,1)}, bf16[16,2048]{1,0:T(8,128)(2,1)}, u32[]{:S(2)}, u32[]{:S(2)}) collective-permute-start(bf16[16,2048]{1,0:T(8,128)(2,1)} %fusion.108), channel_id=1, source_target_pairs={{0,1},{1,2},{2,3},{3,0},{4,5},{5,6},{6,7},{7,4},{8,9},{9,10},{10,1... | collective-permute-start | bytes 196616 | tf_op jit(solution)/shard_map/ppermute | solution.py:321
  150.1 16.8 %copy-start.13 = (bf16[64,128]{1,0:T(8,128)(2,1)S(1)}, bf16[64,128]{1,0:T(8,128)(2,1)}, u32[]{:S(2)}) copy-start(bf16[64,128]{1,0:T(8,128)(2,1)} %copy-done.12) | copy-start | bytes 49156
  150.1 30.6 %all-to-all-start.3 = ((bf16[16,176,128]{2,1,0:T(8,128)(2,1)}), bf16[16,176,128]{2,1,0:T(8,128)(2,1)}, u32[]{:S(2)}, u32[]{:S(2)}) async-start(bf16[16,176,128]{2,1,0:T(8,128)(2,1)} %copy.146), calls=%async_computation.3 | async-start | bytes 1441792 | tf_op jit(solution)/shard_map/all_to_all | solution.py:216
  182.2 12.4 %collective-permute-start.12 = (f32[64,128]{1,0:T(8,128)}, f32[64,128]{1,0:T(8,128)}, u32[]{:S(2)}, u32[]{:S(2)}) collective-permute-start(f32[64,128]{1,0:T(8,128)} %get-tuple-element.33), channel_id=1, source_target_pairs={{0,1},{1,2},{2,3},{3,0},{4,5},{5,6},{6,7},{7,4},{8,9},{9,10},{10,1... | collective-permute-start | bytes 98312 | tf_op jit(solution)/shard_map/ppermute | solution.py:203
  184.0 10.5 %collective-permute-start.14 = (f32[64,128]{1,0:T(8,128)}, f32[64,128]{1,0:T(8,128)}, u32[]{:S(2)}, u32[]{:S(2)}) collective-permute-start(f32[64,128]{1,0:T(8,128)} %get-tuple-element.34), channel_id=1, source_target_pairs={{0,3},{1,0},{2,1},{3,2},{4,7},{5,4},{6,5},{7,6},{8,11},{9,8},{10,9... | collective-permute-start | bytes 98312 | tf_op jit(solution)/shard_map/ppermute | solution.py:203
  186.0 8.5 %collective-permute-start.13 = (f32[64,128]{1,0:T(8,128)}, f32[64,128]{1,0:T(8,128)}, u32[]{:S(2)}, u32[]{:S(2)}) collective-permute-start(f32[64,128]{1,0:T(8,128)} %get-tuple-element.35), channel_id=1, source_target_pairs={{0,2},{1,3},{2,0},{3,1},{4,6},{5,7},{6,4},{7,5},{8,10},{9,11},{10,... | collective-permute-start | bytes 98312 | tf_op jit(solution)/shard_map/ppermute | solution.py:203
  190.2 21.3 %copy-start.11 = (f32[2048]{0:T(1024)S(1)}, f32[2048]{0:T(1024)}, u32[]{:S(2)}) copy-start(f32[2048]{0:T(1024)} %param.26) | copy-start | bytes 24580
  190.2 21.3 %copy-start.18 = (f32[16]{0:T(128)S(1)}, f32[16]{0:T(128)}, u32[]{:S(2)}) copy-start(f32[16]{0:T(128)} %copy-done.17) | copy-start | bytes 196
  192.4 19.4 %copy-start.20 = (f32[16]{0:T(128)S(1)}, f32[16]{0:T(128)}, u32[]{:S(2)}) copy-start(f32[16]{0:T(128)} %copy-done.19) | copy-start | bytes 196
  194.5 17.2 %copy-start.8 = (bf16[16,2048]{1,0:T(8,128)(2,1)S(1)}, bf16[16,2048]{1,0:T(8,128)(2,1)}, u32[]{:S(2)}) copy-start(bf16[16,2048]{1,0:T(8,128)(2,1)} %param.19) | copy-start | bytes 196612
  196.5 8.3 %collective-permute-start.15 = (f32[16,2048]{1,0:T(8,128)S(1)}, f32[16,2048]{1,0:T(8,128)S(1)}, u32[]{:S(2)}, u32[]{:S(2)}) collective-permute-start(f32[16,2048]{1,0:T(8,128)S(1)} %get-tuple-element.27), channel_id=1, source_target_pairs={{0,1},{1,2},{2,3},{3,0},{4,5},{5,6},{6,7},{7,4},{8,9},{9,10},{10,1... | collective-permute-start | bytes 393224 | tf_op jit(solution)/shard_map/ppermute | solution.py:203
  198.0 7.2 %collective-permute-start.17 = (f32[16,2048]{1,0:T(8,128)S(1)}, f32[16,2048]{1,0:T(8,128)S(1)}, u32[]{:S(2)}, u32[]{:S(2)}) collective-permute-start(f32[16,2048]{1,0:T(8,128)S(1)} %get-tuple-element.28), channel_id=1, source_target_pairs={{0,3},{1,0},{2,1},{3,2},{4,7},{5,4},{6,5},{7,6},{8,11},{9,8},{10,9... | collective-permute-start | bytes 393224 | tf_op jit(solution)/shard_map/ppermute | solution.py:203
  200.4 11.1 %collective-permute-start.16 = (f32[16,2048]{1,0:T(8,128)S(1)}, f32[16,2048]{1,0:T(8,128)S(1)}, u32[]{:S(2)}, u32[]{:S(2)}) collective-permute-start(f32[16,2048]{1,0:T(8,128)S(1)} %get-tuple-element.29), channel_id=1, source_target_pairs={{0,2},{1,3},{2,0},{3,1},{4,6},{5,7},{6,4},{7,5},{8,10},{9,11},{10,... | collective-permute-start | bytes 393224 | tf_op jit(solution)/shard_map/ppermute | solution.py:203

commit v17 on v15

--- a/solution.py
+++ b/solution.py
@@ -308,9 +308,9 @@
     )
     grad_back = grad_back.astype(jnp.bfloat16)
     grad_home = from_experts(grad_back.reshape(flat_shape)).reshape(split_shape)
-    grad_moe = jnp.einsum(
-        "dct,dckl->tkl", placement, grad_home, preferred_element_type=jnp.float32
-    ).reshape(owned, width)
+    slots = target.reshape(owned, TOP)
+    grad_picked = jnp.take(grad_home.reshape(slot_total, pieces, lanes), slots, axis=0)
+    grad_moe = jnp.sum(grad_picked.astype(jnp.float32), axis=1).reshape(owned, width)
     grad_hidden = cotangent + rms_backward(hidden, moe_gain, inverse_two, grad_moe)
     grad_low = grad_hidden.astype(jnp.bfloat16)
     count = lax.axis_size("head")
@@ -335,11 +335,9 @@
     input_grad = (
         grad_hidden + rms_backward(hidden_in, attn_gain, inverse_one, grad_attn_rows)
     ).astype(jnp.bfloat16)
-    moe_sum = jnp.einsum(
-        "dct,dckl->tkl",
-        weighting,
-        result_home.astype(jnp.float32),
-        precision=highest_prec,
+    result_picked = jnp.take(result_home.reshape(slot_total, pieces, lanes), slots, axis=0)
+    moe_sum = jnp.sum(
+        gate_weights[:, :, None, None] * result_picked.astype(jnp.float32), axis=1
     ).reshape(owned, width)
     layer_out = (hidden.astype(jnp.float32) + moe_sum).astype(jnp.bfloat16)
     return (layer_out, input_grad)

time: 193 us -> 195 us (1.010)
  other arithmetic: 14 us -> 17.6 us
  matrix products: 39.2 us -> 36.5 us
    gather x0 -> x2, local copies, waits for them, and re-layouts: none -> 5.22 us  [the longest x1 2.61 us: body(): jnp.take(result_home.reshape(slot_total, pieces, lanes), slots, axis=0)]
    dot_general x2 -> x0, local copies, waits for them, and re-layouts: 4.31 us -> none  [the longest x1 2.16 us: body(): jnp.einsum('dct,dckl->tkl', placement, grad_home, preferred_element_type=...]
    dot_general x2 -> x0, matrix products: 4.31 us -> none  [the longest x1 2.57 us: body(): jnp.einsum('dct,dckl->tkl', weighting, result_home.astype(jnp.float32), p...]
    reduce_sum x0 -> x2, other arithmetic: none -> 2.67 us  [the longest x1 1.41 us: body(): jnp.sum(gate_weights[:, :, None, None] * result_picked.astype(jnp.float32...]
    optimization_barrier x1 -> x0, local copies, waits for them, and re-layouts: 2.19 us -> none  [attention_backward(): placed, carried = lax.optimization_barrier((placed, carried))]
    reshape x2 -> x1, local copies, waits for them, and re-layouts: 3.21 us -> 1.06 us  [body(): grad_home = from_experts(grad_back.reshape(flat_shape)).reshape(split_shape)]
    unnamed x68 -> x71, local copies, waits for them, and re-layouts: 7.37 us -> 8.09 us
  transfers between devices with their start and end apart: 22 -> 22, of which waited for: 10 -> 9; matrix products, arithmetic and copies ran while one was open for 35% -> 37% of each run, Pallas kernels for 0% -> 0%
where the time goes in v17:
time: 195 us; the launch traced here: 193 us
  waiting for transfers between devices  54.2 us (28%)
  starting transfers between devices  45.6 us (23%)
  local copies, waits for them, and re-layouts  37.8 us (19%)
  matrix products  36.5 us (19%)
  other arithmetic  17.6 us (9%)
    ppermute x9, waiting for transfers between devices, head_sums(): lax.ppermute(chunk((me + shift) % count), 'head', perm=[(j, (j + shift) %...  19 us
    all_to_all x2, waiting for transfers between devices, from_experts(): lax.all_to_all(results, ('expert', 'head'), split_axis=0, concat_axis=0,...  15.6 us
    all_to_all x2, waiting for transfers between devices, to_experts(): lax.all_to_all(outgoing, ('expert', 'head'), split_axis=0, concat_axis=0,...  13.1 us
    ppermute x9, starting transfers between devices, head_sums(): lax.ppermute(chunk((me + shift) % count), 'head', perm=[(j, (j + shift) %...  12.7 us
    ppermute x6, starting transfers between devices, head_gather(): lax.ppermute(block, 'head', perm=[(j, (j + shift) % count) for j in range...  12.6 us
    all_to_all x2, starting transfers between devices, from_experts(): lax.all_to_all(results, ('expert', 'head'), split_axis=0, concat_axis=0,...  9.67 us
    all_to_all x2, starting transfers between devices, to_experts(): lax.all_to_all(outgoing, ('expert', 'head'), split_axis=0, concat_axis=0,...  8.54 us
    unnamed x71, local copies, waits for them, and re-layouts  8.09 us
  transfers between devices with their start and end apart: 22, of which 9 were waited for; matrix products, arithmetic and copies ran while one was open for 37% of the time, Pallas kernels for 0%

profile of v17, /device:TPU:0, one launch (start us, length us, event | category | flops | bytes accessed | tf_op | source)
XLA Modules:
  0.0 193.0 jit_solution(14172300987634194705)
XLA Ops:
  2.7 4.1 %collective-permute-start.1 = (bf16[16,2048]{1,0:T(8,128)(2,1)S(1)}, bf16[16,2048]{1,0:T(8,128)(2,1)}, u32[]{:S(2)}, u32[]{:S(2)}) collective-permute-start(bf16[16,2048]{1,0:T(8,128)(2,1)S(1)} %fusion.45), channel_id=1, source_target_pairs={{0,2},{1,3},{2,0},{3,1},{4,6},{5,7},{6,4},{7,5},{8,10},{9,11},{10,... | collective-permute-start | bytes 196616 | tf_op jit(solution)/shard_map/ppermute | solution.py:166
  6.8 1.6 collective-permute-start
  8.4 2.2 %collective-permute-start.2 = (bf16[16,2048]{1,0:T(8,128)(2,1)S(1)}, bf16[16,2048]{1,0:T(8,128)(2,1)}, u32[]{:S(2)}, u32[]{:S(2)}) collective-permute-start(bf16[16,2048]{1,0:T(8,128)(2,1)S(1)} %fusion.45), channel_id=1, source_target_pairs={{0,3},{1,0},{2,1},{3,2},{4,7},{5,4},{6,5},{7,6},{8,11},{9,8},{10,9... | collective-permute-start | bytes 196616 | tf_op jit(solution)/shard_map/ppermute | solution.py:166
  14.4 2.2 %convolution_convert_fusion = bf16[16,11,16,128]{3,0,2,1:T(8,128)(2,1)S(1)} fusion(f32[16,11,16,1]{2,1,0,3:T(8,128)S(1)} %bitcast.204, bf16[16,2048]{1,0:T(8,128)(2,1)} %param.21, f32[16]{0:T(128)S(1)} %convert_element_type.115), kind=kOutput, calls=%fused_computation.16 | convolution fusion | flops 69632000 | bytes 797760 | tf_op jit(solution)/shard_map/dct,tkl->dckl/dot_general | solution.py:276
  17.6 4.3 %all-to-all-start = ((bf16[16,176,128]{2,1,0:T(8,128)(2,1)}), bf16[16,176,128]{2,1,0:T(8,128)(2,1)}, u32[]{:S(2)}, u32[]{:S(2)}) async-start(bf16[16,176,128]{2,1,0:T(8,128)(2,1)} %copy.77), calls=%async_computation | async-start | bytes 1441792 | tf_op jit(solution)/shard_map/all_to_all | solution.py:212
  23.4 1.4 constant_dynamic-slice_fusion.10
  24.9 1.7 pad_maximum_fusion
  26.5 1.5 gather_fusion.1
  29.4 3.6 %collective-permute-start.5 = (bf16[64,128]{1,0:T(8,128)(2,1)S(1)}, bf16[64,128]{1,0:T(8,128)(2,1)S(1)}, u32[]{:S(2)}, u32[]{:S(2)}) collective-permute-start(bf16[64,128]{1,0:T(8,128)(2,1)S(1)} %convolution_convert_fusion.6), channel_id=1, source_target_pairs={{0,3},{1,0},{2,1},{3,2},{4,7},{5,4},{6,5},{7,6},{8,11},{9,8},{10,9... | collective-permute-start | bytes 49160 | tf_op jit(solution)/shard_map/ppermute | solution.py:166
  34.1 2.1 %convolution_convert_fusion.5 = bf16[64,512]{1,0:T(8,128)(2,1)S(1)} fusion(bf16[64,2048]{1,0:T(8,128)(2,1)S(1)} %bitcast.196, bf16[2048,512]{1,0:T(8,128)(2,1)} %param.30), kind=kOutput, calls=%fused_computation.37 | convolution fusion | flops 134250496 | bytes 2424832 | tf_op jit(solution)/shard_map/dot_general | solution.py:82
  36.3 6.4 %collective-permute-done.4 = bf16[64,128]{1,0:T(8,128)(2,1)S(1)} collective-permute-done((bf16[64,128]{1,0:T(8,128)(2,1)S(1)}, bf16[64,128]{1,0:T(8,128)(2,1)S(1)}, u32[]{:S(2)}, u32[]{:S(2)}) %collective-permute-start.4) | collective-permute-done | bytes 16416 | tf_op jit(solution)/shard_map/ppermute | solution.py:166
  44.2 1.6 fusion.106
  46.7 2.1 %fusion.63 = f32[64,2048]{1,0:T(8,128)S(1)} fusion(bf16[512,2048]{1,0:T(8,128)(2,1)} %param.32, bf16[8,8,4,128]{3,2,1,0:T(4,128)(2,1)S(1)} %bitcast.207), kind=kOutput, calls=%fused_computation.100 | convolution fusion | flops 134217728 | bytes 2686976 | tf_op jit(solution)/shard_map/dot_general | solution.py:248
  50.7 3.4 %collective-permute-start.8 = (f32[16,2048]{1,0:T(8,128)}, f32[16,2048]{1,0:T(8,128)S(1)}, u32[]{:S(2)}, u32[]{:S(2)}) collective-permute-start(f32[16,2048]{1,0:T(8,128)} %get-tuple-element.30), channel_id=1, source_target_pairs={{0,3},{1,0},{2,1},{3,2},{4,7},{5,4},{6,5},{7,6},{8,11},{9,8},{10,9... | collective-permute-start | bytes 393224 | tf_op jit(solution)/shard_map/ppermute | solution.py:203
  55.2 3.6 %collective-permute-done.6 = f32[16,2048]{1,0:T(8,128)S(1)} collective-permute-done((f32[16,2048]{1,0:T(8,128)}, f32[16,2048]{1,0:T(8,128)S(1)}, u32[]{:S(2)}, u32[]{:S(2)}) %collective-permute-start.6) | collective-permute-done | bytes 131104 | tf_op jit(solution)/shard_map/ppermute | solution.py:203
  59.4 5.3 %collective-permute-done.7 = f32[16,2048]{1,0:T(8,128)} collective-permute-done((f32[16,2048]{1,0:T(8,128)}, f32[16,2048]{1,0:T(8,128)}, u32[]{:S(2)}, u32[]{:S(2)}) %collective-permute-start.7) | collective-permute-done | bytes 131104 | tf_op jit(solution)/shard_map/ppermute | solution.py:203
  67.3 4.3 %all-to-all-start.1 = ((bf16[16,176,128]{2,1,0:T(8,128)(2,1)}), bf16[16,176,128]{2,1,0:T(8,128)(2,1)}, u32[]{:S(2)}, u32[]{:S(2)}) async-start(bf16[16,176,128]{2,1,0:T(8,128)(2,1)} %copy.82), calls=%async_computation.1 | async-start | bytes 1441792 | tf_op jit(solution)/shard_map/all_to_all | solution.py:212
  71.6 2.9 %copy.111 = bf16[96,8,16,128]{3,2,1,0:T(8,128)(2,1)S(1)} copy(bf16[96,8,16,128]{3,1,2,0:T(8,128)(2,1)} %bitcast.189) | data formatting | bytes 6291456
  74.5 1.8 copy.78
  76.3 2.0 %fusion.12 = f32[16,11,768]{2,0,1:T(8,128)} fusion(bf16[16,11,16,128]{3,0,2,1:T(8,128)(2,1)S(1)} %bitcast.202, bf16[768,16,128]{2,1,0:T(8,128)(2,1)S(1)} %bitcast.190), kind=kOutput, calls=%fused_computation.19 | convolution fusion | flops 553648128 | bytes 4407296 | tf_op jit(solution)/shard_map/sckl,fkl->scf/dot_general | solution.py:298
  78.3 13.1 %all-to-all-done.1 = bf16[16,176,128]{2,1,0:T(8,128)(2,1)} async-done(((bf16[16,176,128]{2,1,0:T(8,128)(2,1)}), bf16[16,176,128]{2,1,0:T(8,128)(2,1)}, u32[]{:S(2)}, u32[]{:S(2)}) %all-to-all-start.1) | async-done | bytes 720928 | tf_op jit(solution)/shard_map/all_to_all | solution.py:212
  99.9 4.5 %all-to-all-start.2 = ((bf16[16,176,128]{2,1,0:T(8,128)(2,1)}), bf16[16,176,128]{2,1,0:T(8,128)(2,1)}, u32[]{:S(2)}, u32[]{:S(2)}) async-start(bf16[16,176,128]{2,1,0:T(8,128)(2,1)} %copy.84), calls=%async_computation.2 | async-start | bytes 1441792 | tf_op jit(solution)/shard_map/all_to_all | solution.py:216
  104.5 3.9 %fusion.8 = bf16[16,11,16,128]{3,0,2,1:T(8,128)(2,1)} fusion(bf16[768,16,128]{2,1,0:T(8,128)(2,1)} %bitcast.191, f32[16,11,768]{2,0,1:T(8,128)} %copy-done.6, f32[16,11,768]{2,0,1:T(8,128)} %copy-done.2), kind=kOutput, calls=%fused_computation.15 | convolution fusion | flops 554819584 | bytes 4947968 | tf_op jit(solution)/shard_map/scf,fkl->sckl/dot_general | solution.py:295
  108.4 15.6 %all-to-all-done.2 = bf16[16,176,128]{2,1,0:T(8,128)(2,1)} async-done(((bf16[16,176,128]{2,1,0:T(8,128)(2,1)}), bf16[16,176,128]{2,1,0:T(8,128)(2,1)}, u32[]{:S(2)}, u32[]{:S(2)}) %all-to-all-start.2) | async-done | bytes 720928 | tf_op jit(solution)/shard_map/all_to_all | solution.py:216
  124.0 2.6 %gather_fusion.2 = bf16[128,16,128]{2,1,0:T(8,128)(2,1)} fusion(bf16[176,16,128]{2,1,0:T(8,128)(2,1)} %bitcast.45, s32[1024]{0:T(1024)S(1)} %pad_clamp_fusion), kind=kCustom, calls=%fused_computation.1.clone | custom fusion | bytes 1049088 | tf_op jit(solution)/shard_map/jit(_take)/gather | solution.py:312
  131.0 1.3 copy.71
  132.4 2.2 %copy.89 = bf16[16,176,128]{2,1,0:T(8,128)(2,1)} copy(bf16[16,176,128]{2,0,1:T(8,128)(2,1)} %bitcast.201) | data formatting | bytes 1441792 | tf_op jit(solution)/shard_map/reshape | solution.py:322
  134.6 5.2 %all-to-all-start.3 = ((bf16[16,176,128]{2,1,0:T(8,128)(2,1)}), bf16[16,176,128]{2,1,0:T(8,128)(2,1)}, u32[]{:S(2)}, u32[]{:S(2)}) async-start(bf16[16,176,128]{2,1,0:T(8,128)(2,1)} %copy.89), calls=%async_computation.3 | async-start | bytes 1441792 | tf_op jit(solution)/shard_map/all_to_all | solution.py:216
  139.8 1.6 pad_maximum_fusion.1
  141.5 2.3 %gather_fusion.3 = bf16[4,16,2048]{2,1,0:T(8,128)(2,1)} fusion(bf16[4,16,2048]{2,1,0:T(8,128)(2,1)} %pad_maximum_fusion.1, s32[1024]{0:T(1024)} %copy-done.26), kind=kCustom, calls=%fused_computation.2.clone | custom fusion | bytes 524304 | tf_op jit(solution)/shard_map/jit(_take)/gather | solution.py:176
  144.9 2.3 %convolution_convert_fusion.3 = bf16[64,512]{1,0:T(8,128)(2,1)S(1)} fusion(bf16[64,2048]{1,0:T(8,128)(2,1)S(1)} %bitcast.200, bf16[512,2048]{1,0:T(8,128)(2,1)} %param.32), kind=kOutput, calls=%fused_computation.35 | convolution fusion | flops 134250496 | bytes 2424832 | tf_op jit(solution)/shard_map/td,fd->tf/dot_general | solution.py:132
  149.7 1.7 convolution_bitcast_fusion.2
  151.4 3.0 %convolution_bitcast_fusion.4 = f32[4,48,128]{2,1,0:T(8,128)} fusion(f32[4,4,16,48]{3,2,1,0:T(8,128)} %convolution_bitcast_fusion.2, bf16[4,16,4,128]{3,2,1,0:T(4,128)(2,1)} %copy-done.15, f32[4,4,16,48]{3,2,1,0:T(8,128)} %copy-done.33, f32[4,4,16]{2,1,0:T(4,128)} %get-tuple-element.39), kind=kOutput, calls=%fused_computation.34 | convolution fusion | flops 3232047 | bytes 263168 | tf_op jit(solution)/shard_map/shbk,sbhd->skd/dot_general | solution.py:58
  154.4 1.4 slice.18
  155.8 2.9 %fusion.24 = bf16[4,16,4,128]{3,1,2,0:T(8,128)(2,1)} fusion(f32[4,4,16,48]{3,2,1,0:T(8,128)} %convolution_bitcast_fusion.2, bf16[4,16,128]{2,1,0:T(8,128)(2,1)} %bitcast.215, bf16[4,32,128]{2,1,0:T(8,128)(2,1)} %get-tuple-element.41, f32[4,4,16,48]{3,2,1,0:T(8,128)} %copy-done.33, f32[4,4,16]{2,1,0:T(4,128)} %get-tuple-element.39), kind=kOutput, calls=%fused_computation.39 | convolution fusion | flops 3363119 | bytes 214016 | tf_op jit(solution)/shard_map/shbk,skd->sbhd/dot_general | solution.py:55
  160.2 1.4 constant_dynamic-update-slice_fusion.1
  161.6 1.4 constant_dynamic-update-slice_fusion
  163.0 1.4 constant_dynamic-slice_fusion.5
  164.4 1.9 collective-permute-start.12
  166.3 2.0 %collective-permute-start.14 = (f32[64,128]{1,0:T(8,128)}, f32[64,128]{1,0:T(8,128)}, u32[]{:S(2)}, u32[]{:S(2)}) collective-permute-start(f32[64,128]{1,0:T(8,128)} %get-tuple-element.33), channel_id=1, source_target_pairs={{0,3},{1,0},{2,1},{3,2},{4,7},{5,4},{6,5},{7,6},{8,11},{9,8},{10,9... | collective-permute-start | bytes 98312 | tf_op jit(solution)/shard_map/ppermute | solution.py:203
  169.2 3.1 %fusion.60 = f32[64,2048]{1,0:T(8,128)} fusion(bf16[2048,512]{1,0:T(8,128)(2,1)} %param.30, bf16[8,8,4,128]{3,2,1,0:T(4,128)(2,1)S(1)} %bitcast.206), kind=kOutput, calls=%fused_computation.97 | convolution fusion | flops 134217728 | bytes 2686976 | tf_op jit(solution)/shard_map/tf,df->td/dot_general | solution.py:156
  172.4 2.6 %gather_fusion.4 = bf16[128,16,128]{2,1,0:T(8,128)(2,1)} fusion(bf16[176,16,128]{2,1,0:T(8,128)(2,1)} %bitcast.64, s32[1024]{0:T(1024)S(1)} %pad_clamp_fusion), kind=kCustom, calls=%fused_computation.3.clone | custom fusion | bytes 1049088 | tf_op jit(solution)/shard_map/jit(_take)/gather | solution.py:338
  175.0 1.9 %convolution_add_fusion = f32[64,2048]{1,0:T(8,128)S(1)} fusion(f32[64,2048]{1,0:T(8,128)} %fusion.60, bf16[2048,128]{1,0:T(8,128)(2,1)} %param.31, f32[64,128]{1,0:T(8,128)} %collective-permute-done.14, f32[64,128]{1,0:T(8,128)} %collective-permute-done.13, f32[64,128]{1,0:T(8,128)} %collective-permute-done.12, ...), kind=kOutput, calls=%fused_computation.13 | convolution fusion | flops 201482240 | bytes 1703940 | tf_op jit(solution)/shard_map/tc,dc->td/dot_general | solution.py:152
  177.0 1.5 collective-permute-start.15
  178.5 2.4 %collective-permute-start.17 = (f32[16,2048]{1,0:T(8,128)S(1)}, f32[16,2048]{1,0:T(8,128)S(1)}, u32[]{:S(2)}, u32[]{:S(2)}) collective-permute-start(f32[16,2048]{1,0:T(8,128)S(1)} %get-tuple-element.27), channel_id=1, source_target_pairs={{0,3},{1,0},{2,1},{3,2},{4,7},{5,4},{6,5},{7,6},{8,11},{9,8},{10,9... | collective-permute-start | bytes 393224 | tf_op jit(solution)/shard_map/ppermute | solution.py:203
  181.0 1.4 multiply_reduce_fusion
  182.4 2.9 %collective-permute-done.15 = f32[16,2048]{1,0:T(8,128)S(1)} collective-permute-done((f32[16,2048]{1,0:T(8,128)S(1)}, f32[16,2048]{1,0:T(8,128)S(1)}, u32[]{:S(2)}, u32[]{:S(2)}) %collective-permute-start.15) | collective-permute-done | bytes 131104 | tf_op jit(solution)/shard_map/ppermute | solution.py:203
  185.7 6.2 %collective-permute-done.16 = f32[16,2048]{1,0:T(8,128)S(1)} collective-permute-done((f32[16,2048]{1,0:T(8,128)S(1)}, f32[16,2048]{1,0:T(8,128)S(1)}, u32[]{:S(2)}, u32[]{:S(2)}) %collective-permute-start.16) | collective-permute-done | bytes 131104 | tf_op jit(solution)/shard_map/ppermute | solution.py:203
  (153 shorter events, 39.8 us)
Async XLA Ops:
  0.6 92.1 %copy-start = (bf16[1,2048,768]{2,1,0:T(8,128)(2,1)S(1)}, bf16[1,2048,768]{2,1,0:T(8,128)(2,1)}, u32[]{:S(2)}) copy-start(bf16[1,2048,768]{2,1,0:T(8,128)(2,1)} %param.33) | copy-start | bytes 9437188
  0.6 21.4 %copy-start.4 = (bf16[16,2048]{1,0:T(8,128)(2,1)S(1)}, bf16[16,2048]{1,0:T(8,128)(2,1)}, u32[]{:S(2)}) copy-start(bf16[16,2048]{1,0:T(8,128)(2,1)} %param.20) | copy-start | bytes 196612
  0.7 21.4 %copy-start.11 = (f32[2048]{0:T(1024)S(1)}, f32[2048]{0:T(1024)}, u32[]{:S(2)}) copy-start(f32[2048]{0:T(1024)} %param.28) | copy-start | bytes 24580
  0.7 21.5 %copy-start.32 = (s32[4]{0:T(128)S(1)}, s32[4]{0:T(128)}, u32[]{:S(2)}) copy-start(s32[4]{0:T(128)} %param.25) | copy-start | bytes 52
  1.8 23.0 %copy-start.22 = (f32[16]{0:T(128)}, f32[16]{0:T(128)S(1)}, u32[]{:S(2)}) copy-start(f32[16]{0:T(128)S(1)} %add_rsqrt_fusion.1) | copy-start | bytes 196
  2.7 22.1 %collective-permute-start.1 = (bf16[16,2048]{1,0:T(8,128)(2,1)S(1)}, bf16[16,2048]{1,0:T(8,128)(2,1)}, u32[]{:S(2)}, u32[]{:S(2)}) collective-permute-start(bf16[16,2048]{1,0:T(8,128)(2,1)S(1)} %fusion.45), channel_id=1, source_target_pairs={{0,2},{1,3},{2,0},{3,1},{4,6},{5,7},{6,4},{7,5},{8,10},{9,11},{10,... | collective-permute-start | bytes 196616 | tf_op jit(solution)/shard_map/ppermute | solution.py:166
  6.8 18.0 %collective-permute-start = (bf16[16,2048]{1,0:T(8,128)(2,1)S(1)}, bf16[16,2048]{1,0:T(8,128)(2,1)}, u32[]{:S(2)}, u32[]{:S(2)}) collective-permute-start(bf16[16,2048]{1,0:T(8,128)(2,1)S(1)} %fusion.45), channel_id=1, source_target_pairs={{0,1},{1,2},{2,3},{3,0},{4,5},{5,6},{6,7},{7,4},{8,9},{9,10},{10,1... | collective-permute-start | bytes 196616 | tf_op jit(solution)/shard_map/ppermute | solution.py:166
  8.4 16.4 %collective-permute-start.2 = (bf16[16,2048]{1,0:T(8,128)(2,1)S(1)}, bf16[16,2048]{1,0:T(8,128)(2,1)}, u32[]{:S(2)}, u32[]{:S(2)}) collective-permute-start(bf16[16,2048]{1,0:T(8,128)(2,1)S(1)} %fusion.45), channel_id=1, source_target_pairs={{0,3},{1,0},{2,1},{3,2},{4,7},{5,4},{6,5},{7,6},{8,11},{9,8},{10,9... | collective-permute-start | bytes 196616 | tf_op jit(solution)/shard_map/ppermute | solution.py:166
  11.3 13.5 %copy-start.27 = (f32[16]{0:T(128)}, f32[16]{0:T(128)S(1)}, u32[]{:S(2)}) copy-start(f32[16]{0:T(128)S(1)} %convert_element_type.115) | copy-start | bytes 196
  12.5 10.9 %copy-start.20 = (bf16[4,32,256]{2,1,0:T(8,128)(2,1)S(1)}, bf16[4,32,256]{2,1,0:T(8,128)(2,1)}, u32[]{:S(2)}) copy-start(bf16[4,32,256]{2,1,0:T(8,128)(2,1)} %param.26) | copy-start | bytes 196612
  13.3 8.6 %copy-start.13 = (s32[16,8]{1,0:T(8,128)}, s32[16,8]{1,0:T(8,128)S(1)}, u32[]{:S(2)}) copy-start(s32[16,8]{1,0:T(8,128)S(1)} %get-tuple-element.23) | copy-start | bytes 1540
  13.4 11.4 %copy-start.17 = (s32[16,8]{0,1:T(8,128)}, s32[16,8]{0,1:T(8,128)S(1)}, u32[]{:S(2)}) copy-start(s32[16,8]{0,1:T(8,128)S(1)} %copy.74) | copy-start | bytes 1540
  17.6 49.6 %all-to-all-start = ((bf16[16,176,128]{2,1,0:T(8,128)(2,1)}), bf16[16,176,128]{2,1,0:T(8,128)(2,1)}, u32[]{:S(2)}, u32[]{:S(2)}) async-start(bf16[16,176,128]{2,1,0:T(8,128)(2,1)} %copy.77), calls=%async_computation | async-start | bytes 1441792 | tf_op jit(solution)/shard_map/all_to_all | solution.py:212
  22.2 5.9 %copy-start.26 = (s32[1024]{0:T(1024)}, s32[1024]{0:T(1024)S(1)}, u32[]{:S(2)}) copy-start(s32[1024]{0:T(1024)S(1)} %pad_clamp_fusion.2) | copy-start | bytes 12292
  24.8 21.9 %copy-start.10 = (bf16[4,32,128]{2,1,0:T(8,128)(2,1)}, bf16[4,32,128]{2,1,0:T(8,128)(2,1)S(1)}, u32[]{:S(2)}) copy-start(bf16[4,32,128]{2,1,0:T(8,128)(2,1)S(1)} %get-tuple-element.42) | copy-start | bytes 98308
  28.1 16.0 %copy-start.19 = (bf16[4,32,128]{2,1,0:T(8,128)(2,1)S(1)}, bf16[4,32,128]{2,1,0:T(8,128)(2,1)}, u32[]{:S(2)}) copy-start(bf16[4,32,128]{2,1,0:T(8,128)(2,1)} %get-tuple-element.41) | copy-start | bytes 98308
  29.4 6.8 %collective-permute-start.5 = (bf16[64,128]{1,0:T(8,128)(2,1)S(1)}, bf16[64,128]{1,0:T(8,128)(2,1)S(1)}, u32[]{:S(2)}, u32[]{:S(2)}) collective-permute-start(bf16[64,128]{1,0:T(8,128)(2,1)S(1)} %convolution_convert_fusion.6), channel_id=1, source_target_pairs={{0,3},{1,0},{2,1},{3,2},{4,7},{5,4},{6,5},{7,6},{8,11},{9,8},{10,9... | collective-permute-start | bytes 49160 | tf_op jit(solution)/shard_map/ppermute | solution.py:166
  33.0 9.6 %collective-permute-start.4 = (bf16[64,128]{1,0:T(8,128)(2,1)S(1)}, bf16[64,128]{1,0:T(8,128)(2,1)S(1)}, u32[]{:S(2)}, u32[]{:S(2)}) collective-permute-start(bf16[64,128]{1,0:T(8,128)(2,1)S(1)} %convolution_convert_fusion.6), channel_id=1, source_target_pairs={{0,2},{1,3},{2,0},{3,1},{4,6},{5,7},{6,4},{7,5},{8,10},{9,11},{10,... | collective-permute-start | bytes 49160 | tf_op jit(solution)/shard_map/ppermute | solution.py:166
  33.0 9.6 %collective-permute-start.3 = (bf16[64,128]{1,0:T(8,128)(2,1)S(1)}, bf16[64,128]{1,0:T(8,128)(2,1)S(1)}, u32[]{:S(2)}, u32[]{:S(2)}) collective-permute-start(bf16[64,128]{1,0:T(8,128)(2,1)S(1)} %convolution_convert_fusion.6), channel_id=1, source_target_pairs={{0,1},{1,2},{2,3},{3,0},{4,5},{5,6},{6,7},{7,4},{8,9},{9,10},{10,1... | collective-permute-start | bytes 49160 | tf_op jit(solution)/shard_map/ppermute | solution.py:166
  36.2 29.6 %copy-start.9 = (f32[2048]{0:T(1024)S(1)}, f32[2048]{0:T(1024)}, u32[]{:S(2)}) copy-start(f32[2048]{0:T(1024)} %param.29) | copy-start | bytes 24580
  36.2 23.1 %copy-start.15 = (bf16[4,16,4,128]{3,2,1,0:T(4,128)(2,1)}, bf16[4,16,4,128]{3,2,1,0:T(4,128)(2,1)S(1)}, u32[]{:S(2)}) copy-start(bf16[4,16,4,128]{3,2,1,0:T(4,128)(2,1)S(1)} %reshape.202) | copy-start | bytes 196612
  44.1 6.6 %copy-start.16 = (bf16[64,128]{1,0:T(8,128)(2,1)}, bf16[64,128]{1,0:T(8,128)(2,1)S(1)}, u32[]{:S(2)}) copy-start(bf16[64,128]{1,0:T(8,128)(2,1)S(1)} %get-tuple-element.38) | copy-start | bytes 49156
  44.1 6.6 %copy-start.21 = (bf16[64,128]{1,0:T(8,128)(2,1)}, bf16[64,128]{1,0:T(8,128)(2,1)S(1)}, u32[]{:S(2)}) copy-start(bf16[64,128]{1,0:T(8,128)(2,1)S(1)} %get-tuple-element.37) | copy-start | bytes 49156
  45.7 4.6 %copy-start.33 = (f32[4,4,16,48]{3,2,1,0:T(8,128)}, f32[4,4,16,48]{3,2,1,0:T(8,128)S(1)}, u32[]{:S(2)}) copy-start(f32[4,4,16,48]{3,2,1,0:T(8,128)S(1)} %get-tuple-element.40) | copy-start | bytes 147460
  50.3 8.4 %collective-permute-start.6 = (f32[16,2048]{1,0:T(8,128)}, f32[16,2048]{1,0:T(8,128)S(1)}, u32[]{:S(2)}, u32[]{:S(2)}) collective-permute-start(f32[16,2048]{1,0:T(8,128)} %get-tuple-element.29), channel_id=1, source_target_pairs={{0,1},{1,2},{2,3},{3,0},{4,5},{5,6},{6,7},{7,4},{8,9},{9,10},{10,1... | collective-permute-start | bytes 393224 | tf_op jit(solution)/shard_map/ppermute | solution.py:203
  50.7 8.6 %collective-permute-start.8 = (f32[16,2048]{1,0:T(8,128)}, f32[16,2048]{1,0:T(8,128)S(1)}, u32[]{:S(2)}, u32[]{:S(2)}) collective-permute-start(f32[16,2048]{1,0:T(8,128)} %get-tuple-element.30), channel_id=1, source_target_pairs={{0,3},{1,0},{2,1},{3,2},{4,7},{5,4},{6,5},{7,6},{8,11},{9,8},{10,9... | collective-permute-start | bytes 393224 | tf_op jit(solution)/shard_map/ppermute | solution.py:203
  54.2 10.5 %collective-permute-start.7 = (f32[16,2048]{1,0:T(8,128)}, f32[16,2048]{1,0:T(8,128)}, u32[]{:S(2)}, u32[]{:S(2)}) collective-permute-start(f32[16,2048]{1,0:T(8,128)} %get-tuple-element.31), channel_id=1, source_target_pairs={{0,2},{1,3},{2,0},{3,1},{4,6},{5,7},{6,4},{7,5},{8,10},{9,11},{10,... | collective-permute-start | bytes 393224 | tf_op jit(solution)/shard_map/ppermute | solution.py:203
  65.8 62.1 %copy-start.24 = (f32[16]{0:T(128)}, f32[16]{0:T(128)S(1)}, u32[]{:S(2)}) copy-start(f32[16]{0:T(128)S(1)} %add_rsqrt_fusion) | copy-start | bytes 196
  67.3 24.2 %all-to-all-start.1 = ((bf16[16,176,128]{2,1,0:T(8,128)(2,1)}), bf16[16,176,128]{2,1,0:T(8,128)(2,1)}, u32[]{:S(2)}, u32[]{:S(2)}) async-start(bf16[16,176,128]{2,1,0:T(8,128)(2,1)} %copy.82), calls=%async_computation.1 | async-start | bytes 1441792 | tf_op jit(solution)/shard_map/all_to_all | solution.py:212
  97.6 6.7 %copy-start.18 = (s32[16,8]{1,0:T(8,128)S(1)}, s32[16,8]{1,0:T(8,128)}, u32[]{:S(2)}) copy-start(s32[16,8]{1,0:T(8,128)} %get-tuple-element.22) | copy-start | bytes 1540
  97.6 6.8 %copy-start.14 = (s32[16,8]{1,0:T(8,128)S(1)}, s32[16,8]{1,0:T(8,128)}, u32[]{:S(2)}) copy-start(s32[16,8]{1,0:T(8,128)} %copy-done.13) | copy-start | bytes 1540
  99.9 24.2 %all-to-all-start.2 = ((bf16[16,176,128]{2,1,0:T(8,128)(2,1)}), bf16[16,176,128]{2,1,0:T(8,128)(2,1)}, u32[]{:S(2)}, u32[]{:S(2)}) async-start(bf16[16,176,128]{2,1,0:T(8,128)(2,1)} %copy.84), calls=%async_computation.2 | async-start | bytes 1441792 | tf_op jit(solution)/shard_map/all_to_all | solution.py:216
  104.5 23.7 %copy-start.8 = (bf16[16,2048]{1,0:T(8,128)(2,1)S(1)}, bf16[16,2048]{1,0:T(8,128)(2,1)}, u32[]{:S(2)}) copy-start(bf16[16,2048]{1,0:T(8,128)(2,1)} %param.21) | copy-start | bytes 196612
  128.9 10.9 %collective-permute-start.11 = (bf16[16,2048]{1,0:T(8,128)(2,1)S(1)}, bf16[16,2048]{1,0:T(8,128)(2,1)}, u32[]{:S(2)}, u32[]{:S(2)}) collective-permute-start(bf16[16,2048]{1,0:T(8,128)(2,1)S(1)} %fusion.104), channel_id=1, source_target_pairs={{0,3},{1,0},{2,1},{3,2},{4,7},{5,4},{6,5},{7,6},{8,11},{9,8},{10,9... | collective-permute-start | bytes 196616 | tf_op jit(solution)/shard_map/ppermute | solution.py:319
  129.8 10.0 %collective-permute-start.10 = (bf16[16,2048]{1,0:T(8,128)(2,1)S(1)}, bf16[16,2048]{1,0:T(8,128)(2,1)}, u32[]{:S(2)}, u32[]{:S(2)}) collective-permute-start(bf16[16,2048]{1,0:T(8,128)(2,1)S(1)} %fusion.104), channel_id=1, source_target_pairs={{0,2},{1,3},{2,0},{3,1},{4,6},{5,7},{6,4},{7,5},{8,10},{9,11},{10,... | collective-permute-start | bytes 196616 | tf_op jit(solution)/shard_map/ppermute | solution.py:319
  130.1 9.8 %collective-permute-start.9 = (bf16[16,2048]{1,0:T(8,128)(2,1)S(1)}, bf16[16,2048]{1,0:T(8,128)(2,1)}, u32[]{:S(2)}, u32[]{:S(2)}) collective-permute-start(bf16[16,2048]{1,0:T(8,128)(2,1)S(1)} %fusion.104), channel_id=1, source_target_pairs={{0,1},{1,2},{2,3},{3,0},{4,5},{5,6},{6,7},{7,4},{8,9},{9,10},{10,1... | collective-permute-start | bytes 196616 | tf_op jit(solution)/shard_map/ppermute | solution.py:319
  134.6 28.4 %all-to-all-start.3 = ((bf16[16,176,128]{2,1,0:T(8,128)(2,1)}), bf16[16,176,128]{2,1,0:T(8,128)(2,1)}, u32[]{:S(2)}, u32[]{:S(2)}) async-start(bf16[16,176,128]{2,1,0:T(8,128)(2,1)} %copy.89), calls=%async_computation.3 | async-start | bytes 1441792 | tf_op jit(solution)/shard_map/all_to_all | solution.py:216
  164.4 10.6 %collective-permute-start.12 = (f32[64,128]{1,0:T(8,128)}, f32[64,128]{1,0:T(8,128)}, u32[]{:S(2)}, u32[]{:S(2)}) collective-permute-start(f32[64,128]{1,0:T(8,128)} %get-tuple-element.32), channel_id=1, source_target_pairs={{0,1},{1,2},{2,3},{3,0},{4,5},{5,6},{6,7},{7,4},{8,9},{9,10},{10,1... | collective-permute-start | bytes 98312 | tf_op jit(solution)/shard_map/ppermute | solution.py:203
  166.3 8.7 %collective-permute-start.14 = (f32[64,128]{1,0:T(8,128)}, f32[64,128]{1,0:T(8,128)}, u32[]{:S(2)}, u32[]{:S(2)}) collective-permute-start(f32[64,128]{1,0:T(8,128)} %get-tuple-element.33), channel_id=1, source_target_pairs={{0,3},{1,0},{2,1},{3,2},{4,7},{5,4},{6,5},{7,6},{8,11},{9,8},{10,9... | collective-permute-start | bytes 98312 | tf_op jit(solution)/shard_map/ppermute | solution.py:203
  168.2 6.8 %collective-permute-start.13 = (f32[64,128]{1,0:T(8,128)}, f32[64,128]{1,0:T(8,128)}, u32[]{:S(2)}, u32[]{:S(2)}) collective-permute-start(f32[64,128]{1,0:T(8,128)} %get-tuple-element.34), channel_id=1, source_target_pairs={{0,2},{1,3},{2,0},{3,1},{4,6},{5,7},{6,4},{7,5},{8,10},{9,11},{10,... | collective-permute-start | bytes 98312 | tf_op jit(solution)/shard_map/ppermute | solution.py:203
  172.3 19.6 %copy-start.12 = (f32[2048]{0:T(1024)S(1)}, f32[2048]{0:T(1024)}, u32[]{:S(2)}) copy-start(f32[2048]{0:T(1024)} %param.28) | copy-start | bytes 24580
  172.3 19.6 %copy-start.23 = (f32[16]{0:T(128)S(1)}, f32[16]{0:T(128)}, u32[]{:S(2)}) copy-start(f32[16]{0:T(128)} %copy-done.22) | copy-start | bytes 196
  172.3 19.8 %copy-start.25 = (f32[16]{0:T(128)S(1)}, f32[16]{0:T(128)}, u32[]{:S(2)}) copy-start(f32[16]{0:T(128)} %copy-done.24) | copy-start | bytes 196
  172.4 19.8 %copy-start.28 = (f32[16]{0:T(128)S(1)}, f32[16]{0:T(128)}, u32[]{:S(2)}) copy-start(f32[16]{0:T(128)} %copy-done.27) | copy-start | bytes 196
  172.4 19.9 %copy-start.31 = (f32[16]{0:T(128)S(1)}, f32[16]{0:T(128)}, u32[]{:S(2)}) copy-start(f32[16]{0:T(128)} %copy-done.30) | copy-start | bytes 196
  177.0 8.3 %collective-permute-start.15 = (f32[16,2048]{1,0:T(8,128)S(1)}, f32[16,2048]{1,0:T(8,128)S(1)}, u32[]{:S(2)}, u32[]{:S(2)}) collective-permute-start(f32[16,2048]{1,0:T(8,128)S(1)} %get-tuple-element.26), channel_id=1, source_target_pairs={{0,1},{1,2},{2,3},{3,0},{4,5},{5,6},{6,7},{7,4},{8,9},{9,10},{10,1... | collective-permute-start | bytes 393224 | tf_op jit(solution)/shard_map/ppermute | solution.py:203
  178.5 7.2 %collective-permute-start.17 = (f32[16,2048]{1,0:T(8,128)S(1)}, f32[16,2048]{1,0:T(8,128)S(1)}, u32[]{:S(2)}, u32[]{:S(2)}) collective-permute-start(f32[16,2048]{1,0:T(8,128)S(1)} %get-tuple-element.27), channel_id=1, source_target_pairs={{0,3},{1,0},{2,1},{3,2},{4,7},{5,4},{6,5},{7,6},{8,11},{9,8},{10,9... | collective-permute-start | bytes 393224 | tf_op jit(solution)/shard_map/ppermute | solution.py:203
  180.9 11.1 %collective-permute-start.16 = (f32[16,2048]{1,0:T(8,128)S(1)}, f32[16,2048]{1,0:T(8,128)S(1)}, u32[]{:S(2)}, u32[]{:S(2)}) collective-permute-start(f32[16,2048]{1,0:T(8,128)S(1)} %get-tuple-element.28), channel_id=1, source_target_pairs={{0,2},{1,3},{2,0},{3,1},{4,6},{5,7},{6,4},{7,5},{8,10},{9,11},{10,... | collective-permute-start | bytes 393224 | tf_op jit(solution)/shard_map/ppermute | solution.py:203
  (8 other events, 16.2 us)

commit v18 on v15

--- a/solution.py
+++ b/solution.py
@@ -173,7 +173,14 @@
     count = lax.axis_size("head")
     me = lax.axis_index("head")
     block = parts[0]
-    ordered = jnp.take(jnp.stack(parts), (me - jnp.arange(count)) % count, axis=0)
+    slots = []
+    for slot in range(count):
+        source_shift = (me - slot) % count
+        chosen = parts[0]
+        for shift in range(1, count):
+            chosen = jnp.where(source_shift == shift, parts[shift], chosen)
+        slots.append(chosen)
+    ordered = jnp.stack(slots)
     ordered = jnp.moveaxis(ordered, 0, axis)
     merged = list(block.shape)
     merged[axis] = count * block.shape[axis]

time: 193 us -> 200 us (1.036)
  matrix products: 39.2 us -> 42.4 us
  local copies, waits for them, and re-layouts: 36 us -> 38.9 us
    gather x3 -> x0, local copies, waits for them, and re-layouts: 4.41 us -> none  [head_order(): jnp.take(jnp.stack(parts), (me - jnp.arange(count)) % count, axis=0)]
    unnamed x68 -> x58, local copies, waits for them, and re-layouts: 7.37 us -> 9 us
where the time goes in v18:
time: 200 us; the launch traced here: 197 us
  waiting for transfers between devices  55 us (28%)
  starting transfers between devices  45.4 us (23%)
  matrix products  42.4 us (21%)
  local copies, waits for them, and re-layouts  38.9 us (19%)
  other arithmetic  14.5 us (7%)
    ppermute x9, waiting for transfers between devices, head_sums(): lax.ppermute(chunk((me + shift) % count), 'head', perm=[(j, (j + shift) %...  18.2 us
    all_to_all x2, waiting for transfers between devices, from_experts(): lax.all_to_all(results, ('expert', 'head'), split_axis=0, concat_axis=0,...  15.8 us
    all_to_all x2, waiting for transfers between devices, to_experts(): lax.all_to_all(outgoing, ('expert', 'head'), split_axis=0, concat_axis=0,...  13.1 us
    ppermute x9, starting transfers between devices, head_sums(): lax.ppermute(chunk((me + shift) % count), 'head', perm=[(j, (j + shift) %...  12.7 us
    ppermute x6, starting transfers between devices, head_gather(): lax.ppermute(block, 'head', perm=[(j, (j + shift) % count) for j in range...  12.4 us
    all_to_all x2, starting transfers between devices, from_experts(): lax.all_to_all(results, ('expert', 'head'), split_axis=0, concat_axis=0,...  9.67 us
    unnamed x58, local copies, waits for them, and re-layouts  9 us
    all_to_all x2, starting transfers between devices, to_experts(): lax.all_to_all(outgoing, ('expert', 'head'), split_axis=0, concat_axis=0,...  8.55 us
  transfers between devices with their start and end apart: 22, of which 10 were waited for; matrix products, arithmetic and copies ran while one was open for 35% of the time, Pallas kernels for 0%

profile of v18, /device:TPU:0, one launch (start us, length us, event | category | flops | bytes accessed | tf_op | source)
XLA Modules:
  0.0 197.4 jit_solution(6159745452720523649)
XLA Ops:
  1.8 1.6 fusion.50
  3.4 3.0 %collective-permute-start.2 = (bf16[16,2048]{1,0:T(8,128)(2,1)}, bf16[16,2048]{1,0:T(8,128)(2,1)S(1)}, u32[]{:S(2)}, u32[]{:S(2)}) collective-permute-start(bf16[16,2048]{1,0:T(8,128)(2,1)} %fusion.50), channel_id=1, source_target_pairs={{0,1},{1,2},{2,3},{3,0},{4,5},{5,6},{6,7},{7,4},{8,9},{9,10},{10,1... | collective-permute-start | bytes 196616 | tf_op jit(solution)/shard_map/ppermute | solution.py:166
  6.4 2.6 %collective-permute-start.1 = (bf16[16,2048]{1,0:T(8,128)(2,1)}, bf16[16,2048]{1,0:T(8,128)(2,1)}, u32[]{:S(2)}, u32[]{:S(2)}) collective-permute-start(bf16[16,2048]{1,0:T(8,128)(2,1)} %fusion.50), channel_id=1, source_target_pairs={{0,2},{1,3},{2,0},{3,1},{4,6},{5,7},{6,4},{7,5},{8,10},{9,11},{10,... | collective-permute-start | bytes 196616 | tf_op jit(solution)/shard_map/ppermute | solution.py:166
  14.7 2.2 %convolution_convert_fusion = bf16[16,11,16,128]{3,0,2,1:T(8,128)(2,1)S(1)} fusion(f32[16,11,16,1]{2,1,0,3:T(8,128)S(1)} %bitcast.216, bf16[16,2048]{1,0:T(8,128)(2,1)} %param.17, f32[16]{0:T(128)} %convert_element_type.111), kind=kOutput, calls=%fused_computation.16 | convolution fusion | flops 69632000 | bytes 797760 | tf_op jit(solution)/shard_map/dct,tkl->dckl/dot_general | solution.py:283
  18.0 4.3 %all-to-all-start = ((bf16[16,176,128]{2,1,0:T(8,128)(2,1)}), bf16[16,176,128]{2,1,0:T(8,128)(2,1)}, u32[]{:S(2)}, u32[]{:S(2)}) async-start(bf16[16,176,128]{2,1,0:T(8,128)(2,1)} %copy.131), calls=%async_computation | async-start | bytes 1441792 | tf_op jit(solution)/shard_map/all_to_all | solution.py:219
  27.4 1.7 collective-permute-start.5
  29.1 2.4 %collective-permute-start.4 = (bf16[64,128]{1,0:T(8,128)(2,1)S(1)}, bf16[64,128]{1,0:T(8,128)(2,1)}, u32[]{:S(2)}, u32[]{:S(2)}) collective-permute-start(bf16[64,128]{1,0:T(8,128)(2,1)S(1)} %convolution_convert_fusion.6), channel_id=1, source_target_pairs={{0,2},{1,3},{2,0},{3,1},{4,6},{5,7},{6,4},{7,5},{8,10},{9,11},{10,... | collective-permute-start | bytes 49160 | tf_op jit(solution)/shard_map/ppermute | solution.py:166
  31.5 1.5 collective-permute-start.3
  32.9 2.1 %convolution_convert_fusion.5 = bf16[64,512]{1,0:T(8,128)(2,1)S(1)} fusion(bf16[64,2048]{1,0:T(8,128)(2,1)S(1)} %bitcast.214, bf16[2048,512]{1,0:T(8,128)(2,1)} %param.26), kind=kOutput, calls=%fused_computation.37 | convolution fusion | flops 134250496 | bytes 2424832 | tf_op jit(solution)/shard_map/dot_general | solution.py:82
  35.0 4.3 %collective-permute-done.5 = bf16[64,128]{1,0:T(8,128)(2,1)S(1)} collective-permute-done((bf16[64,128]{1,0:T(8,128)(2,1)S(1)}, bf16[64,128]{1,0:T(8,128)(2,1)S(1)}, u32[]{:S(2)}, u32[]{:S(2)}) %collective-permute-start.5) | collective-permute-done | bytes 16416 | tf_op jit(solution)/shard_map/ppermute | solution.py:166
  39.3 3.5 %collective-permute-done.4 = bf16[64,128]{1,0:T(8,128)(2,1)} collective-permute-done((bf16[64,128]{1,0:T(8,128)(2,1)S(1)}, bf16[64,128]{1,0:T(8,128)(2,1)}, u32[]{:S(2)}, u32[]{:S(2)}) %collective-permute-start.4) | collective-permute-done | bytes 16416 | tf_op jit(solution)/shard_map/ppermute | solution.py:166
  43.7 1.7 fusion.107
  47.2 2.1 %fusion.67 = f32[64,2048]{1,0:T(8,128)S(1)} fusion(bf16[512,2048]{1,0:T(8,128)(2,1)} %param.28, bf16[8,8,4,128]{3,2,1,0:T(4,128)(2,1)S(1)} %bitcast.220), kind=kOutput, calls=%fused_computation.97 | convolution fusion | flops 134217728 | bytes 2686976 | tf_op jit(solution)/shard_map/dot_general | solution.py:255
  51.6 3.1 %collective-permute-start.8 = (f32[16,2048]{1,0:T(8,128)}, f32[16,2048]{1,0:T(8,128)}, u32[]{:S(2)}, u32[]{:S(2)}) collective-permute-start(f32[16,2048]{1,0:T(8,128)} %get-tuple-element.26), channel_id=1, source_target_pairs={{0,3},{1,0},{2,1},{3,2},{4,7},{5,4},{6,5},{7,6},{8,11},{9,8},{10,9... | collective-permute-start | bytes 393224 | tf_op jit(solution)/shard_map/ppermute | solution.py:210
  55.7 3.7 %collective-permute-done.6 = f32[16,2048]{1,0:T(8,128)} collective-permute-done((f32[16,2048]{1,0:T(8,128)}, f32[16,2048]{1,0:T(8,128)}, u32[]{:S(2)}, u32[]{:S(2)}) %collective-permute-start.6) | collective-permute-done | bytes 131104 | tf_op jit(solution)/shard_map/ppermute | solution.py:210
  59.5 6.0 %collective-permute-done.7 = f32[16,2048]{1,0:T(8,128)} collective-permute-done((f32[16,2048]{1,0:T(8,128)}, f32[16,2048]{1,0:T(8,128)}, u32[]{:S(2)}, u32[]{:S(2)}) %collective-permute-start.7) | collective-permute-done | bytes 131104 | tf_op jit(solution)/shard_map/ppermute | solution.py:210
  69.5 4.3 %all-to-all-start.1 = ((bf16[16,176,128]{2,1,0:T(8,128)(2,1)}), bf16[16,176,128]{2,1,0:T(8,128)(2,1)}, u32[]{:S(2)}, u32[]{:S(2)}) async-start(bf16[16,176,128]{2,1,0:T(8,128)(2,1)} %copy.136), calls=%async_computation.1 | async-start | bytes 1441792 | tf_op jit(solution)/shard_map/all_to_all | solution.py:219
  73.8 2.9 %copy.173 = bf16[96,8,16,128]{3,2,1,0:T(8,128)(2,1)S(1)} copy(bf16[96,8,16,128]{3,1,2,0:T(8,128)(2,1)} %bitcast.205) | data formatting | bytes 6291456
  76.7 1.8 copy.132
  78.5 2.0 %fusion.15 = f32[16,11,768]{2,0,1:T(8,128)} fusion(bf16[16,11,16,128]{3,0,2,1:T(8,128)(2,1)S(1)} %bitcast.218, bf16[768,16,128]{2,1,0:T(8,128)(2,1)S(1)} %bitcast.206), kind=kOutput, calls=%fused_computation.19 | convolution fusion | flops 553648128 | bytes 4407296 | tf_op jit(solution)/shard_map/sckl,fkl->scf/dot_general | solution.py:305
  80.5 13.1 %all-to-all-done.1 = bf16[16,176,128]{2,1,0:T(8,128)(2,1)} async-done(((bf16[16,176,128]{2,1,0:T(8,128)(2,1)}), bf16[16,176,128]{2,1,0:T(8,128)(2,1)}, u32[]{:S(2)}, u32[]{:S(2)}) %all-to-all-start.1) | async-done | bytes 720928 | tf_op jit(solution)/shard_map/all_to_all | solution.py:219
  102.0 4.4 %all-to-all-start.2 = ((bf16[16,176,128]{2,1,0:T(8,128)(2,1)}), bf16[16,176,128]{2,1,0:T(8,128)(2,1)}, u32[]{:S(2)}, u32[]{:S(2)}) async-start(bf16[16,176,128]{2,1,0:T(8,128)(2,1)} %copy.138), calls=%async_computation.2 | async-start | bytes 1441792 | tf_op jit(solution)/shard_map/all_to_all | solution.py:223
  106.5 3.9 %fusion.11 = bf16[16,11,16,128]{3,0,2,1:T(8,128)(2,1)} fusion(bf16[768,16,128]{2,1,0:T(8,128)(2,1)} %bitcast.207, f32[16,11,768]{2,0,1:T(8,128)} %copy-done.6, f32[16,11,768]{2,0,1:T(8,128)} %copy-done.2), kind=kOutput, calls=%fused_computation.15 | convolution fusion | flops 554819584 | bytes 4947968 | tf_op jit(solution)/shard_map/scf,fkl->sckl/dot_general | solution.py:302
  110.4 15.8 %all-to-all-done.2 = bf16[16,176,128]{2,1,0:T(8,128)(2,1)} async-done(((bf16[16,176,128]{2,1,0:T(8,128)(2,1)}), bf16[16,176,128]{2,1,0:T(8,128)(2,1)}, u32[]{:S(2)}, u32[]{:S(2)}) %all-to-all-start.2) | async-done | bytes 720928 | tf_op jit(solution)/shard_map/all_to_all | solution.py:223
  126.2 2.1 %copy.231 = bf16[16,11,16,128]{3,2,0,1:T(8,128)(2,1)} copy(bf16[16,11,16,128]{3,2,1,0:T(8,128)(2,1)} %bitcast.44) | data formatting | bytes 1441792 | tf_op jit(solution)/shard_map/reshape | solution.py:317
  128.3 2.2 %dot_general.87 = bf16[2048,11,16]{0,2,1:T(8,128)(2,1)} reshape(bf16[16,128,11,16]{1,0,3,2:T(8,128)(2,1)} %bitcast.209) | data formatting | bytes 1441792 | tf_op jit(solution)/shard_map/dct,dckl->tkl/dot_general | solution.py:318
  130.5 1.7 fusion.46
  132.8 1.6 fusion.105
  136.4 2.2 %copy.146 = bf16[16,176,128]{2,1,0:T(8,128)(2,1)} copy(bf16[16,176,128]{2,0,1:T(8,128)(2,1)} %bitcast.217) | data formatting | bytes 1441792 | tf_op jit(solution)/shard_map/reshape | solution.py:329
  138.6 5.2 %all-to-all-start.3 = ((bf16[16,176,128]{2,1,0:T(8,128)(2,1)}), bf16[16,176,128]{2,1,0:T(8,128)(2,1)}, u32[]{:S(2)}, u32[]{:S(2)}) async-start(bf16[16,176,128]{2,1,0:T(8,128)(2,1)} %copy.146), calls=%async_computation.3 | async-start | bytes 1441792 | tf_op jit(solution)/shard_map/all_to_all | solution.py:223
  144.9 3.0 %convolution_convert_fusion.3 = bf16[64,512]{1,0:T(8,128)(2,1)} fusion(bf16[64,2048]{1,0:T(8,128)(2,1)S(1)} %bitcast.215, bf16[512,2048]{1,0:T(8,128)(2,1)} %param.28), kind=kOutput, calls=%fused_computation.35 | convolution fusion | flops 134250496 | bytes 2424832 | tf_op jit(solution)/shard_map/td,fd->tf/dot_general | solution.py:132
  147.9 1.5 reshape.144
  151.2 1.7 convolution_bitcast_fusion.4
  152.9 3.0 %convolution_bitcast_fusion.6 = f32[4,48,128]{2,1,0:T(8,128)} fusion(f32[4,4,16,48]{3,2,1,0:T(8,128)} %convolution_bitcast_fusion.4, bf16[4,16,4,128]{3,2,1,0:T(4,128)(2,1)} %copy-done.13, f32[4,4,16,48]{3,2,1,0:T(8,128)} %get-tuple-element.46, f32[4,4,16]{2,1,0:T(4,128)S(1)} %copy-done.27), kind=kOutput, calls=%fused_computation.34 | convolution fusion | flops 3232047 | bytes 263168 | tf_op jit(solution)/shard_map/shbk,sbhd->skd/dot_general | solution.py:58
  157.2 2.9 %fusion.27 = bf16[4,16,4,128]{3,1,2,0:T(8,128)(2,1)} fusion(f32[4,4,16,48]{3,2,1,0:T(8,128)} %convolution_bitcast_fusion.4, bf16[4,16,128]{2,1,0:T(8,128)(2,1)} %bitcast.227, bf16[4,32,128]{2,1,0:T(8,128)(2,1)} %get-tuple-element.49, f32[4,4,16,48]{3,2,1,0:T(8,128)} %get-tuple-element.46, f32[4,4,16]{2,1,0:T(4,128)S(1)} %copy-done.27), kind=kOutput, calls=%fused_computation.39 | convolution fusion | flops 3363119 | bytes 214016 | tf_op jit(solution)/shard_map/shbk,skd->sbhd/dot_general | solution.py:55
  160.1 1.5 copy.150
  166.4 1.9 collective-permute-start.12
  168.3 2.0 collective-permute-start.14
  171.3 3.2 %fusion.64 = f32[64,2048]{1,0:T(8,128)} fusion(bf16[2048,512]{1,0:T(8,128)(2,1)} %param.26, bf16[8,8,4,128]{3,2,1,0:T(4,128)(2,1)} %bitcast.219), kind=kOutput, calls=%fused_computation.94 | convolution fusion | flops 134217728 | bytes 2686976 | tf_op jit(solution)/shard_map/tf,df->td/dot_general | solution.py:156
  174.5 2.2 %copy.230 = bf16[16,11,16,128]{3,2,0,1:T(8,128)(2,1)} copy(bf16[16,11,16,128]{3,2,1,0:T(8,128)(2,1)} %bitcast.63) | data formatting | bytes 1441792 | tf_op jit(solution)/shard_map/optimization_barrier | solution.py:150
  176.6 2.1 %dot_general.95 = bf16[2048,11,16]{0,2,1:T(8,128)(2,1)} reshape(bf16[16,128,11,16]{1,0,3,2:T(8,128)(2,1)} %bitcast.210) | data formatting | bytes 1441792 | tf_op jit(solution)/shard_map/dct,dckl->tkl/dot_general | solution.py:345
  178.8 1.9 convolution_add_fusion
  180.8 1.5 collective-permute-start.15
  182.3 2.4 %collective-permute-start.17 = (f32[16,2048]{1,0:T(8,128)S(1)}, f32[16,2048]{1,0:T(8,128)S(1)}, u32[]{:S(2)}, u32[]{:S(2)}) collective-permute-start(f32[16,2048]{1,0:T(8,128)S(1)} %get-tuple-element.23), channel_id=1, source_target_pairs={{0,3},{1,0},{2,1},{3,2},{4,7},{5,4},{6,5},{7,6},{8,11},{9,8},{10,9... | collective-permute-start | bytes 393224 | tf_op jit(solution)/shard_map/ppermute | solution.py:210
  184.8 2.6 %fusion.10 = bf16[16,2048]{1,0:T(8,128)(2,1)} fusion(f32[16,11,16]{2,1,0:T(8,128)S(1)} %fusion.30, bf16[2048,11,16]{0,2,1:T(8,128)(2,1)} %dot_general.95, bf16[16,2048]{1,0:T(8,128)(2,1)S(1)} %get-tuple-element.21), kind=kOutput, calls=%fused_computation.13 | convolution fusion | flops 69304320 | bytes 863232 | tf_op jit(solution)/shard_map/dct,dckl->tkl/dot_general | solution.py:345
  187.4 1.7 collective-permute-done.15
  189.5 6.2 %collective-permute-done.16 = f32[16,2048]{1,0:T(8,128)S(1)} collective-permute-done((f32[16,2048]{1,0:T(8,128)S(1)}, f32[16,2048]{1,0:T(8,128)S(1)}, u32[]{:S(2)}, u32[]{:S(2)}) %collective-permute-start.16) | collective-permute-done | bytes 131104 | tf_op jit(solution)/shard_map/ppermute | solution.py:210
  196.0 1.4 fusion.55
  (129 shorter events, 44.6 us)
Async XLA Ops:
  0.6 94.3 %copy-start = (bf16[1,2048,768]{2,1,0:T(8,128)(2,1)S(1)}, bf16[1,2048,768]{2,1,0:T(8,128)(2,1)}, u32[]{:S(2)}) copy-start(bf16[1,2048,768]{2,1,0:T(8,128)(2,1)} %param.29) | copy-start | bytes 9437188
  0.6 24.4 %copy-start.4 = (bf16[16,2048]{1,0:T(8,128)(2,1)S(1)}, bf16[16,2048]{1,0:T(8,128)(2,1)}, u32[]{:S(2)}) copy-start(bf16[16,2048]{1,0:T(8,128)(2,1)} %param.16) | copy-start | bytes 196612
  0.7 24.4 %copy-start.11 = (f32[2048]{0:T(1024)S(1)}, f32[2048]{0:T(1024)}, u32[]{:S(2)}) copy-start(f32[2048]{0:T(1024)} %param.24) | copy-start | bytes 24580
  1.8 8.5 %copy-start.20 = (f32[16]{0:T(128)}, f32[16]{0:T(128)S(1)}, u32[]{:S(2)}) copy-start(f32[16]{0:T(128)S(1)} %add_rsqrt_fusion.1) | copy-start | bytes 196
  3.4 21.1 %collective-permute-start.2 = (bf16[16,2048]{1,0:T(8,128)(2,1)}, bf16[16,2048]{1,0:T(8,128)(2,1)S(1)}, u32[]{:S(2)}, u32[]{:S(2)}) collective-permute-start(bf16[16,2048]{1,0:T(8,128)(2,1)} %fusion.50), channel_id=1, source_target_pairs={{0,1},{1,2},{2,3},{3,0},{4,5},{5,6},{6,7},{7,4},{8,9},{9,10},{10,1... | collective-permute-start | bytes 196616 | tf_op jit(solution)/shard_map/ppermute | solution.py:166
  6.4 18.1 %collective-permute-start.1 = (bf16[16,2048]{1,0:T(8,128)(2,1)}, bf16[16,2048]{1,0:T(8,128)(2,1)}, u32[]{:S(2)}, u32[]{:S(2)}) collective-permute-start(bf16[16,2048]{1,0:T(8,128)(2,1)} %fusion.50), channel_id=1, source_target_pairs={{0,2},{1,3},{2,0},{3,1},{4,6},{5,7},{6,4},{7,5},{8,10},{9,11},{10,... | collective-permute-start | bytes 196616 | tf_op jit(solution)/shard_map/ppermute | solution.py:166
  9.0 16.1 %collective-permute-start = (bf16[16,2048]{1,0:T(8,128)(2,1)}, bf16[16,2048]{1,0:T(8,128)(2,1)}, u32[]{:S(2)}, u32[]{:S(2)}) collective-permute-start(bf16[16,2048]{1,0:T(8,128)(2,1)} %fusion.50), channel_id=1, source_target_pairs={{0,3},{1,0},{2,1},{3,2},{4,7},{5,4},{6,5},{7,6},{8,11},{9,8},{10,9... | collective-permute-start | bytes 196616 | tf_op jit(solution)/shard_map/ppermute | solution.py:166
  12.7 10.4 %copy-start.18 = (bf16[4,32,256]{2,1,0:T(8,128)(2,1)S(1)}, bf16[4,32,256]{2,1,0:T(8,128)(2,1)}, u32[]{:S(2)}) copy-start(bf16[4,32,256]{2,1,0:T(8,128)(2,1)} %param.22) | copy-start | bytes 196612
  12.9 9.5 %copy-start.25 = (s32[4]{0:T(128)S(1)}, s32[4]{0:T(128)}, u32[]{:S(2)}) copy-start(s32[4]{0:T(128)} %param.21) | copy-start | bytes 52
  13.7 10.7 %copy-start.15 = (s32[16,8]{0,1:T(8,128)}, s32[16,8]{0,1:T(8,128)S(1)}, u32[]{:S(2)}) copy-start(s32[16,8]{0,1:T(8,128)S(1)} %multiply_add_fusion.1) | copy-start | bytes 1540
  18.0 51.5 %all-to-all-start = ((bf16[16,176,128]{2,1,0:T(8,128)(2,1)}), bf16[16,176,128]{2,1,0:T(8,128)(2,1)}, u32[]{:S(2)}, u32[]{:S(2)}) async-start(bf16[16,176,128]{2,1,0:T(8,128)(2,1)} %copy.131), calls=%async_computation | async-start | bytes 1441792 | tf_op jit(solution)/shard_map/all_to_all | solution.py:219
  24.4 0.6 copy-start.12
  26.2 19.9 %copy-start.10 = (bf16[4,32,128]{2,1,0:T(8,128)(2,1)S(1)}, bf16[4,32,128]{2,1,0:T(8,128)(2,1)}, u32[]{:S(2)}) copy-start(bf16[4,32,128]{2,1,0:T(8,128)(2,1)} %get-tuple-element.50) | copy-start | bytes 98308
  27.4 11.9 %collective-permute-start.5 = (bf16[64,128]{1,0:T(8,128)(2,1)S(1)}, bf16[64,128]{1,0:T(8,128)(2,1)S(1)}, u32[]{:S(2)}, u32[]{:S(2)}) collective-permute-start(bf16[64,128]{1,0:T(8,128)(2,1)S(1)} %convolution_convert_fusion.6), channel_id=1, source_target_pairs={{0,1},{1,2},{2,3},{3,0},{4,5},{5,6},{6,7},{7,4},{8,9},{9,10},{10,1... | collective-permute-start | bytes 49160 | tf_op jit(solution)/shard_map/ppermute | solution.py:166
  29.1 13.8 %collective-permute-start.4 = (bf16[64,128]{1,0:T(8,128)(2,1)S(1)}, bf16[64,128]{1,0:T(8,128)(2,1)}, u32[]{:S(2)}, u32[]{:S(2)}) collective-permute-start(bf16[64,128]{1,0:T(8,128)(2,1)S(1)} %convolution_convert_fusion.6), channel_id=1, source_target_pairs={{0,2},{1,3},{2,0},{3,1},{4,6},{5,7},{6,4},{7,5},{8,10},{9,11},{10,... | collective-permute-start | bytes 49160 | tf_op jit(solution)/shard_map/ppermute | solution.py:166
  31.5 11.4 %collective-permute-start.3 = (bf16[64,128]{1,0:T(8,128)(2,1)S(1)}, bf16[64,128]{1,0:T(8,128)(2,1)}, u32[]{:S(2)}, u32[]{:S(2)}) collective-permute-start(bf16[64,128]{1,0:T(8,128)(2,1)S(1)} %convolution_convert_fusion.6), channel_id=1, source_target_pairs={{0,3},{1,0},{2,1},{3,2},{4,7},{5,4},{6,5},{7,6},{8,11},{9,8},{10,9... | collective-permute-start | bytes 49160 | tf_op jit(solution)/shard_map/ppermute | solution.py:166
  35.0 33.4 %copy-start.13 = (bf16[4,16,4,128]{3,2,1,0:T(4,128)(2,1)}, bf16[4,16,4,128]{3,2,1,0:T(4,128)(2,1)S(1)}, u32[]{:S(2)}) copy-start(bf16[4,16,4,128]{3,2,1,0:T(4,128)(2,1)S(1)} %reshape.133) | copy-start | bytes 196612
  39.3 3.5 %copy-start.17 = (bf16[64,128]{1,0:T(8,128)(2,1)}, bf16[64,128]{1,0:T(8,128)(2,1)S(1)}, u32[]{:S(2)}) copy-start(bf16[64,128]{1,0:T(8,128)(2,1)S(1)} %collective-permute-done.5) | copy-start | bytes 49156
  43.7 25.8 %copy-start.14 = (bf16[64,128]{1,0:T(8,128)(2,1)}, bf16[64,128]{1,0:T(8,128)(2,1)S(1)}, u32[]{:S(2)}) copy-start(bf16[64,128]{1,0:T(8,128)(2,1)S(1)} %get-tuple-element.40) | copy-start | bytes 49156
  43.7 25.7 %copy-start.19 = (bf16[64,128]{1,0:T(8,128)(2,1)}, bf16[64,128]{1,0:T(8,128)(2,1)S(1)}, u32[]{:S(2)}) copy-start(bf16[64,128]{1,0:T(8,128)(2,1)S(1)} %get-tuple-element.39) | copy-start | bytes 49156
  45.4 0.6 copy-start.26
  49.2 0.8 copy-start.7
  50.8 8.6 %collective-permute-start.6 = (f32[16,2048]{1,0:T(8,128)}, f32[16,2048]{1,0:T(8,128)}, u32[]{:S(2)}, u32[]{:S(2)}) collective-permute-start(f32[16,2048]{1,0:T(8,128)} %get-tuple-element.25), channel_id=1, source_target_pairs={{0,1},{1,2},{2,3},{3,0},{4,5},{5,6},{6,7},{7,4},{8,9},{9,10},{10,1... | collective-permute-start | bytes 393224 | tf_op jit(solution)/shard_map/ppermute | solution.py:210
  51.6 7.9 %collective-permute-start.8 = (f32[16,2048]{1,0:T(8,128)}, f32[16,2048]{1,0:T(8,128)}, u32[]{:S(2)}, u32[]{:S(2)}) collective-permute-start(f32[16,2048]{1,0:T(8,128)} %get-tuple-element.26), channel_id=1, source_target_pairs={{0,3},{1,0},{2,1},{3,2},{4,7},{5,4},{6,5},{7,6},{8,11},{9,8},{10,9... | collective-permute-start | bytes 393224 | tf_op jit(solution)/shard_map/ppermute | solution.py:210
  54.7 10.8 %collective-permute-start.7 = (f32[16,2048]{1,0:T(8,128)}, f32[16,2048]{1,0:T(8,128)}, u32[]{:S(2)}, u32[]{:S(2)}) collective-permute-start(f32[16,2048]{1,0:T(8,128)} %get-tuple-element.27), channel_id=1, source_target_pairs={{0,2},{1,3},{2,0},{3,1},{4,6},{5,7},{6,4},{7,5},{8,10},{9,11},{10,... | collective-permute-start | bytes 393224 | tf_op jit(solution)/shard_map/ppermute | solution.py:210
  55.7 21.0 %copy-start.9 = (pred[16,11,16]{2,1,0:T(8,128)(4,1)}, pred[16,11,16]{2,1,0:T(8,128)(4,1)S(1)}, u32[]{:S(2)}) copy-start(pred[16,11,16]{2,1,0:T(8,128)(4,1)S(1)} %compare_reduce_fusion) | copy-start | bytes 8452
  69.5 24.2 %all-to-all-start.1 = ((bf16[16,176,128]{2,1,0:T(8,128)(2,1)}), bf16[16,176,128]{2,1,0:T(8,128)(2,1)}, u32[]{:S(2)}, u32[]{:S(2)}) async-start(bf16[16,176,128]{2,1,0:T(8,128)(2,1)} %copy.136), calls=%async_computation.1 | async-start | bytes 1441792 | tf_op jit(solution)/shard_map/all_to_all | solution.py:219
  76.7 1.8 copy-start.3
  95.0 2.1 %copy-start.1 = (bf16[1,2048,768]{2,1,0:T(8,128)(2,1)S(1)}, bf16[1,2048,768]{2,1,0:T(8,128)(2,1)}, u32[]{:S(2)}) copy-start(bf16[1,2048,768]{2,1,0:T(8,128)(2,1)} %param.30) | copy-start | bytes 9437188
  95.7 4.1 %copy-start.2 = (f32[16,11,768]{2,0,1:T(8,128)}, f32[16,11,768]{2,0,1:T(8,128)S(1)}, u32[]{:S(2)}) copy-start(f32[16,11,768]{2,0,1:T(8,128)S(1)} %convolution_bitcast_fusion.2) | copy-start | bytes 1622020
  97.1 1.6 copy-start.5
  97.8 0.8 copy-start.6
  102.0 24.2 %all-to-all-start.2 = ((bf16[16,176,128]{2,1,0:T(8,128)(2,1)}), bf16[16,176,128]{2,1,0:T(8,128)(2,1)}, u32[]{:S(2)}, u32[]{:S(2)}) async-start(bf16[16,176,128]{2,1,0:T(8,128)(2,1)} %copy.138), calls=%async_computation.2 | async-start | bytes 1441792 | tf_op jit(solution)/shard_map/all_to_all | solution.py:223
  106.5 24.0 %copy-start.16 = (f32[2048]{0:T(1024)S(1)}, f32[2048]{0:T(1024)}, u32[]{:S(2)}) copy-start(f32[2048]{0:T(1024)} %param.25) | copy-start | bytes 24580
  134.4 9.5 %collective-permute-start.11 = (bf16[16,2048]{1,0:T(8,128)(2,1)}, bf16[16,2048]{1,0:T(8,128)(2,1)}, u32[]{:S(2)}, u32[]{:S(2)}) collective-permute-start(bf16[16,2048]{1,0:T(8,128)(2,1)} %fusion.105), channel_id=1, source_target_pairs={{0,3},{1,0},{2,1},{3,2},{4,7},{5,4},{6,5},{7,6},{8,11},{9,8},{10,9... | collective-permute-start | bytes 196616 | tf_op jit(solution)/shard_map/ppermute | solution.py:326
  135.2 8.7 %collective-permute-start.10 = (bf16[16,2048]{1,0:T(8,128)(2,1)}, bf16[16,2048]{1,0:T(8,128)(2,1)}, u32[]{:S(2)}, u32[]{:S(2)}) collective-permute-start(bf16[16,2048]{1,0:T(8,128)(2,1)} %fusion.105), channel_id=1, source_target_pairs={{0,2},{1,3},{2,0},{3,1},{4,6},{5,7},{6,4},{7,5},{8,10},{9,11},{10,... | collective-permute-start | bytes 196616 | tf_op jit(solution)/shard_map/ppermute | solution.py:326
  135.4 8.4 %collective-permute-start.9 = (bf16[16,2048]{1,0:T(8,128)(2,1)}, bf16[16,2048]{1,0:T(8,128)(2,1)}, u32[]{:S(2)}, u32[]{:S(2)}) collective-permute-start(bf16[16,2048]{1,0:T(8,128)(2,1)} %fusion.105), channel_id=1, source_target_pairs={{0,1},{1,2},{2,3},{3,0},{4,5},{5,6},{6,7},{7,4},{8,9},{9,10},{10,1... | collective-permute-start | bytes 196616 | tf_op jit(solution)/shard_map/ppermute | solution.py:326
  136.4 13.0 %copy-start.27 = (f32[4,4,16]{2,1,0:T(4,128)S(1)}, f32[4,4,16]{2,1,0:T(4,128)}, u32[]{:S(2)}) copy-start(f32[4,4,16]{2,1,0:T(4,128)} %copy-done.26) | copy-start | bytes 3076
  138.6 26.4 %all-to-all-start.3 = ((bf16[16,176,128]{2,1,0:T(8,128)(2,1)}), bf16[16,176,128]{2,1,0:T(8,128)(2,1)}, u32[]{:S(2)}, u32[]{:S(2)}) async-start(bf16[16,176,128]{2,1,0:T(8,128)(2,1)} %copy.146), calls=%async_computation.3 | async-start | bytes 1441792 | tf_op jit(solution)/shard_map/all_to_all | solution.py:223
  166.4 12.3 %collective-permute-start.12 = (f32[64,128]{1,0:T(8,128)}, f32[64,128]{1,0:T(8,128)}, u32[]{:S(2)}, u32[]{:S(2)}) collective-permute-start(f32[64,128]{1,0:T(8,128)} %get-tuple-element.36), channel_id=1, source_target_pairs={{0,1},{1,2},{2,3},{3,0},{4,5},{5,6},{6,7},{7,4},{8,9},{9,10},{10,1... | collective-permute-start | bytes 98312 | tf_op jit(solution)/shard_map/ppermute | solution.py:210
  168.3 10.4 %collective-permute-start.14 = (f32[64,128]{1,0:T(8,128)}, f32[64,128]{1,0:T(8,128)}, u32[]{:S(2)}, u32[]{:S(2)}) collective-permute-start(f32[64,128]{1,0:T(8,128)} %get-tuple-element.37), channel_id=1, source_target_pairs={{0,3},{1,0},{2,1},{3,2},{4,7},{5,4},{6,5},{7,6},{8,11},{9,8},{10,9... | collective-permute-start | bytes 98312 | tf_op jit(solution)/shard_map/ppermute | solution.py:210
  170.3 8.5 %collective-permute-start.13 = (f32[64,128]{1,0:T(8,128)}, f32[64,128]{1,0:T(8,128)}, u32[]{:S(2)}, u32[]{:S(2)}) collective-permute-start(f32[64,128]{1,0:T(8,128)} %get-tuple-element.38), channel_id=1, source_target_pairs={{0,2},{1,3},{2,0},{3,1},{4,6},{5,7},{6,4},{7,5},{8,10},{9,11},{10,... | collective-permute-start | bytes 98312 | tf_op jit(solution)/shard_map/ppermute | solution.py:210
  174.5 21.3 %copy-start.21 = (f32[16]{0:T(128)S(1)}, f32[16]{0:T(128)}, u32[]{:S(2)}) copy-start(f32[16]{0:T(128)} %copy-done.20) | copy-start | bytes 196
  176.6 19.4 %copy-start.23 = (f32[16]{0:T(128)S(1)}, f32[16]{0:T(128)}, u32[]{:S(2)}) copy-start(f32[16]{0:T(128)} %copy-done.22) | copy-start | bytes 196
  178.8 17.2 %copy-start.8 = (bf16[16,2048]{1,0:T(8,128)(2,1)S(1)}, bf16[16,2048]{1,0:T(8,128)(2,1)}, u32[]{:S(2)}) copy-start(bf16[16,2048]{1,0:T(8,128)(2,1)} %param.17) | copy-start | bytes 196612
  180.8 8.3 %collective-permute-start.15 = (f32[16,2048]{1,0:T(8,128)S(1)}, f32[16,2048]{1,0:T(8,128)S(1)}, u32[]{:S(2)}, u32[]{:S(2)}) collective-permute-start(f32[16,2048]{1,0:T(8,128)S(1)} %get-tuple-element.22), channel_id=1, source_target_pairs={{0,1},{1,2},{2,3},{3,0},{4,5},{5,6},{6,7},{7,4},{8,9},{9,10},{10,1... | collective-permute-start | bytes 393224 | tf_op jit(solution)/shard_map/ppermute | solution.py:210
  182.3 7.2 %collective-permute-start.17 = (f32[16,2048]{1,0:T(8,128)S(1)}, f32[16,2048]{1,0:T(8,128)S(1)}, u32[]{:S(2)}, u32[]{:S(2)}) collective-permute-start(f32[16,2048]{1,0:T(8,128)S(1)} %get-tuple-element.23), channel_id=1, source_target_pairs={{0,3},{1,0},{2,1},{3,2},{4,7},{5,4},{6,5},{7,6},{8,11},{9,8},{10,9... | collective-permute-start | bytes 393224 | tf_op jit(solution)/shard_map/ppermute | solution.py:210
  184.7 11.1 %collective-permute-start.16 = (f32[16,2048]{1,0:T(8,128)S(1)}, f32[16,2048]{1,0:T(8,128)S(1)}, u32[]{:S(2)}, u32[]{:S(2)}) collective-permute-start(f32[16,2048]{1,0:T(8,128)S(1)} %get-tuple-element.24), channel_id=1, source_target_pairs={{0,2},{1,3},{2,0},{3,1},{4,6},{5,7},{6,4},{7,5},{8,10},{9,11},{10,... | collective-permute-start | bytes 393224 | tf_op jit(solution)/shard_map/ppermute | solution.py:210
  (2 other events, 1.1 us)

commit v19 on v16

--- a/solution.py
+++ b/solution.py
@@ -72,6 +72,7 @@
     prefix_value_cache,
     lengths,
     first_head,
+    carried,
 ):
     heads_here = query_weights.shape[1] // HEAD_SIZE
     query_group_count = QUERY_HEADS // KEY_VALUE_HEADS
@@ -94,6 +95,7 @@
     own_rows = jnp.dot(row_block, own_kv_weights, preferred_element_type=jnp.float32).astype(
         jnp.bfloat16
     )
+    own_rows, carried = lax.optimization_barrier((own_rows, carried))
     kv_rows = head_gather(own_rows, 1)
     pair_rows = jnp.concatenate(
         [
@@ -119,7 +121,7 @@
     probabilities, probs_low, attended = attend_forward(queries, key_rows, value_rows, usable)
     saved = [(queries, key_rows, value_rows, probabilities, probs_low)]
     joined = attended.reshape(row_count, heads_here * HEAD_SIZE)
-    return (joined, saved)
+    return (joined, saved, carried)
 
 
 def attention_backward(
@@ -242,9 +244,6 @@
     heads_here = w_query.shape[1] // HEAD_SIZE
     first_head = lax.axis_index("head") * heads_here
     gathered_rows = head_rows(attn_rows)
-    attended, saved = attention_forward(
-        gathered_rows, w_query, key_value_weight, key_cache, prefix_value_cache, cache_lengths, first_head
-    )
     device_count = lax.axis_size("expert") * lax.axis_size("head")
     capacity = (owned * TOP * 4 + 3 * device_count - 1) // (3 * device_count)
     slot_total = device_count * capacity
@@ -269,9 +268,10 @@
         cotangent.reshape(owned, pieces, lanes),
         precision=highest_prec,
     ).astype(jnp.bfloat16)
-    partial_mixed = jnp.dot(attended, w_output, preferred_element_type=jnp.float32)
-    partial_mixed, grad_out = lax.optimization_barrier((partial_mixed, grad_out))
-    mixed = head_sums(partial_mixed)
+    attended, saved, grad_out = attention_forward(
+        gathered_rows, w_query, key_value_weight, key_cache, prefix_value_cache, cache_lengths, first_head, grad_out
+    )
+    mixed = head_sums(jnp.dot(attended, w_output, preferred_element_type=jnp.float32))
     hidden = (hidden_in.astype(jnp.float32) + mixed).astype(jnp.bfloat16)
     normed_two, inverse_two = rms_forward(hidden, moe_gain)
     moe_rows = normed_two.astype(jnp.bfloat16)

time: 215 us -> 208 us (0.967)
  waiting for transfers between devices: 63.2 us -> 54.9 us
    ppermute x9, waiting for transfers between devices: 32.2 us -> 25.9 us  [head_sums(): lax.ppermute(chunk((me + shift) % count), 'head', perm=[(j, (j + shift) %...]
    unnamed x52 -> x56, local copies, waits for them, and re-layouts: 6.56 us -> 7.3 us
  transfers between devices with their start and end apart: 22 -> 22, of which waited for: 8 -> 7; matrix products, arithmetic and copies ran while one was open for 32% -> 36% of each run, Pallas kernels for 0% -> 0%
where the time goes in v19:
time: 208 us; the launch traced here: 206 us
  waiting for transfers between devices  54.9 us (26%)
  starting transfers between devices  45.3 us (22%)
  local copies, waits for them, and re-layouts  43.6 us (21%)
  matrix products  42.7 us (21%)
  other arithmetic  18.3 us (9%)
    ppermute x9, waiting for transfers between devices, head_sums(): lax.ppermute(chunk((me + shift) % count), 'head', perm=[(j, (j + shift) %...  25.9 us
    all_to_all x2, waiting for transfers between devices, from_experts(): lax.all_to_all(results, ('expert', 'head'), split_axis=0, concat_axis=0,...  15.8 us
    ppermute x9, starting transfers between devices, head_sums(): lax.ppermute(chunk((me + shift) % count), 'head', perm=[(j, (j + shift) %...  13.6 us
    all_to_all x2, waiting for transfers between devices, to_experts(): lax.all_to_all(outgoing, ('expert', 'head'), split_axis=0, concat_axis=0,...  13.1 us
    ppermute x6, starting transfers between devices, head_gather(): lax.ppermute(block, 'head', perm=[(j, (j + shift) % count) for j in range...  10 us
    all_to_all x2, starting transfers between devices, from_experts(): lax.all_to_all(results, ('expert', 'head'), split_axis=0, concat_axis=0,...  9.8 us
    all_to_all x2, starting transfers between devices, to_experts(): lax.all_to_all(outgoing, ('expert', 'head'), split_axis=0, concat_axis=0,...  9.8 us
    unnamed x56, local copies, waits for them, and re-layouts  7.3 us
  transfers between devices with their start and end apart: 22, of which 7 were waited for; matrix products, arithmetic and copies ran while one was open for 36% of the time, Pallas kernels for 0%

profile of v19, /device:TPU:0, one launch (start us, length us, event | category | flops | bytes accessed | tf_op | source)
XLA Modules:
  0.0 206.0 jit_solution(11878212094517677686)
XLA Ops:
  2.7 4.1 %collective-permute-start.1 = (bf16[16,2048]{1,0:T(8,128)(2,1)S(1)}, bf16[16,2048]{1,0:T(8,128)(2,1)}, u32[]{:S(2)}, u32[]{:S(2)}) collective-permute-start(bf16[16,2048]{1,0:T(8,128)(2,1)S(1)} %fusion.50), channel_id=1, source_target_pairs={{0,2},{1,3},{2,0},{3,1},{4,6},{5,7},{6,4},{7,5},{8,10},{9,11},{10,... | collective-permute-start | bytes 196616 | tf_op jit(solution)/shard_map/ppermute | solution.py:168
  6.8 1.6 collective-permute-start
  8.4 2.2 %collective-permute-start.2 = (bf16[16,2048]{1,0:T(8,128)(2,1)S(1)}, bf16[16,2048]{1,0:T(8,128)(2,1)}, u32[]{:S(2)}, u32[]{:S(2)}) collective-permute-start(bf16[16,2048]{1,0:T(8,128)(2,1)S(1)} %fusion.50), channel_id=1, source_target_pairs={{0,3},{1,0},{2,1},{3,2},{4,7},{5,4},{6,5},{7,6},{8,11},{9,8},{10,9... | collective-permute-start | bytes 196616 | tf_op jit(solution)/shard_map/ppermute | solution.py:168
  19.3 3.1 %convolution_convert_fusion = bf16[16,11,16,128]{3,0,2,1:T(8,128)(2,1)} fusion(f32[16,11,16,1]{2,1,0,3:T(8,128)S(1)} %bitcast.207, bf16[16,2048]{1,0:T(8,128)(2,1)} %param.19, f32[16]{0:T(128)} %convert_element_type.105), kind=kOutput, calls=%fused_computation.19 | convolution fusion | flops 69632000 | bytes 797760 | tf_op jit(solution)/shard_map/dct,tkl->dckl/dot_general | solution.py:265
  23.0 1.6 pad_maximum_fusion
  24.7 1.5 gather_fusion.1
  30.3 2.1 %convolution_convert_fusion.5 = bf16[64,512]{1,0:T(8,128)(2,1)S(1)} fusion(bf16[64,2048]{1,0:T(8,128)(2,1)S(1)} %bitcast.205, bf16[2048,512]{1,0:T(8,128)(2,1)} %param.28), kind=kOutput, calls=%fused_computation.40 | convolution fusion | flops 134250496 | bytes 2424832 | tf_op jit(solution)/shard_map/dot_general | solution.py:83
  33.1 2.2 %copy.131 = bf16[16,176,128]{2,1,0:T(8,128)(2,1)} copy(bf16[16,176,128]{2,0,1:T(8,128)(2,1)} %bitcast.200) | data formatting | bytes 1441792 | tf_op jit(solution)/shard_map/reshape | solution.py:287
  35.3 5.5 %all-to-all-start = ((bf16[16,176,128]{2,1,0:T(8,128)(2,1)}), bf16[16,176,128]{2,1,0:T(8,128)(2,1)}, u32[]{:S(2)}, u32[]{:S(2)}) async-start(bf16[16,176,128]{2,1,0:T(8,128)(2,1)} %copy.131), calls=%async_computation | async-start | bytes 1441792 | tf_op jit(solution)/shard_map/all_to_all | solution.py:214
  41.7 1.8 fusion.110
  45.2 2.1 %fusion.67 = f32[64,2048]{1,0:T(8,128)S(1)} fusion(bf16[512,2048]{1,0:T(8,128)(2,1)} %param.30, bf16[8,8,4,128]{3,2,1,0:T(4,128)(2,1)S(1)} %bitcast.211), kind=kOutput, calls=%fused_computation.102 | convolution fusion | flops 134217728 | bytes 2686976 | tf_op jit(solution)/shard_map/dot_general | solution.py:274
  48.9 1.9 collective-permute-start.6
  50.7 2.0 collective-permute-start.8
  54.0 6.7 %collective-permute-done.6 = f32[16,2048]{1,0:T(8,128)} collective-permute-done((f32[16,2048]{1,0:T(8,128)}, f32[16,2048]{1,0:T(8,128)}, u32[]{:S(2)}, u32[]{:S(2)}) %collective-permute-start.6) | collective-permute-done | bytes 131104 | tf_op jit(solution)/shard_map/ppermute | solution.py:205
  60.7 10.9 %collective-permute-done.7 = f32[16,2048]{1,0:T(8,128)} collective-permute-done((f32[16,2048]{1,0:T(8,128)}, f32[16,2048]{1,0:T(8,128)}, u32[]{:S(2)}, u32[]{:S(2)}) %collective-permute-start.7) | collective-permute-done | bytes 131104 | tf_op jit(solution)/shard_map/ppermute | solution.py:205
  74.3 4.3 %all-to-all-start.1 = ((bf16[16,176,128]{2,1,0:T(8,128)(2,1)}), bf16[16,176,128]{2,1,0:T(8,128)(2,1)}, u32[]{:S(2)}, u32[]{:S(2)}) async-start(bf16[16,176,128]{2,1,0:T(8,128)(2,1)} %copy.136), calls=%async_computation.1 | async-start | bytes 1441792 | tf_op jit(solution)/shard_map/all_to_all | solution.py:214
  78.6 2.9 %copy.173 = bf16[96,8,16,128]{3,2,1,0:T(8,128)(2,1)S(1)} copy(bf16[96,8,16,128]{3,1,2,0:T(8,128)(2,1)} %bitcast.196) | data formatting | bytes 6291456
  81.5 1.8 copy.132
  83.3 2.0 fusion.15
  85.3 13.1 %all-to-all-done.1 = bf16[16,176,128]{2,1,0:T(8,128)(2,1)} async-done(((bf16[16,176,128]{2,1,0:T(8,128)(2,1)}), bf16[16,176,128]{2,1,0:T(8,128)(2,1)}, u32[]{:S(2)}, u32[]{:S(2)}) %all-to-all-start.1) | async-done | bytes 720928 | tf_op jit(solution)/shard_map/all_to_all | solution.py:214
  106.9 4.5 %all-to-all-start.2 = ((bf16[16,176,128]{2,1,0:T(8,128)(2,1)}), bf16[16,176,128]{2,1,0:T(8,128)(2,1)}, u32[]{:S(2)}, u32[]{:S(2)}) async-start(bf16[16,176,128]{2,1,0:T(8,128)(2,1)} %copy.138), calls=%async_computation.2 | async-start | bytes 1441792 | tf_op jit(solution)/shard_map/all_to_all | solution.py:218
  111.3 3.9 %fusion.11 = bf16[16,11,16,128]{3,0,2,1:T(8,128)(2,1)} fusion(bf16[768,16,128]{2,1,0:T(8,128)(2,1)} %bitcast.198, f32[16,11,768]{2,0,1:T(8,128)} %copy-done.6, f32[16,11,768]{2,0,1:T(8,128)} %copy-done.2), kind=kOutput, calls=%fused_computation.18 | convolution fusion | flops 554819584 | bytes 4947968 | tf_op jit(solution)/shard_map/scf,fkl->sckl/dot_general | solution.py:297
  115.3 15.8 %all-to-all-done.2 = bf16[16,176,128]{2,1,0:T(8,128)(2,1)} async-done(((bf16[16,176,128]{2,1,0:T(8,128)(2,1)}), bf16[16,176,128]{2,1,0:T(8,128)(2,1)}, u32[]{:S(2)}, u32[]{:S(2)}) %all-to-all-start.2) | async-done | bytes 720928 | tf_op jit(solution)/shard_map/all_to_all | solution.py:218
  131.0 2.1 %copy.231 = bf16[16,11,16,128]{3,2,0,1:T(8,128)(2,1)} copy(bf16[16,11,16,128]{3,2,1,0:T(8,128)(2,1)} %bitcast.45) | data formatting | bytes 1441792 | tf_op jit(solution)/shard_map/reshape | solution.py:312
  133.2 2.2 %dot_general.87 = bf16[2048,11,16]{0,2,1:T(8,128)(2,1)} reshape(bf16[16,128,11,16]{1,0,3,2:T(8,128)(2,1)} %bitcast.201) | data formatting | bytes 1441792 | tf_op jit(solution)/shard_map/dct,dckl->tkl/dot_general | solution.py:313
  135.4 1.8 fusion.46
  137.1 1.6 fusion.108
  140.8 2.2 %copy.146 = bf16[16,176,128]{2,1,0:T(8,128)(2,1)} copy(bf16[16,176,128]{2,0,1:T(8,128)(2,1)} %bitcast.208) | data formatting | bytes 1441792 | tf_op jit(solution)/shard_map/reshape | solution.py:324
  142.9 5.4 %all-to-all-start.3 = ((bf16[16,176,128]{2,1,0:T(8,128)(2,1)}), bf16[16,176,128]{2,1,0:T(8,128)(2,1)}, u32[]{:S(2)}, u32[]{:S(2)}) async-start(bf16[16,176,128]{2,1,0:T(8,128)(2,1)} %copy.146), calls=%async_computation.3 | async-start | bytes 1441792 | tf_op jit(solution)/shard_map/all_to_all | solution.py:218
  148.3 1.7 pad_maximum_fusion.1
  150.0 2.4 %gather_fusion.2 = bf16[4,16,2048]{2,1,0:T(8,128)(2,1)} fusion(bf16[4,16,2048]{2,1,0:T(8,128)(2,1)} %pad_maximum_fusion.1, s32[1024]{0:T(1024)} %copy-done.21), kind=kCustom, calls=%fused_computation.1.clone | custom fusion | bytes 524304 | tf_op jit(solution)/shard_map/jit(_take)/gather | solution.py:178
  153.4 3.0 %convolution_convert_fusion.3 = bf16[64,512]{1,0:T(8,128)(2,1)} fusion(bf16[64,2048]{1,0:T(8,128)(2,1)S(1)} %bitcast.206, bf16[512,2048]{1,0:T(8,128)(2,1)} %param.30), kind=kOutput, calls=%fused_computation.38 | convolution fusion | flops 134250496 | bytes 2424832 | tf_op jit(solution)/shard_map/td,fd->tf/dot_general | solution.py:134
  156.4 1.5 reshape.203
  159.7 1.7 convolution_bitcast_fusion.4
  161.4 3.0 %convolution_bitcast_fusion.6 = f32[4,48,128]{2,1,0:T(8,128)} fusion(f32[4,4,16,48]{3,2,1,0:T(8,128)} %convolution_bitcast_fusion.4, bf16[4,16,4,128]{3,2,1,0:T(4,128)(2,1)} %reshape.193, f32[4,4,16,48]{3,2,1,0:T(8,128)} %get-tuple-element.39, f32[4,4,16]{2,1,0:T(4,128)} %copy-done.26), kind=kOutput, calls=%fused_computation.37 | convolution fusion | flops 3232047 | bytes 263168 | tf_op jit(solution)/shard_map/shbk,sbhd->skd/dot_general | solution.py:58
  165.7 2.9 %fusion.27 = bf16[4,16,4,128]{3,1,2,0:T(8,128)(2,1)} fusion(f32[4,4,16,48]{3,2,1,0:T(8,128)} %convolution_bitcast_fusion.4, bf16[4,16,128]{2,1,0:T(8,128)(2,1)} %bitcast.219, bf16[4,32,128]{2,1,0:T(8,128)(2,1)} %get-tuple-element.42, f32[4,4,16,48]{3,2,1,0:T(8,128)} %get-tuple-element.39, f32[4,4,16]{2,1,0:T(4,128)} %copy-done.26), kind=kOutput, calls=%fused_computation.42 | convolution fusion | flops 3363119 | bytes 214016 | tf_op jit(solution)/shard_map/shbk,skd->sbhd/dot_general | solution.py:55
  168.6 1.5 copy.150
  175.0 1.9 collective-permute-start.12
  176.9 2.0 collective-permute-start.14
  179.8 3.2 %fusion.64 = f32[64,2048]{1,0:T(8,128)} fusion(bf16[2048,512]{1,0:T(8,128)(2,1)} %param.28, bf16[8,8,4,128]{3,2,1,0:T(4,128)(2,1)} %bitcast.210), kind=kOutput, calls=%fused_computation.99 | convolution fusion | flops 134217728 | bytes 2686976 | tf_op jit(solution)/shard_map/tf,df->td/dot_general | solution.py:158
  183.0 2.2 %copy.230 = bf16[16,11,16,128]{3,2,0,1:T(8,128)(2,1)} copy(bf16[16,11,16,128]{3,2,1,0:T(8,128)(2,1)} %bitcast.64) | data formatting | bytes 1441792 | tf_op jit(solution)/shard_map/optimization_barrier | solution.py:152
  185.2 2.1 %dot_general.95 = bf16[2048,11,16]{0,2,1:T(8,128)(2,1)} reshape(bf16[16,128,11,16]{1,0,3,2:T(8,128)(2,1)} %bitcast.202) | data formatting | bytes 1441792 | tf_op jit(solution)/shard_map/dct,dckl->tkl/dot_general | solution.py:340
  187.3 1.9 convolution_add_fusion
  189.3 1.5 collective-permute-start.15
  190.8 2.4 %collective-permute-start.17 = (f32[16,2048]{1,0:T(8,128)S(1)}, f32[16,2048]{1,0:T(8,128)S(1)}, u32[]{:S(2)}, u32[]{:S(2)}) collective-permute-start(f32[16,2048]{1,0:T(8,128)S(1)} %get-tuple-element.28), channel_id=1, source_target_pairs={{0,3},{1,0},{2,1},{3,2},{4,7},{5,4},{6,5},{7,6},{8,11},{9,8},{10,9... | collective-permute-start | bytes 393224 | tf_op jit(solution)/shard_map/ppermute | solution.py:205
  193.4 2.6 %fusion.10 = bf16[16,2048]{1,0:T(8,128)(2,1)} fusion(f32[16,11,16]{2,1,0:T(8,128)S(1)} %fusion.30, bf16[2048,11,16]{0,2,1:T(8,128)(2,1)} %dot_general.95, bf16[16,2048]{1,0:T(8,128)(2,1)S(1)} %get-tuple-element.26), kind=kOutput, calls=%fused_computation.16 | convolution fusion | flops 69304320 | bytes 863232 | tf_op jit(solution)/shard_map/dct,dckl->tkl/dot_general | solution.py:340
  195.9 1.7 collective-permute-done.15
  198.1 6.2 %collective-permute-done.16 = f32[16,2048]{1,0:T(8,128)S(1)} collective-permute-done((f32[16,2048]{1,0:T(8,128)S(1)}, f32[16,2048]{1,0:T(8,128)S(1)}, u32[]{:S(2)}, u32[]{:S(2)}) %collective-permute-start.16) | collective-permute-done | bytes 131104 | tf_op jit(solution)/shard_map/ppermute | solution.py:205
  (136 shorter events, 46.9 us)
Async XLA Ops:
  0.6 99.2 %copy-start = (bf16[1,2048,768]{2,1,0:T(8,128)(2,1)S(1)}, bf16[1,2048,768]{2,1,0:T(8,128)(2,1)}, u32[]{:S(2)}) copy-start(bf16[1,2048,768]{2,1,0:T(8,128)(2,1)} %param.31) | copy-start | bytes 9437188
  1.8 11.8 %copy-start.17 = (f32[16]{0:T(128)}, f32[16]{0:T(128)S(1)}, u32[]{:S(2)}) copy-start(f32[16]{0:T(128)S(1)} %add_rsqrt_fusion.1) | copy-start | bytes 196
  2.7 20.3 %collective-permute-start.1 = (bf16[16,2048]{1,0:T(8,128)(2,1)S(1)}, bf16[16,2048]{1,0:T(8,128)(2,1)}, u32[]{:S(2)}, u32[]{:S(2)}) collective-permute-start(bf16[16,2048]{1,0:T(8,128)(2,1)S(1)} %fusion.50), channel_id=1, source_target_pairs={{0,2},{1,3},{2,0},{3,1},{4,6},{5,7},{6,4},{7,5},{8,10},{9,11},{10,... | collective-permute-start | bytes 196616 | tf_op jit(solution)/shard_map/ppermute | solution.py:168
  6.8 16.2 %collective-permute-start = (bf16[16,2048]{1,0:T(8,128)(2,1)S(1)}, bf16[16,2048]{1,0:T(8,128)(2,1)}, u32[]{:S(2)}, u32[]{:S(2)}) collective-permute-start(bf16[16,2048]{1,0:T(8,128)(2,1)S(1)} %fusion.50), channel_id=1, source_target_pairs={{0,1},{1,2},{2,3},{3,0},{4,5},{5,6},{6,7},{7,4},{8,9},{9,10},{10,1... | collective-permute-start | bytes 196616 | tf_op jit(solution)/shard_map/ppermute | solution.py:168
  8.4 14.6 %collective-permute-start.2 = (bf16[16,2048]{1,0:T(8,128)(2,1)S(1)}, bf16[16,2048]{1,0:T(8,128)(2,1)}, u32[]{:S(2)}, u32[]{:S(2)}) collective-permute-start(bf16[16,2048]{1,0:T(8,128)(2,1)S(1)} %fusion.50), channel_id=1, source_target_pairs={{0,3},{1,0},{2,1},{3,2},{4,7},{5,4},{6,5},{7,6},{8,11},{9,8},{10,9... | collective-permute-start | bytes 196616 | tf_op jit(solution)/shard_map/ppermute | solution.py:168
  13.6 18.9 %copy-start.21 = (s32[1024]{0:T(1024)}, s32[1024]{0:T(1024)S(1)}, u32[]{:S(2)}) copy-start(s32[1024]{0:T(1024)S(1)} %pad_clamp_fusion.1) | copy-start | bytes 12292
  27.0 14.6 %copy-start.23 = (pred[4]{0:T(512)(128)(4,1)S(1)}, pred[4]{0:T(512)(128)(4,1)}, u32[]{:S(2)}) copy-start(pred[4]{0:T(512)(128)(4,1)} %compare_and_fusion) | copy-start | bytes 16
  28.2 13.4 %copy-start.25 = (pred[4,48]{1,0:T(4,128)(4,1)S(1)}, pred[4,48]{1,0:T(4,128)(4,1)}, u32[]{:S(2)}) copy-start(pred[4,48]{1,0:T(4,128)(4,1)} %concatenate.10) | copy-start | bytes 580
  28.3 15.8 %copy-start.10 = (bf16[4,32,128]{2,1,0:T(8,128)(2,1)S(1)}, bf16[4,32,128]{2,1,0:T(8,128)(2,1)}, u32[]{:S(2)}) copy-start(bf16[4,32,128]{2,1,0:T(8,128)(2,1)} %get-tuple-element.43) | copy-start | bytes 98308
  28.3 12.5 %collective-permute-start.5 = (bf16[64,128]{1,0:T(8,128)(2,1)S(1)}, bf16[64,128]{1,0:T(8,128)(2,1)S(1)}, u32[]{:S(2)}, u32[]{:S(2)}) collective-permute-start(bf16[64,128]{1,0:T(8,128)(2,1)S(1)} %convolution_convert_fusion.6), channel_id=1, source_target_pairs={{0,3},{1,0},{2,1},{3,2},{4,7},{5,4},{6,5},{7,6},{8,11},{9,8},{10,9... | collective-permute-start | bytes 49160 | tf_op jit(solution)/shard_map/ppermute | solution.py:168
  28.3 12.5 %collective-permute-start.4 = (bf16[64,128]{1,0:T(8,128)(2,1)S(1)}, bf16[64,128]{1,0:T(8,128)(2,1)S(1)}, u32[]{:S(2)}, u32[]{:S(2)}) collective-permute-start(bf16[64,128]{1,0:T(8,128)(2,1)S(1)} %convolution_convert_fusion.6), channel_id=1, source_target_pairs={{0,2},{1,3},{2,0},{3,1},{4,6},{5,7},{6,4},{7,5},{8,10},{9,11},{10,... | collective-permute-start | bytes 49160 | tf_op jit(solution)/shard_map/ppermute | solution.py:168
  29.6 11.3 %collective-permute-start.3 = (bf16[64,128]{1,0:T(8,128)(2,1)S(1)}, bf16[64,128]{1,0:T(8,128)(2,1)S(1)}, u32[]{:S(2)}, u32[]{:S(2)}) collective-permute-start(bf16[64,128]{1,0:T(8,128)(2,1)S(1)} %convolution_convert_fusion.6), channel_id=1, source_target_pairs={{0,1},{1,2},{2,3},{3,0},{4,5},{5,6},{6,7},{7,4},{8,9},{9,10},{10,1... | collective-permute-start | bytes 49160 | tf_op jit(solution)/shard_map/ppermute | solution.py:168
  35.2 36.3 %copy-start.4 = (bf16[16,2048]{1,0:T(8,128)(2,1)S(1)}, bf16[16,2048]{1,0:T(8,128)(2,1)}, u32[]{:S(2)}) copy-start(bf16[16,2048]{1,0:T(8,128)(2,1)} %param.18) | copy-start | bytes 196612
  35.3 39.0 %all-to-all-start = ((bf16[16,176,128]{2,1,0:T(8,128)(2,1)}), bf16[16,176,128]{2,1,0:T(8,128)(2,1)}, u32[]{:S(2)}, u32[]{:S(2)}) async-start(bf16[16,176,128]{2,1,0:T(8,128)(2,1)} %copy.131), calls=%async_computation | async-start | bytes 1441792 | tf_op jit(solution)/shard_map/all_to_all | solution.py:214
  40.8 32.0 %copy-start.14 = (f32[2048]{0:T(1024)S(1)}, f32[2048]{0:T(1024)}, u32[]{:S(2)}) copy-start(f32[2048]{0:T(1024)} %param.27) | copy-start | bytes 24580
  41.6 1.8 copy-start.16
  41.7 32.6 %copy-start.12 = (bf16[64,128]{1,0:T(8,128)(2,1)}, bf16[64,128]{1,0:T(8,128)(2,1)S(1)}, u32[]{:S(2)}) copy-start(bf16[64,128]{1,0:T(8,128)(2,1)S(1)} %get-tuple-element.37) | copy-start | bytes 49156
  47.3 0.8 copy-start.7
  48.9 11.8 %collective-permute-start.6 = (f32[16,2048]{1,0:T(8,128)}, f32[16,2048]{1,0:T(8,128)}, u32[]{:S(2)}, u32[]{:S(2)}) collective-permute-start(f32[16,2048]{1,0:T(8,128)} %get-tuple-element.30), channel_id=1, source_target_pairs={{0,1},{1,2},{2,3},{3,0},{4,5},{5,6},{6,7},{7,4},{8,9},{9,10},{10,1... | collective-permute-start | bytes 393224 | tf_op jit(solution)/shard_map/ppermute | solution.py:205
  50.7 9.9 %collective-permute-start.8 = (f32[16,2048]{1,0:T(8,128)}, f32[16,2048]{1,0:T(8,128)}, u32[]{:S(2)}, u32[]{:S(2)}) collective-permute-start(f32[16,2048]{1,0:T(8,128)} %get-tuple-element.31), channel_id=1, source_target_pairs={{0,3},{1,0},{2,1},{3,2},{4,7},{5,4},{6,5},{7,6},{8,11},{9,8},{10,9... | collective-permute-start | bytes 393224 | tf_op jit(solution)/shard_map/ppermute | solution.py:205
  52.7 18.9 %collective-permute-start.7 = (f32[16,2048]{1,0:T(8,128)}, f32[16,2048]{1,0:T(8,128)}, u32[]{:S(2)}, u32[]{:S(2)}) collective-permute-start(f32[16,2048]{1,0:T(8,128)} %get-tuple-element.32), channel_id=1, source_target_pairs={{0,2},{1,3},{2,0},{3,1},{4,6},{5,7},{6,4},{7,5},{8,10},{9,11},{10,... | collective-permute-start | bytes 393224 | tf_op jit(solution)/shard_map/ppermute | solution.py:205
  54.0 27.5 %copy-start.9 = (pred[16,11,16]{2,1,0:T(8,128)(4,1)}, pred[16,11,16]{2,1,0:T(8,128)(4,1)S(1)}, u32[]{:S(2)}) copy-start(pred[16,11,16]{2,1,0:T(8,128)(4,1)S(1)} %compare_reduce_fusion) | copy-start | bytes 8452
  72.8 64.3 %copy-start.19 = (f32[16]{0:T(128)}, f32[16]{0:T(128)S(1)}, u32[]{:S(2)}) copy-start(f32[16]{0:T(128)S(1)} %add_rsqrt_fusion) | copy-start | bytes 196
  74.3 24.2 %all-to-all-start.1 = ((bf16[16,176,128]{2,1,0:T(8,128)(2,1)}), bf16[16,176,128]{2,1,0:T(8,128)(2,1)}, u32[]{:S(2)}, u32[]{:S(2)}) async-start(bf16[16,176,128]{2,1,0:T(8,128)(2,1)} %copy.136), calls=%async_computation.1 | async-start | bytes 1441792 | tf_op jit(solution)/shard_map/all_to_all | solution.py:214
  81.5 1.8 copy-start.3
  99.8 2.1 %copy-start.1 = (bf16[1,2048,768]{2,1,0:T(8,128)(2,1)S(1)}, bf16[1,2048,768]{2,1,0:T(8,128)(2,1)}, u32[]{:S(2)}) copy-start(bf16[1,2048,768]{2,1,0:T(8,128)(2,1)} %param.32) | copy-start | bytes 9437188
  100.5 4.1 %copy-start.2 = (f32[16,11,768]{2,0,1:T(8,128)}, f32[16,11,768]{2,0,1:T(8,128)S(1)}, u32[]{:S(2)}) copy-start(f32[16,11,768]{2,0,1:T(8,128)S(1)} %convolution_bitcast_fusion.2) | copy-start | bytes 1622020
  101.9 1.6 copy-start.5
  102.6 0.8 copy-start.6
  106.9 24.2 %all-to-all-start.2 = ((bf16[16,176,128]{2,1,0:T(8,128)(2,1)}), bf16[16,176,128]{2,1,0:T(8,128)(2,1)}, u32[]{:S(2)}, u32[]{:S(2)}) async-start(bf16[16,176,128]{2,1,0:T(8,128)(2,1)} %copy.138), calls=%async_computation.2 | async-start | bytes 1441792 | tf_op jit(solution)/shard_map/all_to_all | solution.py:218
  111.3 24.0 %copy-start.15 = (f32[2048]{0:T(1024)S(1)}, f32[2048]{0:T(1024)}, u32[]{:S(2)}) copy-start(f32[2048]{0:T(1024)} %param.27) | copy-start | bytes 24580
  115.3 21.9 %copy-start.22 = (f32[16]{0:T(128)S(1)}, f32[16]{0:T(128)}, u32[]{:S(2)}) copy-start(f32[16]{0:T(128)} %convert_element_type.105) | copy-start | bytes 196
  137.1 3.6 %copy-start.24 = (f32[16]{0:T(128)}, f32[16]{0:T(128)S(1)}, u32[]{:S(2)}) copy-start(f32[16]{0:T(128)S(1)} %broadcast_multiply_fusion.1) | copy-start | bytes 196
  138.7 9.6 %collective-permute-start.11 = (bf16[16,2048]{1,0:T(8,128)(2,1)}, bf16[16,2048]{1,0:T(8,128)(2,1)}, u32[]{:S(2)}, u32[]{:S(2)}) collective-permute-start(bf16[16,2048]{1,0:T(8,128)(2,1)} %fusion.108), channel_id=1, source_target_pairs={{0,3},{1,0},{2,1},{3,2},{4,7},{5,4},{6,5},{7,6},{8,11},{9,8},{10,9... | collective-permute-start | bytes 196616 | tf_op jit(solution)/shard_map/ppermute | solution.py:321
  139.5 8.8 %collective-permute-start.10 = (bf16[16,2048]{1,0:T(8,128)(2,1)}, bf16[16,2048]{1,0:T(8,128)(2,1)}, u32[]{:S(2)}, u32[]{:S(2)}) collective-permute-start(bf16[16,2048]{1,0:T(8,128)(2,1)} %fusion.108), channel_id=1, source_target_pairs={{0,2},{1,3},{2,0},{3,1},{4,6},{5,7},{6,4},{7,5},{8,10},{9,11},{10,... | collective-permute-start | bytes 196616 | tf_op jit(solution)/shard_map/ppermute | solution.py:321
  139.8 8.6 %collective-permute-start.9 = (bf16[16,2048]{1,0:T(8,128)(2,1)}, bf16[16,2048]{1,0:T(8,128)(2,1)}, u32[]{:S(2)}, u32[]{:S(2)}) collective-permute-start(bf16[16,2048]{1,0:T(8,128)(2,1)} %fusion.108), channel_id=1, source_target_pairs={{0,1},{1,2},{2,3},{3,0},{4,5},{5,6},{6,7},{7,4},{8,9},{9,10},{10,1... | collective-permute-start | bytes 196616 | tf_op jit(solution)/shard_map/ppermute | solution.py:321
  142.9 16.8 %copy-start.13 = (bf16[64,128]{1,0:T(8,128)(2,1)S(1)}, bf16[64,128]{1,0:T(8,128)(2,1)}, u32[]{:S(2)}) copy-start(bf16[64,128]{1,0:T(8,128)(2,1)} %copy-done.12) | copy-start | bytes 49156
  142.9 30.6 %all-to-all-start.3 = ((bf16[16,176,128]{2,1,0:T(8,128)(2,1)}), bf16[16,176,128]{2,1,0:T(8,128)(2,1)}, u32[]{:S(2)}, u32[]{:S(2)}) async-start(bf16[16,176,128]{2,1,0:T(8,128)(2,1)} %copy.146), calls=%async_computation.3 | async-start | bytes 1441792 | tf_op jit(solution)/shard_map/all_to_all | solution.py:218
  175.0 12.3 %collective-permute-start.12 = (f32[64,128]{1,0:T(8,128)}, f32[64,128]{1,0:T(8,128)}, u32[]{:S(2)}, u32[]{:S(2)}) collective-permute-start(f32[64,128]{1,0:T(8,128)} %get-tuple-element.33), channel_id=1, source_target_pairs={{0,1},{1,2},{2,3},{3,0},{4,5},{5,6},{6,7},{7,4},{8,9},{9,10},{10,1... | collective-permute-start | bytes 98312 | tf_op jit(solution)/shard_map/ppermute | solution.py:205
  176.9 10.5 %collective-permute-start.14 = (f32[64,128]{1,0:T(8,128)}, f32[64,128]{1,0:T(8,128)}, u32[]{:S(2)}, u32[]{:S(2)}) collective-permute-start(f32[64,128]{1,0:T(8,128)} %get-tuple-element.34), channel_id=1, source_target_pairs={{0,3},{1,0},{2,1},{3,2},{4,7},{5,4},{6,5},{7,6},{8,11},{9,8},{10,9... | collective-permute-start | bytes 98312 | tf_op jit(solution)/shard_map/ppermute | solution.py:205
  178.8 8.5 %collective-permute-start.13 = (f32[64,128]{1,0:T(8,128)}, f32[64,128]{1,0:T(8,128)}, u32[]{:S(2)}, u32[]{:S(2)}) collective-permute-start(f32[64,128]{1,0:T(8,128)} %get-tuple-element.35), channel_id=1, source_target_pairs={{0,2},{1,3},{2,0},{3,1},{4,6},{5,7},{6,4},{7,5},{8,10},{9,11},{10,... | collective-permute-start | bytes 98312 | tf_op jit(solution)/shard_map/ppermute | solution.py:205
  183.0 21.3 %copy-start.11 = (f32[2048]{0:T(1024)S(1)}, f32[2048]{0:T(1024)}, u32[]{:S(2)}) copy-start(f32[2048]{0:T(1024)} %param.26) | copy-start | bytes 24580
  183.0 21.3 %copy-start.18 = (f32[16]{0:T(128)S(1)}, f32[16]{0:T(128)}, u32[]{:S(2)}) copy-start(f32[16]{0:T(128)} %copy-done.17) | copy-start | bytes 196
  185.2 19.4 %copy-start.20 = (f32[16]{0:T(128)S(1)}, f32[16]{0:T(128)}, u32[]{:S(2)}) copy-start(f32[16]{0:T(128)} %copy-done.19) | copy-start | bytes 196
  187.3 17.2 %copy-start.8 = (bf16[16,2048]{1,0:T(8,128)(2,1)S(1)}, bf16[16,2048]{1,0:T(8,128)(2,1)}, u32[]{:S(2)}) copy-start(bf16[16,2048]{1,0:T(8,128)(2,1)} %param.19) | copy-start | bytes 196612
  189.3 8.3 %collective-permute-start.15 = (f32[16,2048]{1,0:T(8,128)S(1)}, f32[16,2048]{1,0:T(8,128)S(1)}, u32[]{:S(2)}, u32[]{:S(2)}) collective-permute-start(f32[16,2048]{1,0:T(8,128)S(1)} %get-tuple-element.27), channel_id=1, source_target_pairs={{0,1},{1,2},{2,3},{3,0},{4,5},{5,6},{6,7},{7,4},{8,9},{9,10},{10,1... | collective-permute-start | bytes 393224 | tf_op jit(solution)/shard_map/ppermute | solution.py:205
  190.8 7.2 %collective-permute-start.17 = (f32[16,2048]{1,0:T(8,128)S(1)}, f32[16,2048]{1,0:T(8,128)S(1)}, u32[]{:S(2)}, u32[]{:S(2)}) collective-permute-start(f32[16,2048]{1,0:T(8,128)S(1)} %get-tuple-element.28), channel_id=1, source_target_pairs={{0,3},{1,0},{2,1},{3,2},{4,7},{5,4},{6,5},{7,6},{8,11},{9,8},{10,9... | collective-permute-start | bytes 393224 | tf_op jit(solution)/shard_map/ppermute | solution.py:205
  193.2 11.1 %collective-permute-start.16 = (f32[16,2048]{1,0:T(8,128)S(1)}, f32[16,2048]{1,0:T(8,128)S(1)}, u32[]{:S(2)}, u32[]{:S(2)}) collective-permute-start(f32[16,2048]{1,0:T(8,128)S(1)} %get-tuple-element.29), channel_id=1, source_target_pairs={{0,2},{1,3},{2,0},{3,1},{4,6},{5,7},{6,4},{7,5},{8,10},{9,11},{10,... | collective-permute-start | bytes 393224 | tf_op jit(solution)/shard_map/ppermute | solution.py:205
  (1 other events, 0.6 us)

commit v20 on v19

--- a/solution.py
+++ b/solution.py
@@ -95,7 +95,6 @@
     own_rows = jnp.dot(row_block, own_kv_weights, preferred_element_type=jnp.float32).astype(
         jnp.bfloat16
     )
-    own_rows, carried = lax.optimization_barrier((own_rows, carried))
     kv_rows = head_gather(own_rows, 1)
     pair_rows = jnp.concatenate(
         [
@@ -243,7 +242,7 @@
     attn_rows = normed_one.astype(jnp.bfloat16)
     heads_here = w_query.shape[1] // HEAD_SIZE
     first_head = lax.axis_index("head") * heads_here
-    gathered_rows = head_rows(attn_rows)
+
     device_count = lax.axis_size("expert") * lax.axis_size("head")
     capacity = (owned * TOP * 4 + 3 * device_count - 1) // (3 * device_count)
     slot_total = device_count * capacity
@@ -268,6 +267,8 @@
         cotangent.reshape(owned, pieces, lanes),
         precision=highest_prec,
     ).astype(jnp.bfloat16)
+    attn_rows, grad_out = lax.optimization_barrier((attn_rows, grad_out))
+    gathered_rows = head_rows(attn_rows)
     attended, saved, grad_out = attention_forward(
         gathered_rows, w_query, key_value_weight, key_cache, prefix_value_cache, cache_lengths, first_head, grad_out
     )

time: 208 us -> 202 us (0.971)
  waiting for transfers between devices: 54.9 us -> 49.4 us
    ppermute x9, waiting for transfers between devices: 25.9 us -> 18.3 us  [head_sums(): lax.ppermute(chunk((me + shift) % count), 'head', perm=[(j, (j + shift) %...]
    ppermute x6, waiting for transfers between devices: 0.02 us -> 2.19 us  [head_gather(): lax.ppermute(block, 'head', perm=[(j, (j + shift) % count) for j in range...]
    another operation x4 -> x3, other arithmetic: 4.26 us -> 2.42 us  [head_order(): jnp.stack(parts)]
    unnamed x56 -> x52, local copies, waits for them, and re-layouts: 7.3 us -> 6.72 us
  transfers between devices with their start and end apart: 22 -> 22, of which waited for: 7 -> 9; matrix products, arithmetic and copies ran while one was open for 36% -> 37% of each run, Pallas kernels for 0% -> 0%
where the time goes in v20:
time: 202 us; the launch traced here: 200 us
  waiting for transfers between devices  49.4 us (24%)
  starting transfers between devices  44.9 us (22%)
  local copies, waits for them, and re-layouts  42.6 us (21%)
  matrix products  42.6 us (21%)
  other arithmetic  19.5 us (10%)
    ppermute x9, waiting for transfers between devices, head_sums(): lax.ppermute(chunk((me + shift) % count), 'head', perm=[(j, (j + shift) %...  18.3 us
    all_to_all x2, waiting for transfers between devices, from_experts(): lax.all_to_all(results, ('expert', 'head'), split_axis=0, concat_axis=0,...  15.8 us
    all_to_all x2, waiting for transfers between devices, to_experts(): lax.all_to_all(outgoing, ('expert', 'head'), split_axis=0, concat_axis=0,...  13.1 us
    ppermute x9, starting transfers between devices, head_sums(): lax.ppermute(chunk((me + shift) % count), 'head', perm=[(j, (j + shift) %...  12.7 us
    ppermute x6, starting transfers between devices, head_gather(): lax.ppermute(block, 'head', perm=[(j, (j + shift) % count) for j in range...  10.9 us
    all_to_all x2, starting transfers between devices, from_experts(): lax.all_to_all(results, ('expert', 'head'), split_axis=0, concat_axis=0,...  9.8 us
    all_to_all x2, starting transfers between devices, to_experts(): lax.all_to_all(outgoing, ('expert', 'head'), split_axis=0, concat_axis=0,...  9.44 us
    unnamed x52, local copies, waits for them, and re-layouts  6.72 us
  transfers between devices with their start and end apart: 22, of which 9 were waited for; matrix products, arithmetic and copies ran while one was open for 37% of the time, Pallas kernels for 0%

profile of v20, /device:TPU:0, one launch (start us, length us, event | category | flops | bytes accessed | tf_op | source)
XLA Modules:
  0.0 200.1 jit_solution(302015174061479992)
XLA Ops:
  6.7 2.2 %convolution_convert_fusion = bf16[16,11,16,128]{3,0,2,1:T(8,128)(2,1)S(1)} fusion(f32[16,11,16,1]{2,1,0,3:T(8,128)S(1)} %bitcast.206, bf16[16,2048]{1,0:T(8,128)(2,1)} %param.19, f32[16]{0:T(128)S(1)} %convert_element_type.104), kind=kOutput, calls=%fused_computation.19 | convolution fusion | flops 69632000 | bytes 797760 | tf_op jit(solution)/shard_map/dct,tkl->dckl/dot_general | solution.py:264
  8.9 5.1 %collective-permute-start.2 = (bf16[16,2048]{1,0:T(8,128)(2,1)S(1)}, bf16[16,2048]{1,0:T(8,128)(2,1)S(1)}, u32[]{:S(2)}, u32[]{:S(2)}) collective-permute-start(bf16[16,2048]{1,0:T(8,128)(2,1)S(1)} %fusion.50), channel_id=1, source_target_pairs={{0,3},{1,0},{2,1},{3,2},{4,7},{5,4},{6,5},{7,6},{8,11},{9,8},{10,9... | collective-permute-start | bytes 196616 | tf_op jit(solution)/shard_map/ppermute | solution.py:167
  16.1 5.2 %all-to-all-start = ((bf16[16,176,128]{2,1,0:T(8,128)(2,1)}), bf16[16,176,128]{2,1,0:T(8,128)(2,1)}, u32[]{:S(2)}, u32[]{:S(2)}) async-start(bf16[16,176,128]{2,1,0:T(8,128)(2,1)} %copy.131), calls=%async_computation | async-start | bytes 1441792 | tf_op jit(solution)/shard_map/all_to_all | solution.py:213
  26.2 1.4 constant_dynamic-slice_fusion.9
  28.8 1.5 gather_fusion.1
  32.3 3.7 %collective-permute-start.5 = (bf16[64,128]{1,0:T(8,128)(2,1)S(1)}, bf16[64,128]{1,0:T(8,128)(2,1)S(1)}, u32[]{:S(2)}, u32[]{:S(2)}) collective-permute-start(bf16[64,128]{1,0:T(8,128)(2,1)S(1)} %convolution_convert_fusion.6), channel_id=1, source_target_pairs={{0,3},{1,0},{2,1},{3,2},{4,7},{5,4},{6,5},{7,6},{8,11},{9,8},{10,9... | collective-permute-start | bytes 49160 | tf_op jit(solution)/shard_map/ppermute | solution.py:167
  37.2 2.1 %convolution_convert_fusion.5 = bf16[64,512]{1,0:T(8,128)(2,1)S(1)} fusion(bf16[64,2048]{1,0:T(8,128)(2,1)S(1)} %bitcast.204, bf16[2048,512]{1,0:T(8,128)(2,1)} %param.28), kind=kOutput, calls=%fused_computation.40 | convolution fusion | flops 134250496 | bytes 2424832 | tf_op jit(solution)/shard_map/dot_general | solution.py:83
  39.9 2.2 %collective-permute-done.4 = bf16[64,128]{1,0:T(8,128)(2,1)S(1)} collective-permute-done((bf16[64,128]{1,0:T(8,128)(2,1)S(1)}, bf16[64,128]{1,0:T(8,128)(2,1)S(1)}, u32[]{:S(2)}, u32[]{:S(2)}) %collective-permute-start.4) | collective-permute-done | bytes 16416 | tf_op jit(solution)/shard_map/ppermute | solution.py:167
  43.5 1.8 fusion.110
  46.5 2.1 %fusion.67 = f32[64,2048]{1,0:T(8,128)S(1)} fusion(bf16[512,2048]{1,0:T(8,128)(2,1)} %param.30, bf16[8,8,4,128]{3,2,1,0:T(4,128)(2,1)S(1)} %bitcast.211), kind=kOutput, calls=%fused_computation.102 | convolution fusion | flops 134217728 | bytes 2686976 | tf_op jit(solution)/shard_map/dot_general | solution.py:275
  50.6 3.4 %collective-permute-start.8 = (f32[16,2048]{1,0:T(8,128)}, f32[16,2048]{1,0:T(8,128)}, u32[]{:S(2)}, u32[]{:S(2)}) collective-permute-start(f32[16,2048]{1,0:T(8,128)} %get-tuple-element.31), channel_id=1, source_target_pairs={{0,3},{1,0},{2,1},{3,2},{4,7},{5,4},{6,5},{7,6},{8,11},{9,8},{10,9... | collective-permute-start | bytes 393224 | tf_op jit(solution)/shard_map/ppermute | solution.py:204
  54.3 4.4 %collective-permute-done.6 = f32[16,2048]{1,0:T(8,128)} collective-permute-done((f32[16,2048]{1,0:T(8,128)}, f32[16,2048]{1,0:T(8,128)}, u32[]{:S(2)}, u32[]{:S(2)}) %collective-permute-start.6) | collective-permute-done | bytes 131104 | tf_op jit(solution)/shard_map/ppermute | solution.py:204
  59.2 5.1 %collective-permute-done.7 = f32[16,2048]{1,0:T(8,128)} collective-permute-done((f32[16,2048]{1,0:T(8,128)}, f32[16,2048]{1,0:T(8,128)}, u32[]{:S(2)}, u32[]{:S(2)}) %collective-permute-start.7) | collective-permute-done | bytes 131104 | tf_op jit(solution)/shard_map/ppermute | solution.py:204
  67.7 4.3 %all-to-all-start.1 = ((bf16[16,176,128]{2,1,0:T(8,128)(2,1)}), bf16[16,176,128]{2,1,0:T(8,128)(2,1)}, u32[]{:S(2)}, u32[]{:S(2)}) async-start(bf16[16,176,128]{2,1,0:T(8,128)(2,1)} %copy.136), calls=%async_computation.1 | async-start | bytes 1441792 | tf_op jit(solution)/shard_map/all_to_all | solution.py:213
  72.0 2.9 %copy.173 = bf16[96,8,16,128]{3,2,1,0:T(8,128)(2,1)S(1)} copy(bf16[96,8,16,128]{3,1,2,0:T(8,128)(2,1)} %bitcast.195) | data formatting | bytes 6291456
  74.9 1.8 copy.132
  76.8 2.0 %fusion.15 = f32[16,11,768]{2,0,1:T(8,128)} fusion(bf16[16,11,16,128]{3,0,2,1:T(8,128)(2,1)S(1)} %bitcast.208, bf16[768,16,128]{2,1,0:T(8,128)(2,1)S(1)} %bitcast.196), kind=kOutput, calls=%fused_computation.22 | convolution fusion | flops 553648128 | bytes 4407296 | tf_op jit(solution)/shard_map/sckl,fkl->scf/dot_general | solution.py:301
  78.8 13.1 %all-to-all-done.1 = bf16[16,176,128]{2,1,0:T(8,128)(2,1)} async-done(((bf16[16,176,128]{2,1,0:T(8,128)(2,1)}), bf16[16,176,128]{2,1,0:T(8,128)(2,1)}, u32[]{:S(2)}, u32[]{:S(2)}) %all-to-all-start.1) | async-done | bytes 720928 | tf_op jit(solution)/shard_map/all_to_all | solution.py:213
  100.3 4.5 %all-to-all-start.2 = ((bf16[16,176,128]{2,1,0:T(8,128)(2,1)}), bf16[16,176,128]{2,1,0:T(8,128)(2,1)}, u32[]{:S(2)}, u32[]{:S(2)}) async-start(bf16[16,176,128]{2,1,0:T(8,128)(2,1)} %copy.138), calls=%async_computation.2 | async-start | bytes 1441792 | tf_op jit(solution)/shard_map/all_to_all | solution.py:217
  104.8 3.9 %fusion.11 = bf16[16,11,16,128]{3,0,2,1:T(8,128)(2,1)} fusion(bf16[768,16,128]{2,1,0:T(8,128)(2,1)} %bitcast.197, f32[16,11,768]{2,0,1:T(8,128)} %copy-done.5, f32[16,11,768]{2,0,1:T(8,128)} %copy-done.2), kind=kOutput, calls=%fused_computation.18 | convolution fusion | flops 554819584 | bytes 4947968 | tf_op jit(solution)/shard_map/scf,fkl->sckl/dot_general | solution.py:298
  108.7 15.8 %all-to-all-done.2 = bf16[16,176,128]{2,1,0:T(8,128)(2,1)} async-done(((bf16[16,176,128]{2,1,0:T(8,128)(2,1)}), bf16[16,176,128]{2,1,0:T(8,128)(2,1)}, u32[]{:S(2)}, u32[]{:S(2)}) %all-to-all-start.2) | async-done | bytes 720928 | tf_op jit(solution)/shard_map/all_to_all | solution.py:217
  124.5 2.1 %copy.231 = bf16[16,11,16,128]{3,2,0,1:T(8,128)(2,1)} copy(bf16[16,11,16,128]{3,2,1,0:T(8,128)(2,1)} %bitcast.45) | data formatting | bytes 1441792 | tf_op jit(solution)/shard_map/reshape | solution.py:313
  126.6 2.2 %dot_general.87 = bf16[2048,11,16]{0,2,1:T(8,128)(2,1)} reshape(bf16[16,128,11,16]{1,0,3,2:T(8,128)(2,1)} %bitcast.200) | data formatting | bytes 1441792 | tf_op jit(solution)/shard_map/dct,dckl->tkl/dot_general | solution.py:314
  128.8 1.8 fusion.46
  130.6 1.6 fusion.108
  134.2 2.2 %copy.146 = bf16[16,176,128]{2,1,0:T(8,128)(2,1)} copy(bf16[16,176,128]{2,0,1:T(8,128)(2,1)} %bitcast.207) | data formatting | bytes 1441792 | tf_op jit(solution)/shard_map/reshape | solution.py:325
  136.4 5.4 %all-to-all-start.3 = ((bf16[16,176,128]{2,1,0:T(8,128)(2,1)}), bf16[16,176,128]{2,1,0:T(8,128)(2,1)}, u32[]{:S(2)}, u32[]{:S(2)}) async-start(bf16[16,176,128]{2,1,0:T(8,128)(2,1)} %copy.146), calls=%async_computation.3 | async-start | bytes 1441792 | tf_op jit(solution)/shard_map/all_to_all | solution.py:217
  141.8 1.7 pad_maximum_fusion.1
  143.5 2.4 %gather_fusion.2 = bf16[4,16,2048]{2,1,0:T(8,128)(2,1)} fusion(bf16[4,16,2048]{2,1,0:T(8,128)(2,1)} %pad_maximum_fusion.1, s32[1024]{0:T(1024)} %copy-done.17), kind=kCustom, calls=%fused_computation.1.clone | custom fusion | bytes 524304 | tf_op jit(solution)/shard_map/jit(_take)/gather | solution.py:177
  146.9 3.0 %convolution_convert_fusion.3 = bf16[64,512]{1,0:T(8,128)(2,1)} fusion(bf16[64,2048]{1,0:T(8,128)(2,1)S(1)} %bitcast.205, bf16[512,2048]{1,0:T(8,128)(2,1)} %param.30), kind=kOutput, calls=%fused_computation.38 | convolution fusion | flops 134250496 | bytes 2424832 | tf_op jit(solution)/shard_map/td,fd->tf/dot_general | solution.py:133
  149.9 1.5 reshape.203
  153.2 1.7 convolution_bitcast_fusion.4
  154.8 3.0 %convolution_bitcast_fusion.6 = f32[4,48,128]{2,1,0:T(8,128)} fusion(f32[4,4,16,48]{3,2,1,0:T(8,128)} %convolution_bitcast_fusion.4, bf16[4,16,4,128]{3,2,1,0:T(4,128)(2,1)} %reshape.193, f32[4,4,16,48]{3,2,1,0:T(8,128)} %get-tuple-element.39, f32[4,4,16]{2,1,0:T(4,128)} %copy-done.24), kind=kOutput, calls=%fused_computation.37 | convolution fusion | flops 3232047 | bytes 263168 | tf_op jit(solution)/shard_map/shbk,sbhd->skd/dot_general | solution.py:58
  159.2 2.9 %fusion.27 = bf16[4,16,4,128]{3,1,2,0:T(8,128)(2,1)} fusion(f32[4,4,16,48]{3,2,1,0:T(8,128)} %convolution_bitcast_fusion.4, bf16[4,16,128]{2,1,0:T(8,128)(2,1)} %bitcast.222, bf16[4,32,128]{2,1,0:T(8,128)(2,1)} %get-tuple-element.42, f32[4,4,16,48]{3,2,1,0:T(8,128)} %get-tuple-element.39, f32[4,4,16]{2,1,0:T(4,128)} %copy-done.24), kind=kOutput, calls=%fused_computation.42 | convolution fusion | flops 3363119 | bytes 214016 | tf_op jit(solution)/shard_map/shbk,skd->sbhd/dot_general | solution.py:55
  162.1 1.5 copy.150
  167.0 1.4 constant_dynamic-slice_fusion.4
  168.4 1.9 collective-permute-start.12
  170.3 2.0 collective-permute-start.14
  173.2 3.2 %fusion.64 = f32[64,2048]{1,0:T(8,128)} fusion(bf16[2048,512]{1,0:T(8,128)(2,1)} %param.28, bf16[8,8,4,128]{3,2,1,0:T(4,128)(2,1)} %bitcast.210), kind=kOutput, calls=%fused_computation.99 | convolution fusion | flops 134217728 | bytes 2686976 | tf_op jit(solution)/shard_map/tf,df->td/dot_general | solution.py:157
  176.5 2.2 %copy.230 = bf16[16,11,16,128]{3,2,0,1:T(8,128)(2,1)} copy(bf16[16,11,16,128]{3,2,1,0:T(8,128)(2,1)} %bitcast.64) | data formatting | bytes 1441792 | tf_op jit(solution)/shard_map/optimization_barrier | solution.py:151
  178.6 2.1 %dot_general.95 = bf16[2048,11,16]{0,2,1:T(8,128)(2,1)} reshape(bf16[16,128,11,16]{1,0,3,2:T(8,128)(2,1)} %bitcast.201) | data formatting | bytes 1441792 | tf_op jit(solution)/shard_map/dct,dckl->tkl/dot_general | solution.py:341
  180.8 1.9 convolution_add_fusion
  182.8 1.5 collective-permute-start.15
  184.3 2.4 %collective-permute-start.17 = (f32[16,2048]{1,0:T(8,128)S(1)}, f32[16,2048]{1,0:T(8,128)S(1)}, u32[]{:S(2)}, u32[]{:S(2)}) collective-permute-start(f32[16,2048]{1,0:T(8,128)S(1)} %get-tuple-element.28), channel_id=1, source_target_pairs={{0,3},{1,0},{2,1},{3,2},{4,7},{5,4},{6,5},{7,6},{8,11},{9,8},{10,9... | collective-permute-start | bytes 393224 | tf_op jit(solution)/shard_map/ppermute | solution.py:204
  186.8 2.6 %fusion.10 = bf16[16,2048]{1,0:T(8,128)(2,1)} fusion(f32[16,11,16]{2,1,0:T(8,128)S(1)} %fusion.30, bf16[2048,11,16]{0,2,1:T(8,128)(2,1)} %dot_general.95, bf16[16,2048]{1,0:T(8,128)(2,1)S(1)} %get-tuple-element.26), kind=kOutput, calls=%fused_computation.16 | convolution fusion | flops 69304320 | bytes 863232 | tf_op jit(solution)/shard_map/dct,dckl->tkl/dot_general | solution.py:341
  189.4 1.7 collective-permute-done.15
  191.6 6.2 %collective-permute-done.16 = f32[16,2048]{1,0:T(8,128)S(1)} collective-permute-done((f32[16,2048]{1,0:T(8,128)S(1)}, f32[16,2048]{1,0:T(8,128)S(1)}, u32[]{:S(2)}, u32[]{:S(2)}) %collective-permute-start.16) | collective-permute-done | bytes 131104 | tf_op jit(solution)/shard_map/ppermute | solution.py:204
  198.7 1.4 fusion.55
  (131 shorter events, 47.3 us)
Async XLA Ops:
  0.6 92.6 %copy-start = (bf16[1,2048,768]{2,1,0:T(8,128)(2,1)S(1)}, bf16[1,2048,768]{2,1,0:T(8,128)(2,1)}, u32[]{:S(2)}) copy-start(bf16[1,2048,768]{2,1,0:T(8,128)(2,1)} %param.31) | copy-start | bytes 9437188
  0.6 21.7 %copy-start.23 = (s32[4]{0:T(128)S(1)}, s32[4]{0:T(128)}, u32[]{:S(2)}) copy-start(s32[4]{0:T(128)} %param.23) | copy-start | bytes 52
  1.5 7.4 %copy-start.18 = (f32[16]{0:T(128)}, f32[16]{0:T(128)S(1)}, u32[]{:S(2)}) copy-start(f32[16]{0:T(128)S(1)} %convert_element_type.104) | copy-start | bytes 196
  2.6 6.3 %copy-start.21 = (f32[16]{0:T(128)}, f32[16]{0:T(128)S(1)}, u32[]{:S(2)}) copy-start(f32[16]{0:T(128)S(1)} %add_rsqrt_fusion.1) | copy-start | bytes 196
  8.9 19.2 %collective-permute-start.2 = (bf16[16,2048]{1,0:T(8,128)(2,1)S(1)}, bf16[16,2048]{1,0:T(8,128)(2,1)S(1)}, u32[]{:S(2)}, u32[]{:S(2)}) collective-permute-start(bf16[16,2048]{1,0:T(8,128)(2,1)S(1)} %fusion.50), channel_id=1, source_target_pairs={{0,3},{1,0},{2,1},{3,2},{4,7},{5,4},{6,5},{7,6},{8,11},{9,8},{10,9... | collective-permute-start | bytes 196616 | tf_op jit(solution)/shard_map/ppermute | solution.py:167
  14.0 14.1 %collective-permute-start.1 = (bf16[16,2048]{1,0:T(8,128)(2,1)S(1)}, bf16[16,2048]{1,0:T(8,128)(2,1)S(1)}, u32[]{:S(2)}, u32[]{:S(2)}) collective-permute-start(bf16[16,2048]{1,0:T(8,128)(2,1)S(1)} %fusion.50), channel_id=1, source_target_pairs={{0,2},{1,3},{2,0},{3,1},{4,6},{5,7},{6,4},{7,5},{8,10},{9,11},{10,... | collective-permute-start | bytes 196616 | tf_op jit(solution)/shard_map/ppermute | solution.py:167
  14.0 14.1 %collective-permute-start = (bf16[16,2048]{1,0:T(8,128)(2,1)S(1)}, bf16[16,2048]{1,0:T(8,128)(2,1)S(1)}, u32[]{:S(2)}, u32[]{:S(2)}) collective-permute-start(bf16[16,2048]{1,0:T(8,128)(2,1)S(1)} %fusion.50), channel_id=1, source_target_pairs={{0,1},{1,2},{2,3},{3,0},{4,5},{5,6},{6,7},{7,4},{8,9},{9,10},{10,1... | collective-permute-start | bytes 196616 | tf_op jit(solution)/shard_map/ppermute | solution.py:167
  16.1 51.7 %all-to-all-start = ((bf16[16,176,128]{2,1,0:T(8,128)(2,1)}), bf16[16,176,128]{2,1,0:T(8,128)(2,1)}, u32[]{:S(2)}, u32[]{:S(2)}) async-start(bf16[16,176,128]{2,1,0:T(8,128)(2,1)} %copy.131), calls=%async_computation | async-start | bytes 1441792 | tf_op jit(solution)/shard_map/all_to_all | solution.py:213
  23.7 22.8 %copy-start.17 = (s32[1024]{0:T(1024)}, s32[1024]{0:T(1024)S(1)}, u32[]{:S(2)}) copy-start(s32[1024]{0:T(1024)S(1)} %pad_clamp_fusion.1) | copy-start | bytes 12292
  32.3 7.5 %collective-permute-start.5 = (bf16[64,128]{1,0:T(8,128)(2,1)S(1)}, bf16[64,128]{1,0:T(8,128)(2,1)S(1)}, u32[]{:S(2)}, u32[]{:S(2)}) collective-permute-start(bf16[64,128]{1,0:T(8,128)(2,1)S(1)} %convolution_convert_fusion.6), channel_id=1, source_target_pairs={{0,3},{1,0},{2,1},{3,2},{4,7},{5,4},{6,5},{7,6},{8,11},{9,8},{10,9... | collective-permute-start | bytes 49160 | tf_op jit(solution)/shard_map/ppermute | solution.py:167
  36.0 6.0 %collective-permute-start.4 = (bf16[64,128]{1,0:T(8,128)(2,1)S(1)}, bf16[64,128]{1,0:T(8,128)(2,1)S(1)}, u32[]{:S(2)}, u32[]{:S(2)}) collective-permute-start(bf16[64,128]{1,0:T(8,128)(2,1)S(1)} %convolution_convert_fusion.6), channel_id=1, source_target_pairs={{0,2},{1,3},{2,0},{3,1},{4,6},{5,7},{6,4},{7,5},{8,10},{9,11},{10,... | collective-permute-start | bytes 49160 | tf_op jit(solution)/shard_map/ppermute | solution.py:167
  36.0 6.0 %collective-permute-start.3 = (bf16[64,128]{1,0:T(8,128)(2,1)S(1)}, bf16[64,128]{1,0:T(8,128)(2,1)S(1)}, u32[]{:S(2)}, u32[]{:S(2)}) collective-permute-start(bf16[64,128]{1,0:T(8,128)(2,1)S(1)} %convolution_convert_fusion.6), channel_id=1, source_target_pairs={{0,1},{1,2},{2,3},{3,0},{4,5},{5,6},{6,7},{7,4},{8,9},{9,10},{10,1... | collective-permute-start | bytes 49160 | tf_op jit(solution)/shard_map/ppermute | solution.py:167
  39.2 25.1 %copy-start.7 = (bf16[16,2048]{1,0:T(8,128)(2,1)S(1)}, bf16[16,2048]{1,0:T(8,128)(2,1)}, u32[]{:S(2)}) copy-start(bf16[16,2048]{1,0:T(8,128)(2,1)} %param.18) | copy-start | bytes 196612
  43.5 15.7 %copy-start.10 = (bf16[64,128]{1,0:T(8,128)(2,1)}, bf16[64,128]{1,0:T(8,128)(2,1)S(1)}, u32[]{:S(2)}) copy-start(bf16[64,128]{1,0:T(8,128)(2,1)S(1)} %get-tuple-element.37) | copy-start | bytes 49156
  43.5 15.7 %copy-start.14 = (bf16[64,128]{1,0:T(8,128)(2,1)}, bf16[64,128]{1,0:T(8,128)(2,1)S(1)}, u32[]{:S(2)}) copy-start(bf16[64,128]{1,0:T(8,128)(2,1)S(1)} %get-tuple-element.36) | copy-start | bytes 49156
  45.3 13.9 %copy-start.24 = (f32[4,4,16]{2,1,0:T(4,128)}, f32[4,4,16]{2,1,0:T(4,128)S(1)}, u32[]{:S(2)}) copy-start(f32[4,4,16]{2,1,0:T(4,128)S(1)} %get-tuple-element.38) | copy-start | bytes 3076
  48.6 0.8 copy-start.6
  50.2 8.5 %collective-permute-start.6 = (f32[16,2048]{1,0:T(8,128)}, f32[16,2048]{1,0:T(8,128)}, u32[]{:S(2)}, u32[]{:S(2)}) collective-permute-start(f32[16,2048]{1,0:T(8,128)} %get-tuple-element.30), channel_id=1, source_target_pairs={{0,1},{1,2},{2,3},{3,0},{4,5},{5,6},{6,7},{7,4},{8,9},{9,10},{10,1... | collective-permute-start | bytes 393224 | tf_op jit(solution)/shard_map/ppermute | solution.py:204
  50.6 8.6 %collective-permute-start.8 = (f32[16,2048]{1,0:T(8,128)}, f32[16,2048]{1,0:T(8,128)}, u32[]{:S(2)}, u32[]{:S(2)}) collective-permute-start(f32[16,2048]{1,0:T(8,128)} %get-tuple-element.31), channel_id=1, source_target_pairs={{0,3},{1,0},{2,1},{3,2},{4,7},{5,4},{6,5},{7,6},{8,11},{9,8},{10,9... | collective-permute-start | bytes 393224 | tf_op jit(solution)/shard_map/ppermute | solution.py:204
  54.0 10.3 %collective-permute-start.7 = (f32[16,2048]{1,0:T(8,128)}, f32[16,2048]{1,0:T(8,128)}, u32[]{:S(2)}, u32[]{:S(2)}) collective-permute-start(f32[16,2048]{1,0:T(8,128)} %get-tuple-element.32), channel_id=1, source_target_pairs={{0,2},{1,3},{2,0},{3,1},{4,6},{5,7},{6,4},{7,5},{8,10},{9,11},{10,... | collective-permute-start | bytes 393224 | tf_op jit(solution)/shard_map/ppermute | solution.py:204
  54.3 20.6 %copy-start.9 = (pred[16,11,16]{2,1,0:T(8,128)(4,1)}, pred[16,11,16]{2,1,0:T(8,128)(4,1)S(1)}, u32[]{:S(2)}) copy-start(pred[16,11,16]{2,1,0:T(8,128)(4,1)S(1)} %compare_reduce_fusion) | copy-start | bytes 8452
  65.5 65.0 %copy-start.15 = (f32[16]{0:T(128)}, f32[16]{0:T(128)S(1)}, u32[]{:S(2)}) copy-start(f32[16]{0:T(128)S(1)} %add_rsqrt_fusion) | copy-start | bytes 196
  67.7 24.2 %all-to-all-start.1 = ((bf16[16,176,128]{2,1,0:T(8,128)(2,1)}), bf16[16,176,128]{2,1,0:T(8,128)(2,1)}, u32[]{:S(2)}, u32[]{:S(2)}) async-start(bf16[16,176,128]{2,1,0:T(8,128)(2,1)} %copy.136), calls=%async_computation.1 | async-start | bytes 1441792 | tf_op jit(solution)/shard_map/all_to_all | solution.py:213
  74.9 1.8 copy-start.3
  93.2 2.1 %copy-start.1 = (bf16[1,2048,768]{2,1,0:T(8,128)(2,1)S(1)}, bf16[1,2048,768]{2,1,0:T(8,128)(2,1)}, u32[]{:S(2)}) copy-start(bf16[1,2048,768]{2,1,0:T(8,128)(2,1)} %param.32) | copy-start | bytes 9437188
  94.0 4.1 %copy-start.2 = (f32[16,11,768]{2,0,1:T(8,128)}, f32[16,11,768]{2,0,1:T(8,128)S(1)}, u32[]{:S(2)}) copy-start(f32[16,11,768]{2,0,1:T(8,128)S(1)} %convolution_bitcast_fusion.2) | copy-start | bytes 1622020
  95.3 1.6 copy-start.4
  96.1 0.8 copy-start.5
  100.3 24.2 %all-to-all-start.2 = ((bf16[16,176,128]{2,1,0:T(8,128)(2,1)}), bf16[16,176,128]{2,1,0:T(8,128)(2,1)}, u32[]{:S(2)}, u32[]{:S(2)}) async-start(bf16[16,176,128]{2,1,0:T(8,128)(2,1)} %copy.138), calls=%async_computation.2 | async-start | bytes 1441792 | tf_op jit(solution)/shard_map/all_to_all | solution.py:217
  104.8 24.0 %copy-start.12 = (f32[2048]{0:T(1024)S(1)}, f32[2048]{0:T(1024)}, u32[]{:S(2)}) copy-start(f32[2048]{0:T(1024)} %param.27) | copy-start | bytes 24580
  108.7 21.9 %copy-start.19 = (f32[16]{0:T(128)S(1)}, f32[16]{0:T(128)}, u32[]{:S(2)}) copy-start(f32[16]{0:T(128)} %copy-done.18) | copy-start | bytes 196
  130.6 3.6 %copy-start.22 = (f32[16]{0:T(128)}, f32[16]{0:T(128)S(1)}, u32[]{:S(2)}) copy-start(f32[16]{0:T(128)S(1)} %broadcast_multiply_fusion.1) | copy-start | bytes 196
  132.2 9.6 %collective-permute-start.11 = (bf16[16,2048]{1,0:T(8,128)(2,1)}, bf16[16,2048]{1,0:T(8,128)(2,1)}, u32[]{:S(2)}, u32[]{:S(2)}) collective-permute-start(bf16[16,2048]{1,0:T(8,128)(2,1)} %fusion.108), channel_id=1, source_target_pairs={{0,3},{1,0},{2,1},{3,2},{4,7},{5,4},{6,5},{7,6},{8,11},{9,8},{10,9... | collective-permute-start | bytes 196616 | tf_op jit(solution)/shard_map/ppermute | solution.py:322
  133.0 8.8 %collective-permute-start.10 = (bf16[16,2048]{1,0:T(8,128)(2,1)}, bf16[16,2048]{1,0:T(8,128)(2,1)}, u32[]{:S(2)}, u32[]{:S(2)}) collective-permute-start(bf16[16,2048]{1,0:T(8,128)(2,1)} %fusion.108), channel_id=1, source_target_pairs={{0,2},{1,3},{2,0},{3,1},{4,6},{5,7},{6,4},{7,5},{8,10},{9,11},{10,... | collective-permute-start | bytes 196616 | tf_op jit(solution)/shard_map/ppermute | solution.py:322
  133.2 8.6 %collective-permute-start.9 = (bf16[16,2048]{1,0:T(8,128)(2,1)}, bf16[16,2048]{1,0:T(8,128)(2,1)}, u32[]{:S(2)}, u32[]{:S(2)}) collective-permute-start(bf16[16,2048]{1,0:T(8,128)(2,1)} %fusion.108), channel_id=1, source_target_pairs={{0,1},{1,2},{2,3},{3,0},{4,5},{5,6},{6,7},{7,4},{8,9},{9,10},{10,1... | collective-permute-start | bytes 196616 | tf_op jit(solution)/shard_map/ppermute | solution.py:322
  136.4 16.8 %copy-start.11 = (bf16[64,128]{1,0:T(8,128)(2,1)S(1)}, bf16[64,128]{1,0:T(8,128)(2,1)}, u32[]{:S(2)}) copy-start(bf16[64,128]{1,0:T(8,128)(2,1)} %copy-done.10) | copy-start | bytes 49156
  136.4 30.6 %all-to-all-start.3 = ((bf16[16,176,128]{2,1,0:T(8,128)(2,1)}), bf16[16,176,128]{2,1,0:T(8,128)(2,1)}, u32[]{:S(2)}, u32[]{:S(2)}) async-start(bf16[16,176,128]{2,1,0:T(8,128)(2,1)} %copy.146), calls=%async_computation.3 | async-start | bytes 1441792 | tf_op jit(solution)/shard_map/all_to_all | solution.py:217
  168.4 12.4 %collective-permute-start.12 = (f32[64,128]{1,0:T(8,128)}, f32[64,128]{1,0:T(8,128)}, u32[]{:S(2)}, u32[]{:S(2)}) collective-permute-start(f32[64,128]{1,0:T(8,128)} %get-tuple-element.33), channel_id=1, source_target_pairs={{0,1},{1,2},{2,3},{3,0},{4,5},{5,6},{6,7},{7,4},{8,9},{9,10},{10,1... | collective-permute-start | bytes 98312 | tf_op jit(solution)/shard_map/ppermute | solution.py:204
  170.3 10.5 %collective-permute-start.14 = (f32[64,128]{1,0:T(8,128)}, f32[64,128]{1,0:T(8,128)}, u32[]{:S(2)}, u32[]{:S(2)}) collective-permute-start(f32[64,128]{1,0:T(8,128)} %get-tuple-element.34), channel_id=1, source_target_pairs={{0,3},{1,0},{2,1},{3,2},{4,7},{5,4},{6,5},{7,6},{8,11},{9,8},{10,9... | collective-permute-start | bytes 98312 | tf_op jit(solution)/shard_map/ppermute | solution.py:204
  172.3 8.5 %collective-permute-start.13 = (f32[64,128]{1,0:T(8,128)}, f32[64,128]{1,0:T(8,128)}, u32[]{:S(2)}, u32[]{:S(2)}) collective-permute-start(f32[64,128]{1,0:T(8,128)} %get-tuple-element.35), channel_id=1, source_target_pairs={{0,2},{1,3},{2,0},{3,1},{4,6},{5,7},{6,4},{7,5},{8,10},{9,11},{10,... | collective-permute-start | bytes 98312 | tf_op jit(solution)/shard_map/ppermute | solution.py:204
  176.5 21.3 %copy-start.13 = (f32[2048]{0:T(1024)S(1)}, f32[2048]{0:T(1024)}, u32[]{:S(2)}) copy-start(f32[2048]{0:T(1024)} %param.26) | copy-start | bytes 24580
  178.6 20.0 %copy-start.16 = (f32[16]{0:T(128)S(1)}, f32[16]{0:T(128)}, u32[]{:S(2)}) copy-start(f32[16]{0:T(128)} %copy-done.15) | copy-start | bytes 196
  178.6 20.0 %copy-start.20 = (f32[16]{0:T(128)S(1)}, f32[16]{0:T(128)}, u32[]{:S(2)}) copy-start(f32[16]{0:T(128)} %copy-done.18) | copy-start | bytes 196
  180.8 17.9 %copy-start.8 = (bf16[16,2048]{1,0:T(8,128)(2,1)S(1)}, bf16[16,2048]{1,0:T(8,128)(2,1)}, u32[]{:S(2)}) copy-start(bf16[16,2048]{1,0:T(8,128)(2,1)} %param.19) | copy-start | bytes 196612
  182.8 8.3 %collective-permute-start.15 = (f32[16,2048]{1,0:T(8,128)S(1)}, f32[16,2048]{1,0:T(8,128)S(1)}, u32[]{:S(2)}, u32[]{:S(2)}) collective-permute-start(f32[16,2048]{1,0:T(8,128)S(1)} %get-tuple-element.27), channel_id=1, source_target_pairs={{0,1},{1,2},{2,3},{3,0},{4,5},{5,6},{6,7},{7,4},{8,9},{9,10},{10,1... | collective-permute-start | bytes 393224 | tf_op jit(solution)/shard_map/ppermute | solution.py:204
  184.3 7.2 %collective-permute-start.17 = (f32[16,2048]{1,0:T(8,128)S(1)}, f32[16,2048]{1,0:T(8,128)S(1)}, u32[]{:S(2)}, u32[]{:S(2)}) collective-permute-start(f32[16,2048]{1,0:T(8,128)S(1)} %get-tuple-element.28), channel_id=1, source_target_pairs={{0,3},{1,0},{2,1},{3,2},{4,7},{5,4},{6,5},{7,6},{8,11},{9,8},{10,9... | collective-permute-start | bytes 393224 | tf_op jit(solution)/shard_map/ppermute | solution.py:204
  186.7 11.1 %collective-permute-start.16 = (f32[16,2048]{1,0:T(8,128)S(1)}, f32[16,2048]{1,0:T(8,128)S(1)}, u32[]{:S(2)}, u32[]{:S(2)}) collective-permute-start(f32[16,2048]{1,0:T(8,128)S(1)} %get-tuple-element.29), channel_id=1, source_target_pairs={{0,2},{1,3},{2,0},{3,1},{4,6},{5,7},{6,4},{7,5},{8,10},{9,11},{10,... | collective-permute-start | bytes 393224 | tf_op jit(solution)/shard_map/ppermute | solution.py:204
